TPU v7x, 128 devices: a whole 4x4x4 slice. The times are simulated.
128 devices in a mesh: seq: 32 (over z, x, y_lo), type: 4 (over y_hi, core).
Axes of the slice: x: 4, y: 4 (y_hi: 2, y_lo: 2; y = y_hi * 2 + y_lo), z: 4, core: 2. Of those that a mesh axis runs over, the one named last changes fastest.
Arguments:
- tokens: bfloat16 [17408, 1024], P(('seq', 'type')), may hold values from -60 to 60
- shift_scale: float32 [2, 1024], replicated, may hold values from -0.8 to 0.8
- branch_gate: float32 [1024], replicated, may hold values from 0.25 to 1.75
- final_gain: float32 [1024], replicated, may hold values from 0.5 to 1.5
- w_qkv: bfloat16 [3, 1024, 1024], P(None, None, 'type'), may hold values from -1 to 1
- w_out: bfloat16 [1024, 1024], P('type'), may hold values from -0.375 to 0.375
- type_ids: int32 [17408, 1], P(('seq', 'type')), may hold values from 0 to 7; in each aligned block of 136 rows (0 to 135, 136 to 271, ...) at most 51 rows name the same one
- head_w1: bfloat16 [8, 1024, 1024], P('type'), may hold values from -0.1875 to 0.1875
- head_b1: bfloat16 [8, 1024], P('type'), may hold values from -3 to 3
- head_w2: bfloat16 [8, 1024, 16], P('type'), may hold values from -0.1875 to 0.1875
Outputs:
- updated: bfloat16 [17408, 1024], P(('seq', 'type'))
- head_out: float32 [17408, 16], P(('seq', 'type'))
Inputs may be any that keep to these rules, and one draw needn't show every extreme that they name: `type_ids`: among the 136 tokens of one device no type occurs more than 51 times; some type occurs exactly 51 times on some devices.
All inputs are finite; a program needn't handle non-finite values.
Results may differ from a plain program's by a relative error of at most 0.014.
Values may be sent and summed in bfloat16 or wider, within the bound.
No kernel may reach another device: no remote copies, remote signals or barrier semaphores. Data moves between devices by JAX's collectives and lax.ppermute only.
A program may use at most 192 MiB of HBM per device.

v0:
```python
import jax
import jax.numpy as jnp
from jax import lax
from jax.sharding import PartitionSpec as P

HD = 64


def rms_normalize(values):
    squares = jnp.mean(values * values, axis=-1, keepdims=True)
    return values * lax.rsqrt(squares + 1e-06)


def absorb_block(state, query_heads, key_heads, value_heads):
    largest, totals, numer = state
    scores = jnp.einsum(
        "qhd,khd->hqk", query_heads, key_heads, preferred_element_type=jnp.float32
    ) * HD ** (-0.5)
    newmax = jnp.maximum(largest, jnp.max(scores, axis=-1))
    decay = jnp.exp(largest - newmax)
    weights = jnp.exp(scores - newmax[:, :, None])
    totals = totals * decay + jnp.sum(weights, axis=-1)
    update = jnp.einsum(
        "hqk,khd->qhd",
        weights.astype(jnp.bfloat16),
        value_heads,
        preferred_element_type=jnp.float32,
    )
    numer = numer * jnp.transpose(decay)[:, :, None] + update
    return (newmax, totals, numer)


def apply_heads(feature_slots, first_w, first_b, second_w):
    hidden = jnp.einsum(
        "...tcd,tdh->...tch", feature_slots, first_w, preferred_element_type=jnp.float32
    )
    hidden = jax.nn.gelu(hidden + first_b.astype(jnp.float32)[:, None, :]).astype(jnp.bfloat16)
    return jnp.einsum("...tch,tho->...tco", hidden, second_w, preferred_element_type=jnp.float32)


def body(
    tokens, shift_scale, branch_gate, final_gain, w_qkv, w_out, type_ids, head_w1, head_b1, head_w2
):
    inputs = tokens.astype(jnp.float32)
    modulated = (rms_normalize(inputs) * (1.0 + shift_scale[1]) + shift_scale[0]).astype(
        jnp.bfloat16
    )
    projected = jnp.einsum(
        "rd,ide->ire",
        lax.all_gather(modulated, "type", axis=0, tiled=True),
        w_qkv,
        preferred_element_type=jnp.float32,
    ).astype(jnp.bfloat16)
    queries = projected[0]
    local_keys = projected[1]
    local_values = projected[2]
    query_count = queries.shape[0]
    width = queries.shape[1]
    local_heads = width // HD
    query_heads = queries.reshape(query_count, local_heads, HD)
    initial = (
        jnp.full((local_heads, query_count), -1e30, jnp.float32),
        jnp.zeros((local_heads, query_count), jnp.float32),
        jnp.zeros((query_count, local_heads, HD), jnp.float32),
    )
    running = initial
    key_part = lax.all_gather(local_keys, "seq", axis=0, tiled=True)
    value_part = lax.all_gather(local_values, "seq", axis=0, tiled=True)
    row_total = key_part.shape[0]
    key_blocks = key_part.reshape(row_total // 512, 512, local_heads, HD)
    value_blocks = value_part.reshape(row_total // 512, 512, local_heads, HD)

    def advance(state, pair):
        return (absorb_block(state, query_heads, pair[0], pair[1]), None)

    running, unused = lax.scan(advance, running, (key_blocks, value_blocks))
    largest, totals, numer = running
    attended = (
        (numer / jnp.transpose(totals)[:, :, None]).astype(jnp.bfloat16).reshape(query_count, width)
    )
    mixed = lax.psum_scatter(
        jnp.dot(attended, w_out, preferred_element_type=jnp.float32),
        "type",
        scatter_dimension=0,
        tiled=True,
    )
    updated = (inputs + branch_gate * mixed).astype(jnp.bfloat16)
    final = (rms_normalize(updated.astype(jnp.float32)) * final_gain).astype(jnp.bfloat16)
    owned = head_w1.shape[0]
    owners = lax.axis_size("type")
    kinds_all = owned * owners
    capacity = 3 * tokens.shape[0] // 8
    kinds = type_ids[:, 0]
    onehot = (kinds[:, None] == jnp.arange(kinds_all, dtype=jnp.int32)[None, :]).astype(jnp.int32)
    ranks = jnp.sum((jnp.cumsum(onehot, axis=0) - onehot) * onehot, axis=1)
    slots = kinds * capacity + ranks
    slot_ids = jnp.arange(kinds_all * capacity, dtype=jnp.int32)
    dispatch = (slot_ids[:, None] == slots[None, :]).astype(jnp.bfloat16)
    packed = jnp.dot(dispatch, final, preferred_element_type=jnp.float32).astype(jnp.bfloat16)
    packed = packed.reshape(kinds_all, capacity, final.shape[1])
    first_w, first_b, second_w = (
        lax.all_gather(head_w1, "type", axis=0, tiled=True),
        lax.all_gather(head_b1, "type", axis=0, tiled=True),
        lax.all_gather(head_w2, "type", axis=0, tiled=True),
    )
    answers = apply_heads(packed, first_w, first_b, second_w)
    answers = answers.reshape(kinds_all * capacity, head_w2.shape[2])
    gather_back = (slots[:, None] == slot_ids[None, :]).astype(jnp.float32)
    head_out = jnp.dot(
        gather_back, answers, precision=lax.Precision.HIGHEST, preferred_element_type=jnp.float32
    )
    return (updated, head_out)


def solution(mesh):
    in_specs = (
        P(("seq", "type"), None),
        P(),
        P(),
        P(),
        P(None, None, "type"),
        P("type", None),
        P(("seq", "type"), None),
        P("type", None, None),
        P("type", None),
        P("type", None, None),
    )
    out_specs = (P(("seq", "type"), None), P(("seq", "type"), None))
    return jax.shard_map(body, mesh=mesh, in_specs=in_specs, out_specs=out_specs, check_vma=False)
```

profile of v0, /device:TPU:1, one launch (start us, length us, event | category | flops | bytes accessed | tf_op | source)
XLA Modules:
  0.0 957.8 jit_solution(635125774649194052)
XLA Ops:
  11.1 24.9 %all-gather.8.cloned.1.call-done = bf16[544,1024]{1,0:T(8,128)(2,1)} async-done(((bf16[136,1024]{1,0:T(8,128)(2,1)}), bf16[544,1024]{1,0:T(8,128)(2,1)}) %all-gather.8.cloned.1.call-update) | async-done | bytes 1114128 | tf_op jit(solution)/shard_map/all_gather | solution.py:50
  40.1 196.5 %all-gather.12.cloned.1.call-done = bf16[1,17408,256]{2,1,0:T(8,128)(2,1)} async-done(((bf16[1,544,256]{2,1,0:T(8,128)(2,1)}), bf16[1,17408,256]{2,1,0:T(8,128)(2,1)}) %all-gather.12.cloned.1.call-update) | async-done | bytes 8912912 | tf_op jit(solution)/shard_map/all_gather | solution.py:67
  236.6 25.9 %reshape.77 = bf16[34,512,4,64]{3,2,1,0:T(4,128)(2,1)} reshape(bf16[1,17408,256]{2,1,0:T(8,128)(2,1)} %all-gather.12.cloned.1.call-done) | data formatting | bytes 17825792 | tf_op jit(solution)/shard_map/reshape | solution.py:70
  262.5 25.6 %copy.24 = bf16[34,512,4,64]{1,3,2,0:T(8,128)(2,1)} copy(bf16[34,512,4,64]{3,2,1,0:T(4,128)(2,1)} %reshape.77) | data formatting | bytes 17825792
  288.2 150.6 %all-gather.14.cloned.1.call-done = bf16[1,17408,256]{2,1,0:T(8,128)(2,1)} async-done(((bf16[1,544,256]{2,1,0:T(8,128)(2,1)}), bf16[1,17408,256]{2,1,0:T(8,128)(2,1)}) %all-gather.14.cloned.1.call-update) | async-done | bytes 8912912 | tf_op jit(solution)/shard_map/all_gather | solution.py:68
  438.8 25.9 %reshape.78 = bf16[34,512,4,64]{3,2,1,0:T(4,128)(2,1)} reshape(bf16[1,17408,256]{2,1,0:T(8,128)(2,1)} %all-gather.14.cloned.1.call-done) | data formatting | bytes 17825792 | tf_op jit(solution)/shard_map/reshape | solution.py:71
  464.7 25.6 %copy.25 = bf16[34,512,4,64]{1,3,2,0:T(8,128)(2,1)} copy(bf16[34,512,4,64]{3,2,1,0:T(4,128)(2,1)} %reshape.78) | data formatting | bytes 17825792
  490.3 298.6 %while.15 = (s32[]{:T(128)}, f32[4,544]{1,0:T(4,128)S(1)}, f32[4,544]{1,0:T(4,128)S(1)}, f32[544,4,64]{0,2,1:T(8,128)S(1)}, bf16[34,512,4,64]{1,3,2,0:T(8,128)(2...) while((s32[]{:T(128)}, f32[4,544]{1,0:T(4,128)S(1)}, ...), condition=%wide.region_4.5_spmd.clone, body=%wide.region_1.4_spmd.clone.sunk | while | flops 294556416 | bytes 33252484 | solution.py:76
  490.3 3.8 bitcast_reduce_fusion.2
  499.2 3.8 bitcast_reduce_fusion.2
  503.0 3.6 fusion.83
  507.9 3.8 bitcast_reduce_fusion.2
  511.7 3.6 fusion.83
  516.7 3.8 bitcast_reduce_fusion.2
  520.5 3.6 fusion.83
  525.5 3.8 bitcast_reduce_fusion.2
  534.3 3.8 bitcast_reduce_fusion.2
  543.1 3.8 bitcast_reduce_fusion.2
  546.9 3.6 fusion.83
  551.9 3.8 bitcast_reduce_fusion.2
  555.6 3.6 fusion.83
  560.6 3.8 bitcast_reduce_fusion.2
  564.4 3.6 fusion.83
  569.4 3.8 bitcast_reduce_fusion.2
  578.2 3.8 bitcast_reduce_fusion.2
  587.0 3.8 bitcast_reduce_fusion.2
  595.8 3.8 bitcast_reduce_fusion.2
  599.5 3.6 fusion.83
  604.5 3.8 bitcast_reduce_fusion.2
  608.3 3.6 fusion.83
  613.3 3.8 bitcast_reduce_fusion.2
  622.1 3.8 bitcast_reduce_fusion.2
  630.9 3.8 bitcast_reduce_fusion.2
  639.7 3.8 bitcast_reduce_fusion.2
  643.5 3.6 fusion.83
  648.4 3.8 bitcast_reduce_fusion.2
  652.2 3.6 fusion.83
  657.2 3.8 bitcast_reduce_fusion.2
  666.0 3.8 bitcast_reduce_fusion.2
  674.8 3.8 bitcast_reduce_fusion.2
  683.6 3.8 bitcast_reduce_fusion.2
  687.4 3.6 fusion.83
  692.4 3.8 bitcast_reduce_fusion.2
  696.1 3.6 fusion.83
  701.1 3.8 bitcast_reduce_fusion.2
  709.9 3.8 bitcast_reduce_fusion.2
  718.7 3.8 bitcast_reduce_fusion.2
  722.5 3.6 fusion.83
  727.5 3.8 bitcast_reduce_fusion.2
  731.3 3.6 fusion.83
  736.3 3.8 bitcast_reduce_fusion.2
  740.1 3.6 fusion.83
  745.0 3.8 bitcast_reduce_fusion.2
  753.8 3.8 bitcast_reduce_fusion.2
  762.6 3.8 bitcast_reduce_fusion.2
  771.4 3.8 bitcast_reduce_fusion.2
  775.2 3.6 fusion.83
  780.2 3.8 bitcast_reduce_fusion.2
  784.0 3.6 fusion.83
  792.4 11.0 %all-gather.2 = bf16[4,2,1024]{2,1,0:T(2,128)(2,1)S(1)} all-gather(bf16[1,2,1024]{2,1,0:T(2,128)(2,1)S(1)} %bitcast.83), channel_id=1, replica_groups=mesh['seq'=32,'type'=4] {'type'}, dimensions={0}, use_global_device_ids=true | all-gather | bytes 20480 | tf_op jit(solution)/shard_map/all_gather | solution.py:103
  803.5 7.4 all_gather.23
  811.0 20.2 %reduce-scatter.2.cloned.1.call-done = f32[136,1024]{1,0:T(8,128)} async-done(((f32[544,1024]{1,0:T(8,128)}), f32[136,1024]{1,0:T(8,128)}) %reduce-scatter.2.cloned.1.call-update) | async-done | bytes 557072 | tf_op jit(solution)/shard_map/reduce_scatter | solution.py:81
  833.3 109.4 %all-gather.10.cloned.1.call-done = bf16[8,1024,1024]{2,1,0:T(8,128)(2,1)} async-done(((bf16[2,1024,1024]{2,1,0:T(8,128)(2,1)}), bf16[8,1024,1024]{2,1,0:T(8,128)(2,1)}) %all-gather.10.cloned.1.call-update) | async-done | bytes 16777232 | tf_op jit(solution)/shard_map/all_gather | solution.py:102
  942.7 7.6 fusion.32
  (281 shorter events, 122.0 us)
Async XLA Ops:
  7.2 28.8 %copy-start = (bf16[3,1024,256]{2,1,0:T(8,128)(2,1)S(1)}, bf16[3,1024,256]{2,1,0:T(8,128)(2,1)}, u32[]{:S(2)}) copy-start(bf16[3,1024,256]{2,1,0:T(8,128)(2,1)} %param.16) | copy-start | bytes 4718596
  7.2 28.7 %all-gather.8.cloned.1.call-start = ((), (), s32[]{:S(2)}) async-start(), calls=%async_computation.1 | async-start | bytes 1392640 | tf_op jit(solution)/shard_map/all_gather | solution.py:50
  11.0 225.6 %all-gather.12.cloned.1.call-start = ((), (), s32[]{:S(2)}) async-start(), calls=%async_computation.4 | async-start | bytes 9191424 | tf_op jit(solution)/shard_map/all_gather | solution.py:67
  39.1 399.7 %all-gather.14.cloned.1.call-start = ((), (), s32[]{:S(2)}) async-start(), calls=%async_computation.5 | async-start | bytes 9191424 | tf_op jit(solution)/shard_map/all_gather | solution.py:68
  39.8 791.4 %reduce-scatter.2.cloned.1.call-start = ((), (), s32[]{:S(2)}) async-start(), calls=%async_computation.2 | async-start | bytes 2785280 | tf_op jit(solution)/shard_map/reduce_scatter | solution.py:81
  490.3 298.7 %copy-start.5 = (bf16[256,1024]{1,0:T(8,128)(2,1)S(1)}, bf16[256,1024]{1,0:T(8,128)(2,1)}, u32[]{:S(2)}) copy-start(bf16[256,1024]{1,0:T(8,128)(2,1)} %param.17) | copy-start | bytes 1572868
  494.2 3.7 copy-start.2
  502.9 3.7 copy-start.2
  511.7 3.7 copy-start.2
  520.5 3.7 copy-start.2
  529.3 3.7 copy-start.2
  538.1 3.7 copy-start.2
  546.8 3.7 copy-start.2
  555.6 3.7 copy-start.2
  564.4 3.7 copy-start.2
  573.2 3.7 copy-start.2
  582.0 3.7 copy-start.2
  590.7 3.7 copy-start.2
  599.5 3.7 copy-start.2
  608.3 3.7 copy-start.2
  617.1 3.7 copy-start.2
  625.9 3.7 copy-start.2
  634.7 3.7 copy-start.2
  643.4 3.7 copy-start.2
  652.2 3.7 copy-start.2
  661.0 3.7 copy-start.2
  669.8 3.7 copy-start.2
  678.6 3.7 copy-start.2
  687.3 3.7 copy-start.2
  696.1 3.7 copy-start.2
  704.9 3.7 copy-start.2
  713.7 3.7 copy-start.2
  722.5 3.7 copy-start.2
  731.3 3.7 copy-start.2
  740.0 3.7 copy-start.2
  748.8 3.7 copy-start.2
  757.6 3.7 copy-start.2
  766.4 3.7 copy-start.2
  775.2 3.7 copy-start.2
  783.9 3.7 copy-start.2
  789.0 2.5 copy-start.7
  789.0 3.4 copy-start.10
  789.0 14.4 %copy-start.6 = (bf16[2,1024,16]{1,2,0:T(8,128)(2,1)S(1)}, bf16[2,1024,16]{1,2,0:T(8,128)(2,1)}, u32[]{:S(2)}) copy-start(bf16[2,1024,16]{1,2,0:T(8,128)(2,1)} %param.21) | copy-start | bytes 196612
  789.1 42.2 %copy-start.3 = (bf16[136,1024]{1,0:T(8,128)(2,1)S(1)}, bf16[136,1024]{1,0:T(8,128)(2,1)}, u32[]{:S(2)}) copy-start(bf16[136,1024]{1,0:T(8,128)(2,1)} %param.12) | copy-start | bytes 835588
  789.1 42.2 %copy-start.8 = (f32[1024]{0:T(1024)S(1)}, f32[1024]{0:T(1024)}, u32[]{:S(2)}) copy-start(f32[1024]{0:T(1024)} %param.14) | copy-start | bytes 12292
  790.9 41.6 %copy-start.9 = (f32[1024]{0:T(1024)S(1)}, f32[1024]{0:T(1024)}, u32[]{:S(2)}) copy-start(f32[1024]{0:T(1024)} %param.15) | copy-start | bytes 12292
  791.0 151.7 %all-gather.10.cloned.1.call-start = ((), (), s32[]{:S(2)}) async-start(), calls=%async_computation.3 | async-start | bytes 20971520 | tf_op jit(solution)/shard_map/all_gather | solution.py:102
  832.5 117.8 %copy-start.4 = (bf16[136,1024]{1,0:T(8,128)(2,1)}, bf16[136,1024]{1,0:T(8,128)(2,1)S(1)}, u32[]{:S(2)}) copy-start(bf16[136,1024]{1,0:T(8,128)(2,1)S(1)} %get-tuple-element.104) | copy-start | bytes 835588
  942.7 8.6 copy-start.1
Sparse Core Ops, SparseCore 0:
  11.1 24.7 all-gather.7
  39.2 197.3 all-gather.11
  238.8 199.9 all-gather.13
  791.1 40.1 reduce-scatter.1
  832.8 109.7 all-gather.9
where the time goes:
time: 962 us; the launch traced here: 958 us
  waiting for transfers between devices  503 us (52%)
  matrix products  264 us (27%)
  local copies, waits for them, and re-layouts  106 us (11%)
  other arithmetic  50.4 us (5%)
  blocking collectives  18.4 us (2%)
  between operations  14 us (1%)
    all_gather x1, waiting for transfers between devices, body(): key_part = lax.all_gather(local_keys, 'seq', axis=0, tiled=True)  197 us
    all_gather x1, waiting for transfers between devices, body(): value_part = lax.all_gather(local_values, 'seq', axis=0, tiled=True)  151 us
    dot_general x34, matrix products, absorb_block(): jnp.einsum('qhd,khd->hqk', query_heads, key_heads, preferred_element_type...  128 us
    dot_general x34, matrix products, absorb_block(): jnp.einsum('hqk,khd->qhd', weights.astype(jnp.bfloat16), value_heads, pre...  123 us
    all_gather x1, waiting for transfers between devices, body(): lax.all_gather(head_w1, 'type', axis=0, tiled=True)  109 us
    unnamed x22, local copies, waits for them, and re-layouts  51.3 us
    reduce_sum x34, other arithmetic, absorb_block(): totals = totals * decay + jnp.sum(weights, axis=-1)  43.5 us
    reshape x1, local copies, waits for them, and re-layouts, body(): key_blocks = key_part.reshape(row_total // 512, 512, local_heads, HD)  25.9 us
  transfers between devices with their start and end apart: 5, of which 5 were waited for; matrix products, arithmetic and copies ran while one was open for 6% of the time, Pallas kernels for 0%

commit v1 on v0

v1 whole, which is shorter than its diff:
```python
import jax
import jax.numpy as jnp
from jax import lax
from jax.experimental import pallas as pl
from jax.experimental.pallas import tpu as pltpu
from jax.sharding import Mesh
from jax.sharding import PartitionSpec as P

HD = 64
SCALE = HD ** (-0.5)
SUB = 4
QUERY_BLOCK = 544


def rms_normalize(values):
    squares = jnp.mean(values * values, axis=-1, keepdims=True)
    return values * lax.rsqrt(squares + 1e-06)


def flash_kernel(q_ref, kv_ref, o_ref, m_ref, l_ref, acc_ref):
    step = pl.program_id(1)

    @pl.when(step == 0)
    def _():
        m_ref[...] = jnp.full(m_ref.shape, -jnp.inf, jnp.float32)
        l_ref[...] = jnp.zeros(l_ref.shape, jnp.float32)
        acc_ref[...] = jnp.zeros(acc_ref.shape, jnp.float32)

    q = q_ref[...]
    kv = kv_ref[...]
    scores = lax.dot_general(q, kv, (((1,), (1,)), ((), ())), preferred_element_type=jnp.float32)
    m_old = m_ref[...]
    m_new = jnp.maximum(m_old, jnp.max(scores, axis=1, keepdims=True))
    decay = jnp.exp((m_old - m_new) * SCALE)
    weights = jnp.exp((scores - m_new) * SCALE)
    l_ref[...] = decay * l_ref[...] + jnp.sum(weights, axis=1, keepdims=True)
    acc_ref[...] = decay * acc_ref[...] + jnp.dot(
        weights.astype(jnp.bfloat16), kv, preferred_element_type=jnp.float32
    )
    m_ref[...] = m_new

    @pl.when(step == pl.num_programs(1) - 1)
    def _():
        o_ref[...] = (acc_ref[...] / l_ref[...]).astype(o_ref.dtype)


def flash(q_pad, kv_all):
    rows, width = q_pad.shape
    chunks, chunk, _ = kv_all.shape
    block = QUERY_BLOCK
    return pl.pallas_call(
        flash_kernel,
        grid=(rows // block, chunks),
        in_specs=[
            pl.BlockSpec((block, width), lambda i, k: (i, 0)),
            pl.BlockSpec((None, chunk, width), lambda i, k: (k, 0, 0)),
        ],
        out_specs=pl.BlockSpec((block, width), lambda i, k: (i, 0)),
        out_shape=jax.ShapeDtypeStruct((rows, width), jnp.bfloat16),
        scratch_shapes=[
            pltpu.VMEM((block, 1), jnp.float32),
            pltpu.VMEM((block, 1), jnp.float32),
            pltpu.VMEM((block, width), jnp.float32),
        ],
        compiler_params=pltpu.CompilerParams(dimension_semantics=("parallel", "arbitrary")),
        cost_estimate=pl.CostEstimate(
            flops=4 * rows * chunks * chunk * width,
            transcendentals=rows * chunks * chunk,
            bytes_accessed=2 * (rows * width * 2 + (rows // block) * chunks * chunk * width),
        ),
    )(q_pad, kv_all)


def body(
    tokens, shift_scale, branch_gate, final_gain, w_qkv, w_out, type_ids, head_w1, head_b1, head_w2
):
    inputs = tokens.astype(jnp.float32)
    modulated = (rms_normalize(inputs) * (1.0 + shift_scale[1]) + shift_scale[0]).astype(
        jnp.bfloat16
    )
    gathered = lax.all_gather(modulated, "type", axis=0, tiled=True)
    dim = w_qkv.shape[1]
    local_heads = w_qkv.shape[2] // HD
    parts = w_qkv.reshape(3, dim, local_heads, HD)
    arranged = jnp.stack([parts[0], jnp.zeros_like(parts[0]), parts[1], parts[2]], axis=2)
    arranged = arranged.reshape(dim, local_heads, 4 * HD)
    projected = jnp.einsum(
        "rd,dje->jre", gathered, arranged, preferred_element_type=jnp.float32
    ).astype(jnp.bfloat16)
    mine = lax.all_to_all(projected, "sub", 0, 0, tiled=True)
    mine = mine.reshape(-1, 4 * HD)
    q_pad = mine[:, : 2 * HD]
    kv_local = mine[:, 2 * HD :]
    kv_all = lax.all_gather(kv_local, "grp", axis=0, tiled=False)
    attended = flash(q_pad, kv_all)[:, HD:]
    attended = attended.reshape(local_heads, -1, HD)
    back = lax.all_to_all(attended, "sub", 0, 0, tiled=True)
    rows = back.shape[1]
    back = jnp.transpose(back, (1, 0, 2)).reshape(rows, local_heads * HD)
    mixed = lax.psum_scatter(
        jnp.dot(back, w_out, preferred_element_type=jnp.float32),
        "type",
        scatter_dimension=0,
        tiled=True,
    )
    updated = (inputs + branch_gate * mixed).astype(jnp.bfloat16)
    final = (rms_normalize(updated.astype(jnp.float32)) * final_gain).astype(jnp.bfloat16)
    final_all = lax.all_gather(final, "type", axis=0, tiled=True)
    kinds_all = lax.all_gather(type_ids[:, 0], "type", axis=0, tiled=True)
    owned = head_w1.shape[0]
    first_kind = lax.axis_index("type") * owned
    result = jnp.zeros((final_all.shape[0], head_w2.shape[2]), jnp.float32)
    for which in range(owned):
        hidden = jnp.dot(final_all, head_w1[which], preferred_element_type=jnp.float32)
        hidden = jax.nn.gelu(hidden + head_b1[which].astype(jnp.float32)).astype(jnp.bfloat16)
        answer = jnp.dot(hidden, head_w2[which], preferred_element_type=jnp.float32)
        result = jnp.where((kinds_all == first_kind + which)[:, None], answer, result)
    head_out = lax.psum_scatter(result, "type", scatter_dimension=0, tiled=True)
    return (updated, head_out)


def solution(mesh):
    seq = mesh.shape["seq"]
    kinds = mesh.shape["type"]
    split = Mesh(mesh.devices.reshape(seq // SUB, SUB, kinds), ("grp", "sub", "type"))
    rows = P(("grp", "sub", "type"), None)
    in_specs = (
        rows,
        P(),
        P(),
        P(),
        P(None, None, "type"),
        P("type", None),
        rows,
        P("type", None, None),
        P("type", None),
        P("type", None, None),
    )
    out_specs = (rows, rows)
    return jax.shard_map(body, mesh=split, in_specs=in_specs, out_specs=out_specs, check_vma=False)
```

time: 962 us -> 342 us (0.36)
  waiting for transfers between devices: 503 us -> 150 us
  matrix products: 264 us -> 11.9 us
  Pallas kernels: 0 us -> 108 us
  local copies, waits for them, and re-layouts: 106 us -> 6.6 us
  other arithmetic: 50.4 us -> 6.07 us
  blocking collectives: 18.4 us -> 42.3 us
    all_gather x4 -> x3, waiting for transfers between devices: 481 us -> 111 us  [the longest x1 74.4 us: body(): kv_all = lax.all_gather(kv_local, 'grp', axis=0, tiled=False)]
    dot_general x73 -> x4, matrix products: 264 us -> 11.9 us  [the longest x2 7.47 us: body(): answer = jnp.dot(hidden, head_w2[which], preferred_element_type=jnp.float32)]
    pallas_call x0 -> x1, Pallas kernels: none -> 108 us  [flash(): pl.pallas_call(flash_kernel, grid=(rows // block, chunks), in_specs=[pl.B...]
    reshape x4 -> x1, local copies, waits for them, and re-layouts: 52.2 us -> 0.25 us  [body(): attended = attended.reshape(local_heads, -1, HD)]
    unnamed x22 -> x27, local copies, waits for them, and re-layouts: 51.3 us -> 2.19 us
    reduce_sum x35 -> x0, other arithmetic: 43.5 us -> none  [the longest x34 43.5 us: absorb_block(): totals = totals * decay + jnp.sum(weights, axis=-1)]
    all_to_all x0 -> x2, blocking collectives: none -> 24.1 us  [the longest x1 16.6 us: body(): mine = lax.all_to_all(projected, 'sub', 0, 0, tiled=True)]
    reduce_scatter x1, waiting for transfers between devices: 20.2 us -> 39.4 us  [body(): lax.psum_scatter(jnp.dot(back, w_out, preferred_element_type=jnp.float32)...]
  transfers between devices with their start and end apart: 5 -> 4, of which waited for: 5 -> 4; matrix products, arithmetic and copies ran while one was open for 6% -> 1% of each run, Pallas kernels for 0% -> 0%
where the time goes in v1:
time: 342 us; the launch traced here: 341 us
  waiting for transfers between devices  150 us (44%)
  Pallas kernels  108 us (32%)
  blocking collectives  42.3 us (12%)
  between operations  15.1 us (4%)
  matrix products  11.9 us (3%)
  local copies, waits for them, and re-layouts  6.6 us (2%)
  other arithmetic  6.07 us (2%)
    pallas_call x1, Pallas kernels, flash(): pl.pallas_call(flash_kernel, grid=(rows // block, chunks), in_specs=[pl.B...  108 us
    all_gather x1, waiting for transfers between devices, body(): kv_all = lax.all_gather(kv_local, 'grp', axis=0, tiled=False)  74.4 us
    reduce_scatter x1, waiting for transfers between devices, body(): lax.psum_scatter(jnp.dot(back, w_out, preferred_element_type=jnp.float32)...  39.4 us
    all_gather x1, waiting for transfers between devices, body(): gathered = lax.all_gather(modulated, 'type', axis=0, tiled=True)  22.2 us
    unnamed x2, blocking collectives  18.2 us
    all_to_all x1, blocking collectives, body(): mine = lax.all_to_all(projected, 'sub', 0, 0, tiled=True)  16.6 us
    all_gather x1, waiting for transfers between devices, body(): final_all = lax.all_gather(final, 'type', axis=0, tiled=True)  14.4 us
    all_to_all x1, blocking collectives, body(): back = lax.all_to_all(attended, 'sub', 0, 0, tiled=True)  7.49 us
  transfers between devices with their start and end apart: 4, of which 4 were waited for; matrix products, arithmetic and copies ran while one was open for 1% of the time, Pallas kernels for 0%

profile of v1, /device:TPU:1, one launch (start us, length us, event | category | flops | bytes accessed | tf_op | source)
XLA Modules:
  0.0 341.0 jit_solution(4138734210159931922)
XLA Ops:
  7.2 0.0 copy-start
  7.2 0.0 all-gather.6.cloned.1.call-start
  7.2 0.8 slice_add_fusion
  8.0 1.1 fusion.53
  9.1 1.8 fusion.56
  10.9 0.0 all-gather.6.cloned.1.call-update
  11.0 0.0 all-gather.10.cloned.1.call-start
  11.0 1.5 fusion.71
  12.5 0.2 copy.32
  12.7 0.2 copy.31
  12.9 0.2 copy.30
  13.1 0.1 pad.1.clone
  13.2 0.2 pad_maximum_fusion
  13.4 0.2 copy.24
  13.7 22.2 %all-gather.6.cloned.1.call-done = bf16[544,1024]{1,0:T(8,128)(2,1)} async-done(((bf16[136,1024]{1,0:T(8,128)(2,1)}), bf16[544,1024]{1,0:T(8,128)(2,1)}) %all-gather.6.cloned.1.call-update) | async-done | bytes 1114128 | tf_op jit(solution)/shard_map/all_gather | solution.py:81
  35.9 2.6 fusion.22
  38.5 16.6 %all_to_all.10 = bf16[4,544,256]{2,1,0:T(8,128)(2,1)S(1)} all-to-all(bf16[4,544,256]{2,1,0:T(8,128)(2,1)S(1)} %fusion.22), channel_id=1, replica_groups=mesh['grp'=8,'sub'=4,'type'=4] {'sub'}, dimensions={0} | all-to-all | bytes 2228224 | tf_op jit(solution)/shard_map/all_to_all | solution.py:90
  55.1 1.1 fusion.72
  56.3 0.0 all-gather.10.cloned.1.call-update
  56.3 0.0 reduce-scatter.3.cloned.1.call-start
  56.3 74.4 %all-gather.10.cloned.1.call-done = bf16[17408,128]{1,0:T(8,128)(2,1)} async-done(((bf16[2176,128]{1,0:T(8,128)(2,1)}), bf16[17408,128]{1,0:T(8,128)(2,1)}) %all-gather.10.cloned.1.call-update) | async-done | bytes 4456464 | tf_op jit(solution)/shard_map/all_gather | solution.py:94
  130.7 108.4 %shard_map.113 = bf16[2176,128]{1,0:T(8,128)(2,1)} custom-call(bf16[2176,128]{1,0:T(8,128)(2,1)} %get-tuple-element.8.q_ref, bf16[8,2176,128]{2,1,0:T(8,128)(2,1)} %bitcast.66), custom_call_target="tpu_custom_call" | custom-call | flops 19394461696 | bytes 18939904 | tf_op jit(solution)/shard_map/pallas_call | solution.py:51
  239.2 1.3 slice.61
  240.4 0.3 copy.26
  240.7 7.5 %all_to_all.11 = bf16[4,544,64]{1,2,0:T(8,128)(2,1)S(1)} all-to-all(bf16[4,544,64]{1,2,0:T(8,128)(2,1)S(1)} %copy.26), channel_id=1, replica_groups=mesh['grp'=8,'sub'=4,'type'=4] {'sub'}, dimensions={0} | all-to-all | bytes 557056 | tf_op jit(solution)/shard_map/all_to_all | solution.py:97
  248.2 0.0 copy-done
  248.2 0.0 copy-start.1
  248.2 0.0 copy-start.4
  248.2 1.8 fusion.74
  250.0 0.0 copy-start.5
  250.0 0.0 copy-start.6
  250.0 0.0 copy-start.7
  250.0 0.0 copy-start.3
  250.0 0.0 copy-start.9
  250.1 0.0 reduce-scatter.3.cloned.1.call-update
  250.1 0.0 all-gather.8.cloned.1.call-start
  250.1 39.4 %reduce-scatter.3.cloned.1.call-done = f32[136,1024]{1,0:T(8,128)} async-done(((f32[544,1024]{1,0:T(8,128)}), f32[136,1024]{1,0:T(8,128)}) %reduce-scatter.3.cloned.1.call-update) | async-done | bytes 557072 | tf_op jit(solution)/shard_map/reduce_scatter | solution.py:100
  289.5 0.0 copy-done.1
  289.5 0.0 copy-done.4
  289.5 1.2 fusion.50
  290.8 0.0 copy-start.2
  290.8 0.0 copy-done.5
  290.8 0.9 fusion.52
  291.6 0.0 all-gather.8.cloned.1.call-update
  291.7 0.0 copy-done.6
  291.7 0.6 fusion.73
  293.5 0.0 copy-done.7
  293.5 0.2 dynamic-update-slice
  293.7 4.6 %all-reduce = s32[544]{0:T(1024)S(1)} all-reduce(s32[544]{0:T(1024)S(1)} %dynamic-update-slice), channel_id=3, replica_groups=mesh['grp'=8,'sub'=4,'type'=4] {'type'}, use_global_device_ids=true, to_apply=%add | all-reduce | flops 544 | bytes 4352
  298.4 0.0 copy-done.3
  298.4 14.4 %all-gather.8.cloned.1.call-done = bf16[544,1024]{1,0:T(8,128)(2,1)} async-done(((bf16[136,1024]{1,0:T(8,128)(2,1)}), bf16[544,1024]{1,0:T(8,128)(2,1)}) %all-gather.8.cloned.1.call-update) | async-done | bytes 1114128 | tf_op jit(solution)/shard_map/all_gather | solution.py:108
  312.8 0.0 copy-done.9
  312.8 0.0 copy-start.8
  312.8 3.9 %fusion.44 = f32[544,16]{0,1:T(8,128)S(1)} fusion(bf16[544,1024]{1,0:T(8,128)(2,1)} %all-gather.8.cloned.1.call-done, bf16[2,1024,1024]{2,1,0:T(8,128)(2,1)} %param.17, f32[1024]{0:T(1024)S(1)} %bitcast.64, bf16[2,1024,16]{1,2,0:T(8,128)(2,1)S(1)} %copy-done.9, pred[544]{0:T(1024)(128)(4,1)S(1)} %get-tuple-element.12), kind=kOutput, calls=%fused_computation.40 | convolution fusion | flops 1164255744 | bytes 3283968 | tf_op jit(solution)/shard_map/dot_general | solution.py:116
  316.7 0.0 copy-done.2
  316.7 0.0 copy-done.8
  316.7 3.5 %fusion.47 = f32[544,16]{0,1:T(8,128)S(1)} fusion(f32[544,16]{0,1:T(8,128)S(1)} %fusion.44, bf16[544,1024]{1,0:T(8,128)(2,1)S(1)} %copy-done.8, bf16[2,1024,1024]{2,1,0:T(8,128)(2,1)} %param.17, f32[1024]{0:T(1024)S(1)} %bitcast.63, bf16[2,1024,16]{1,2,0:T(8,128)(2,1)S(1)} %copy-done.9, pred[544]{0:T(1024)(128)(4,1)S(1)} %get-tuple-element.11), kind=kOutput, calls=%fused_computation.41 | convolution fusion | flops 1164255744 | bytes 3324928 | tf_op jit(solution)/shard_map/dot_general | solution.py:116
  320.3 13.6 %all-reduce.1 = f32[544,16]{0,1:T(8,128)S(1)} all-reduce(f32[544,16]{0,1:T(8,128)S(1)} %fusion.47), channel_id=5, replica_groups=mesh['grp'=8,'sub'=4,'type'=4] {'type'}, use_global_device_ids=true, to_apply=%region_3.4.clone | all-reduce | flops 8704 | bytes 69632
  333.8 0.7 constant_dynamic-slice_fusion
  (5 shorter events, 0.0 us)
Async XLA Ops:
  7.2 241.0 %copy-start = (bf16[256,1024]{1,0:T(8,128)(2,1)S(1)}, bf16[256,1024]{1,0:T(8,128)(2,1)}, u32[]{:S(2)}) copy-start(bf16[256,1024]{1,0:T(8,128)(2,1)} %param.15) | copy-start | bytes 1572868
  7.2 28.7 %all-gather.6.cloned.1.call-start = ((), (), s32[]{:S(2)}) async-start(), calls=%async_computation.3 | async-start | bytes 1392640 | tf_op jit(solution)/shard_map/all_gather | solution.py:81
  11.0 119.8 %all-gather.10.cloned.1.call-start = ((), (), s32[]{:S(2)}) async-start(), calls=%async_computation.6 | async-start | bytes 5013504 | tf_op jit(solution)/shard_map/all_gather | solution.py:94
  56.3 233.2 %reduce-scatter.3.cloned.1.call-start = ((), (), s32[]{:S(2)}) async-start(), calls=%async_computation.4 | async-start | bytes 2785280 | tf_op jit(solution)/shard_map/reduce_scatter | solution.py:100
  248.2 41.3 %copy-start.1 = (bf16[136,1024]{1,0:T(8,128)(2,1)S(1)}, bf16[136,1024]{1,0:T(8,128)(2,1)}, u32[]{:S(2)}) copy-start(bf16[136,1024]{1,0:T(8,128)(2,1)} %param.10) | copy-start | bytes 835588
  248.2 41.3 %copy-start.4 = (f32[1024]{0:T(1024)S(1)}, f32[1024]{0:T(1024)}, u32[]{:S(2)}) copy-start(f32[1024]{0:T(1024)} %param.12) | copy-start | bytes 12292
  250.0 40.7 %copy-start.5 = (f32[1024]{0:T(1024)S(1)}, f32[1024]{0:T(1024)}, u32[]{:S(2)}) copy-start(f32[1024]{0:T(1024)} %param.13) | copy-start | bytes 12292
  250.0 41.6 %copy-start.6 = (u32[128]{0:T(128)S(1)}, u32[128]{0:T(128)}, u32[]{:S(2)}) copy-start(u32[128]{0:T(128)} %constant.35) | copy-start | bytes 1540
  250.0 43.4 %copy-start.7 = (s32[136,1]{0,1:T(1,128)S(1)}, s32[136,1]{0,1:T(1,128)}, u32[]{:S(2)}) copy-start(s32[136,1]{0,1:T(1,128)} %param.16) | copy-start | bytes 1636
  250.0 48.3 %copy-start.3 = (bf16[2,1024]{1,0:T(2,128)(2,1)S(1)}, bf16[2,1024]{1,0:T(2,128)(2,1)}, u32[]{:S(2)}) copy-start(bf16[2,1024]{1,0:T(2,128)(2,1)} %param.18) | copy-start | bytes 12292
  250.0 62.7 %copy-start.9 = (bf16[2,1024,16]{1,2,0:T(8,128)(2,1)S(1)}, bf16[2,1024,16]{1,2,0:T(8,128)(2,1)}, u32[]{:S(2)}) copy-start(bf16[2,1024,16]{1,2,0:T(8,128)(2,1)} %param.19) | copy-start | bytes 196612
  250.1 62.7 %all-gather.8.cloned.1.call-start = ((), (), s32[]{:S(2)}) async-start(), calls=%async_computation.5 | async-start | bytes 1392640 | tf_op jit(solution)/shard_map/all_gather | solution.py:108
  290.8 26.0 %copy-start.2 = (bf16[136,1024]{1,0:T(8,128)(2,1)}, bf16[136,1024]{1,0:T(8,128)(2,1)S(1)}, u32[]{:S(2)}) copy-start(bf16[136,1024]{1,0:T(8,128)(2,1)S(1)} %get-tuple-element.3) | copy-start | bytes 835588
  312.8 4.0 %copy-start.8 = (bf16[544,1024]{1,0:T(8,128)(2,1)S(1)}, bf16[544,1024]{1,0:T(8,128)(2,1)}, u32[]{:S(2)}) copy-start(bf16[544,1024]{1,0:T(8,128)(2,1)} %all-gather.8.cloned.1.call-done) | copy-start | bytes 3342340
Sparse Core Ops, SparseCore 0:
  11.1 24.7 all-gather.5
  56.4 74.2 all-gather.9
  250.2 39.2 reduce-scatter.2
  291.8 20.9 all-gather.7

commit v2 on v1

v2 whole, which is shorter than its diff:
```python
import functools

import jax
import jax.numpy as jnp
from jax import lax
from jax.experimental import pallas as pl
from jax.experimental.pallas import tpu as pltpu
from jax.sharding import Mesh
from jax.sharding import PartitionSpec as P

HD = 64
SCALE = HD ** (-0.5)
QUERY_BLOCK = 544
KEY_BLOCK = 544
RING = ("z", "y")


def rms_normalize(values):
    squares = jnp.mean(values * values, axis=-1, keepdims=True)
    return values * lax.rsqrt(squares + 1e-06)


def step_kernel(first, last, *refs):
    if first:
        q_ref, kv_ref = refs[:2]
        rest = refs[2:]
    else:
        q_ref, kv_ref, m_in, l_in, acc_in = refs[:5]
        rest = refs[5:]
    m_s, l_s, acc_s = rest[-3:]
    outs = rest[:-3]
    if first:
        m_s[...] = jnp.full(m_s.shape, -jnp.inf, jnp.float32)
        l_s[...] = jnp.zeros(l_s.shape, jnp.float32)
        acc_s[...] = jnp.zeros(acc_s.shape, jnp.float32)
    else:
        m_s[...] = m_in[...]
        l_s[...] = l_in[...]
        acc_s[...] = acc_in[...]
    q = q_ref[...]

    def absorb(c, carry):
        start = pl.multiple_of(c * KEY_BLOCK, KEY_BLOCK)
        kv = kv_ref[pl.ds(start, KEY_BLOCK), :]
        scores = lax.dot_general(
            q, kv, (((1,), (1,)), ((), ())), preferred_element_type=jnp.float32
        )
        m_old = m_s[...]
        m_new = jnp.maximum(m_old, jnp.max(scores, axis=1, keepdims=True))
        decay = jnp.exp((m_old - m_new) * SCALE)
        weights = jnp.exp((scores - m_new) * SCALE)
        l_s[...] = decay * l_s[...] + jnp.sum(weights, axis=1, keepdims=True)
        acc_s[...] = decay * acc_s[...] + jnp.dot(
            weights.astype(jnp.bfloat16), kv, preferred_element_type=jnp.float32
        )
        m_s[...] = m_new
        return carry

    lax.fori_loop(0, kv_ref.shape[0] // KEY_BLOCK, absorb, 0)
    if last:
        outs[0][...] = (acc_s[...] / l_s[...]).astype(outs[0].dtype)
    else:
        outs[0][...] = m_s[...]
        outs[1][...] = l_s[...]
        outs[2][...] = acc_s[...]


def flash_step(q_pad, kv, state, first, last):
    rows, width = q_pad.shape
    chunk = kv.shape[0]
    block = QUERY_BLOCK
    row_block = pl.BlockSpec((block, width), lambda i: (i, 0))
    stat_block = pl.BlockSpec((block, 1), lambda i: (i, 0))
    in_specs = [row_block, pl.BlockSpec((chunk, width), lambda i: (0, 0))]
    operands = [q_pad, kv]
    if not first:
        in_specs += [stat_block, stat_block, row_block]
        operands += list(state)
    if last:
        out_specs = row_block
        out_shape = jax.ShapeDtypeStruct((rows, width), jnp.bfloat16)
    else:
        out_specs = [stat_block, stat_block, row_block]
        out_shape = [
            jax.ShapeDtypeStruct((rows, 1), jnp.float32),
            jax.ShapeDtypeStruct((rows, 1), jnp.float32),
            jax.ShapeDtypeStruct((rows, width), jnp.float32),
        ]
    return pl.pallas_call(
        functools.partial(step_kernel, first, last),
        grid=(rows // block,),
        in_specs=in_specs,
        out_specs=out_specs,
        out_shape=out_shape,
        scratch_shapes=[
            pltpu.VMEM((block, 1), jnp.float32),
            pltpu.VMEM((block, 1), jnp.float32),
            pltpu.VMEM((block, width), jnp.float32),
        ],
        compiler_params=pltpu.CompilerParams(dimension_semantics=("arbitrary",)),
        cost_estimate=pl.CostEstimate(
            flops=4 * rows * chunk * width,
            transcendentals=rows * chunk,
            bytes_accessed=rows * width * 14 + chunk * width * 2,
        ),
    )(*operands)


def body(
    tokens, shift_scale, branch_gate, final_gain, w_qkv, w_out, type_ids, head_w1, head_b1, head_w2
):
    inputs = tokens.astype(jnp.float32)
    modulated = (rms_normalize(inputs) * (1.0 + shift_scale[1]) + shift_scale[0]).astype(
        jnp.bfloat16
    )
    gathered = lax.all_gather(modulated, "type", axis=0, tiled=True)
    dim = w_qkv.shape[1]
    local_heads = w_qkv.shape[2] // HD
    kinds = lax.axis_size("type")
    parts = w_qkv.reshape(3, dim, local_heads, HD)
    arranged = jnp.stack([parts[0], jnp.zeros_like(parts[0]), parts[1], parts[2]], axis=2)
    arranged = arranged.reshape(dim, local_heads, 4 * HD)
    projected = jnp.einsum(
        "rd,dje->jre", gathered, arranged, preferred_element_type=jnp.float32
    ).astype(jnp.bfloat16)
    mine = lax.all_to_all(projected, "x", 0, 0, tiled=True)
    mine = mine.reshape(-1, 4 * HD)
    q_pad = mine[:, : 2 * HD]
    chunk = mine[:, 2 * HD :]
    w_out_dep, chunk = lax.optimization_barrier((w_out, chunk))
    w_out_all = lax.all_gather(w_out_dep, "type", axis=0, tiled=True)
    z_n = lax.axis_size("z")
    y_n = lax.axis_size("y")
    order = [z * y_n for z in range(z_n)] + [z * y_n + 1 for z in reversed(range(z_n))]
    if y_n != 2:
        order = list(range(z_n * y_n))
    pairs = [(order[i], order[(i + 1) % len(order)]) for i in range(len(order))]
    steps = len(order)
    state = None
    for step in range(steps):
        if step < steps - 1:
            coming = lax.ppermute(chunk, RING, pairs)
        state = flash_step(q_pad, chunk, state, step == 0, step == steps - 1)
        if step < steps - 1:
            chunk, state = lax.optimization_barrier((coming, state))
    attended = state[:, HD:]
    rows = tokens.shape[0]
    attended = attended.reshape(-1, kinds, rows, HD).reshape(-1, rows, HD)
    back = lax.all_to_all(attended, ("x", "type"), 0, 0, tiled=True)
    back = back.reshape(-1, kinds, rows, HD)
    back = jnp.transpose(back, (2, 1, 0, 3)).reshape(rows, -1)
    mixed = jnp.dot(back, w_out_all, preferred_element_type=jnp.float32)
    updated = (inputs + branch_gate * mixed).astype(jnp.bfloat16)
    final = (rms_normalize(updated.astype(jnp.float32)) * final_gain).astype(jnp.bfloat16)
    final_all = lax.all_gather(final, "type", axis=0, tiled=True)
    kinds_all = lax.all_gather(type_ids[:, 0], "type", axis=0, tiled=True)
    owned = head_w1.shape[0]
    first_kind = lax.axis_index("type") * owned
    result = jnp.zeros((final_all.shape[0], head_w2.shape[2]), jnp.float32)
    for which in range(owned):
        hidden = jnp.dot(final_all, head_w1[which], preferred_element_type=jnp.float32)
        hidden = jax.nn.gelu(hidden + head_b1[which].astype(jnp.float32)).astype(jnp.bfloat16)
        answer = jnp.dot(hidden, head_w2[which], preferred_element_type=jnp.float32)
        result = jnp.where((kinds_all == first_kind + which)[:, None], answer, result)
    head_out = lax.psum_scatter(result, "type", scatter_dimension=0, tiled=True)
    return (updated, head_out)


def solution(mesh):
    seq = mesh.shape["seq"]
    kinds = mesh.shape["type"]
    y_n = 2
    x_n = 4
    z_n = seq // (x_n * y_n)
    split = Mesh(mesh.devices.reshape(z_n, x_n, y_n, kinds), ("z", "x", "y", "type"))
    rows = P(("z", "x", "y", "type"), None)
    in_specs = (
        rows,
        P(),
        P(),
        P(),
        P(None, None, "type"),
        P("type", None),
        rows,
        P("type", None, None),
        P("type", None),
        P("type", None, None),
    )
    out_specs = (rows, rows)
    return jax.shard_map(body, mesh=split, in_specs=in_specs, out_specs=out_specs, check_vma=False)
```

time: 342 us -> 300 us (0.88)
  waiting for transfers between devices: 150 us -> 34.1 us
  Pallas kernels: 108 us -> 163 us
  blocking collectives: 42.3 us -> 54.3 us
  starting transfers between devices: 0.16 us -> 7.23 us
    all_gather x1, waiting for transfers between devices: 74.4 us -> 0.02 us  [body(): w_out_all = lax.all_gather(w_out_dep, 'type', axis=0, tiled=True)]
    pallas_call x1 -> x8, Pallas kernels: 108 us -> 163 us  [flash_step(): pl.pallas_call(functools.partial(step_kernel, first, last), grid=(rows //...]
    reduce_scatter x1 -> x0, waiting for transfers between devices: 39.4 us -> none  [body(): lax.psum_scatter(jnp.dot(back, w_out, preferred_element_type=jnp.float32)...]
    all_to_all x2, blocking collectives: 24.1 us -> 36.1 us  [the longest x1 19 us: body(): mine = lax.all_to_all(projected, 'x', 0, 0, tiled=True)]
    ppermute x0 -> x7, starting transfers between devices: none -> 7.11 us  [body(): coming = lax.ppermute(chunk, RING, pairs)]
  transfers between devices with their start and end apart: 4 -> 10, of which waited for: 4 -> 2; matrix products, arithmetic and copies ran while one was open for 1% -> 2% of each run, Pallas kernels for 0% -> 54%
where the time goes in v2:
time: 300 us; the launch traced here: 299 us
  Pallas kernels  163 us (54%)
  blocking collectives  54.3 us (18%)
  waiting for transfers between devices  34.1 us (11%)
  between operations  15.3 us (5%)
  matrix products  12.3 us (4%)
  local copies, waits for them, and re-layouts  8.23 us (3%)
  starting transfers between devices  7.23 us (2%)
  other arithmetic  4.81 us (2%)
    pallas_call x8, Pallas kernels, flash_step(): pl.pallas_call(functools.partial(step_kernel, first, last), grid=(rows //...  163 us
    all_gather x1, waiting for transfers between devices, body(): gathered = lax.all_gather(modulated, 'type', axis=0, tiled=True)  22.2 us
    all_to_all x1, blocking collectives, body(): mine = lax.all_to_all(projected, 'x', 0, 0, tiled=True)  19 us
    unnamed x2, blocking collectives  18.2 us
    all_to_all x1, blocking collectives, body(): back = lax.all_to_all(attended, ('x', 'type'), 0, 0, tiled=True)  17.1 us
    all_gather x1, waiting for transfers between devices, body(): final_all = lax.all_gather(final, 'type', axis=0, tiled=True)  11.8 us
    dot_general x2, matrix products, body(): answer = jnp.dot(hidden, head_w2[which], preferred_element_type=jnp.float32)  7.44 us
    ppermute x7, starting transfers between devices, body(): coming = lax.ppermute(chunk, RING, pairs)  7.11 us
  transfers between devices with their start and end apart: 10, of which 2 were waited for; matrix products, arithmetic and copies ran while one was open for 2% of the time, Pallas kernels for 54%

profile of v2, /device:TPU:1, one launch (start us, length us, event | category | flops | bytes accessed | tf_op | source)
XLA Modules:
  0.0 299.4 jit_solution(14627027730974767183)
XLA Ops:
  7.2 0.0 all-gather.5.cloned.1.call-start
  7.2 0.8 slice_add_fusion
  8.0 1.1 fusion.55
  9.1 1.8 fusion.58
  10.9 0.0 all-gather.5.cloned.1.call-update
  10.9 0.0 all-gather.7.cloned.1.call-start
  11.0 1.5 fusion.71
  12.5 0.2 copy.37
  12.7 0.2 copy.38
  12.9 0.2 copy.39
  13.1 0.1 pad.1.clone
  13.2 0.2 pad_maximum_fusion
  13.4 0.2 copy.30
  13.6 22.2 %all-gather.5.cloned.1.call-done = bf16[544,1024]{1,0:T(8,128)(2,1)} async-done(((bf16[136,1024]{1,0:T(8,128)(2,1)}), bf16[544,1024]{1,0:T(8,128)(2,1)}) %all-gather.5.cloned.1.call-update) | async-done | bytes 1114128 | tf_op jit(solution)/shard_map/all_gather | solution.py:116
  35.9 2.6 fusion.22
  38.5 19.0 %all_to_all.10 = bf16[4,544,256]{2,1,0:T(8,128)(2,1)S(1)} all-to-all(bf16[4,544,256]{2,1,0:T(8,128)(2,1)S(1)} %fusion.22), channel_id=1, replica_groups=mesh['z'=4,'x'=4,'y'=2,'type'=4] {'x'}, dimensions={0} | all-to-all | bytes 2228224 | tf_op jit(solution)/shard_map/all_to_all | solution.py:126
  57.5 0.9 fusion.72
  58.4 1.3 collective-permute-start
  59.6 20.0 %shard_map.113 = (f32[2176,1]{1,0:T(8,128)}, f32[2176,1]{1,0:T(8,128)}, f32[2176,128]{1,0:T(8,128)}) custom-call(bf16[2176,128]{1,0:T(8,128)(2,1)} %get-tuple-element.108.refs_0_, bf16[2176,128]{1,0:T(8,128)(2,1)} %copy-done.2), custom_call_target="tpu_custom_call" | custom-call | flops 2424307712 | bytes 4456448 | tf_op jit(solution)/shard_map/pallas_call | solution.py:89
  79.6 0.0 collective-permute-done.refs_1_
  79.6 1.3 collective-permute-start.1
  81.0 20.4 %shard_map.114 = (f32[2176,1]{1,0:T(8,128)}, f32[2176,1]{1,0:T(8,128)}, f32[2176,128]{1,0:T(8,128)}) custom-call(bf16[2176,128]{1,0:T(8,128)(2,1)} %get-tuple-element.108.refs_0_, bf16[2176,128]{1,0:T(8,128)(2,1)} %copy-done.14, f32[2176,1]{1,0:T(8,128)} %get-tuple-element.58.refs_2_, f32[2176,1]{1,0:T(8,128)} %get-tuple-element.59.refs_3_, ...), custom_call_target="tpu_custom_call" | custom-call | flops 2424307712 | bytes 4456448 | tf_op jit(solution)/shard_map/pallas_call | solution.py:89
  101.4 0.0 collective-permute-done.1.refs_1_
  101.4 1.0 collective-permute-start.2
  102.4 0.0 all-gather.7.cloned.1.call-update
  102.5 0.0 all-gather.9.cloned.1.call-start
  102.5 20.5 %shard_map.115 = (f32[2176,1]{1,0:T(8,128)}, f32[2176,1]{1,0:T(8,128)}, f32[2176,128]{1,0:T(8,128)}) custom-call(bf16[2176,128]{1,0:T(8,128)(2,1)} %get-tuple-element.108.refs_0_, bf16[2176,128]{1,0:T(8,128)(2,1)} %copy-done.9, f32[2176,1]{1,0:T(8,128)} %get-tuple-element.65.refs_2_, f32[2176,1]{1,0:T(8,128)} %get-tuple-element.66.refs_3_, ...), custom_call_target="tpu_custom_call" | custom-call | flops 2424307712 | bytes 4456448 | tf_op jit(solution)/shard_map/pallas_call | solution.py:89
  123.0 0.9 collective-permute-start.3
  123.9 20.4 %shard_map.116 = (f32[2176,1]{1,0:T(8,128)}, f32[2176,1]{1,0:T(8,128)}, f32[2176,128]{1,0:T(8,128)}) custom-call(bf16[2176,128]{1,0:T(8,128)(2,1)} %get-tuple-element.108.refs_0_, bf16[2176,128]{1,0:T(8,128)(2,1)} %copy-done.10, f32[2176,1]{1,0:T(8,128)} %get-tuple-element.72.refs_2_, f32[2176,1]{1,0:T(8,128)} %get-tuple-element.73.refs_3_, ...), custom_call_target="tpu_custom_call" | custom-call | flops 2424307712 | bytes 4456448 | tf_op jit(solution)/shard_map/pallas_call | solution.py:89
  144.3 0.8 collective-permute-start.4
  145.1 20.5 %shard_map.117 = (f32[2176,1]{1,0:T(8,128)}, f32[2176,1]{1,0:T(8,128)}, f32[2176,128]{1,0:T(8,128)}) custom-call(bf16[2176,128]{1,0:T(8,128)(2,1)} %get-tuple-element.108.refs_0_, bf16[2176,128]{1,0:T(8,128)(2,1)} %copy-done.11, f32[2176,1]{1,0:T(8,128)} %get-tuple-element.79.refs_2_, f32[2176,1]{1,0:T(8,128)} %get-tuple-element.80.refs_3_, ...), custom_call_target="tpu_custom_call" | custom-call | flops 2424307712 | bytes 4456448 | tf_op jit(solution)/shard_map/pallas_call | solution.py:89
  165.6 1.0 collective-permute-start.5
  166.6 20.4 %shard_map.118 = (f32[2176,1]{1,0:T(8,128)}, f32[2176,1]{1,0:T(8,128)}, f32[2176,128]{1,0:T(8,128)}) custom-call(bf16[2176,128]{1,0:T(8,128)(2,1)} %get-tuple-element.108.refs_0_, bf16[2176,128]{1,0:T(8,128)(2,1)} %copy-done.12, f32[2176,1]{1,0:T(8,128)} %get-tuple-element.86.refs_2_, f32[2176,1]{1,0:T(8,128)} %get-tuple-element.87.refs_3_, ...), custom_call_target="tpu_custom_call" | custom-call | flops 2424307712 | bytes 4456448 | tf_op jit(solution)/shard_map/pallas_call | solution.py:89
  187.0 0.8 collective-permute-start.6
  187.7 0.0 copy-done.13
  187.8 20.4 %shard_map.119 = (f32[2176,1]{1,0:T(8,128)}, f32[2176,1]{1,0:T(8,128)}, f32[2176,128]{1,0:T(8,128)}) custom-call(bf16[2176,128]{1,0:T(8,128)(2,1)} %get-tuple-element.108.refs_0_, bf16[2176,128]{1,0:T(8,128)(2,1)} %copy-done.13, f32[2176,1]{1,0:T(8,128)} %get-tuple-element.93.refs_2_, f32[2176,1]{1,0:T(8,128)} %get-tuple-element.94.refs_3_, ...), custom_call_target="tpu_custom_call" | custom-call | flops 2424307712 | bytes 4456448 | tf_op jit(solution)/shard_map/pallas_call | solution.py:89
  208.2 0.8 copy-done.15
  209.0 20.6 %shard_map.120 = bf16[2176,128]{1,0:T(8,128)(2,1)} custom-call(bf16[2176,128]{1,0:T(8,128)(2,1)} %get-tuple-element.108.refs_0_, bf16[2176,128]{1,0:T(8,128)(2,1)} %copy-done.15, f32[2176,1]{1,0:T(8,128)} %get-tuple-element.100.refs_2_, f32[2176,1]{1,0:T(8,128)} %get-tuple-element.101.refs_3_, f32[2176,128]{1,0:T(8,128)} %get-tuple-element.102.refs_4_), custom_call_target="tpu_custom_call" | custom-call | flops 2424307712 | bytes 4456448 | tf_op jit(solution)/shard_map/pallas_call | solution.py:89
  229.6 1.3 slice.61
  230.8 0.0 copy-start
  230.9 0.0 copy-start.4
  230.9 0.3 copy.32
  231.2 17.1 %all_to_all.11 = bf16[16,136,64]{1,2,0:T(8,128)(2,1)S(1)} all-to-all(bf16[16,136,64]{1,2,0:T(8,128)(2,1)S(1)} %copy.32), channel_id=1, replica_groups=mesh['z'=4,'x'=4,'y'=2,'type'=4] {'x','type'}, dimensions={0} | all-to-all | bytes 557056 | tf_op jit(solution)/shard_map/all_to_all | solution.py:149
  248.3 0.6 copy.33
  248.9 0.0 copy-start.5
  248.9 0.4 reshape.46
  249.3 0.0 copy-start.6
  249.3 0.0 copy-start.7
  249.3 0.0 copy-start.3
  249.3 0.0 copy-start.16
  249.3 0.0 all-gather.7.cloned.1.call-done
  249.4 2.2 fusion.52
  251.6 0.0 copy-start.1
  251.6 0.8 fusion.54
  252.5 0.0 all-gather.9.cloned.1.call-update
  252.5 0.7 fusion.73
  254.5 0.2 dynamic-update-slice
  254.7 4.6 %all-reduce = s32[544]{0:T(1024)S(1)} all-reduce(s32[544]{0:T(1024)S(1)} %dynamic-update-slice), channel_id=2, replica_groups=mesh['z'=4,'x'=4,'y'=2,'type'=4] {'type'}, use_global_device_ids=true, to_apply=%add | all-reduce | flops 544 | bytes 4352
  259.4 11.8 %all-gather.9.cloned.1.call-done = bf16[544,1024]{1,0:T(8,128)(2,1)} async-done(((bf16[136,1024]{1,0:T(8,128)(2,1)}), bf16[544,1024]{1,0:T(8,128)(2,1)}) %all-gather.9.cloned.1.call-update) | async-done | bytes 1114128 | tf_op jit(solution)/shard_map/all_gather | solution.py:155
  271.2 3.9 %fusion.46 = f32[544,16]{0,1:T(8,128)S(1)} fusion(bf16[544,1024]{1,0:T(8,128)(2,1)} %all-gather.9.cloned.1.call-done, bf16[2,1024,1024]{2,1,0:T(8,128)(2,1)} %param.17, f32[1024]{0:T(1024)S(1)} %bitcast.63, bf16[2,1024,16]{1,2,0:T(8,128)(2,1)S(1)} %copy-done.16, pred[544]{0:T(1024)(128)(4,1)S(1)} %get-tuple-element.112), kind=kOutput, calls=%fused_computation.43 | convolution fusion | flops 1164255744 | bytes 3283968 | tf_op jit(solution)/shard_map/dot_general | solution.py:163
  275.1 0.0 copy-done.8
  275.1 3.5 %fusion.49 = f32[544,16]{0,1:T(8,128)S(1)} fusion(f32[544,16]{0,1:T(8,128)S(1)} %fusion.46, bf16[544,1024]{1,0:T(8,128)(2,1)S(1)} %copy-done.8, bf16[2,1024,1024]{2,1,0:T(8,128)(2,1)} %param.17, f32[1024]{0:T(1024)S(1)} %bitcast.62, bf16[2,1024,16]{1,2,0:T(8,128)(2,1)S(1)} %copy-done.16, pred[544]{0:T(1024)(128)(4,1)S(1)} %get-tuple-element.111), kind=kOutput, calls=%fused_computation.44 | convolution fusion | flops 1164255744 | bytes 3324928 | tf_op jit(solution)/shard_map/dot_general | solution.py:163
  278.6 13.6 %all-reduce.1 = f32[544,16]{0,1:T(8,128)S(1)} all-reduce(f32[544,16]{0,1:T(8,128)S(1)} %fusion.49), channel_id=3, replica_groups=mesh['z'=4,'x'=4,'y'=2,'type'=4] {'type'}, use_global_device_ids=true, to_apply=%region_2.3.clone | all-reduce | flops 8704 | bytes 69632
  292.2 0.7 constant_dynamic-slice_fusion
  (33 shorter events, 0.1 us)
Async XLA Ops:
  7.2 28.7 %all-gather.5.cloned.1.call-start = ((), (), s32[]{:S(2)}) async-start(), calls=%async_computation.2 | async-start | bytes 1392640 | tf_op jit(solution)/shard_map/all_gather | solution.py:116
  10.9 238.4 %all-gather.7.cloned.1.call-start = ((), (), s32[]{:S(2)}) async-start(), calls=%async_computation.3 | async-start | bytes 2621440 | tf_op jit(solution)/shard_map/all_gather | solution.py:131
  58.4 1.3 copy-start.2
  58.4 21.3 %collective-permute-start = (bf16[2176,128]{1,0:T(8,128)(2,1)S(1)}, bf16[2176,128]{1,0:T(8,128)(2,1)S(1)}, u32[]{:S(2)}, u32[]{:S(2)}) collective-permute-start(bf16[2176,128]{1,0:T(8,128)(2,1)S(1)} %get-tuple-element.53.refs_1_), channel_id=1, source_target_pairs={{0,32},{32,64},{64,96},{96,100},{100,68},{68,36},{36,4},{4,0},{1,3... | collective-permute-start | bytes 1671176 | tf_op jit(solution)/shard_map/ppermute | solution.py:142
  79.6 1.4 copy-start.14
  79.6 21.7 %collective-permute-start.1 = (bf16[2176,128]{1,0:T(8,128)(2,1)S(1)}, bf16[2176,128]{1,0:T(8,128)(2,1)S(1)}, u32[]{:S(2)}, u32[]{:S(2)}) collective-permute-start(bf16[2176,128]{1,0:T(8,128)(2,1)S(1)} %collective-permute-done.refs_1_), channel_id=1, source_target_pairs={{0,32},{32,64},{64,96},{96,100},{100,68},{68,36},{36,4},{4,0},{1,3... | collective-permute-start | bytes 1671176 | tf_op jit(solution)/shard_map/ppermute | solution.py:142
  101.4 1.1 copy-start.9
  101.4 21.6 %collective-permute-start.2 = (bf16[2176,128]{1,0:T(8,128)(2,1)S(1)}, bf16[2176,128]{1,0:T(8,128)(2,1)S(1)}, u32[]{:S(2)}, u32[]{:S(2)}) collective-permute-start(bf16[2176,128]{1,0:T(8,128)(2,1)S(1)} %collective-permute-done.1.refs_1_), channel_id=1, source_target_pairs={{0,32},{32,64},{64,96},{96,100},{100,68},{68,36},{36,4},{4,0},{1,3... | collective-permute-start | bytes 1671176 | tf_op jit(solution)/shard_map/ppermute | solution.py:142
  102.5 168.7 %all-gather.9.cloned.1.call-start = ((), (), s32[]{:S(2)}) async-start(), calls=%async_computation.4 | async-start | bytes 1392640 | tf_op jit(solution)/shard_map/all_gather | solution.py:155
  123.0 0.9 copy-start.10
  123.0 21.3 %collective-permute-start.3 = (bf16[2176,128]{1,0:T(8,128)(2,1)S(1)}, bf16[2176,128]{1,0:T(8,128)(2,1)S(1)}, u32[]{:S(2)}, u32[]{:S(2)}) collective-permute-start(bf16[2176,128]{1,0:T(8,128)(2,1)S(1)} %collective-permute-done.2.refs_1_), channel_id=1, source_target_pairs={{0,32},{32,64},{64,96},{96,100},{100,68},{68,36},{36,4},{4,0},{1,3... | collective-permute-start | bytes 1671176 | tf_op jit(solution)/shard_map/ppermute | solution.py:142
  144.3 0.8 copy-start.11
  144.3 21.3 %collective-permute-start.4 = (bf16[2176,128]{1,0:T(8,128)(2,1)S(1)}, bf16[2176,128]{1,0:T(8,128)(2,1)S(1)}, u32[]{:S(2)}, u32[]{:S(2)}) collective-permute-start(bf16[2176,128]{1,0:T(8,128)(2,1)S(1)} %collective-permute-done.3.refs_1_), channel_id=1, source_target_pairs={{0,32},{32,64},{64,96},{96,100},{100,68},{68,36},{36,4},{4,0},{1,3... | collective-permute-start | bytes 1671176 | tf_op jit(solution)/shard_map/ppermute | solution.py:142
  165.6 1.0 copy-start.12
  165.6 21.3 %collective-permute-start.5 = (bf16[2176,128]{1,0:T(8,128)(2,1)S(1)}, bf16[2176,128]{1,0:T(8,128)(2,1)S(1)}, u32[]{:S(2)}, u32[]{:S(2)}) collective-permute-start(bf16[2176,128]{1,0:T(8,128)(2,1)S(1)} %collective-permute-done.4.refs_1_), channel_id=1, source_target_pairs={{0,32},{32,64},{64,96},{96,100},{100,68},{68,36},{36,4},{4,0},{1,3... | collective-permute-start | bytes 1671176 | tf_op jit(solution)/shard_map/ppermute | solution.py:142
  187.0 0.8 copy-start.13
  187.0 21.2 %collective-permute-start.6 = (bf16[2176,128]{1,0:T(8,128)(2,1)S(1)}, bf16[2176,128]{1,0:T(8,128)(2,1)S(1)}, u32[]{:S(2)}, u32[]{:S(2)}) collective-permute-start(bf16[2176,128]{1,0:T(8,128)(2,1)S(1)} %collective-permute-done.5.refs_1_), channel_id=1, source_target_pairs={{0,32},{32,64},{64,96},{96,100},{100,68},{68,36},{36,4},{4,0},{1,3... | collective-permute-start | bytes 1671176 | tf_op jit(solution)/shard_map/ppermute | solution.py:142
  208.2 0.8 copy-start.15
  230.8 18.5 %copy-start = (bf16[136,1024]{1,0:T(8,128)(2,1)S(1)}, bf16[136,1024]{1,0:T(8,128)(2,1)}, u32[]{:S(2)}) copy-start(bf16[136,1024]{1,0:T(8,128)(2,1)} %param.10) | copy-start | bytes 835588
  230.9 18.5 %copy-start.4 = (f32[1024]{0:T(1024)S(1)}, f32[1024]{0:T(1024)}, u32[]{:S(2)}) copy-start(f32[1024]{0:T(1024)} %param.12) | copy-start | bytes 12292
  248.9 2.7 copy-start.5
  249.3 3.2 %copy-start.6 = (u32[128]{0:T(128)S(1)}, u32[128]{0:T(128)}, u32[]{:S(2)}) copy-start(u32[128]{0:T(128)} %constant.35) | copy-start | bytes 1540
  249.3 5.2 %copy-start.7 = (s32[136,1]{0,1:T(1,128)S(1)}, s32[136,1]{0,1:T(1,128)}, u32[]{:S(2)}) copy-start(s32[136,1]{0,1:T(1,128)} %param.16) | copy-start | bytes 1636
  249.3 10.1 %copy-start.3 = (bf16[2,1024]{1,0:T(2,128)(2,1)S(1)}, bf16[2,1024]{1,0:T(2,128)(2,1)}, u32[]{:S(2)}) copy-start(bf16[2,1024]{1,0:T(2,128)(2,1)} %param.18) | copy-start | bytes 12292
  249.3 21.9 %copy-start.16 = (bf16[2,1024,16]{1,2,0:T(8,128)(2,1)S(1)}, bf16[2,1024,16]{1,2,0:T(8,128)(2,1)}, u32[]{:S(2)}) copy-start(bf16[2,1024,16]{1,2,0:T(8,128)(2,1)} %param.19) | copy-start | bytes 196612
  251.6 23.5 %copy-start.1 = (bf16[136,1024]{1,0:T(8,128)(2,1)}, bf16[136,1024]{1,0:T(8,128)(2,1)S(1)}, u32[]{:S(2)}) copy-start(bf16[136,1024]{1,0:T(8,128)(2,1)S(1)} %get-tuple-element.118) | copy-start | bytes 835588
  271.2 3.9 %copy-start.8 = (bf16[544,1024]{1,0:T(8,128)(2,1)S(1)}, bf16[544,1024]{1,0:T(8,128)(2,1)}, u32[]{:S(2)}) copy-start(bf16[544,1024]{1,0:T(8,128)(2,1)} %all-gather.9.cloned.1.call-done) | copy-start | bytes 3342340
Sparse Core Ops, SparseCore 0:
  11.1 24.7 all-gather.4
  102.6 25.4 all-gather.6
  252.6 18.5 all-gather.8

commit v3 on v2

--- a/solution.py
+++ b/solution.py
@@ -10,8 +10,8 @@
 
 HD = 64
 SCALE = HD ** (-0.5)
-QUERY_BLOCK = 544
-KEY_BLOCK = 544
+QUERY_BLOCK = 272
+KEY_BLOCK = 2176
 RING = ("z", "y")
 
 

time: 300 us -> 257 us (0.86)
  Pallas kernels: 163 us -> 113 us
  waiting for transfers between devices: 34.1 us -> 40.7 us
    pallas_call x8, Pallas kernels: 163 us -> 113 us  [flash_step(): pl.pallas_call(functools.partial(step_kernel, first, last), grid=(rows //...]
    ppermute x7, waiting for transfers between devices: 0.02 us -> 5.71 us  [body(): coming = lax.ppermute(chunk, RING, pairs)]
  transfers between devices with their start and end apart: 10 -> 10, of which waited for: 2 -> 3; matrix products, arithmetic and copies ran while one was open for 2% -> 2% of each run, Pallas kernels for 54% -> 44%
where the time goes in v3:
time: 257 us
  Pallas kernels  113 us (44%)
  blocking collectives  54.9 us (21%)
  waiting for transfers between devices  40.7 us (16%)
  between operations  15.3 us (6%)
  matrix products  12.3 us (5%)
  local copies, waits for them, and re-layouts  10.2 us (4%)
  starting transfers between devices  5.02 us (2%)
  other arithmetic  4.81 us (2%)
    pallas_call x8, Pallas kernels, flash_step(): pl.pallas_call(functools.partial(step_kernel, first, last), grid=(rows //...  113 us
    all_gather x1, waiting for transfers between devices, body(): gathered = lax.all_gather(modulated, 'type', axis=0, tiled=True)  22.2 us
    all_to_all x1, blocking collectives, body(): mine = lax.all_to_all(projected, 'x', 0, 0, tiled=True)  19 us
    unnamed x2, blocking collectives  18.2 us
    all_to_all x1, blocking collectives, body(): back = lax.all_to_all(attended, ('x', 'type'), 0, 0, tiled=True)  17.6 us
    all_gather x1, waiting for transfers between devices, body(): final_all = lax.all_gather(final, 'type', axis=0, tiled=True)  12.7 us
    dot_general x2, matrix products, body(): answer = jnp.dot(hidden, head_w2[which], preferred_element_type=jnp.float32)  7.45 us
    ppermute x7, waiting for transfers between devices, body(): coming = lax.ppermute(chunk, RING, pairs)  5.71 us
  transfers between devices with their start and end apart: 10, of which 3 were waited for; matrix products, arithmetic and copies ran while one was open for 2% of the time, Pallas kernels for 44%

profile of v3, /device:TPU:1, one launch (start us, length us, event | category | flops | bytes accessed | tf_op | source)
XLA Modules:
  0.0 256.7 jit_solution(14490022880495093394)
XLA Ops:
  7.2 0.0 all-gather.5.cloned.1.call-start
  7.2 0.8 slice_add_fusion
  8.0 1.1 fusion.55
  9.1 1.8 fusion.58
  10.9 0.0 all-gather.5.cloned.1.call-update
  10.9 0.0 all-gather.7.cloned.1.call-start
  11.0 1.5 fusion.71
  12.5 0.2 copy.37
  12.7 0.2 copy.38
  12.9 0.2 copy.39
  13.1 0.1 pad.1.clone
  13.2 0.2 pad_maximum_fusion
  13.4 0.2 copy.30
  13.6 22.2 %all-gather.5.cloned.1.call-done = bf16[544,1024]{1,0:T(8,128)(2,1)} async-done(((bf16[136,1024]{1,0:T(8,128)(2,1)}), bf16[544,1024]{1,0:T(8,128)(2,1)}) %all-gather.5.cloned.1.call-update) | async-done | bytes 1114128 | tf_op jit(solution)/shard_map/all_gather | solution.py:116
  35.9 2.6 %fusion.22 = bf16[4,544,256]{2,1,0:T(8,128)(2,1)S(1)} fusion(bf16[1024,4,256]{0,2,1:T(8,128)(2,1)S(1)} %bitcast.55, bf16[544,1024]{1,0:T(8,128)(2,1)} %all-gather.5.cloned.1.call-done), kind=kOutput, calls=%fused_computation.26 | convolution fusion | flops 1141407744 | bytes 4325376 | tf_op jit(solution)/shard_map/rd,dje->jre/dot_general | solution.py:123
  38.5 19.0 %all_to_all.10 = bf16[4,544,256]{2,1,0:T(8,128)(2,1)S(1)} all-to-all(bf16[4,544,256]{2,1,0:T(8,128)(2,1)S(1)} %fusion.22), channel_id=1, replica_groups=mesh['z'=4,'x'=4,'y'=2,'type'=4] {'x'}, dimensions={0} | all-to-all | bytes 2228224 | tf_op jit(solution)/shard_map/all_to_all | solution.py:126
  57.5 0.9 fusion.72
  58.4 1.3 collective-permute-start
  59.6 13.8 %shard_map.113 = (f32[2176,1]{1,0:T(8,128)}, f32[2176,1]{1,0:T(8,128)}, f32[2176,128]{1,0:T(8,128)}) custom-call(bf16[2176,128]{1,0:T(8,128)(2,1)} %get-tuple-element.108.refs_0_, bf16[2176,128]{1,0:T(8,128)(2,1)} %copy-done.2), custom_call_target="tpu_custom_call" | custom-call | flops 2424307712 | bytes 4456448 | tf_op jit(solution)/shard_map/pallas_call | solution.py:89
  73.4 1.3 collective-permute-start.1
  74.8 14.3 %shard_map.114 = (f32[2176,1]{1,0:T(8,128)}, f32[2176,1]{1,0:T(8,128)}, f32[2176,128]{1,0:T(8,128)}) custom-call(bf16[2176,128]{1,0:T(8,128)(2,1)} %get-tuple-element.108.refs_0_, bf16[2176,128]{1,0:T(8,128)(2,1)} %copy-done.14, f32[2176,1]{1,0:T(8,128)} %get-tuple-element.58.refs_2_, f32[2176,1]{1,0:T(8,128)} %get-tuple-element.59.refs_3_, ...), custom_call_target="tpu_custom_call" | custom-call | flops 2424307712 | bytes 4456448 | tf_op jit(solution)/shard_map/pallas_call | solution.py:89
  89.1 1.0 collective-permute-start.2
  90.1 0.0 all-gather.7.cloned.1.call-update
  90.2 0.0 all-gather.9.cloned.1.call-start
  90.2 14.3 %shard_map.115 = (f32[2176,1]{1,0:T(8,128)}, f32[2176,1]{1,0:T(8,128)}, f32[2176,128]{1,0:T(8,128)}) custom-call(bf16[2176,128]{1,0:T(8,128)(2,1)} %get-tuple-element.108.refs_0_, bf16[2176,128]{1,0:T(8,128)(2,1)} %copy-done.9, f32[2176,1]{1,0:T(8,128)} %get-tuple-element.65.refs_2_, f32[2176,1]{1,0:T(8,128)} %get-tuple-element.66.refs_3_, ...), custom_call_target="tpu_custom_call" | custom-call | flops 2424307712 | bytes 4456448 | tf_op jit(solution)/shard_map/pallas_call | solution.py:89
  104.5 0.9 collective-permute-start.3
  105.4 14.3 %shard_map.116 = (f32[2176,1]{1,0:T(8,128)}, f32[2176,1]{1,0:T(8,128)}, f32[2176,128]{1,0:T(8,128)}) custom-call(bf16[2176,128]{1,0:T(8,128)(2,1)} %get-tuple-element.108.refs_0_, bf16[2176,128]{1,0:T(8,128)(2,1)} %copy-done.10, f32[2176,1]{1,0:T(8,128)} %get-tuple-element.72.refs_2_, f32[2176,1]{1,0:T(8,128)} %get-tuple-element.73.refs_3_, ...), custom_call_target="tpu_custom_call" | custom-call | flops 2424307712 | bytes 4456448 | tf_op jit(solution)/shard_map/pallas_call | solution.py:89
  119.7 5.7 %collective-permute-done.3.refs_1_ = bf16[2176,128]{1,0:T(8,128)(2,1)S(1)} collective-permute-done((bf16[2176,128]{1,0:T(8,128)(2,1)S(1)}, bf16[2176,128]{1,0:T(8,128)(2,1)S(1)}, u32[]{:S(2)}, u32[]{:S(2)}) %collective-permute-start.3) | collective-permute-done | bytes 557088 | tf_op jit(solution)/shard_map/ppermute | solution.py:142
  125.4 0.8 copy-done.11
  126.2 14.3 %shard_map.117 = (f32[2176,1]{1,0:T(8,128)}, f32[2176,1]{1,0:T(8,128)}, f32[2176,128]{1,0:T(8,128)}) custom-call(bf16[2176,128]{1,0:T(8,128)(2,1)} %get-tuple-element.108.refs_0_, bf16[2176,128]{1,0:T(8,128)(2,1)} %copy-done.11, f32[2176,1]{1,0:T(8,128)} %get-tuple-element.79.refs_2_, f32[2176,1]{1,0:T(8,128)} %get-tuple-element.80.refs_3_, ...), custom_call_target="tpu_custom_call" | custom-call | flops 2424307712 | bytes 4456448 | tf_op jit(solution)/shard_map/pallas_call | solution.py:89
  140.5 0.3 collective-permute-start.5
  140.8 0.5 copy-done.12
  141.3 14.3 %shard_map.118 = (f32[2176,1]{1,0:T(8,128)}, f32[2176,1]{1,0:T(8,128)}, f32[2176,128]{1,0:T(8,128)}) custom-call(bf16[2176,128]{1,0:T(8,128)(2,1)} %get-tuple-element.108.refs_0_, bf16[2176,128]{1,0:T(8,128)(2,1)} %copy-done.12, f32[2176,1]{1,0:T(8,128)} %get-tuple-element.86.refs_2_, f32[2176,1]{1,0:T(8,128)} %get-tuple-element.87.refs_3_, ...), custom_call_target="tpu_custom_call" | custom-call | flops 2424307712 | bytes 4456448 | tf_op jit(solution)/shard_map/pallas_call | solution.py:89
  155.6 0.1 collective-permute-start.6
  155.7 0.7 copy-done.13
  156.4 14.3 %shard_map.119 = (f32[2176,1]{1,0:T(8,128)}, f32[2176,1]{1,0:T(8,128)}, f32[2176,128]{1,0:T(8,128)}) custom-call(bf16[2176,128]{1,0:T(8,128)(2,1)} %get-tuple-element.108.refs_0_, bf16[2176,128]{1,0:T(8,128)(2,1)} %copy-done.13, f32[2176,1]{1,0:T(8,128)} %get-tuple-element.93.refs_2_, f32[2176,1]{1,0:T(8,128)} %get-tuple-element.94.refs_3_, ...), custom_call_target="tpu_custom_call" | custom-call | flops 2424307712 | bytes 4456448 | tf_op jit(solution)/shard_map/pallas_call | solution.py:89
  170.6 0.8 copy-done.15
  171.4 14.0 %shard_map.120 = bf16[2176,128]{1,0:T(8,128)(2,1)} custom-call(bf16[2176,128]{1,0:T(8,128)(2,1)} %get-tuple-element.108.refs_0_, bf16[2176,128]{1,0:T(8,128)(2,1)} %copy-done.15, f32[2176,1]{1,0:T(8,128)} %get-tuple-element.100.refs_2_, f32[2176,1]{1,0:T(8,128)} %get-tuple-element.101.refs_3_, f32[2176,128]{1,0:T(8,128)} %get-tuple-element.102.refs_4_), custom_call_target="tpu_custom_call" | custom-call | flops 2424307712 | bytes 4456448 | tf_op jit(solution)/shard_map/pallas_call | solution.py:89
  185.4 1.3 slice.61
  186.7 0.0 copy-start
  186.7 0.0 copy-start.4
  186.7 0.3 copy.32
  187.1 17.6 %all_to_all.11 = bf16[16,136,64]{1,2,0:T(8,128)(2,1)S(1)} all-to-all(bf16[16,136,64]{1,2,0:T(8,128)(2,1)S(1)} %copy.32), channel_id=1, replica_groups=mesh['z'=4,'x'=4,'y'=2,'type'=4] {'x','type'}, dimensions={0} | all-to-all | bytes 557056 | tf_op jit(solution)/shard_map/all_to_all | solution.py:149
  204.7 0.6 copy.33
  205.2 0.0 copy-start.5
  205.3 0.4 reshape.46
  205.6 0.0 copy-start.6
  205.6 0.0 copy-start.7
  205.6 0.0 copy-start.3
  205.7 0.0 copy-start.16
  205.7 0.0 all-gather.7.cloned.1.call-done
  205.7 2.2 fusion.52
  208.0 0.0 copy-start.1
  208.0 0.8 fusion.54
  208.8 0.0 all-gather.9.cloned.1.call-update
  208.9 0.7 fusion.73
  210.8 0.2 dynamic-update-slice
  211.1 4.6 %all-reduce = s32[544]{0:T(1024)S(1)} all-reduce(s32[544]{0:T(1024)S(1)} %dynamic-update-slice), channel_id=2, replica_groups=mesh['z'=4,'x'=4,'y'=2,'type'=4] {'type'}, use_global_device_ids=true, to_apply=%add | all-reduce | flops 544 | bytes 4352
  215.7 12.7 %all-gather.9.cloned.1.call-done = bf16[544,1024]{1,0:T(8,128)(2,1)} async-done(((bf16[136,1024]{1,0:T(8,128)(2,1)}), bf16[544,1024]{1,0:T(8,128)(2,1)}) %all-gather.9.cloned.1.call-update) | async-done | bytes 1114128 | tf_op jit(solution)/shard_map/all_gather | solution.py:155
  228.4 3.9 %fusion.46 = f32[544,16]{0,1:T(8,128)S(1)} fusion(bf16[544,1024]{1,0:T(8,128)(2,1)} %all-gather.9.cloned.1.call-done, bf16[2,1024,1024]{2,1,0:T(8,128)(2,1)} %param.17, f32[1024]{0:T(1024)S(1)} %bitcast.63, bf16[2,1024,16]{1,2,0:T(8,128)(2,1)S(1)} %copy-done.16, pred[544]{0:T(1024)(128)(4,1)S(1)} %get-tuple-element.112), kind=kOutput, calls=%fused_computation.43 | convolution fusion | flops 1164255744 | bytes 3283968 | tf_op jit(solution)/shard_map/dot_general | solution.py:163
  232.3 0.0 copy-done.8
  232.4 3.5 %fusion.49 = f32[544,16]{0,1:T(8,128)S(1)} fusion(f32[544,16]{0,1:T(8,128)S(1)} %fusion.46, bf16[544,1024]{1,0:T(8,128)(2,1)S(1)} %copy-done.8, bf16[2,1024,1024]{2,1,0:T(8,128)(2,1)} %param.17, f32[1024]{0:T(1024)S(1)} %bitcast.62, bf16[2,1024,16]{1,2,0:T(8,128)(2,1)S(1)} %copy-done.16, pred[544]{0:T(1024)(128)(4,1)S(1)} %get-tuple-element.111), kind=kOutput, calls=%fused_computation.44 | convolution fusion | flops 1164255744 | bytes 3324928 | tf_op jit(solution)/shard_map/dot_general | solution.py:163
  235.9 13.6 %all-reduce.1 = f32[544,16]{0,1:T(8,128)S(1)} all-reduce(f32[544,16]{0,1:T(8,128)S(1)} %fusion.49), channel_id=3, replica_groups=mesh['z'=4,'x'=4,'y'=2,'type'=4] {'type'}, use_global_device_ids=true, to_apply=%region_2.3.clone | all-reduce | flops 8704 | bytes 69632
  249.5 0.7 constant_dynamic-slice_fusion
  (33 shorter events, 0.1 us)
Async XLA Ops:
  7.2 28.7 %all-gather.5.cloned.1.call-start = ((), (), s32[]{:S(2)}) async-start(), calls=%async_computation.2 | async-start | bytes 1392640 | tf_op jit(solution)/shard_map/all_gather | solution.py:116
  10.9 194.7 %all-gather.7.cloned.1.call-start = ((), (), s32[]{:S(2)}) async-start(), calls=%async_computation.3 | async-start | bytes 2621440 | tf_op jit(solution)/shard_map/all_gather | solution.py:131
  58.4 1.3 copy-start.2
  58.4 15.1 %collective-permute-start = (bf16[2176,128]{1,0:T(8,128)(2,1)S(1)}, bf16[2176,128]{1,0:T(8,128)(2,1)S(1)}, u32[]{:S(2)}, u32[]{:S(2)}) collective-permute-start(bf16[2176,128]{1,0:T(8,128)(2,1)S(1)} %get-tuple-element.53.refs_1_), channel_id=1, source_target_pairs={{0,32},{32,64},{64,96},{96,100},{100,68},{68,36},{36,4},{4,0},{1,3... | collective-permute-start | bytes 1671176 | tf_op jit(solution)/shard_map/ppermute | solution.py:142
  73.4 1.4 copy-start.14
  73.4 15.6 %collective-permute-start.1 = (bf16[2176,128]{1,0:T(8,128)(2,1)S(1)}, bf16[2176,128]{1,0:T(8,128)(2,1)S(1)}, u32[]{:S(2)}, u32[]{:S(2)}) collective-permute-start(bf16[2176,128]{1,0:T(8,128)(2,1)S(1)} %collective-permute-done.refs_1_), channel_id=1, source_target_pairs={{0,32},{32,64},{64,96},{96,100},{100,68},{68,36},{36,4},{4,0},{1,3... | collective-permute-start | bytes 1671176 | tf_op jit(solution)/shard_map/ppermute | solution.py:142
  89.1 1.1 copy-start.9
  89.1 15.4 %collective-permute-start.2 = (bf16[2176,128]{1,0:T(8,128)(2,1)S(1)}, bf16[2176,128]{1,0:T(8,128)(2,1)S(1)}, u32[]{:S(2)}, u32[]{:S(2)}) collective-permute-start(bf16[2176,128]{1,0:T(8,128)(2,1)S(1)} %collective-permute-done.1.refs_1_), channel_id=1, source_target_pairs={{0,32},{32,64},{64,96},{96,100},{100,68},{68,36},{36,4},{4,0},{1,3... | collective-permute-start | bytes 1671176 | tf_op jit(solution)/shard_map/ppermute | solution.py:142
  90.2 138.2 %all-gather.9.cloned.1.call-start = ((), (), s32[]{:S(2)}) async-start(), calls=%async_computation.4 | async-start | bytes 1392640 | tf_op jit(solution)/shard_map/all_gather | solution.py:155
  104.5 0.9 copy-start.10
  104.5 20.9 %collective-permute-start.3 = (bf16[2176,128]{1,0:T(8,128)(2,1)S(1)}, bf16[2176,128]{1,0:T(8,128)(2,1)S(1)}, u32[]{:S(2)}, u32[]{:S(2)}) collective-permute-start(bf16[2176,128]{1,0:T(8,128)(2,1)S(1)} %collective-permute-done.2.refs_1_), channel_id=1, source_target_pairs={{0,32},{32,64},{64,96},{96,100},{100,68},{68,36},{36,4},{4,0},{1,3... | collective-permute-start | bytes 1671176 | tf_op jit(solution)/shard_map/ppermute | solution.py:142
  125.4 0.8 copy-start.11
  125.4 15.1 %collective-permute-start.4 = (bf16[2176,128]{1,0:T(8,128)(2,1)S(1)}, bf16[2176,128]{1,0:T(8,128)(2,1)S(1)}, u32[]{:S(2)}, u32[]{:S(2)}) collective-permute-start(bf16[2176,128]{1,0:T(8,128)(2,1)S(1)} %collective-permute-done.3.refs_1_), channel_id=1, source_target_pairs={{0,32},{32,64},{64,96},{96,100},{100,68},{68,36},{36,4},{4,0},{1,3... | collective-permute-start | bytes 1671176 | tf_op jit(solution)/shard_map/ppermute | solution.py:142
  140.5 0.8 copy-start.12
  140.5 15.1 %collective-permute-start.5 = (bf16[2176,128]{1,0:T(8,128)(2,1)S(1)}, bf16[2176,128]{1,0:T(8,128)(2,1)S(1)}, u32[]{:S(2)}, u32[]{:S(2)}) collective-permute-start(bf16[2176,128]{1,0:T(8,128)(2,1)S(1)} %collective-permute-done.4.refs_1_), channel_id=1, source_target_pairs={{0,32},{32,64},{64,96},{96,100},{100,68},{68,36},{36,4},{4,0},{1,3... | collective-permute-start | bytes 1671176 | tf_op jit(solution)/shard_map/ppermute | solution.py:142
  155.6 0.8 copy-start.13
  155.6 15.1 %collective-permute-start.6 = (bf16[2176,128]{1,0:T(8,128)(2,1)S(1)}, bf16[2176,128]{1,0:T(8,128)(2,1)S(1)}, u32[]{:S(2)}, u32[]{:S(2)}) collective-permute-start(bf16[2176,128]{1,0:T(8,128)(2,1)S(1)} %collective-permute-done.5.refs_1_), channel_id=1, source_target_pairs={{0,32},{32,64},{64,96},{96,100},{100,68},{68,36},{36,4},{4,0},{1,3... | collective-permute-start | bytes 1671176 | tf_op jit(solution)/shard_map/ppermute | solution.py:142
  170.6 0.8 copy-start.15
  186.7 19.0 %copy-start = (bf16[136,1024]{1,0:T(8,128)(2,1)S(1)}, bf16[136,1024]{1,0:T(8,128)(2,1)}, u32[]{:S(2)}) copy-start(bf16[136,1024]{1,0:T(8,128)(2,1)} %param.10) | copy-start | bytes 835588
  186.7 19.0 %copy-start.4 = (f32[1024]{0:T(1024)S(1)}, f32[1024]{0:T(1024)}, u32[]{:S(2)}) copy-start(f32[1024]{0:T(1024)} %param.12) | copy-start | bytes 12292
  205.2 2.7 %copy-start.5 = (f32[1024]{0:T(1024)S(1)}, f32[1024]{0:T(1024)}, u32[]{:S(2)}) copy-start(f32[1024]{0:T(1024)} %param.13) | copy-start | bytes 12292
  205.6 3.2 %copy-start.6 = (u32[128]{0:T(128)S(1)}, u32[128]{0:T(128)}, u32[]{:S(2)}) copy-start(u32[128]{0:T(128)} %constant.35) | copy-start | bytes 1540
  205.6 5.2 %copy-start.7 = (s32[136,1]{0,1:T(1,128)S(1)}, s32[136,1]{0,1:T(1,128)}, u32[]{:S(2)}) copy-start(s32[136,1]{0,1:T(1,128)} %param.16) | copy-start | bytes 1636
  205.6 10.1 %copy-start.3 = (bf16[2,1024]{1,0:T(2,128)(2,1)S(1)}, bf16[2,1024]{1,0:T(2,128)(2,1)}, u32[]{:S(2)}) copy-start(bf16[2,1024]{1,0:T(2,128)(2,1)} %param.18) | copy-start | bytes 12292
  205.7 22.7 %copy-start.16 = (bf16[2,1024,16]{1,2,0:T(8,128)(2,1)S(1)}, bf16[2,1024,16]{1,2,0:T(8,128)(2,1)}, u32[]{:S(2)}) copy-start(bf16[2,1024,16]{1,2,0:T(8,128)(2,1)} %param.19) | copy-start | bytes 196612
  208.0 24.4 %copy-start.1 = (bf16[136,1024]{1,0:T(8,128)(2,1)}, bf16[136,1024]{1,0:T(8,128)(2,1)S(1)}, u32[]{:S(2)}) copy-start(bf16[136,1024]{1,0:T(8,128)(2,1)S(1)} %get-tuple-element.118) | copy-start | bytes 835588
  228.4 3.9 %copy-start.8 = (bf16[544,1024]{1,0:T(8,128)(2,1)S(1)}, bf16[544,1024]{1,0:T(8,128)(2,1)}, u32[]{:S(2)}) copy-start(bf16[544,1024]{1,0:T(8,128)(2,1)} %all-gather.9.cloned.1.call-done) | copy-start | bytes 3342340
Sparse Core Ops, SparseCore 0:
  11.1 24.7 all-gather.4
  90.3 25.4 all-gather.6
  209.0 19.3 all-gather.8

commit v4 on v2

--- a/solution.py
+++ b/solution.py
@@ -11,7 +11,7 @@
 HD = 64
 SCALE = HD ** (-0.5)
 QUERY_BLOCK = 544
-KEY_BLOCK = 544
+ROW_SPLIT = 2
 RING = ("z", "y")
 
 
@@ -37,26 +37,29 @@
         m_s[...] = m_in[...]
         l_s[...] = l_in[...]
         acc_s[...] = acc_in[...]
-    q = q_ref[...]
-
-    def absorb(c, carry):
-        start = pl.multiple_of(c * KEY_BLOCK, KEY_BLOCK)
-        kv = kv_ref[pl.ds(start, KEY_BLOCK), :]
-        scores = lax.dot_general(
-            q, kv, (((1,), (1,)), ((), ())), preferred_element_type=jnp.float32
+    kv = kv_ref[...]
+    rows = q_ref.shape[0] // ROW_SPLIT
+    scores = []
+    for g in range(ROW_SPLIT):
+        scores.append(
+            lax.dot_general(
+                q_ref[g * rows : (g + 1) * rows, :],
+                kv,
+                (((1,), (1,)), ((), ())),
+                preferred_element_type=jnp.float32,
+            )
         )
-        m_old = m_s[...]
-        m_new = jnp.maximum(m_old, jnp.max(scores, axis=1, keepdims=True))
-        decay = jnp.exp((m_old - m_new) * SCALE)
-        weights = jnp.exp((scores - m_new) * SCALE)
-        l_s[...] = decay * l_s[...] + jnp.sum(weights, axis=1, keepdims=True)
-        acc_s[...] = decay * acc_s[...] + jnp.dot(
+    for g in range(ROW_SPLIT):
+        part = slice(g * rows, (g + 1) * rows)
+        m_old = m_s[part, :]
+        m_new = jnp.maximum(m_old, jnp.max(scores[g], axis=1, keepdims=True))
+        decay = jnp.exp(m_old - m_new)
+        weights = jnp.exp(scores[g] - m_new)
+        l_s[part, :] = decay * l_s[part, :] + jnp.sum(weights, axis=1, keepdims=True)
+        acc_s[part, :] = decay * acc_s[part, :] + jnp.dot(
             weights.astype(jnp.bfloat16), kv, preferred_element_type=jnp.float32
         )
-        m_s[...] = m_new
-        return carry
-
-    lax.fori_loop(0, kv_ref.shape[0] // KEY_BLOCK, absorb, 0)
+        m_s[part, :] = m_new
     if last:
         outs[0][...] = (acc_s[...] / l_s[...]).astype(outs[0].dtype)
     else:
@@ -118,7 +121,8 @@
     local_heads = w_qkv.shape[2] // HD
     kinds = lax.axis_size("type")
     parts = w_qkv.reshape(3, dim, local_heads, HD)
-    arranged = jnp.stack([parts[0], jnp.zeros_like(parts[0]), parts[1], parts[2]], axis=2)
+    scaled = (parts[0] * SCALE).astype(parts.dtype)
+    arranged = jnp.stack([scaled, jnp.zeros_like(scaled), parts[1], parts[2]], axis=2)
     arranged = arranged.reshape(dim, local_heads, 4 * HD)
     projected = jnp.einsum(
         "rd,dje->jre", gathered, arranged, preferred_element_type=jnp.float32
@@ -152,8 +156,10 @@
     mixed = jnp.dot(back, w_out_all, preferred_element_type=jnp.float32)
     updated = (inputs + branch_gate * mixed).astype(jnp.bfloat16)
     final = (rms_normalize(updated.astype(jnp.float32)) * final_gain).astype(jnp.bfloat16)
-    final_all = lax.all_gather(final, "type", axis=0, tiled=True)
-    kinds_all = lax.all_gather(type_ids[:, 0], "type", axis=0, tiled=True)
+    ids = jnp.broadcast_to(type_ids.astype(jnp.bfloat16), (rows, 128))
+    joined = lax.all_gather(jnp.concatenate([final, ids], axis=1), "type", axis=0, tiled=True)
+    final_all = joined[:, : final.shape[1]]
+    kinds_all = joined[:, final.shape[1]].astype(jnp.int32)
     owned = head_w1.shape[0]
     first_kind = lax.axis_index("type") * owned
     result = jnp.zeros((final_all.shape[0], head_w2.shape[2]), jnp.float32)

time: 300 us -> 244 us (0.81)
  Pallas kernels: 163 us -> 81.7 us
  waiting for transfers between devices: 34.1 us -> 67.8 us
  blocking collectives: 54.3 us -> 32.6 us
  starting transfers between devices: 7.23 us -> 17.5 us
    pallas_call x8, Pallas kernels: 163 us -> 81.7 us  [flash_step(): pl.pallas_call(functools.partial(step_kernel, first, last), grid=(rows //...]
    all_to_all x1 -> x0, blocking collectives: 17.1 us -> none  [body(): back = lax.all_to_all(attended, ('x', 'type'), 0, 0, tiled=True)]
    ppermute x7, waiting for transfers between devices: 0.02 us -> 15.8 us  [body(): coming = lax.ppermute(chunk, RING, pairs)]
    all_to_all x0 -> x1, starting transfers between devices: none -> 11 us  [body(): back = lax.all_to_all(attended, ('x', 'type'), 0, 0, tiled=True)]
    all_to_all x0 -> x1, waiting for transfers between devices: none -> 10.8 us  [body(): back = lax.all_to_all(attended, ('x', 'type'), 0, 0, tiled=True)]
    all_gather x1, waiting for transfers between devices: 11.8 us -> 19 us  [body(): lax.all_gather(jnp.concatenate([final, ids], axis=1), 'type', axis=0, til...]
    unnamed x2 -> x1, blocking collectives: 18.2 us -> 13.6 us
  transfers between devices with their start and end apart: 10 -> 11, of which waited for: 2 -> 8; matrix products, arithmetic and copies ran while one was open for 2% -> 3% of each run, Pallas kernels for 54% -> 34%
where the time goes in v4:
time: 244 us; the launch traced here: 243 us
  Pallas kernels  81.7 us (33%)
  waiting for transfers between devices  67.8 us (28%)
  blocking collectives  32.6 us (13%)
  starting transfers between devices  17.5 us (7%)
  between operations  14.7 us (6%)
  matrix products  12.3 us (5%)
  local copies, waits for them, and re-layouts  10.4 us (4%)
  other arithmetic  6.09 us (2%)
    pallas_call x8, Pallas kernels, flash_step(): pl.pallas_call(functools.partial(step_kernel, first, last), grid=(rows //...  81.7 us
    all_gather x1, waiting for transfers between devices, body(): gathered = lax.all_gather(modulated, 'type', axis=0, tiled=True)  22.2 us
    all_to_all x1, blocking collectives, body(): mine = lax.all_to_all(projected, 'x', 0, 0, tiled=True)  19 us
    all_gather x1, waiting for transfers between devices, body(): lax.all_gather(jnp.concatenate([final, ids], axis=1), 'type', axis=0, til...  19 us
    ppermute x7, waiting for transfers between devices, body(): coming = lax.ppermute(chunk, RING, pairs)  15.8 us
    unnamed x1, blocking collectives  13.6 us
    all_to_all x1, starting transfers between devices, body(): back = lax.all_to_all(attended, ('x', 'type'), 0, 0, tiled=True)  11 us
    all_to_all x1, waiting for transfers between devices, body(): back = lax.all_to_all(attended, ('x', 'type'), 0, 0, tiled=True)  10.8 us
  transfers between devices with their start and end apart: 11, of which 8 were waited for; matrix products, arithmetic and copies ran while one was open for 3% of the time, Pallas kernels for 34%

profile of v4, /device:TPU:1, one launch (start us, length us, event | category | flops | bytes accessed | tf_op | source)
XLA Modules:
  0.0 243.2 jit_solution(12514207564516221731)
XLA Ops:
  7.2 0.0 all-gather.4.cloned.1.call-start
  7.2 0.8 slice_add_fusion
  8.0 1.1 fusion.59
  9.1 1.8 fusion.62
  10.9 0.0 all-gather.4.cloned.1.call-update
  10.9 0.0 all-gather.6.cloned.1.call-start
  11.0 1.5 fusion.77
  12.5 0.2 copy.37
  12.7 0.2 copy.38
  12.9 0.2 copy.39
  13.1 0.1 pad.3.clone
  13.2 0.2 pad_maximum_fusion
  13.5 0.2 copy.30
  13.7 22.2 %all-gather.4.cloned.1.call-done = bf16[544,1024]{1,0:T(8,128)(2,1)} async-done(((bf16[136,1024]{1,0:T(8,128)(2,1)}), bf16[544,1024]{1,0:T(8,128)(2,1)}) %all-gather.4.cloned.1.call-update) | async-done | bytes 1114128 | tf_op jit(solution)/shard_map/all_gather | solution.py:119
  35.9 2.6 %fusion.22 = bf16[4,544,256]{2,1,0:T(8,128)(2,1)S(1)} fusion(bf16[1024,4,256]{0,2,1:T(8,128)(2,1)S(1)} %bitcast.51, bf16[544,1024]{1,0:T(8,128)(2,1)} %all-gather.4.cloned.1.call-done), kind=kOutput, calls=%fused_computation.26 | convolution fusion | flops 1141407744 | bytes 4325376 | tf_op jit(solution)/shard_map/rd,dje->jre/dot_general | solution.py:127
  38.5 19.0 %all_to_all.10 = bf16[4,544,256]{2,1,0:T(8,128)(2,1)S(1)} all-to-all(bf16[4,544,256]{2,1,0:T(8,128)(2,1)S(1)} %fusion.22), channel_id=1, replica_groups=mesh['z'=4,'x'=4,'y'=2,'type'=4] {'x'}, dimensions={0} | all-to-all | bytes 2228224 | tf_op jit(solution)/shard_map/all_to_all | solution.py:130
  57.5 0.9 fusion.78
  58.4 1.3 collective-permute-start
  59.7 10.0 %shard_map.113 = (f32[2176,1]{1,0:T(8,128)}, f32[2176,1]{1,0:T(8,128)}, f32[2176,128]{1,0:T(8,128)}) custom-call(bf16[2176,128]{1,0:T(8,128)(2,1)} %get-tuple-element.110.refs_0_, bf16[2176,128]{1,0:T(8,128)(2,1)} %copy-done.2), custom_call_target="tpu_custom_call" | custom-call | flops 2424307712 | bytes 4456448 | tf_op jit(solution)/shard_map/pallas_call | solution.py:92
  69.7 1.3 collective-permute-done.refs_1_
  71.0 1.3 collective-permute-start.1
  72.3 10.3 %shard_map.114 = (f32[2176,1]{1,0:T(8,128)}, f32[2176,1]{1,0:T(8,128)}, f32[2176,128]{1,0:T(8,128)}) custom-call(bf16[2176,128]{1,0:T(8,128)(2,1)} %get-tuple-element.110.refs_0_, bf16[2176,128]{1,0:T(8,128)(2,1)} %copy-done.12, f32[2176,1]{1,0:T(8,128)} %get-tuple-element.58.refs_2_, f32[2176,1]{1,0:T(8,128)} %get-tuple-element.59.refs_3_, ...), custom_call_target="tpu_custom_call" | custom-call | flops 2424307712 | bytes 4456448 | tf_op jit(solution)/shard_map/pallas_call | solution.py:92
  82.6 0.1 collective-permute-done.1.refs_1_
  82.7 1.3 collective-permute-start.2
  84.0 0.0 all-gather.6.cloned.1.call-update
  84.0 10.3 %shard_map.115 = (f32[2176,1]{1,0:T(8,128)}, f32[2176,1]{1,0:T(8,128)}, f32[2176,128]{1,0:T(8,128)}) custom-call(bf16[2176,128]{1,0:T(8,128)(2,1)} %get-tuple-element.110.refs_0_, bf16[2176,128]{1,0:T(8,128)(2,1)} %copy-done.7, f32[2176,1]{1,0:T(8,128)} %get-tuple-element.65.refs_2_, f32[2176,1]{1,0:T(8,128)} %get-tuple-element.66.refs_3_, ...), custom_call_target="tpu_custom_call" | custom-call | flops 2424307712 | bytes 4456448 | tf_op jit(solution)/shard_map/pallas_call | solution.py:92
  94.4 1.5 collective-permute-start.3
  95.9 10.3 %shard_map.116 = (f32[2176,1]{1,0:T(8,128)}, f32[2176,1]{1,0:T(8,128)}, f32[2176,128]{1,0:T(8,128)}) custom-call(bf16[2176,128]{1,0:T(8,128)(2,1)} %get-tuple-element.110.refs_0_, bf16[2176,128]{1,0:T(8,128)(2,1)} %copy-done.8, f32[2176,1]{1,0:T(8,128)} %get-tuple-element.72.refs_2_, f32[2176,1]{1,0:T(8,128)} %get-tuple-element.73.refs_3_, ...), custom_call_target="tpu_custom_call" | custom-call | flops 2424307712 | bytes 4456448 | tf_op jit(solution)/shard_map/pallas_call | solution.py:92
  106.2 13.0 %collective-permute-done.3.refs_1_ = bf16[2176,128]{1,0:T(8,128)(2,1)S(1)} collective-permute-done((bf16[2176,128]{1,0:T(8,128)(2,1)S(1)}, bf16[2176,128]{1,0:T(8,128)(2,1)S(1)}, u32[]{:S(2)}, u32[]{:S(2)}) %collective-permute-start.3) | collective-permute-done | bytes 557088 | tf_op jit(solution)/shard_map/ppermute | solution.py:146
  119.3 0.8 copy-done.9
  120.1 10.3 %shard_map.117 = (f32[2176,1]{1,0:T(8,128)}, f32[2176,1]{1,0:T(8,128)}, f32[2176,128]{1,0:T(8,128)}) custom-call(bf16[2176,128]{1,0:T(8,128)(2,1)} %get-tuple-element.110.refs_0_, bf16[2176,128]{1,0:T(8,128)(2,1)} %copy-done.9, f32[2176,1]{1,0:T(8,128)} %get-tuple-element.79.refs_2_, f32[2176,1]{1,0:T(8,128)} %get-tuple-element.80.refs_3_, ...), custom_call_target="tpu_custom_call" | custom-call | flops 2424307712 | bytes 4456448 | tf_op jit(solution)/shard_map/pallas_call | solution.py:92
  130.4 1.1 collective-permute-done.4.refs_1_
  131.5 0.3 collective-permute-start.5
  131.8 0.5 copy-done.10
  132.3 10.3 %shard_map.118 = (f32[2176,1]{1,0:T(8,128)}, f32[2176,1]{1,0:T(8,128)}, f32[2176,128]{1,0:T(8,128)}) custom-call(bf16[2176,128]{1,0:T(8,128)(2,1)} %get-tuple-element.110.refs_0_, bf16[2176,128]{1,0:T(8,128)(2,1)} %copy-done.10, f32[2176,1]{1,0:T(8,128)} %get-tuple-element.86.refs_2_, f32[2176,1]{1,0:T(8,128)} %get-tuple-element.87.refs_3_, ...), custom_call_target="tpu_custom_call" | custom-call | flops 2424307712 | bytes 4456448 | tf_op jit(solution)/shard_map/pallas_call | solution.py:92
  142.6 0.2 collective-permute-done.5.refs_1_
  142.8 0.6 collective-permute-start.6
  143.4 0.3 copy-done.11
  143.6 10.3 %shard_map.119 = (f32[2176,1]{1,0:T(8,128)}, f32[2176,1]{1,0:T(8,128)}, f32[2176,128]{1,0:T(8,128)}) custom-call(bf16[2176,128]{1,0:T(8,128)(2,1)} %get-tuple-element.110.refs_0_, bf16[2176,128]{1,0:T(8,128)(2,1)} %copy-done.11, f32[2176,1]{1,0:T(8,128)} %get-tuple-element.93.refs_2_, f32[2176,1]{1,0:T(8,128)} %get-tuple-element.94.refs_3_, ...), custom_call_target="tpu_custom_call" | custom-call | flops 2424307712 | bytes 4456448 | tf_op jit(solution)/shard_map/pallas_call | solution.py:92
  153.9 0.8 copy-done.13
  154.7 9.8 %shard_map.120 = bf16[2176,128]{1,0:T(8,128)(2,1)} custom-call(bf16[2176,128]{1,0:T(8,128)(2,1)} %get-tuple-element.110.refs_0_, bf16[2176,128]{1,0:T(8,128)(2,1)} %copy-done.13, f32[2176,1]{1,0:T(8,128)} %get-tuple-element.100.refs_2_, f32[2176,1]{1,0:T(8,128)} %get-tuple-element.101.refs_3_, f32[2176,128]{1,0:T(8,128)} %get-tuple-element.102.refs_4_), custom_call_target="tpu_custom_call" | custom-call | flops 2424307712 | bytes 4456448 | tf_op jit(solution)/shard_map/pallas_call | solution.py:92
  164.6 1.3 slice.69
  165.9 1.1 copy.32
  167.0 11.0 %all-to-all-start.1 = ((bf16[16,136,64]{1,2,0:T(8,128)(2,1)}), bf16[16,136,64]{1,2,0:T(8,128)(2,1)S(1)}, u32[]{:S(2)}, u32[]{:S(2)}) async-start(bf16[16,136,64]{1,2,0:T(8,128)(2,1)} %copy.32), calls=%async_computation.1 | async-start | bytes 1048576 | tf_op jit(solution)/shard_map/all_to_all | solution.py:153
  178.0 0.3 all-gather.8.cloned.1.call-start
  178.3 10.8 %all-to-all-done.1 = bf16[16,136,64]{1,2,0:T(8,128)(2,1)S(1)} async-done(((bf16[16,136,64]{1,2,0:T(8,128)(2,1)}), bf16[16,136,64]{1,2,0:T(8,128)(2,1)S(1)}, u32[]{:S(2)}, u32[]{:S(2)}) %all-to-all-start.1) | async-done | bytes 278560 | tf_op jit(solution)/shard_map/all_to_all | solution.py:153
  189.1 0.6 copy.33
  189.7 0.0 copy-start.6
  189.7 0.4 reshape.56
  190.1 0.0 copy-start.16
  190.1 0.0 all-gather.6.cloned.1.call-done
  190.2 2.2 fusion.56
  192.4 0.1 fusion.58
  192.6 0.1 broadcast_in_dim.37
  192.7 0.8 pad_maximum_fusion.1
  193.4 0.0 all-gather.8.cloned.1.call-update
  193.5 0.6 dynamic-slice
  194.7 19.0 %all-gather.8.cloned.1.call-done = bf16[544,1152]{1,0:T(8,128)(2,1)} async-done(((bf16[136,1152]{1,0:T(8,128)(2,1)}), bf16[544,1152]{1,0:T(8,128)(2,1)}) %all-gather.8.cloned.1.call-update) | async-done | bytes 1253392 | tf_op jit(solution)/shard_map/all_gather | solution.py:160
  213.7 1.2 fusion.63
  214.9 3.9 %fusion.46 = f32[544,16]{0,1:T(8,128)S(1)} fusion(bf16[2,1024,1024]{2,1,0:T(8,128)(2,1)} %param.17, f32[1024]{0:T(1024)S(1)} %bitcast.59, bf16[544,1152]{1,0:T(8,128)(2,1)} %all-gather.8.cloned.1.call-done, bf16[2,1024,16]{1,2,0:T(8,128)(2,1)S(1)} %copy-done.14, pred[544]{0:T(1024)(128)(4,1)S(1)} %get-tuple-element.105), kind=kOutput, calls=%fused_computation.43 | convolution fusion | flops 1164255744 | bytes 3283968 | tf_op jit(solution)/shard_map/dot_general | solution.py:169
  218.8 0.0 copy-done.4
  218.8 3.5 %fusion.49 = f32[544,16]{0,1:T(8,128)S(1)} fusion(f32[544,16]{0,1:T(8,128)S(1)} %fusion.46, bf16[2,1024,1024]{2,1,0:T(8,128)(2,1)} %param.17, f32[1024]{0:T(1024)S(1)} %bitcast.58, bf16[544,1152]{1,0:T(8,128)(2,1)S(1)} %copy-done.4, bf16[2,1024,16]{1,2,0:T(8,128)(2,1)S(1)} %copy-done.14, pred[544]{0:T(1024)(128)(4,1)S(1)} %get-tuple-element.104), kind=kOutput, calls=%fused_computation.44 | convolution fusion | flops 1164255744 | bytes 3324928 | tf_op jit(solution)/shard_map/dot_general | solution.py:169
  222.4 13.6 %all-reduce = f32[544,16]{0,1:T(8,128)S(1)} all-reduce(f32[544,16]{0,1:T(8,128)S(1)} %fusion.49), channel_id=2, replica_groups=mesh['z'=4,'x'=4,'y'=2,'type'=4] {'type'}, use_global_device_ids=true, to_apply=%region_2.3.clone | all-reduce | flops 8704 | bytes 69632
  235.9 0.7 constant_dynamic-slice_fusion
  (35 shorter events, 0.2 us)
Async XLA Ops:
  7.2 28.7 %all-gather.4.cloned.1.call-start = ((), (), s32[]{:S(2)}) async-start(), calls=%async_computation.2 | async-start | bytes 1392640 | tf_op jit(solution)/shard_map/all_gather | solution.py:119
  10.9 179.2 %all-gather.6.cloned.1.call-start = ((), (), s32[]{:S(2)}) async-start(), calls=%async_computation.3 | async-start | bytes 2621440 | tf_op jit(solution)/shard_map/all_gather | solution.py:135
  58.4 1.3 copy-start.2
  58.4 12.6 %collective-permute-start = (bf16[2176,128]{1,0:T(8,128)(2,1)S(1)}, bf16[2176,128]{1,0:T(8,128)(2,1)S(1)}, u32[]{:S(2)}, u32[]{:S(2)}) collective-permute-start(bf16[2176,128]{1,0:T(8,128)(2,1)S(1)} %get-tuple-element.53.refs_1_), channel_id=1, source_target_pairs={{0,32},{32,64},{64,96},{96,100},{100,68},{68,36},{36,4},{4,0},{1,3... | collective-permute-start | bytes 1671176 | tf_op jit(solution)/shard_map/ppermute | solution.py:146
  71.0 1.3 copy-start.12
  71.0 11.7 %collective-permute-start.1 = (bf16[2176,128]{1,0:T(8,128)(2,1)S(1)}, bf16[2176,128]{1,0:T(8,128)(2,1)S(1)}, u32[]{:S(2)}, u32[]{:S(2)}) collective-permute-start(bf16[2176,128]{1,0:T(8,128)(2,1)S(1)} %collective-permute-done.refs_1_), channel_id=1, source_target_pairs={{0,32},{32,64},{64,96},{96,100},{100,68},{68,36},{36,4},{4,0},{1,3... | collective-permute-start | bytes 1671176 | tf_op jit(solution)/shard_map/ppermute | solution.py:146
  82.7 1.3 copy-start.7
  82.7 11.7 %collective-permute-start.2 = (bf16[2176,128]{1,0:T(8,128)(2,1)S(1)}, bf16[2176,128]{1,0:T(8,128)(2,1)S(1)}, u32[]{:S(2)}, u32[]{:S(2)}) collective-permute-start(bf16[2176,128]{1,0:T(8,128)(2,1)S(1)} %collective-permute-done.1.refs_1_), channel_id=1, source_target_pairs={{0,32},{32,64},{64,96},{96,100},{100,68},{68,36},{36,4},{4,0},{1,3... | collective-permute-start | bytes 1671176 | tf_op jit(solution)/shard_map/ppermute | solution.py:146
  94.4 1.5 copy-start.8
  94.4 24.9 %collective-permute-start.3 = (bf16[2176,128]{1,0:T(8,128)(2,1)S(1)}, bf16[2176,128]{1,0:T(8,128)(2,1)S(1)}, u32[]{:S(2)}, u32[]{:S(2)}) collective-permute-start(bf16[2176,128]{1,0:T(8,128)(2,1)S(1)} %collective-permute-done.2.refs_1_), channel_id=1, source_target_pairs={{0,32},{32,64},{64,96},{96,100},{100,68},{68,36},{36,4},{4,0},{1,3... | collective-permute-start | bytes 1671176 | tf_op jit(solution)/shard_map/ppermute | solution.py:146
  119.3 0.8 copy-start.9
  119.3 12.2 %collective-permute-start.4 = (bf16[2176,128]{1,0:T(8,128)(2,1)S(1)}, bf16[2176,128]{1,0:T(8,128)(2,1)S(1)}, u32[]{:S(2)}, u32[]{:S(2)}) collective-permute-start(bf16[2176,128]{1,0:T(8,128)(2,1)S(1)} %collective-permute-done.3.refs_1_), channel_id=1, source_target_pairs={{0,32},{32,64},{64,96},{96,100},{100,68},{68,36},{36,4},{4,0},{1,3... | collective-permute-start | bytes 1671176 | tf_op jit(solution)/shard_map/ppermute | solution.py:146
  131.5 0.8 copy-start.10
  131.5 11.3 %collective-permute-start.5 = (bf16[2176,128]{1,0:T(8,128)(2,1)S(1)}, bf16[2176,128]{1,0:T(8,128)(2,1)S(1)}, u32[]{:S(2)}, u32[]{:S(2)}) collective-permute-start(bf16[2176,128]{1,0:T(8,128)(2,1)S(1)} %collective-permute-done.4.refs_1_), channel_id=1, source_target_pairs={{0,32},{32,64},{64,96},{96,100},{100,68},{68,36},{36,4},{4,0},{1,3... | collective-permute-start | bytes 1671176 | tf_op jit(solution)/shard_map/ppermute | solution.py:146
  142.8 0.8 copy-start.11
  142.8 11.1 %collective-permute-start.6 = (bf16[2176,128]{1,0:T(8,128)(2,1)S(1)}, bf16[2176,128]{1,0:T(8,128)(2,1)S(1)}, u32[]{:S(2)}, u32[]{:S(2)}) collective-permute-start(bf16[2176,128]{1,0:T(8,128)(2,1)S(1)} %collective-permute-done.5.refs_1_), channel_id=1, source_target_pairs={{0,32},{32,64},{64,96},{96,100},{100,68},{68,36},{36,4},{4,0},{1,3... | collective-permute-start | bytes 1671176 | tf_op jit(solution)/shard_map/ppermute | solution.py:146
  153.9 0.8 copy-start.13
  164.6 13.7 %copy-start.15 = (s32[136,1]{0,1:T(1,128)S(1)}, s32[136,1]{0,1:T(1,128)}, u32[]{:S(2)}) copy-start(s32[136,1]{0,1:T(1,128)} %param.16) | copy-start | bytes 1636
  165.9 24.3 %copy-start = (bf16[136,1024]{1,0:T(8,128)(2,1)S(1)}, bf16[136,1024]{1,0:T(8,128)(2,1)}, u32[]{:S(2)}) copy-start(bf16[136,1024]{1,0:T(8,128)(2,1)} %param.10) | copy-start | bytes 835588
  165.9 24.3 %copy-start.5 = (f32[1024]{0:T(1024)S(1)}, f32[1024]{0:T(1024)}, u32[]{:S(2)}) copy-start(f32[1024]{0:T(1024)} %param.12) | copy-start | bytes 12292
  167.0 22.1 %all-to-all-start.1 = ((bf16[16,136,64]{1,2,0:T(8,128)(2,1)}), bf16[16,136,64]{1,2,0:T(8,128)(2,1)S(1)}, u32[]{:S(2)}, u32[]{:S(2)}) async-start(bf16[16,136,64]{1,2,0:T(8,128)(2,1)} %copy.32), calls=%async_computation.1 | async-start | bytes 1048576 | tf_op jit(solution)/shard_map/all_to_all | solution.py:153
  178.0 35.7 %all-gather.8.cloned.1.call-start = ((), (), s32[]{:S(2)}) async-start(), calls=%async_computation.4 | async-start | bytes 1566720 | tf_op jit(solution)/shard_map/all_gather | solution.py:160
  189.7 2.7 %copy-start.6 = (f32[1024]{0:T(1024)S(1)}, f32[1024]{0:T(1024)}, u32[]{:S(2)}) copy-start(f32[1024]{0:T(1024)} %param.13) | copy-start | bytes 12292
  190.1 3.4 %copy-start.16 = (u32[128]{0:T(128)S(1)}, u32[128]{0:T(128)}, u32[]{:S(2)}) copy-start(u32[128]{0:T(128)} %constant.37) | copy-start | bytes 1540
  190.1 4.6 %copy-start.3 = (bf16[2,1024]{1,0:T(2,128)(2,1)S(1)}, bf16[2,1024]{1,0:T(2,128)(2,1)}, u32[]{:S(2)}) copy-start(bf16[2,1024]{1,0:T(2,128)(2,1)} %param.18) | copy-start | bytes 12292
  190.1 24.8 %copy-start.14 = (bf16[2,1024,16]{1,2,0:T(8,128)(2,1)S(1)}, bf16[2,1024,16]{1,2,0:T(8,128)(2,1)}, u32[]{:S(2)}) copy-start(bf16[2,1024,16]{1,2,0:T(8,128)(2,1)} %param.19) | copy-start | bytes 196612
  192.4 26.4 %copy-start.1 = (bf16[136,1024]{1,0:T(8,128)(2,1)}, bf16[136,1024]{1,0:T(8,128)(2,1)S(1)}, u32[]{:S(2)}) copy-start(bf16[136,1024]{1,0:T(8,128)(2,1)S(1)} %get-tuple-element.116) | copy-start | bytes 835588
  214.9 4.0 %copy-start.4 = (bf16[544,1152]{1,0:T(8,128)(2,1)S(1)}, bf16[544,1152]{1,0:T(8,128)(2,1)}, u32[]{:S(2)}) copy-start(bf16[544,1152]{1,0:T(8,128)(2,1)} %all-gather.8.cloned.1.call-done) | copy-start | bytes 3760132
Sparse Core Ops, SparseCore 0:
  11.1 24.7 all-gather.3
  84.2 27.4 all-gather.5
  193.6 20.0 all-gather.7

commit v5 on v4

--- a/solution.py
+++ b/solution.py
@@ -109,6 +109,31 @@
     )(*operands)
 
 
+def from_each(pieces, axis):
+    n = len(pieces)
+    me = lax.axis_index(axis)
+    turned = jnp.stack([pieces[(n - j) % n] for j in range(n)])
+    return jnp.roll(turned, me, axis=0)
+
+
+def gather_by_permutes(value, axis):
+    n = lax.axis_size(axis)
+    pieces = [value] + [
+        lax.ppermute(value, axis, [(i, (i + k) % n) for i in range(n)]) for k in range(1, n)
+    ]
+    return from_each(pieces, axis)
+
+
+def exchange_by_permutes(blocks, axis):
+    n = lax.axis_size(axis)
+    me = lax.axis_index(axis)
+    pieces = [lax.dynamic_index_in_dim(blocks, me, 0, keepdims=False)]
+    for k in range(1, n):
+        send = lax.dynamic_index_in_dim(blocks, (me + k) % n, 0, keepdims=False)
+        pieces.append(lax.ppermute(send, axis, [(i, (i + k) % n) for i in range(n)]))
+    return from_each(pieces, axis)
+
+
 def body(
     tokens, shift_scale, branch_gate, final_gain, w_qkv, w_out, type_ids, head_w1, head_b1, head_w2
 ):
@@ -116,7 +141,8 @@
     modulated = (rms_normalize(inputs) * (1.0 + shift_scale[1]) + shift_scale[0]).astype(
         jnp.bfloat16
     )
-    gathered = lax.all_gather(modulated, "type", axis=0, tiled=True)
+    gathered = gather_by_permutes(modulated, "type")
+    gathered = gathered.reshape(-1, gathered.shape[-1])
     dim = w_qkv.shape[1]
     local_heads = w_qkv.shape[2] // HD
     kinds = lax.axis_size("type")
@@ -127,7 +153,7 @@
     projected = jnp.einsum(
         "rd,dje->jre", gathered, arranged, preferred_element_type=jnp.float32
     ).astype(jnp.bfloat16)
-    mine = lax.all_to_all(projected, "x", 0, 0, tiled=True)
+    mine = exchange_by_permutes(projected, "x")
     mine = mine.reshape(-1, 4 * HD)
     q_pad = mine[:, : 2 * HD]
     chunk = mine[:, 2 * HD :]
@@ -138,15 +164,28 @@
     order = [z * y_n for z in range(z_n)] + [z * y_n + 1 for z in reversed(range(z_n))]
     if y_n != 2:
         order = list(range(z_n * y_n))
-    pairs = [(order[i], order[(i + 1) % len(order)]) for i in range(len(order))]
-    steps = len(order)
+    n = len(order)
+    right = [(order[i], order[(i + 1) % n]) for i in range(n)]
+    left = [(order[i], order[(i - 1) % n]) for i in range(n)]
+    plan = [[chunk]]
     state = None
-    for step in range(steps):
-        if step < steps - 1:
-            coming = lax.ppermute(chunk, RING, pairs)
-        state = flash_step(q_pad, chunk, state, step == 0, step == steps - 1)
-        if step < steps - 1:
-            chunk, state = lax.optimization_barrier((coming, state))
+    done = 0
+    incoming = [lax.ppermute(chunk, RING, right), lax.ppermute(chunk, RING, left)]
+    for d in range(n // 2 + 1):
+        held = plan[-1] if d == 0 else incoming_now
+        if d > 0:
+            following = []
+            if d + 1 <= n // 2:
+                following.append(lax.ppermute(held[0], RING, right))
+                if d + 1 < n - (d + 1):
+                    following.append(lax.ppermute(held[1], RING, left))
+        else:
+            following = incoming
+        for piece in held:
+            state = flash_step(q_pad, piece, state, done == 0, done == n - 1)
+            done += 1
+        if following:
+            incoming_now, state = lax.optimization_barrier((following, state))
     attended = state[:, HD:]
     rows = tokens.shape[0]
     attended = attended.reshape(-1, kinds, rows, HD).reshape(-1, rows, HD)

time: 244 us -> 232 us (0.951)
  waiting for transfers between devices: 67.8 us -> 47.7 us
  blocking collectives: 32.6 us -> 13.6 us
  starting transfers between devices: 17.5 us -> 31.1 us
  local copies, waits for them, and re-layouts: 10.4 us -> 23.5 us
    all_gather x1 -> x0, waiting for transfers between devices: 22.2 us -> none  [body(): gathered = lax.all_gather(modulated, 'type', axis=0, tiled=True)]
    all_to_all x1 -> x0, blocking collectives: 19 us -> none  [body(): mine = lax.all_to_all(projected, 'x', 0, 0, tiled=True)]
    ppermute x7 -> x13, starting transfers between devices: 6.23 us -> 17.3 us  [the longest x3 7.27 us: gather_by_permutes(): lax.ppermute(value, axis, [(i, (i + k) % n) for i in range(n)])]
    unnamed x39 -> x54, local copies, waits for them, and re-layouts: 4.37 us -> 12.9 us
    all_to_all x1, starting transfers between devices: 11 us -> 13.7 us  [body(): back = lax.all_to_all(attended, ('x', 'type'), 0, 0, tiled=True)]
    ppermute x7 -> x13, waiting for transfers between devices: 15.8 us -> 16.8 us  [the longest x3 13.8 us: exchange_by_permutes(): lax.ppermute(send, axis, [(i, (i + k) % n) for i in range(n)])]
  transfers between devices with their start and end apart: 11 -> 16, of which waited for: 8 -> 8; matrix products, arithmetic and copies ran while one was open for 3% -> 6% of each run, Pallas kernels for 34% -> 35%
where the time goes in v5:
time: 232 us; the launch traced here: 231 us
  Pallas kernels  81.8 us (35%)
  waiting for transfers between devices  47.7 us (21%)
  starting transfers between devices  31.1 us (13%)
  local copies, waits for them, and re-layouts  23.5 us (10%)
  between operations  15.1 us (7%)
  blocking collectives  13.6 us (6%)
  matrix products  11 us (5%)
  other arithmetic  7.11 us (3%)
    pallas_call x8, Pallas kernels, flash_step(): pl.pallas_call(functools.partial(step_kernel, first, last), grid=(rows //...  81.8 us
    all_gather x1, waiting for transfers between devices, body(): lax.all_gather(jnp.concatenate([final, ids], axis=1), 'type', axis=0, til...  19.8 us
    ppermute x3, waiting for transfers between devices, exchange_by_permutes(): lax.ppermute(send, axis, [(i, (i + k) % n) for i in range(n)])  13.8 us
    all_to_all x1, starting transfers between devices, body(): back = lax.all_to_all(attended, ('x', 'type'), 0, 0, tiled=True)  13.7 us
    unnamed x1, blocking collectives  13.6 us
    unnamed x54, local copies, waits for them, and re-layouts  12.9 us
    all_to_all x1, waiting for transfers between devices, body(): back = lax.all_to_all(attended, ('x', 'type'), 0, 0, tiled=True)  11.1 us
    dot_general x2, matrix products, body(): answer = jnp.dot(hidden, head_w2[which], preferred_element_type=jnp.float32)  7.46 us
  transfers between devices with their start and end apart: 16, of which 8 were waited for; matrix products, arithmetic and copies ran while one was open for 6% of the time, Pallas kernels for 35%

profile of v5, /device:TPU:1, one launch (start us, length us, event | category | flops | bytes accessed | tf_op | source)
XLA Modules:
  0.0 230.9 jit_solution(10361863774513912483)
XLA Ops:
  7.2 0.8 slice_add_fusion
  8.0 1.1 fusion.57
  9.1 1.8 bitcast_dynamic-update-slice_fusion.14
  10.9 1.4 collective-permute-start
  12.3 3.0 %collective-permute-start.1 = (bf16[136,1024]{1,0:T(8,128)(2,1)S(1)}, bf16[136,1024]{1,0:T(8,128)(2,1)}, u32[]{:S(2)}, u32[]{:S(2)}) collective-permute-start(bf16[136,1024]{1,0:T(8,128)(2,1)S(1)} %get-tuple-element.89), channel_id=1, source_target_pairs={{0,2},{1,3},{2,0},{3,1},{4,6},{5,7},{6,4},{7,5},{8,10},{9,11},{10,... | collective-permute-start | bytes 835592 | tf_op jit(solution)/shard_map/ppermute | solution.py:122
  15.3 2.9 %collective-permute-start.2 = (bf16[136,1024]{1,0:T(8,128)(2,1)S(1)}, bf16[136,1024]{1,0:T(8,128)(2,1)}, u32[]{:S(2)}, u32[]{:S(2)}) collective-permute-start(bf16[136,1024]{1,0:T(8,128)(2,1)S(1)} %get-tuple-element.89), channel_id=1, source_target_pairs={{0,1},{1,2},{2,3},{3,0},{4,5},{5,6},{6,7},{7,4},{8,9},{9,10},{10,1... | collective-permute-start | bytes 835592 | tf_op jit(solution)/shard_map/ppermute | solution.py:122
  18.2 1.5 fusion.76
  19.7 0.2 copy.37
  19.9 0.2 copy.38
  20.1 1.0 copy.39
  21.2 1.3 pad_maximum_fusion
  22.6 1.6 copy.30
  24.1 1.7 bitcast_dynamic-update-slice_fusion.12
  25.8 1.7 bitcast_dynamic-update-slice_fusion.10
  27.5 0.3 collective-permute-done.2
  27.8 1.7 bitcast_dynamic-update-slice_fusion.8
  29.5 0.7 bitcast_dynamic-update-slice_fusion.15
  30.2 1.7 bitcast_dynamic-update-slice_fusion.13
  31.9 1.7 bitcast_dynamic-update-slice_fusion.11
  33.6 1.7 bitcast_dynamic-update-slice_fusion.9
  35.3 1.3 constant_dynamic-slice_fusion.1
  36.6 1.4 convolution_convert_fusion
  38.0 2.5 %collective-permute-start.3 = (bf16[544,256]{1,0:T(8,128)(2,1)S(1)}, bf16[544,256]{1,0:T(8,128)(2,1)S(1)}, u32[]{:S(2)}, u32[]{:S(2)}) collective-permute-start(bf16[544,256]{1,0:T(8,128)(2,1)S(1)} %get-tuple-element.97), channel_id=1, source_target_pairs={{0,24},{8,0},{16,8},{24,16},{1,25},{9,1},{17,9},{25,17},{2,26},{10... | collective-permute-start | bytes 835592 | tf_op jit(solution)/shard_map/ppermute | solution.py:133
  40.6 0.5 collective-permute-start.4
  41.1 0.7 collective-permute-start.5
  41.8 4.7 %collective-permute-done.3 = bf16[544,256]{1,0:T(8,128)(2,1)S(1)} collective-permute-done((bf16[544,256]{1,0:T(8,128)(2,1)S(1)}, bf16[544,256]{1,0:T(8,128)(2,1)S(1)}, u32[]{:S(2)}, u32[]{:S(2)}) %collective-permute-start.3) | collective-permute-done | bytes 278560 | tf_op jit(solution)/shard_map/ppermute | solution.py:133
  46.5 1.1 collective-permute-done.4
  47.6 8.0 %collective-permute-done.5 = bf16[544,256]{1,0:T(8,128)(2,1)S(1)} collective-permute-done((bf16[544,256]{1,0:T(8,128)(2,1)S(1)}, bf16[544,256]{1,0:T(8,128)(2,1)S(1)}, u32[]{:S(2)}, u32[]{:S(2)}) %collective-permute-start.5) | collective-permute-done | bytes 278560 | tf_op jit(solution)/shard_map/ppermute | solution.py:133
  55.8 0.1 constant_dynamic-slice_fusion
  55.9 0.9 fusion.77
  56.8 1.7 collective-permute-start.6
  58.5 10.1 %shard_map.113 = (f32[2176,1]{1,0:T(8,128)}, f32[2176,1]{1,0:T(8,128)}, f32[2176,128]{1,0:T(8,128)}) custom-call(bf16[2176,128]{1,0:T(8,128)(2,1)} %get-tuple-element.94.refs_0_, bf16[2176,128]{1,0:T(8,128)(2,1)} %copy-done.3), custom_call_target="tpu_custom_call" | custom-call | flops 2424307712 | bytes 4456448 | tf_op jit(solution)/shard_map/pallas_call | solution.py:92
  68.5 1.7 collective-permute-done.6.refs_1_
  70.3 1.0 collective-permute-done.7.refs_1_
  71.2 1.3 collective-permute-start.8
  72.5 0.9 collective-permute-start.9
  73.4 10.3 %shard_map.114 = (f32[2176,1]{1,0:T(8,128)}, f32[2176,1]{1,0:T(8,128)}, f32[2176,128]{1,0:T(8,128)}) custom-call(bf16[2176,128]{1,0:T(8,128)(2,1)} %get-tuple-element.94.refs_0_, bf16[2176,128]{1,0:T(8,128)(2,1)} %copy-done.11, f32[2176,1]{1,0:T(8,128)} %get-tuple-element.50.refs_2_, f32[2176,1]{1,0:T(8,128)} %get-tuple-element.51.refs_3_, ...), custom_call_target="tpu_custom_call" | custom-call | flops 2424307712 | bytes 4456448 | tf_op jit(solution)/shard_map/pallas_call | solution.py:92
  83.7 10.3 %shard_map.115 = (f32[2176,1]{1,0:T(8,128)}, f32[2176,1]{1,0:T(8,128)}, f32[2176,128]{1,0:T(8,128)}) custom-call(bf16[2176,128]{1,0:T(8,128)(2,1)} %get-tuple-element.94.refs_0_, bf16[2176,128]{1,0:T(8,128)(2,1)} %copy-done.12, f32[2176,1]{1,0:T(8,128)} %get-tuple-element.53.refs_2_, f32[2176,1]{1,0:T(8,128)} %get-tuple-element.54.refs_3_, ...), custom_call_target="tpu_custom_call" | custom-call | flops 2424307712 | bytes 4456448 | tf_op jit(solution)/shard_map/pallas_call | solution.py:92
  94.0 0.7 collective-permute-start.10
  94.8 1.0 collective-permute-start.11
  95.7 10.3 %shard_map.116 = (f32[2176,1]{1,0:T(8,128)}, f32[2176,1]{1,0:T(8,128)}, f32[2176,128]{1,0:T(8,128)}) custom-call(bf16[2176,128]{1,0:T(8,128)(2,1)} %get-tuple-element.94.refs_0_, bf16[2176,128]{1,0:T(8,128)(2,1)} %copy-done.8, f32[2176,1]{1,0:T(8,128)} %get-tuple-element.61.refs_2_, f32[2176,1]{1,0:T(8,128)} %get-tuple-element.62.refs_3_, ...), custom_call_target="tpu_custom_call" | custom-call | flops 2424307712 | bytes 4456448 | tf_op jit(solution)/shard_map/pallas_call | solution.py:92
  106.0 10.3 %shard_map.117 = (f32[2176,1]{1,0:T(8,128)}, f32[2176,1]{1,0:T(8,128)}, f32[2176,128]{1,0:T(8,128)}) custom-call(bf16[2176,128]{1,0:T(8,128)(2,1)} %get-tuple-element.94.refs_0_, bf16[2176,128]{1,0:T(8,128)(2,1)} %copy-done.9, f32[2176,1]{1,0:T(8,128)} %get-tuple-element.64.refs_2_, f32[2176,1]{1,0:T(8,128)} %get-tuple-element.65.refs_3_, ...), custom_call_target="tpu_custom_call" | custom-call | flops 2424307712 | bytes 4456448 | tf_op jit(solution)/shard_map/pallas_call | solution.py:92
  116.4 0.8 collective-permute-start.12
  117.2 10.3 %shard_map.118 = (f32[2176,1]{1,0:T(8,128)}, f32[2176,1]{1,0:T(8,128)}, f32[2176,128]{1,0:T(8,128)}) custom-call(bf16[2176,128]{1,0:T(8,128)(2,1)} %get-tuple-element.94.refs_0_, bf16[2176,128]{1,0:T(8,128)(2,1)} %copy-done.10, f32[2176,1]{1,0:T(8,128)} %get-tuple-element.72.refs_2_, f32[2176,1]{1,0:T(8,128)} %get-tuple-element.73.refs_3_, ...), custom_call_target="tpu_custom_call" | custom-call | flops 2424307712 | bytes 4456448 | tf_op jit(solution)/shard_map/pallas_call | solution.py:92
  127.5 10.3 %shard_map.119 = (f32[2176,1]{1,0:T(8,128)}, f32[2176,1]{1,0:T(8,128)}, f32[2176,128]{1,0:T(8,128)}) custom-call(bf16[2176,128]{1,0:T(8,128)(2,1)} %get-tuple-element.94.refs_0_, bf16[2176,128]{1,0:T(8,128)(2,1)} %copy-done.13, f32[2176,1]{1,0:T(8,128)} %get-tuple-element.75.refs_2_, f32[2176,1]{1,0:T(8,128)} %get-tuple-element.76.refs_3_, ...), custom_call_target="tpu_custom_call" | custom-call | flops 2424307712 | bytes 4456448 | tf_op jit(solution)/shard_map/pallas_call | solution.py:92
  137.8 0.8 copy-done.14
  138.6 9.8 %shard_map.120 = bf16[2176,128]{1,0:T(8,128)(2,1)} custom-call(bf16[2176,128]{1,0:T(8,128)(2,1)} %get-tuple-element.94.refs_0_, bf16[2176,128]{1,0:T(8,128)(2,1)} %copy-done.14, f32[2176,1]{1,0:T(8,128)} %get-tuple-element.82.refs_2_, f32[2176,1]{1,0:T(8,128)} %get-tuple-element.83.refs_3_, f32[2176,128]{1,0:T(8,128)} %get-tuple-element.84.refs_4_), custom_call_target="tpu_custom_call" | custom-call | flops 2424307712 | bytes 4456448 | tf_op jit(solution)/shard_map/pallas_call | solution.py:92
  148.5 1.3 slice.69
  149.8 1.1 copy.32
  150.9 13.7 %all-to-all-start = ((bf16[16,136,64]{1,2,0:T(8,128)(2,1)}), bf16[16,136,64]{1,2,0:T(8,128)(2,1)S(1)}, u32[]{:S(2)}, u32[]{:S(2)}) async-start(bf16[16,136,64]{1,2,0:T(8,128)(2,1)} %copy.32), calls=%async_computation | async-start | bytes 1048576 | tf_op jit(solution)/shard_map/all_to_all | solution.py:192
  164.7 11.1 %all-to-all-done = bf16[16,136,64]{1,2,0:T(8,128)(2,1)S(1)} async-done(((bf16[16,136,64]{1,2,0:T(8,128)(2,1)}), bf16[16,136,64]{1,2,0:T(8,128)(2,1)S(1)}, u32[]{:S(2)}, u32[]{:S(2)}) %all-to-all-start) | async-done | bytes 278560 | tf_op jit(solution)/shard_map/all_to_all | solution.py:192
  175.8 0.6 copy.33
  176.4 0.4 reshape.60
  176.8 2.2 fusion.54
  179.1 0.1 fusion.56
  179.2 0.1 broadcast_in_dim.37
  179.3 0.7 pad_maximum_fusion.1
  180.1 0.6 dynamic-slice.16
  181.3 19.8 %all-gather.5.cloned.1.call-done = bf16[544,1152]{1,0:T(8,128)(2,1)} async-done(((bf16[136,1152]{1,0:T(8,128)(2,1)}), bf16[544,1152]{1,0:T(8,128)(2,1)}) %all-gather.5.cloned.1.call-update) | async-done | bytes 1253392 | tf_op jit(solution)/shard_map/all_gather | solution.py:199
  201.1 1.2 fusion.61
  202.3 3.9 %fusion.44 = f32[544,16]{0,1:T(8,128)S(1)} fusion(bf16[2,1024,1024]{2,1,0:T(8,128)(2,1)} %param.17, f32[1024]{0:T(1024)S(1)} %bitcast.95, bf16[544,1152]{1,0:T(8,128)(2,1)} %all-gather.5.cloned.1.call-done, bf16[2,1024,16]{1,2,0:T(8,128)(2,1)S(1)} %copy-done.15, pred[544]{0:T(1024)(128)(4,1)S(1)} %get-tuple-element.87), kind=kOutput, calls=%fused_computation.41 | convolution fusion | flops 1164255744 | bytes 3283968 | tf_op jit(solution)/shard_map/dot_general | solution.py:208
  206.3 3.5 %fusion.47 = f32[544,16]{0,1:T(8,128)S(1)} fusion(f32[544,16]{0,1:T(8,128)S(1)} %fusion.44, bf16[2,1024,1024]{2,1,0:T(8,128)(2,1)} %param.17, f32[1024]{0:T(1024)S(1)} %bitcast.94, bf16[544,1152]{1,0:T(8,128)(2,1)S(1)} %copy-done.5, bf16[2,1024,16]{1,2,0:T(8,128)(2,1)S(1)} %copy-done.15, pred[544]{0:T(1024)(128)(4,1)S(1)} %get-tuple-element.86), kind=kOutput, calls=%fused_computation.42 | convolution fusion | flops 1164255744 | bytes 3324928 | tf_op jit(solution)/shard_map/dot_general | solution.py:208
  209.8 13.6 %all-reduce = f32[544,16]{0,1:T(8,128)S(1)} all-reduce(f32[544,16]{0,1:T(8,128)S(1)} %fusion.47), channel_id=2, replica_groups=mesh['z'=4,'x'=4,'y'=2,'type'=4] {'type'}, use_global_device_ids=true, to_apply=%region_2.3.clone | all-reduce | flops 8704 | bytes 69632
  223.4 0.7 constant_dynamic-slice_fusion.2
  (63 shorter events, 0.6 us)
Async XLA Ops:
  7.2 169.6 %all-gather.3.cloned.1.call-start = ((), (), s32[]{:S(2)}) async-start(), calls=%async_computation.1 | async-start | bytes 2621440 | tf_op jit(solution)/shard_map/all_gather | solution.py:161
  10.9 13.2 %collective-permute-start = (bf16[136,1024]{1,0:T(8,128)(2,1)S(1)}, bf16[136,1024]{1,0:T(8,128)(2,1)}, u32[]{:S(2)}, u32[]{:S(2)}) collective-permute-start(bf16[136,1024]{1,0:T(8,128)(2,1)S(1)} %get-tuple-element.89), channel_id=1, source_target_pairs={{0,3},{1,0},{2,1},{3,2},{4,7},{5,4},{6,5},{7,6},{8,11},{9,8},{10,9... | collective-permute-start | bytes 835592 | tf_op jit(solution)/shard_map/ppermute | solution.py:122
  12.3 13.5 %collective-permute-start.1 = (bf16[136,1024]{1,0:T(8,128)(2,1)S(1)}, bf16[136,1024]{1,0:T(8,128)(2,1)}, u32[]{:S(2)}, u32[]{:S(2)}) collective-permute-start(bf16[136,1024]{1,0:T(8,128)(2,1)S(1)} %get-tuple-element.89), channel_id=1, source_target_pairs={{0,2},{1,3},{2,0},{3,1},{4,6},{5,7},{6,4},{7,5},{8,10},{9,11},{10,... | collective-permute-start | bytes 835592 | tf_op jit(solution)/shard_map/ppermute | solution.py:122
  15.3 12.4 %collective-permute-start.2 = (bf16[136,1024]{1,0:T(8,128)(2,1)S(1)}, bf16[136,1024]{1,0:T(8,128)(2,1)}, u32[]{:S(2)}, u32[]{:S(2)}) collective-permute-start(bf16[136,1024]{1,0:T(8,128)(2,1)S(1)} %get-tuple-element.89), channel_id=1, source_target_pairs={{0,1},{1,2},{2,3},{3,0},{4,5},{5,6},{6,7},{7,4},{8,9},{9,10},{10,1... | collective-permute-start | bytes 835592 | tf_op jit(solution)/shard_map/ppermute | solution.py:122
  29.5 7.1 %copy-start.1 = (bf16[1024,4,4,64]{0,3,2,1:T(8,128)(2,1)S(1)}, bf16[1024,4,4,64]{0,3,2,1:T(8,128)(2,1)}, u32[]{:S(2)}) copy-start(bf16[1024,4,4,64]{0,3,2,1:T(8,128)(2,1)} %copy.30) | copy-start | bytes 6291460
  38.0 8.5 %collective-permute-start.3 = (bf16[544,256]{1,0:T(8,128)(2,1)S(1)}, bf16[544,256]{1,0:T(8,128)(2,1)S(1)}, u32[]{:S(2)}, u32[]{:S(2)}) collective-permute-start(bf16[544,256]{1,0:T(8,128)(2,1)S(1)} %get-tuple-element.97), channel_id=1, source_target_pairs={{0,24},{8,0},{16,8},{24,16},{1,25},{9,1},{17,9},{25,17},{2,26},{10... | collective-permute-start | bytes 835592 | tf_op jit(solution)/shard_map/ppermute | solution.py:133
  40.6 7.0 %collective-permute-start.4 = (bf16[544,256]{1,0:T(8,128)(2,1)S(1)}, bf16[544,256]{1,0:T(8,128)(2,1)S(1)}, u32[]{:S(2)}, u32[]{:S(2)}) collective-permute-start(bf16[544,256]{1,0:T(8,128)(2,1)S(1)} %get-tuple-element.96), channel_id=1, source_target_pairs={{0,16},{8,24},{16,0},{24,8},{1,17},{9,25},{17,1},{25,9},{2,18},{10... | collective-permute-start | bytes 835592 | tf_op jit(solution)/shard_map/ppermute | solution.py:133
  41.1 14.5 %collective-permute-start.5 = (bf16[544,256]{1,0:T(8,128)(2,1)S(1)}, bf16[544,256]{1,0:T(8,128)(2,1)S(1)}, u32[]{:S(2)}, u32[]{:S(2)}) collective-permute-start(bf16[544,256]{1,0:T(8,128)(2,1)S(1)} %get-tuple-element.95), channel_id=1, source_target_pairs={{0,8},{8,16},{16,24},{24,0},{1,9},{9,17},{17,25},{25,1},{2,10},{10... | collective-permute-start | bytes 835592 | tf_op jit(solution)/shard_map/ppermute | solution.py:133
  56.7 1.7 copy-start.3
  56.8 13.5 %collective-permute-start.6 = (bf16[2176,128]{1,0:T(8,128)(2,1)S(1)}, bf16[2176,128]{1,0:T(8,128)(2,1)S(1)}, u32[]{:S(2)}, u32[]{:S(2)}) collective-permute-start(bf16[2176,128]{1,0:T(8,128)(2,1)S(1)} %get-tuple-element.44.refs_1_), channel_id=1, source_target_pairs={{0,32},{32,64},{64,96},{96,100},{100,68},{68,36},{36,4},{4,0},{1,3... | collective-permute-start | bytes 1671176 | tf_op jit(solution)/shard_map/ppermute | solution.py:173
  58.5 12.8 %collective-permute-start.7 = (bf16[2176,128]{1,0:T(8,128)(2,1)S(1)}, bf16[2176,128]{1,0:T(8,128)(2,1)S(1)}, u32[]{:S(2)}, u32[]{:S(2)}) collective-permute-start(bf16[2176,128]{1,0:T(8,128)(2,1)S(1)} %get-tuple-element.44.refs_1_), channel_id=1, source_target_pairs={{0,4},{32,0},{64,32},{96,64},{100,96},{68,100},{36,68},{4,36},{1,5... | collective-permute-start | bytes 1671176 | tf_op jit(solution)/shard_map/ppermute | solution.py:173
  70.3 3.1 %copy-start.11 = (bf16[2176,128]{1,0:T(8,128)(2,1)}, bf16[2176,128]{1,0:T(8,128)(2,1)S(1)}, u32[]{:S(2)}) copy-start(bf16[2176,128]{1,0:T(8,128)(2,1)S(1)} %collective-permute-done.6.refs_1_) | copy-start | bytes 1671172
  71.2 12.5 %copy-start.12 = (bf16[2176,128]{1,0:T(8,128)(2,1)}, bf16[2176,128]{1,0:T(8,128)(2,1)S(1)}, u32[]{:S(2)}) copy-start(bf16[2176,128]{1,0:T(8,128)(2,1)S(1)} %collective-permute-done.7.refs_1_) | copy-start | bytes 1671172
  71.2 22.8 %collective-permute-start.8 = (bf16[2176,128]{1,0:T(8,128)(2,1)S(1)}, bf16[2176,128]{1,0:T(8,128)(2,1)S(1)}, u32[]{:S(2)}, u32[]{:S(2)}) collective-permute-start(bf16[2176,128]{1,0:T(8,128)(2,1)S(1)} %collective-permute-done.6.refs_1_), channel_id=1, source_target_pairs={{0,32},{32,64},{64,96},{96,100},{100,68},{68,36},{36,4},{4,0},{1,3... | collective-permute-start | bytes 1671176 | tf_op jit(solution)/shard_map/ppermute | solution.py:179
  72.5 21.5 %collective-permute-start.9 = (bf16[2176,128]{1,0:T(8,128)(2,1)S(1)}, bf16[2176,128]{1,0:T(8,128)(2,1)S(1)}, u32[]{:S(2)}, u32[]{:S(2)}) collective-permute-start(bf16[2176,128]{1,0:T(8,128)(2,1)S(1)} %collective-permute-done.7.refs_1_), channel_id=1, source_target_pairs={{0,4},{32,0},{64,32},{96,64},{100,96},{68,100},{36,68},{4,36},{1,5... | collective-permute-start | bytes 1671176 | tf_op jit(solution)/shard_map/ppermute | solution.py:181
  94.0 1.7 copy-start.8
  94.0 12.0 %copy-start.9 = (bf16[2176,128]{1,0:T(8,128)(2,1)}, bf16[2176,128]{1,0:T(8,128)(2,1)S(1)}, u32[]{:S(2)}) copy-start(bf16[2176,128]{1,0:T(8,128)(2,1)S(1)} %collective-permute-done.9.refs_1_) | copy-start | bytes 1671172
  94.0 22.3 %collective-permute-start.10 = (bf16[2176,128]{1,0:T(8,128)(2,1)S(1)}, bf16[2176,128]{1,0:T(8,128)(2,1)S(1)}, u32[]{:S(2)}, u32[]{:S(2)}) collective-permute-start(bf16[2176,128]{1,0:T(8,128)(2,1)S(1)} %collective-permute-done.8.refs_1_), channel_id=1, source_target_pairs={{0,32},{32,64},{64,96},{96,100},{100,68},{68,36},{36,4},{4,0},{1,3... | collective-permute-start | bytes 1671176 | tf_op jit(solution)/shard_map/ppermute | solution.py:179
  94.8 21.6 %collective-permute-start.11 = (bf16[2176,128]{1,0:T(8,128)(2,1)S(1)}, bf16[2176,128]{1,0:T(8,128)(2,1)S(1)}, u32[]{:S(2)}, u32[]{:S(2)}) collective-permute-start(bf16[2176,128]{1,0:T(8,128)(2,1)S(1)} %collective-permute-done.9.refs_1_), channel_id=1, source_target_pairs={{0,4},{32,0},{64,32},{96,64},{100,96},{68,100},{36,68},{4,36},{1,5... | collective-permute-start | bytes 1671176 | tf_op jit(solution)/shard_map/ppermute | solution.py:181
  116.3 0.8 copy-start.10
  116.4 11.1 %copy-start.13 = (bf16[2176,128]{1,0:T(8,128)(2,1)}, bf16[2176,128]{1,0:T(8,128)(2,1)S(1)}, u32[]{:S(2)}) copy-start(bf16[2176,128]{1,0:T(8,128)(2,1)S(1)} %collective-permute-done.11.refs_1_) | copy-start | bytes 1671172
  116.4 21.4 %collective-permute-start.12 = (bf16[2176,128]{1,0:T(8,128)(2,1)S(1)}, bf16[2176,128]{1,0:T(8,128)(2,1)S(1)}, u32[]{:S(2)}, u32[]{:S(2)}) collective-permute-start(bf16[2176,128]{1,0:T(8,128)(2,1)S(1)} %collective-permute-done.10.refs_1_), channel_id=1, source_target_pairs={{0,32},{32,64},{64,96},{96,100},{100,68},{68,36},{36,4},{4,0},{1,3... | collective-permute-start | bytes 1671176 | tf_op jit(solution)/shard_map/ppermute | solution.py:179
  137.8 0.8 copy-start.14
  148.5 16.2 %copy-start.16 = (s32[136,1]{0,1:T(1,128)S(1)}, s32[136,1]{0,1:T(1,128)}, u32[]{:S(2)}) copy-start(s32[136,1]{0,1:T(1,128)} %param.16) | copy-start | bytes 1636
  149.7 27.1 %copy-start = (bf16[136,1024]{1,0:T(8,128)(2,1)S(1)}, bf16[136,1024]{1,0:T(8,128)(2,1)}, u32[]{:S(2)}) copy-start(bf16[136,1024]{1,0:T(8,128)(2,1)} %param.10) | copy-start | bytes 835588
  149.8 27.1 %copy-start.6 = (f32[1024]{0:T(1024)S(1)}, f32[1024]{0:T(1024)}, u32[]{:S(2)}) copy-start(f32[1024]{0:T(1024)} %param.12) | copy-start | bytes 12292
  150.9 24.9 %all-to-all-start = ((bf16[16,136,64]{1,2,0:T(8,128)(2,1)}), bf16[16,136,64]{1,2,0:T(8,128)(2,1)S(1)}, u32[]{:S(2)}, u32[]{:S(2)}) async-start(bf16[16,136,64]{1,2,0:T(8,128)(2,1)} %copy.32), calls=%async_computation | async-start | bytes 1048576 | tf_op jit(solution)/shard_map/all_to_all | solution.py:192
  164.6 36.5 %all-gather.5.cloned.1.call-start = ((), (), s32[]{:S(2)}) async-start(), calls=%async_computation.2 | async-start | bytes 1566720 | tf_op jit(solution)/shard_map/all_gather | solution.py:199
  175.8 3.3 %copy-start.7 = (f32[1024]{0:T(1024)S(1)}, f32[1024]{0:T(1024)}, u32[]{:S(2)}) copy-start(f32[1024]{0:T(1024)} %param.13) | copy-start | bytes 12292
  176.7 3.3 %copy-start.17 = (u32[128]{0:T(128)S(1)}, u32[128]{0:T(128)}, u32[]{:S(2)}) copy-start(u32[128]{0:T(128)} %constant.101) | copy-start | bytes 1540
  176.7 4.6 %copy-start.4 = (bf16[2,1024]{1,0:T(2,128)(2,1)S(1)}, bf16[2,1024]{1,0:T(2,128)(2,1)}, u32[]{:S(2)}) copy-start(bf16[2,1024]{1,0:T(2,128)(2,1)} %param.18) | copy-start | bytes 12292
  176.8 25.5 %copy-start.15 = (bf16[2,1024,16]{1,2,0:T(8,128)(2,1)S(1)}, bf16[2,1024,16]{1,2,0:T(8,128)(2,1)}, u32[]{:S(2)}) copy-start(bf16[2,1024,16]{1,2,0:T(8,128)(2,1)} %param.19) | copy-start | bytes 196612
  179.0 27.2 %copy-start.2 = (bf16[136,1024]{1,0:T(8,128)(2,1)}, bf16[136,1024]{1,0:T(8,128)(2,1)S(1)}, u32[]{:S(2)}) copy-start(bf16[136,1024]{1,0:T(8,128)(2,1)S(1)} %get-tuple-element.103) | copy-start | bytes 835588
  202.3 4.0 %copy-start.5 = (bf16[544,1152]{1,0:T(8,128)(2,1)S(1)}, bf16[544,1152]{1,0:T(8,128)(2,1)}, u32[]{:S(2)}) copy-start(bf16[544,1152]{1,0:T(8,128)(2,1)} %all-gather.5.cloned.1.call-done) | copy-start | bytes 3760132
Sparse Core Ops, SparseCore 0:
  56.9 34.4 all-gather.2
  180.2 20.9 all-gather.4

commit v6 on v5

--- a/solution.py
+++ b/solution.py
@@ -109,30 +109,9 @@
     )(*operands)
 
 
-def from_each(pieces, axis):
-    n = len(pieces)
-    me = lax.axis_index(axis)
-    turned = jnp.stack([pieces[(n - j) % n] for j in range(n)])
-    return jnp.roll(turned, me, axis=0)
-
-
-def gather_by_permutes(value, axis):
+def shifted(value, axis, k):
     n = lax.axis_size(axis)
-    pieces = [value] + [
-        lax.ppermute(value, axis, [(i, (i + k) % n) for i in range(n)]) for k in range(1, n)
-    ]
-    return from_each(pieces, axis)
-
-
-def exchange_by_permutes(blocks, axis):
-    n = lax.axis_size(axis)
-    me = lax.axis_index(axis)
-    pieces = [lax.dynamic_index_in_dim(blocks, me, 0, keepdims=False)]
-    for k in range(1, n):
-        send = lax.dynamic_index_in_dim(blocks, (me + k) % n, 0, keepdims=False)
-        pieces.append(lax.ppermute(send, axis, [(i, (i + k) % n) for i in range(n)]))
-    return from_each(pieces, axis)
-
+    return lax.ppermute(value, axis, [(i, (i + k) % n) for i in range(n)])
 
 def body(
     tokens, shift_scale, branch_gate, final_gain, w_qkv, w_out, type_ids, head_w1, head_b1, head_w2
@@ -141,20 +120,23 @@
     modulated = (rms_normalize(inputs) * (1.0 + shift_scale[1]) + shift_scale[0]).astype(
         jnp.bfloat16
     )
-    gathered = gather_by_permutes(modulated, "type")
-    gathered = gathered.reshape(-1, gathered.shape[-1])
+    kinds = lax.axis_size("type")
+    gathered = jnp.concatenate(
+        [modulated] + [shifted(modulated, "type", k) for k in range(1, kinds)], axis=0
+    )
     dim = w_qkv.shape[1]
     local_heads = w_qkv.shape[2] // HD
-    kinds = lax.axis_size("type")
     parts = w_qkv.reshape(3, dim, local_heads, HD)
     scaled = (parts[0] * SCALE).astype(parts.dtype)
     arranged = jnp.stack([scaled, jnp.zeros_like(scaled), parts[1], parts[2]], axis=2)
     arranged = arranged.reshape(dim, local_heads, 4 * HD)
+    arranged = jnp.roll(arranged, -lax.axis_index("x"), axis=1)
     projected = jnp.einsum(
         "rd,dje->jre", gathered, arranged, preferred_element_type=jnp.float32
     ).astype(jnp.bfloat16)
-    mine = exchange_by_permutes(projected, "x")
-    mine = mine.reshape(-1, 4 * HD)
+    mine = jnp.concatenate(
+        [projected[0]] + [shifted(projected[k], "x", k) for k in range(1, local_heads)], axis=0
+    )
     q_pad = mine[:, : 2 * HD]
     chunk = mine[:, 2 * HD :]
     w_out_dep, chunk = lax.optimization_barrier((w_out, chunk))
@@ -188,7 +170,12 @@
             incoming_now, state = lax.optimization_barrier((following, state))
     attended = state[:, HD:]
     rows = tokens.shape[0]
-    attended = attended.reshape(-1, kinds, rows, HD).reshape(-1, rows, HD)
+    attended = attended.reshape(-1, rows, HD)
+    owner = jnp.arange(local_heads * kinds)
+    pick = ((lax.axis_index("x") - owner // kinds) % local_heads) * kinds + (
+        lax.axis_index("type") - owner % kinds
+    ) % kinds
+    attended = jnp.take(attended, pick, axis=0)
     back = lax.all_to_all(attended, ("x", "type"), 0, 0, tiled=True)
     back = back.reshape(-1, kinds, rows, HD)
     back = jnp.transpose(back, (2, 1, 0, 3)).reshape(rows, -1)
@@ -196,7 +183,8 @@
     updated = (inputs + branch_gate * mixed).astype(jnp.bfloat16)
     final = (rms_normalize(updated.astype(jnp.float32)) * final_gain).astype(jnp.bfloat16)
     ids = jnp.broadcast_to(type_ids.astype(jnp.bfloat16), (rows, 128))
-    joined = lax.all_gather(jnp.concatenate([final, ids], axis=1), "type", axis=0, tiled=True)
+    ext = jnp.concatenate([final, ids], axis=1)
+    joined = jnp.concatenate([ext] + [shifted(ext, "type", k) for k in range(1, kinds)], axis=0)
     final_all = joined[:, : final.shape[1]]
     kinds_all = joined[:, final.shape[1]].astype(jnp.int32)
     owned = head_w1.shape[0]
@@ -207,7 +195,10 @@
         hidden = jax.nn.gelu(hidden + head_b1[which].astype(jnp.float32)).astype(jnp.bfloat16)
         answer = jnp.dot(hidden, head_w2[which], preferred_element_type=jnp.float32)
         result = jnp.where((kinds_all == first_kind + which)[:, None], answer, result)
-    head_out = lax.psum_scatter(result, "type", scatter_dimension=0, tiled=True)
+    result = result.reshape(kinds, rows, -1)
+    head_out = result[0]
+    for k in range(1, kinds):
+        head_out = head_out + shifted(result[(-k) % kinds], "type", k)
     return (updated, head_out)
 
 

time: 232 us -> 209 us (0.901)
  blocking collectives: 13.6 us -> 0 us
  local copies, waits for them, and re-layouts: 23.5 us -> 10 us
  waiting for transfers between devices: 47.7 us -> 52.5 us
    ppermute x6 -> x12, waiting for transfers between devices: 14.1 us -> 37.7 us  [shifted(): return lax.ppermute(value, axis, [(i, (i + k) % n) for i in range(n)])]
    all_gather x1 -> x0, waiting for transfers between devices: 19.8 us -> none  [body(): lax.all_gather(jnp.concatenate([final, ids], axis=1), 'type', axis=0, til...]
    unnamed x1 -> x0, blocking collectives: 13.6 us -> none
    unnamed x54 -> x33, local copies, waits for them, and re-layouts: 12.9 us -> 1.5 us
    all_to_all x1, starting transfers between devices: 13.7 us -> 9.17 us  [body(): back = lax.all_to_all(attended, ('x', 'type'), 0, 0, tiled=True)]
    ppermute x6 -> x12, starting transfers between devices: 11 us -> 14.9 us  [shifted(): return lax.ppermute(value, axis, [(i, (i + k) % n) for i in range(n)])]
    reshape x0 -> x2, local copies, waits for them, and re-layouts: none -> 2.91 us  [the longest x1 2.58 us: body(): arranged = arranged.reshape(dim, local_heads, 4 * HD)]
  transfers between devices with their start and end apart: 16 -> 21, of which waited for: 8 -> 14; matrix products, arithmetic and copies ran while one was open for 6% -> 4% of each run, Pallas kernels for 35% -> 39%
where the time goes in v6:
time: 209 us
  Pallas kernels  81.8 us (39%)
  waiting for transfers between devices  52.5 us (25%)
  starting transfers between devices  32.3 us (15%)
  between operations  14.4 us (7%)
  matrix products  12.2 us (6%)
  local copies, waits for them, and re-layouts  10 us (5%)
  other arithmetic  5.4 us (3%)
    pallas_call x8, Pallas kernels, flash_step(): pl.pallas_call(functools.partial(step_kernel, first, last), grid=(rows //...  81.8 us
    ppermute x12, waiting for transfers between devices, shifted(): return lax.ppermute(value, axis, [(i, (i + k) % n) for i in range(n)])  37.7 us
    ppermute x12, starting transfers between devices, shifted(): return lax.ppermute(value, axis, [(i, (i + k) % n) for i in range(n)])  14.9 us
    all_to_all x1, waiting for transfers between devices, body(): back = lax.all_to_all(attended, ('x', 'type'), 0, 0, tiled=True)  11.1 us
    all_to_all x1, starting transfers between devices, body(): back = lax.all_to_all(attended, ('x', 'type'), 0, 0, tiled=True)  9.17 us
    dot_general x2, matrix products, body(): answer = jnp.dot(hidden, head_w2[which], preferred_element_type=jnp.float32)  7.06 us
    ppermute x3, starting transfers between devices, body(): following.append(lax.ppermute(held[0], RING, right))  4.95 us
  transfers between devices with their start and end apart: 21, of which 14 were waited for; matrix products, arithmetic and copies ran while one was open for 4% of the time, Pallas kernels for 39%

profile of v6, /device:TPU:1, one launch (start us, length us, event | category | flops | bytes accessed | tf_op | source)
XLA Modules:
  0.0 208.7 jit_solution(1377595031590382369)
XLA Ops:
  7.2 0.8 slice_add_fusion.1
  8.0 1.1 fusion.68
  9.1 1.1 fusion.71
  10.2 4.4 %collective-permute-start = (bf16[136,1024]{1,0:T(8,128)(2,1)S(1)}, bf16[136,1024]{1,0:T(8,128)(2,1)S(1)}, u32[]{:S(2)}, u32[]{:S(2)}) collective-permute-start(bf16[136,1024]{1,0:T(8,128)(2,1)S(1)} %fusion.71), channel_id=1, source_target_pairs={{0,1},{1,2},{2,3},{3,0},{4,5},{5,6},{6,7},{7,4},{8,9},{9,10},{10,1... | collective-permute-start | bytes 835592 | tf_op jit(solution)/shard_map/ppermute | solution.py:114
  14.6 0.5 collective-permute-start.2
  15.1 1.5 fusion.103
  16.5 0.2 copy.36
  16.8 0.2 copy.37
  17.0 0.2 copy.38
  17.3 0.2 pad_maximum_fusion
  17.6 0.2 copy.31
  17.8 2.6 %copy.32 = bf16[1024,4,256]{2,0,1:T(8,128)(2,1)} copy(bf16[1024,4,256]{0,2,1:T(8,128)(2,1)S(1)} %bitcast.54) | data formatting | bytes 4194304 | tf_op jit(solution)/shard_map/reshape | solution.py:132
  20.3 0.1 collective-permute-done
  20.5 6.4 %collective-permute-done.1 = bf16[136,1024]{1,0:T(8,128)(2,1)S(1)} collective-permute-done((bf16[136,1024]{1,0:T(8,128)(2,1)S(1)}, bf16[136,1024]{1,0:T(8,128)(2,1)S(1)}, u32[]{:S(2)}, u32[]{:S(2)}) %collective-permute-start.1) | collective-permute-done | bytes 278560 | tf_op jit(solution)/shard_map/ppermute | solution.py:114
  26.8 0.6 collective-permute-done.2
  27.4 3.0 %fusion.28 = bf16[4,544,256]{2,1,0:T(8,128)(2,1)S(1)} fusion(s32[]{:T(128)S(6)} %select_n.108, bf16[1024,4,256]{2,0,1:T(8,128)(2,1)} %copy.32, bf16[136,1024]{1,0:T(8,128)(2,1)S(1)} %collective-permute-done.2, bf16[136,1024]{1,0:T(8,128)(2,1)S(1)} %collective-permute-done.1, bf16[136,1024]{1,0:T(8,128)(2,1)S(1)} %collective-permute-done, ...), kind=kOutput, calls=%fused_computation.31 | convolution fusion | flops 1150058496 | bytes 4325380 | tf_op jit(solution)/shard_map/rd,dje->jre/dot_general | solution.py:134
  30.5 1.3 collective-permute-start.3
  31.8 2.5 %collective-permute-start.4 = (bf16[544,256]{1,0:T(8,128)(2,1)S(1)}, bf16[544,256]{1,0:T(8,128)(2,1)S(1)}, u32[]{:S(2)}, u32[]{:S(2)}) collective-permute-start(bf16[544,256]{1,0:T(8,128)(2,1)S(1)} %get-tuple-element.95), channel_id=1, source_target_pairs={{0,16},{8,24},{16,0},{24,8},{1,17},{9,25},{17,1},{25,9},{2,18},{10... | collective-permute-start | bytes 835592 | tf_op jit(solution)/shard_map/ppermute | solution.py:114
  34.3 1.1 collective-permute-start.5
  35.4 4.7 %collective-permute-done.3 = bf16[544,256]{1,0:T(8,128)(2,1)S(1)} collective-permute-done((bf16[544,256]{1,0:T(8,128)(2,1)S(1)}, bf16[544,256]{1,0:T(8,128)(2,1)S(1)}, u32[]{:S(2)}, u32[]{:S(2)}) %collective-permute-start.3) | collective-permute-done | bytes 278560 | tf_op jit(solution)/shard_map/ppermute | solution.py:114
  40.1 7.1 %collective-permute-done.4 = bf16[544,256]{1,0:T(8,128)(2,1)S(1)} collective-permute-done((bf16[544,256]{1,0:T(8,128)(2,1)S(1)}, bf16[544,256]{1,0:T(8,128)(2,1)S(1)}, u32[]{:S(2)}, u32[]{:S(2)}) %collective-permute-start.4) | collective-permute-done | bytes 278560 | tf_op jit(solution)/shard_map/ppermute | solution.py:114
  47.3 0.9 fusion.104
  48.2 1.7 collective-permute-start.6
  49.9 10.0 %shard_map.113 = (f32[2176,1]{1,0:T(8,128)}, f32[2176,1]{1,0:T(8,128)}, f32[2176,128]{1,0:T(8,128)}) custom-call(bf16[2176,128]{1,0:T(8,128)(2,1)} %get-tuple-element.92.refs_0_, bf16[2176,128]{1,0:T(8,128)(2,1)} %copy-done.2), custom_call_target="tpu_custom_call" | custom-call | flops 2424307712 | bytes 4456448 | tf_op jit(solution)/shard_map/pallas_call | solution.py:92
  60.0 2.4 %collective-permute-done.6.refs_1_ = bf16[2176,128]{1,0:T(8,128)(2,1)S(1)} collective-permute-done((bf16[2176,128]{1,0:T(8,128)(2,1)S(1)}, bf16[2176,128]{1,0:T(8,128)(2,1)S(1)}, u32[]{:S(2)}, u32[]{:S(2)}) %collective-permute-start.6) | collective-permute-done | bytes 557088 | tf_op jit(solution)/shard_map/ppermute | solution.py:155
  62.4 1.2 collective-permute-done.7.refs_1_
  63.6 1.3 collective-permute-start.8
  64.8 0.7 collective-permute-start.9
  65.6 10.3 %shard_map.114 = (f32[2176,1]{1,0:T(8,128)}, f32[2176,1]{1,0:T(8,128)}, f32[2176,128]{1,0:T(8,128)}) custom-call(bf16[2176,128]{1,0:T(8,128)(2,1)} %get-tuple-element.92.refs_0_, bf16[2176,128]{1,0:T(8,128)(2,1)} %copy-done.9, f32[2176,1]{1,0:T(8,128)} %get-tuple-element.50.refs_2_, f32[2176,1]{1,0:T(8,128)} %get-tuple-element.51.refs_3_, ...), custom_call_target="tpu_custom_call" | custom-call | flops 2424307712 | bytes 4456448 | tf_op jit(solution)/shard_map/pallas_call | solution.py:92
  75.9 10.3 %shard_map.115 = (f32[2176,1]{1,0:T(8,128)}, f32[2176,1]{1,0:T(8,128)}, f32[2176,128]{1,0:T(8,128)}) custom-call(bf16[2176,128]{1,0:T(8,128)(2,1)} %get-tuple-element.92.refs_0_, bf16[2176,128]{1,0:T(8,128)(2,1)} %copy-done.10, f32[2176,1]{1,0:T(8,128)} %get-tuple-element.53.refs_2_, f32[2176,1]{1,0:T(8,128)} %get-tuple-element.54.refs_3_, ...), custom_call_target="tpu_custom_call" | custom-call | flops 2424307712 | bytes 4456448 | tf_op jit(solution)/shard_map/pallas_call | solution.py:92
  86.3 0.8 collective-permute-start.10
  87.1 0.8 collective-permute-start.11
  88.0 10.3 %shard_map.116 = (f32[2176,1]{1,0:T(8,128)}, f32[2176,1]{1,0:T(8,128)}, f32[2176,128]{1,0:T(8,128)}) custom-call(bf16[2176,128]{1,0:T(8,128)(2,1)} %get-tuple-element.92.refs_0_, bf16[2176,128]{1,0:T(8,128)(2,1)} %copy-done.6, f32[2176,1]{1,0:T(8,128)} %get-tuple-element.61.refs_2_, f32[2176,1]{1,0:T(8,128)} %get-tuple-element.62.refs_3_, ...), custom_call_target="tpu_custom_call" | custom-call | flops 2424307712 | bytes 4456448 | tf_op jit(solution)/shard_map/pallas_call | solution.py:92
  98.3 10.3 %shard_map.117 = (f32[2176,1]{1,0:T(8,128)}, f32[2176,1]{1,0:T(8,128)}, f32[2176,128]{1,0:T(8,128)}) custom-call(bf16[2176,128]{1,0:T(8,128)(2,1)} %get-tuple-element.92.refs_0_, bf16[2176,128]{1,0:T(8,128)(2,1)} %copy-done.7, f32[2176,1]{1,0:T(8,128)} %get-tuple-element.64.refs_2_, f32[2176,1]{1,0:T(8,128)} %get-tuple-element.65.refs_3_, ...), custom_call_target="tpu_custom_call" | custom-call | flops 2424307712 | bytes 4456448 | tf_op jit(solution)/shard_map/pallas_call | solution.py:92
  108.6 2.9 %collective-permute-start.12 = (bf16[2176,128]{1,0:T(8,128)(2,1)S(1)}, bf16[2176,128]{1,0:T(8,128)(2,1)S(1)}, u32[]{:S(2)}, u32[]{:S(2)}) collective-permute-start(bf16[2176,128]{1,0:T(8,128)(2,1)S(1)} %collective-permute-done.10.refs_1_), channel_id=1, source_target_pairs={{0,32},{32,64},{64,96},{96,100},{100,68},{68,36},{36,4},{4,0},{1,3... | collective-permute-start | bytes 1671176 | tf_op jit(solution)/shard_map/ppermute | solution.py:161
  111.5 10.3 %shard_map.118 = (f32[2176,1]{1,0:T(8,128)}, f32[2176,1]{1,0:T(8,128)}, f32[2176,128]{1,0:T(8,128)}) custom-call(bf16[2176,128]{1,0:T(8,128)(2,1)} %get-tuple-element.92.refs_0_, bf16[2176,128]{1,0:T(8,128)(2,1)} %copy-done.8, f32[2176,1]{1,0:T(8,128)} %get-tuple-element.72.refs_2_, f32[2176,1]{1,0:T(8,128)} %get-tuple-element.73.refs_3_, ...), custom_call_target="tpu_custom_call" | custom-call | flops 2424307712 | bytes 4456448 | tf_op jit(solution)/shard_map/pallas_call | solution.py:92
  121.9 10.3 %shard_map.119 = (f32[2176,1]{1,0:T(8,128)}, f32[2176,1]{1,0:T(8,128)}, f32[2176,128]{1,0:T(8,128)}) custom-call(bf16[2176,128]{1,0:T(8,128)(2,1)} %get-tuple-element.92.refs_0_, bf16[2176,128]{1,0:T(8,128)(2,1)} %copy-done.11, f32[2176,1]{1,0:T(8,128)} %get-tuple-element.75.refs_2_, f32[2176,1]{1,0:T(8,128)} %get-tuple-element.76.refs_3_, ...), custom_call_target="tpu_custom_call" | custom-call | flops 2424307712 | bytes 4456448 | tf_op jit(solution)/shard_map/pallas_call | solution.py:92
  132.2 0.8 copy-done.12
  133.0 9.8 %shard_map.120 = bf16[2176,128]{1,0:T(8,128)(2,1)} custom-call(bf16[2176,128]{1,0:T(8,128)(2,1)} %get-tuple-element.92.refs_0_, bf16[2176,128]{1,0:T(8,128)(2,1)} %copy-done.12, f32[2176,1]{1,0:T(8,128)} %get-tuple-element.82.refs_2_, f32[2176,1]{1,0:T(8,128)} %get-tuple-element.83.refs_3_, f32[2176,128]{1,0:T(8,128)} %get-tuple-element.84.refs_4_), custom_call_target="tpu_custom_call" | custom-call | flops 2424307712 | bytes 4456448 | tf_op jit(solution)/shard_map/pallas_call | solution.py:92
  142.8 1.3 slice.111
  144.1 0.3 copy.34
  144.4 0.6 gather_fusion
  145.0 0.9 broadcast_select_fusion
  146.0 9.2 %all-to-all-start = ((bf16[16,136,64]{1,2,0:T(8,128)(2,1)}), bf16[16,136,64]{1,2,0:T(8,128)(2,1)S(1)}, u32[]{:S(2)}, u32[]{:S(2)}) async-start(bf16[16,136,64]{1,2,0:T(8,128)(2,1)} %broadcast_select_fusion), calls=%async_computation | async-start | bytes 1048576 | tf_op jit(solution)/shard_map/all_to_all | solution.py:179
  155.2 11.1 %all-to-all-done = bf16[16,136,64]{1,2,0:T(8,128)(2,1)S(1)} async-done(((bf16[16,136,64]{1,2,0:T(8,128)(2,1)}), bf16[16,136,64]{1,2,0:T(8,128)(2,1)S(1)}, u32[]{:S(2)}, u32[]{:S(2)}) %all-to-all-start) | async-done | bytes 278560 | tf_op jit(solution)/shard_map/all_to_all | solution.py:179
  166.3 0.6 copy.35
  166.8 0.4 reshape.206
  167.3 2.2 %fusion.65 = (f32[136]{0:T(256)S(1)}, bf16[136,1024]{1,0:T(8,128)(2,1)S(1)}) fusion(bf16[136,1024]{1,0:T(8,128)(2,1)S(1)} %reshape.206, bf16[1024,1024]{1,0:T(8,128)(2,1)} %all-gather.2.cloned.1.call-done, f32[1024]{0:T(1024)S(1)} %copy-done.4, bf16[136,1024]{1,0:T(8,128)(2,1)S(1)} %copy-done), kind=kOutput, calls=%fused_computation.65 | convolution fusion | flops 286187392 | bytes 2937376 | tf_op jit(solution)/shard_map/dot_general | solution.py:182
  169.5 0.1 fusion.67
  169.8 1.4 collective-permute-start.13
  171.2 2.9 %collective-permute-start.14 = (bf16[136,1152]{1,0:T(8,128)(2,1)S(1)}, bf16[136,1152]{1,0:T(8,128)(2,1)S(1)}, u32[]{:S(2)}, u32[]{:S(2)}) collective-permute-start(bf16[136,1152]{1,0:T(8,128)(2,1)S(1)} %pad_maximum_fusion.6), channel_id=1, source_target_pairs={{0,2},{1,3},{2,0},{3,1},{4,6},{5,7},{6,4},{7,5},{8,10},{9,11},{10,... | collective-permute-start | bytes 940040 | tf_op jit(solution)/shard_map/ppermute | solution.py:114
  174.1 3.5 %collective-permute-done.13 = bf16[136,1152]{1,0:T(8,128)(2,1)S(1)} collective-permute-done((bf16[136,1152]{1,0:T(8,128)(2,1)S(1)}, bf16[136,1152]{1,0:T(8,128)(2,1)S(1)}, u32[]{:S(2)}, u32[]{:S(2)}) %collective-permute-start.13) | collective-permute-done | bytes 313376 | tf_op jit(solution)/shard_map/ppermute | solution.py:114
  177.5 10.3 %collective-permute-done.14 = bf16[136,1152]{1,0:T(8,128)(2,1)S(1)} collective-permute-done((bf16[136,1152]{1,0:T(8,128)(2,1)S(1)}, bf16[136,1152]{1,0:T(8,128)(2,1)S(1)}, u32[]{:S(2)}, u32[]{:S(2)}) %collective-permute-start.14) | collective-permute-done | bytes 313376 | tf_op jit(solution)/shard_map/ppermute | solution.py:114
  187.8 0.6 collective-permute-done.15
  188.4 0.3 fusion.72
  188.7 3.5 %fusion.59 = f32[544,16]{0,1:T(8,128)S(1)} fusion(bf16[2,1024,1024]{2,1,0:T(8,128)(2,1)} %param.17, f32[1024]{0:T(1024)S(1)} %bitcast.63, bf16[2,1024,16]{1,2,0:T(8,128)(2,1)S(1)} %copy-done.13, pred[544]{0:T(1024)(128)(4,1)S(1)} %get-tuple-element.87, bf16[136,1152]{1,0:T(8,128)(2,1)S(1)} %collective-permute-done.15, ...), kind=kOutput, calls=%fused_computation.59 | convolution fusion | flops 1169826304 | bytes 3423232 | tf_op jit(solution)/shard_map/dot_general | solution.py:196
  192.2 3.5 %fusion.62 = f32[544,16]{0,1:T(8,128)S(1)} fusion(f32[544,16]{0,1:T(8,128)S(1)} %fusion.59, bf16[2,1024,1024]{2,1,0:T(8,128)(2,1)} %param.17, f32[1024]{0:T(1024)S(1)} %bitcast.62, bf16[2,1024,16]{1,2,0:T(8,128)(2,1)S(1)} %copy-done.13, pred[544]{0:T(1024)(128)(4,1)S(1)} %get-tuple-element.86, bf16[136,1152]{1,0:T(8,128)(2,1)S(1)} %collective-permute-done.15, ...), kind=kOutput, calls=%fused_computation.60 | convolution fusion | flops 1169826304 | bytes 3464192 | tf_op jit(solution)/shard_map/dot_general | solution.py:196
  195.8 0.1 fusion.105
  195.9 0.2 collective-permute-start.17
  196.1 0.7 collective-permute-start.18
  196.7 0.3 collective-permute-done.16
  197.1 3.0 %collective-permute-done.17 = f32[136,16]{0,1:T(8,128)S(1)} collective-permute-done((f32[136,16]{0,1:T(8,128)S(1)}, f32[136,16]{0,1:T(8,128)S(1)}, u32[]{:S(2)}, u32[]{:S(2)}) %collective-permute-start.17) | collective-permute-done | bytes 8736 | tf_op jit(solution)/shard_map/ppermute | solution.py:114
  200.1 1.2 collective-permute-done.18
  201.2 0.6 fusion.79
  (55 shorter events, 0.7 us)
Async XLA Ops:
  7.2 160.1 %all-gather.2.cloned.1.call-start = ((), (), s32[]{:S(2)}) async-start(), calls=%async_computation.1 | async-start | bytes 2621440 | tf_op jit(solution)/shard_map/all_gather | solution.py:143
  10.2 10.3 %collective-permute-start = (bf16[136,1024]{1,0:T(8,128)(2,1)S(1)}, bf16[136,1024]{1,0:T(8,128)(2,1)S(1)}, u32[]{:S(2)}, u32[]{:S(2)}) collective-permute-start(bf16[136,1024]{1,0:T(8,128)(2,1)S(1)} %fusion.71), channel_id=1, source_target_pairs={{0,1},{1,2},{2,3},{3,0},{4,5},{5,6},{6,7},{7,4},{8,9},{9,10},{10,1... | collective-permute-start | bytes 835592 | tf_op jit(solution)/shard_map/ppermute | solution.py:114
  14.6 12.2 %collective-permute-start.1 = (bf16[136,1024]{1,0:T(8,128)(2,1)S(1)}, bf16[136,1024]{1,0:T(8,128)(2,1)S(1)}, u32[]{:S(2)}, u32[]{:S(2)}) collective-permute-start(bf16[136,1024]{1,0:T(8,128)(2,1)S(1)} %fusion.71), channel_id=1, source_target_pairs={{0,2},{1,3},{2,0},{3,1},{4,6},{5,7},{6,4},{7,5},{8,10},{9,11},{10,... | collective-permute-start | bytes 835592 | tf_op jit(solution)/shard_map/ppermute | solution.py:114
  14.6 12.8 %collective-permute-start.2 = (bf16[136,1024]{1,0:T(8,128)(2,1)S(1)}, bf16[136,1024]{1,0:T(8,128)(2,1)S(1)}, u32[]{:S(2)}, u32[]{:S(2)}) collective-permute-start(bf16[136,1024]{1,0:T(8,128)(2,1)S(1)} %fusion.71), channel_id=1, source_target_pairs={{0,3},{1,0},{2,1},{3,2},{4,7},{5,4},{6,5},{7,6},{8,11},{9,8},{10,9... | collective-permute-start | bytes 835592 | tf_op jit(solution)/shard_map/ppermute | solution.py:114
  30.5 9.6 %collective-permute-start.3 = (bf16[544,256]{1,0:T(8,128)(2,1)S(1)}, bf16[544,256]{1,0:T(8,128)(2,1)S(1)}, u32[]{:S(2)}, u32[]{:S(2)}) collective-permute-start(bf16[544,256]{1,0:T(8,128)(2,1)S(1)} %get-tuple-element.96), channel_id=1, source_target_pairs={{0,8},{8,16},{16,24},{24,0},{1,9},{9,17},{17,25},{25,1},{2,10},{10... | collective-permute-start | bytes 835592 | tf_op jit(solution)/shard_map/ppermute | solution.py:114
  31.8 15.4 %collective-permute-start.4 = (bf16[544,256]{1,0:T(8,128)(2,1)S(1)}, bf16[544,256]{1,0:T(8,128)(2,1)S(1)}, u32[]{:S(2)}, u32[]{:S(2)}) collective-permute-start(bf16[544,256]{1,0:T(8,128)(2,1)S(1)} %get-tuple-element.95), channel_id=1, source_target_pairs={{0,16},{8,24},{16,0},{24,8},{1,17},{9,25},{17,1},{25,9},{2,18},{10... | collective-permute-start | bytes 835592 | tf_op jit(solution)/shard_map/ppermute | solution.py:114
  34.3 12.9 %collective-permute-start.5 = (bf16[544,256]{1,0:T(8,128)(2,1)S(1)}, bf16[544,256]{1,0:T(8,128)(2,1)S(1)}, u32[]{:S(2)}, u32[]{:S(2)}) collective-permute-start(bf16[544,256]{1,0:T(8,128)(2,1)S(1)} %get-tuple-element.94), channel_id=1, source_target_pairs={{0,24},{8,0},{16,8},{24,16},{1,25},{9,1},{17,9},{25,17},{2,26},{10... | collective-permute-start | bytes 835592 | tf_op jit(solution)/shard_map/ppermute | solution.py:114
  48.2 1.8 copy-start.2
  48.2 14.2 %collective-permute-start.6 = (bf16[2176,128]{1,0:T(8,128)(2,1)S(1)}, bf16[2176,128]{1,0:T(8,128)(2,1)S(1)}, u32[]{:S(2)}, u32[]{:S(2)}) collective-permute-start(bf16[2176,128]{1,0:T(8,128)(2,1)S(1)} %get-tuple-element.44.refs_1_), channel_id=1, source_target_pairs={{0,32},{32,64},{64,96},{96,100},{100,68},{68,36},{36,4},{4,0},{1,3... | collective-permute-start | bytes 1671176 | tf_op jit(solution)/shard_map/ppermute | solution.py:155
  49.9 13.6 %collective-permute-start.7 = (bf16[2176,128]{1,0:T(8,128)(2,1)S(1)}, bf16[2176,128]{1,0:T(8,128)(2,1)S(1)}, u32[]{:S(2)}, u32[]{:S(2)}) collective-permute-start(bf16[2176,128]{1,0:T(8,128)(2,1)S(1)} %get-tuple-element.44.refs_1_), channel_id=1, source_target_pairs={{0,4},{32,0},{64,32},{96,64},{100,96},{68,100},{36,68},{4,36},{1,5... | collective-permute-start | bytes 1671176 | tf_op jit(solution)/shard_map/ppermute | solution.py:155
  62.4 3.2 %copy-start.9 = (bf16[2176,128]{1,0:T(8,128)(2,1)}, bf16[2176,128]{1,0:T(8,128)(2,1)S(1)}, u32[]{:S(2)}) copy-start(bf16[2176,128]{1,0:T(8,128)(2,1)S(1)} %collective-permute-done.6.refs_1_) | copy-start | bytes 1671172
  63.6 12.4 %copy-start.10 = (bf16[2176,128]{1,0:T(8,128)(2,1)}, bf16[2176,128]{1,0:T(8,128)(2,1)S(1)}, u32[]{:S(2)}) copy-start(bf16[2176,128]{1,0:T(8,128)(2,1)S(1)} %collective-permute-done.7.refs_1_) | copy-start | bytes 1671172
  63.6 22.7 %collective-permute-start.8 = (bf16[2176,128]{1,0:T(8,128)(2,1)S(1)}, bf16[2176,128]{1,0:T(8,128)(2,1)S(1)}, u32[]{:S(2)}, u32[]{:S(2)}) collective-permute-start(bf16[2176,128]{1,0:T(8,128)(2,1)S(1)} %collective-permute-done.6.refs_1_), channel_id=1, source_target_pairs={{0,32},{32,64},{64,96},{96,100},{100,68},{68,36},{36,4},{4,0},{1,3... | collective-permute-start | bytes 1671176 | tf_op jit(solution)/shard_map/ppermute | solution.py:161
  64.8 21.4 %collective-permute-start.9 = (bf16[2176,128]{1,0:T(8,128)(2,1)S(1)}, bf16[2176,128]{1,0:T(8,128)(2,1)S(1)}, u32[]{:S(2)}, u32[]{:S(2)}) collective-permute-start(bf16[2176,128]{1,0:T(8,128)(2,1)S(1)} %collective-permute-done.7.refs_1_), channel_id=1, source_target_pairs={{0,4},{32,0},{64,32},{96,64},{100,96},{68,100},{36,68},{4,36},{1,5... | collective-permute-start | bytes 1671176 | tf_op jit(solution)/shard_map/ppermute | solution.py:163
  86.3 1.7 copy-start.6
  86.3 12.0 %copy-start.7 = (bf16[2176,128]{1,0:T(8,128)(2,1)}, bf16[2176,128]{1,0:T(8,128)(2,1)S(1)}, u32[]{:S(2)}) copy-start(bf16[2176,128]{1,0:T(8,128)(2,1)S(1)} %collective-permute-done.9.refs_1_) | copy-start | bytes 1671172
  86.3 22.3 %collective-permute-start.10 = (bf16[2176,128]{1,0:T(8,128)(2,1)S(1)}, bf16[2176,128]{1,0:T(8,128)(2,1)S(1)}, u32[]{:S(2)}, u32[]{:S(2)}) collective-permute-start(bf16[2176,128]{1,0:T(8,128)(2,1)S(1)} %collective-permute-done.8.refs_1_), channel_id=1, source_target_pairs={{0,32},{32,64},{64,96},{96,100},{100,68},{68,36},{36,4},{4,0},{1,3... | collective-permute-start | bytes 1671176 | tf_op jit(solution)/shard_map/ppermute | solution.py:161
  87.1 21.5 %collective-permute-start.11 = (bf16[2176,128]{1,0:T(8,128)(2,1)S(1)}, bf16[2176,128]{1,0:T(8,128)(2,1)S(1)}, u32[]{:S(2)}, u32[]{:S(2)}) collective-permute-start(bf16[2176,128]{1,0:T(8,128)(2,1)S(1)} %collective-permute-done.9.refs_1_), channel_id=1, source_target_pairs={{0,4},{32,0},{64,32},{96,64},{100,96},{68,100},{36,68},{4,36},{1,5... | collective-permute-start | bytes 1671176 | tf_op jit(solution)/shard_map/ppermute | solution.py:163
  108.6 2.9 %copy-start.8 = (bf16[2176,128]{1,0:T(8,128)(2,1)}, bf16[2176,128]{1,0:T(8,128)(2,1)S(1)}, u32[]{:S(2)}) copy-start(bf16[2176,128]{1,0:T(8,128)(2,1)S(1)} %collective-permute-done.10.refs_1_) | copy-start | bytes 1671172
  108.6 13.2 %copy-start.11 = (bf16[2176,128]{1,0:T(8,128)(2,1)}, bf16[2176,128]{1,0:T(8,128)(2,1)S(1)}, u32[]{:S(2)}) copy-start(bf16[2176,128]{1,0:T(8,128)(2,1)S(1)} %collective-permute-done.11.refs_1_) | copy-start | bytes 1671172
  108.6 23.5 %collective-permute-start.12 = (bf16[2176,128]{1,0:T(8,128)(2,1)S(1)}, bf16[2176,128]{1,0:T(8,128)(2,1)S(1)}, u32[]{:S(2)}, u32[]{:S(2)}) collective-permute-start(bf16[2176,128]{1,0:T(8,128)(2,1)S(1)} %collective-permute-done.10.refs_1_), channel_id=1, source_target_pairs={{0,32},{32,64},{64,96},{96,100},{100,68},{68,36},{36,4},{4,0},{1,3... | collective-permute-start | bytes 1671176 | tf_op jit(solution)/shard_map/ppermute | solution.py:161
  132.2 0.8 copy-start.12
  144.1 11.1 %copy-start.14 = (s32[136,1]{0,1:T(1,128)S(1)}, s32[136,1]{0,1:T(1,128)}, u32[]{:S(2)}) copy-start(s32[136,1]{0,1:T(1,128)} %param.16) | copy-start | bytes 1636
  145.0 22.3 %copy-start = (bf16[136,1024]{1,0:T(8,128)(2,1)S(1)}, bf16[136,1024]{1,0:T(8,128)(2,1)}, u32[]{:S(2)}) copy-start(bf16[136,1024]{1,0:T(8,128)(2,1)} %param.10) | copy-start | bytes 835588
  145.0 22.2 %copy-start.4 = (f32[1024]{0:T(1024)S(1)}, f32[1024]{0:T(1024)}, u32[]{:S(2)}) copy-start(f32[1024]{0:T(1024)} %param.12) | copy-start | bytes 12292
  146.0 20.3 %all-to-all-start = ((bf16[16,136,64]{1,2,0:T(8,128)(2,1)}), bf16[16,136,64]{1,2,0:T(8,128)(2,1)S(1)}, u32[]{:S(2)}, u32[]{:S(2)}) async-start(bf16[16,136,64]{1,2,0:T(8,128)(2,1)} %broadcast_select_fusion), calls=%async_computation | async-start | bytes 1048576 | tf_op jit(solution)/shard_map/all_to_all | solution.py:179
  166.8 2.7 %copy-start.5 = (f32[1024]{0:T(1024)S(1)}, f32[1024]{0:T(1024)}, u32[]{:S(2)}) copy-start(f32[1024]{0:T(1024)} %param.13) | copy-start | bytes 12292
  167.2 6.8 %copy-start.3 = (bf16[2,1024]{1,0:T(2,128)(2,1)S(1)}, bf16[2,1024]{1,0:T(2,128)(2,1)}, u32[]{:S(2)}) copy-start(bf16[2,1024]{1,0:T(2,128)(2,1)} %param.18) | copy-start | bytes 12292
  167.2 21.5 %copy-start.13 = (bf16[2,1024,16]{1,2,0:T(8,128)(2,1)S(1)}, bf16[2,1024,16]{1,2,0:T(8,128)(2,1)}, u32[]{:S(2)}) copy-start(bf16[2,1024,16]{1,2,0:T(8,128)(2,1)} %param.19) | copy-start | bytes 196612
  169.5 22.7 %copy-start.1 = (bf16[136,1024]{1,0:T(8,128)(2,1)}, bf16[136,1024]{1,0:T(8,128)(2,1)S(1)}, u32[]{:S(2)}) copy-start(bf16[136,1024]{1,0:T(8,128)(2,1)S(1)} %get-tuple-element.105) | copy-start | bytes 835588
  169.8 7.7 %collective-permute-start.13 = (bf16[136,1152]{1,0:T(8,128)(2,1)S(1)}, bf16[136,1152]{1,0:T(8,128)(2,1)S(1)}, u32[]{:S(2)}, u32[]{:S(2)}) collective-permute-start(bf16[136,1152]{1,0:T(8,128)(2,1)S(1)} %pad_maximum_fusion.6), channel_id=1, source_target_pairs={{0,1},{1,2},{2,3},{3,0},{4,5},{5,6},{6,7},{7,4},{8,9},{9,10},{10,1... | collective-permute-start | bytes 940040 | tf_op jit(solution)/shard_map/ppermute | solution.py:114
  171.2 16.6 %collective-permute-start.14 = (bf16[136,1152]{1,0:T(8,128)(2,1)S(1)}, bf16[136,1152]{1,0:T(8,128)(2,1)S(1)}, u32[]{:S(2)}, u32[]{:S(2)}) collective-permute-start(bf16[136,1152]{1,0:T(8,128)(2,1)S(1)} %pad_maximum_fusion.6), channel_id=1, source_target_pairs={{0,2},{1,3},{2,0},{3,1},{4,6},{5,7},{6,4},{7,5},{8,10},{9,11},{10,... | collective-permute-start | bytes 940040 | tf_op jit(solution)/shard_map/ppermute | solution.py:114
  174.0 14.4 %collective-permute-start.15 = (bf16[136,1152]{1,0:T(8,128)(2,1)S(1)}, bf16[136,1152]{1,0:T(8,128)(2,1)S(1)}, u32[]{:S(2)}, u32[]{:S(2)}) collective-permute-start(bf16[136,1152]{1,0:T(8,128)(2,1)S(1)} %pad_maximum_fusion.6), channel_id=1, source_target_pairs={{0,3},{1,0},{2,1},{3,2},{4,7},{5,4},{6,5},{7,6},{8,11},{9,8},{10,9... | collective-permute-start | bytes 940040 | tf_op jit(solution)/shard_map/ppermute | solution.py:114
  195.9 1.2 collective-permute-start.16
  195.9 4.2 %collective-permute-start.17 = (f32[136,16]{0,1:T(8,128)S(1)}, f32[136,16]{0,1:T(8,128)S(1)}, u32[]{:S(2)}, u32[]{:S(2)}) collective-permute-start(f32[136,16]{0,1:T(8,128)S(1)} %get-tuple-element.99), channel_id=1, source_target_pairs={{0,2},{1,3},{2,0},{3,1},{4,6},{5,7},{6,4},{7,5},{8,10},{9,11},{10,... | collective-permute-start | bytes 26120 | tf_op jit(solution)/shard_map/ppermute | solution.py:114
  196.1 5.2 %collective-permute-start.18 = (f32[136,16]{0,1:T(8,128)S(1)}, f32[136,16]{0,1:T(8,128)S(1)}, u32[]{:S(2)}, u32[]{:S(2)}) collective-permute-start(f32[136,16]{0,1:T(8,128)S(1)} %get-tuple-element.98), channel_id=1, source_target_pairs={{0,3},{1,0},{2,1},{3,2},{4,7},{5,4},{6,5},{7,6},{8,11},{9,8},{10,9... | collective-permute-start | bytes 26120 | tf_op jit(solution)/shard_map/ppermute | solution.py:114
Sparse Core Ops, SparseCore 0:
  48.3 35.0 all-gather.1

commit v7 on v6

--- a/solution.py
+++ b/solution.py
@@ -12,7 +12,6 @@
 SCALE = HD ** (-0.5)
 QUERY_BLOCK = 544
 ROW_SPLIT = 2
-RING = ("z", "y")
 
 
 def rms_normalize(values):
@@ -139,35 +138,40 @@
     )
     q_pad = mine[:, : 2 * HD]
     chunk = mine[:, 2 * HD :]
-    w_out_dep, chunk = lax.optimization_barrier((w_out, chunk))
-    w_out_all = lax.all_gather(w_out_dep, "type", axis=0, tiled=True)
     z_n = lax.axis_size("z")
-    y_n = lax.axis_size("y")
-    order = [z * y_n for z in range(z_n)] + [z * y_n + 1 for z in reversed(range(z_n))]
-    if y_n != 2:
-        order = list(range(z_n * y_n))
-    n = len(order)
-    right = [(order[i], order[(i + 1) % n]) for i in range(n)]
-    left = [(order[i], order[(i - 1) % n]) for i in range(n)]
-    plan = [[chunk]]
+    zr = [(i, (i + 1) % z_n) for i in range(z_n)]
+    zl = [(i, (i - 1) % z_n) for i in range(z_n)]
+    yy = [(0, 1), (1, 0)]
+    held = [chunk]
     state = None
     done = 0
-    incoming = [lax.ppermute(chunk, RING, right), lax.ppermute(chunk, RING, left)]
-    for d in range(n // 2 + 1):
-        held = plan[-1] if d == 0 else incoming_now
-        if d > 0:
+    total = 2 * z_n
+    w_out_all = None
+    for stage in range(4):
+        if stage == 0:
+            following = [
+                lax.ppermute(chunk, "z", zr),
+                lax.ppermute(chunk, "z", zl),
+                lax.ppermute(chunk, "y", yy),
+            ]
+        elif stage == 1:
+            following = [
+                lax.ppermute(held[0], "z", zr),
+                lax.ppermute(held[2], "z", zr),
+                lax.ppermute(held[2], "z", zl),
+            ]
+        elif stage == 2:
+            following = [lax.ppermute(held[1], "z", zr)]
+        else:
             following = []
-            if d + 1 <= n // 2:
-                following.append(lax.ppermute(held[0], RING, right))
-                if d + 1 < n - (d + 1):
-                    following.append(lax.ppermute(held[1], RING, left))
-        else:
-            following = incoming
         for piece in held:
-            state = flash_step(q_pad, piece, state, done == 0, done == n - 1)
+            state = flash_step(q_pad, piece, state, done == 0, done == total - 1)
             done += 1
         if following:
-            incoming_now, state = lax.optimization_barrier((following, state))
+            held, state = lax.optimization_barrier((following, state))
+        if stage == 0:
+            w_out_dep, held = lax.optimization_barrier((w_out, held))
+            w_out_all = lax.all_gather(w_out_dep, "type", axis=0, tiled=True)
     attended = state[:, HD:]
     rows = tokens.shape[0]
     attended = attended.reshape(-1, rows, HD)

time: 209 us -> 206 us (0.986)
  starting transfers between devices: 32.3 us -> 29.9 us
  transfers between devices with their start and end apart: 21 -> 21, of which waited for: 14 -> 14; matrix products, arithmetic and copies ran while one was open for 4% -> 5% of each run, Pallas kernels for 39% -> 40%
where the time goes in v7:
time: 206 us; the launch traced here: 205 us
  Pallas kernels  81.8 us (40%)
  waiting for transfers between devices  51.3 us (25%)
  starting transfers between devices  29.9 us (15%)
  between operations  14.4 us (7%)
  matrix products  12.2 us (6%)
  local copies, waits for them, and re-layouts  10 us (5%)
  other arithmetic  5.41 us (3%)
    pallas_call x8, Pallas kernels, flash_step(): pl.pallas_call(functools.partial(step_kernel, first, last), grid=(rows //...  81.8 us
    ppermute x12, waiting for transfers between devices, shifted(): return lax.ppermute(value, axis, [(i, (i + k) % n) for i in range(n)])  37.7 us
    ppermute x12, starting transfers between devices, shifted(): return lax.ppermute(value, axis, [(i, (i + k) % n) for i in range(n)])  14.9 us
    all_to_all x1, waiting for transfers between devices, body(): back = lax.all_to_all(attended, ('x', 'type'), 0, 0, tiled=True)  11.1 us
    all_to_all x1, starting transfers between devices, body(): back = lax.all_to_all(attended, ('x', 'type'), 0, 0, tiled=True)  7.41 us
    dot_general x2, matrix products, body(): answer = jnp.dot(hidden, head_w2[which], preferred_element_type=jnp.float32)  7.05 us
  transfers between devices with their start and end apart: 21, of which 14 were waited for; matrix products, arithmetic and copies ran while one was open for 5% of the time, Pallas kernels for 40%

profile of v7, /device:TPU:1, one launch (start us, length us, event | category | flops | bytes accessed | tf_op | source)
XLA Modules:
  0.0 205.1 jit_solution(11286110443275985324)
XLA Ops:
  7.2 0.8 slice_add_fusion.1
  8.0 1.1 fusion.68
  9.1 1.1 fusion.71
  10.2 4.4 %collective-permute-start = (bf16[136,1024]{1,0:T(8,128)(2,1)S(1)}, bf16[136,1024]{1,0:T(8,128)(2,1)S(1)}, u32[]{:S(2)}, u32[]{:S(2)}) collective-permute-start(bf16[136,1024]{1,0:T(8,128)(2,1)S(1)} %fusion.71), channel_id=1, source_target_pairs={{0,1},{1,2},{2,3},{3,0},{4,5},{5,6},{6,7},{7,4},{8,9},{9,10},{10,1... | collective-permute-start | bytes 835592 | tf_op jit(solution)/shard_map/ppermute | solution.py:113
  14.6 0.5 collective-permute-start.2
  15.1 1.5 fusion.103
  16.5 0.2 copy.36
  16.8 0.2 copy.37
  17.0 0.2 copy.38
  17.3 0.2 pad_maximum_fusion
  17.6 0.2 copy.31
  17.8 2.6 %copy.32 = bf16[1024,4,256]{2,0,1:T(8,128)(2,1)} copy(bf16[1024,4,256]{0,2,1:T(8,128)(2,1)S(1)} %bitcast.54) | data formatting | bytes 4194304 | tf_op jit(solution)/shard_map/reshape | solution.py:131
  20.4 0.1 collective-permute-done
  20.5 6.4 %collective-permute-done.1 = bf16[136,1024]{1,0:T(8,128)(2,1)S(1)} collective-permute-done((bf16[136,1024]{1,0:T(8,128)(2,1)S(1)}, bf16[136,1024]{1,0:T(8,128)(2,1)S(1)}, u32[]{:S(2)}, u32[]{:S(2)}) %collective-permute-start.1) | collective-permute-done | bytes 278560 | tf_op jit(solution)/shard_map/ppermute | solution.py:113
  26.8 0.6 collective-permute-done.2
  27.4 3.0 %fusion.28 = bf16[4,544,256]{2,1,0:T(8,128)(2,1)S(1)} fusion(s32[]{:T(128)S(6)} %select_n.108, bf16[1024,4,256]{2,0,1:T(8,128)(2,1)} %copy.32, bf16[136,1024]{1,0:T(8,128)(2,1)S(1)} %collective-permute-done.2, bf16[136,1024]{1,0:T(8,128)(2,1)S(1)} %collective-permute-done.1, bf16[136,1024]{1,0:T(8,128)(2,1)S(1)} %collective-permute-done, ...), kind=kOutput, calls=%fused_computation.31 | convolution fusion | flops 1150058496 | bytes 4325380 | tf_op jit(solution)/shard_map/rd,dje->jre/dot_general | solution.py:133
  30.5 1.3 collective-permute-start.3
  31.8 2.5 %collective-permute-start.4 = (bf16[544,256]{1,0:T(8,128)(2,1)S(1)}, bf16[544,256]{1,0:T(8,128)(2,1)S(1)}, u32[]{:S(2)}, u32[]{:S(2)}) collective-permute-start(bf16[544,256]{1,0:T(8,128)(2,1)S(1)} %get-tuple-element.93), channel_id=1, source_target_pairs={{0,16},{8,24},{16,0},{24,8},{1,17},{9,25},{17,1},{25,9},{2,18},{10... | collective-permute-start | bytes 835592 | tf_op jit(solution)/shard_map/ppermute | solution.py:113
  34.3 1.1 collective-permute-start.5
  35.4 4.7 %collective-permute-done.3 = bf16[544,256]{1,0:T(8,128)(2,1)S(1)} collective-permute-done((bf16[544,256]{1,0:T(8,128)(2,1)S(1)}, bf16[544,256]{1,0:T(8,128)(2,1)S(1)}, u32[]{:S(2)}, u32[]{:S(2)}) %collective-permute-start.3) | collective-permute-done | bytes 278560 | tf_op jit(solution)/shard_map/ppermute | solution.py:113
  40.1 7.1 %collective-permute-done.4 = bf16[544,256]{1,0:T(8,128)(2,1)S(1)} collective-permute-done((bf16[544,256]{1,0:T(8,128)(2,1)S(1)}, bf16[544,256]{1,0:T(8,128)(2,1)S(1)}, u32[]{:S(2)}, u32[]{:S(2)}) %collective-permute-start.4) | collective-permute-done | bytes 278560 | tf_op jit(solution)/shard_map/ppermute | solution.py:113
  47.3 0.9 fusion.104
  48.2 1.7 collective-permute-start.6
  49.9 2.1 %collective-permute-start.7 = (bf16[2176,128]{1,0:T(8,128)(2,1)S(1)}, bf16[2176,128]{1,0:T(8,128)(2,1)S(1)}, u32[]{:S(2)}, u32[]{:S(2)}) collective-permute-start(bf16[2176,128]{1,0:T(8,128)(2,1)S(1)} %get-tuple-element.89.refs_1_), channel_id=1, source_target_pairs={{0,96},{32,0},{64,32},{96,64},{1,97},{33,1},{65,33},{97,65},{2,98}... | collective-permute-start | bytes 1671176 | tf_op jit(solution)/shard_map/ppermute | solution.py:154
  52.0 0.7 collective-permute-start.8
  52.7 10.0 %shard_map.113 = (f32[2176,1]{1,0:T(8,128)}, f32[2176,1]{1,0:T(8,128)}, f32[2176,128]{1,0:T(8,128)}) custom-call(bf16[2176,128]{1,0:T(8,128)(2,1)} %get-tuple-element.90.refs_0_, bf16[2176,128]{1,0:T(8,128)(2,1)} %copy-done.2), custom_call_target="tpu_custom_call" | custom-call | flops 2424307712 | bytes 4456448 | tf_op jit(solution)/shard_map/pallas_call | solution.py:91
  62.7 1.6 collective-permute-done.6.refs_1_
  64.4 0.8 collective-permute-done.8.refs_1_
  65.3 2.7 %collective-permute-start.11 = (bf16[2176,128]{1,0:T(8,128)(2,1)S(1)}, bf16[2176,128]{1,0:T(8,128)(2,1)S(1)}, u32[]{:S(2)}, u32[]{:S(2)}) collective-permute-start(bf16[2176,128]{1,0:T(8,128)(2,1)S(1)} %collective-permute-done.8.refs_1_), channel_id=1, source_target_pairs={{0,96},{32,0},{64,32},{96,64},{1,97},{33,1},{65,33},{97,65},{2,98}... | collective-permute-start | bytes 1671176 | tf_op jit(solution)/shard_map/ppermute | solution.py:161
  68.0 10.3 %shard_map.114 = (f32[2176,1]{1,0:T(8,128)}, f32[2176,1]{1,0:T(8,128)}, f32[2176,128]{1,0:T(8,128)}) custom-call(bf16[2176,128]{1,0:T(8,128)(2,1)} %get-tuple-element.90.refs_0_, bf16[2176,128]{1,0:T(8,128)(2,1)} %copy-done.6, f32[2176,1]{1,0:T(8,128)} %get-tuple-element.52.refs_2_, f32[2176,1]{1,0:T(8,128)} %get-tuple-element.53.refs_3_, ...), custom_call_target="tpu_custom_call" | custom-call | flops 2424307712 | bytes 4456448 | tf_op jit(solution)/shard_map/pallas_call | solution.py:91
  78.3 10.3 %shard_map.115 = (f32[2176,1]{1,0:T(8,128)}, f32[2176,1]{1,0:T(8,128)}, f32[2176,128]{1,0:T(8,128)}) custom-call(bf16[2176,128]{1,0:T(8,128)(2,1)} %get-tuple-element.90.refs_0_, bf16[2176,128]{1,0:T(8,128)(2,1)} %copy-done.10, f32[2176,1]{1,0:T(8,128)} %get-tuple-element.55.refs_2_, f32[2176,1]{1,0:T(8,128)} %get-tuple-element.56.refs_3_, ...), custom_call_target="tpu_custom_call" | custom-call | flops 2424307712 | bytes 4456448 | tf_op jit(solution)/shard_map/pallas_call | solution.py:91
  88.7 10.3 %shard_map.116 = (f32[2176,1]{1,0:T(8,128)}, f32[2176,1]{1,0:T(8,128)}, f32[2176,128]{1,0:T(8,128)}) custom-call(bf16[2176,128]{1,0:T(8,128)(2,1)} %get-tuple-element.90.refs_0_, bf16[2176,128]{1,0:T(8,128)(2,1)} %copy-done.8, f32[2176,1]{1,0:T(8,128)} %get-tuple-element.58.refs_2_, f32[2176,1]{1,0:T(8,128)} %get-tuple-element.59.refs_3_, ...), custom_call_target="tpu_custom_call" | custom-call | flops 2424307712 | bytes 4456448 | tf_op jit(solution)/shard_map/pallas_call | solution.py:91
  99.0 0.3 collective-permute-start.12
  99.3 10.4 %shard_map.117 = (f32[2176,1]{1,0:T(8,128)}, f32[2176,1]{1,0:T(8,128)}, f32[2176,128]{1,0:T(8,128)}) custom-call(bf16[2176,128]{1,0:T(8,128)(2,1)} %get-tuple-element.90.refs_0_, bf16[2176,128]{1,0:T(8,128)(2,1)} %collective-permute-done.9.refs_1_, f32[2176,1]{1,0:T(8,128)} %get-tuple-element.67.refs_2_, f32[2176,1]{1,0:T(8,128)} %get-tuple-element.68.refs_3_, ...), custom_call_target="tpu_custom_call" | custom-call | flops 2424307712 | bytes 4456448 | tf_op jit(solution)/shard_map/pallas_call | solution.py:91
  109.7 10.3 %shard_map.118 = (f32[2176,1]{1,0:T(8,128)}, f32[2176,1]{1,0:T(8,128)}, f32[2176,128]{1,0:T(8,128)}) custom-call(bf16[2176,128]{1,0:T(8,128)(2,1)} %get-tuple-element.90.refs_0_, bf16[2176,128]{1,0:T(8,128)(2,1)} %copy-done.7, f32[2176,1]{1,0:T(8,128)} %get-tuple-element.70.refs_2_, f32[2176,1]{1,0:T(8,128)} %get-tuple-element.71.refs_3_, ...), custom_call_target="tpu_custom_call" | custom-call | flops 2424307712 | bytes 4456448 | tf_op jit(solution)/shard_map/pallas_call | solution.py:91
  120.0 10.3 %shard_map.119 = (f32[2176,1]{1,0:T(8,128)}, f32[2176,1]{1,0:T(8,128)}, f32[2176,128]{1,0:T(8,128)}) custom-call(bf16[2176,128]{1,0:T(8,128)(2,1)} %get-tuple-element.90.refs_0_, bf16[2176,128]{1,0:T(8,128)(2,1)} %copy-done.9, f32[2176,1]{1,0:T(8,128)} %get-tuple-element.73.refs_2_, f32[2176,1]{1,0:T(8,128)} %get-tuple-element.74.refs_3_, ...), custom_call_target="tpu_custom_call" | custom-call | flops 2424307712 | bytes 4456448 | tf_op jit(solution)/shard_map/pallas_call | solution.py:91
  130.3 0.8 copy-done.11
  131.2 9.8 %shard_map.120 = bf16[2176,128]{1,0:T(8,128)(2,1)} custom-call(bf16[2176,128]{1,0:T(8,128)(2,1)} %get-tuple-element.90.refs_0_, bf16[2176,128]{1,0:T(8,128)(2,1)} %copy-done.11, f32[2176,1]{1,0:T(8,128)} %get-tuple-element.80.refs_2_, f32[2176,1]{1,0:T(8,128)} %get-tuple-element.81.refs_3_, f32[2176,128]{1,0:T(8,128)} %get-tuple-element.82.refs_4_), custom_call_target="tpu_custom_call" | custom-call | flops 2424307712 | bytes 4456448 | tf_op jit(solution)/shard_map/pallas_call | solution.py:91
  141.0 1.3 slice.111
  142.3 0.3 copy.34
  142.6 0.6 gather_fusion
  143.2 0.9 broadcast_select_fusion
  144.1 7.4 %all-to-all-start = ((bf16[16,136,64]{1,2,0:T(8,128)(2,1)}), bf16[16,136,64]{1,2,0:T(8,128)(2,1)S(1)}, u32[]{:S(2)}, u32[]{:S(2)}) async-start(bf16[16,136,64]{1,2,0:T(8,128)(2,1)} %broadcast_select_fusion), calls=%async_computation | async-start | bytes 1048576 | tf_op jit(solution)/shard_map/all_to_all | solution.py:183
  151.6 11.1 %all-to-all-done = bf16[16,136,64]{1,2,0:T(8,128)(2,1)S(1)} async-done(((bf16[16,136,64]{1,2,0:T(8,128)(2,1)}), bf16[16,136,64]{1,2,0:T(8,128)(2,1)S(1)}, u32[]{:S(2)}, u32[]{:S(2)}) %all-to-all-start) | async-done | bytes 278560 | tf_op jit(solution)/shard_map/all_to_all | solution.py:183
  162.7 0.6 copy.35
  163.3 0.4 reshape.206
  163.7 2.2 %fusion.65 = (f32[136]{0:T(256)S(1)}, bf16[136,1024]{1,0:T(8,128)(2,1)S(1)}) fusion(bf16[136,1024]{1,0:T(8,128)(2,1)S(1)} %reshape.206, bf16[1024,1024]{1,0:T(8,128)(2,1)} %all-gather.2.cloned.1.call-done, f32[1024]{0:T(1024)S(1)} %copy-done.4, bf16[136,1024]{1,0:T(8,128)(2,1)S(1)} %copy-done), kind=kOutput, calls=%fused_computation.65 | convolution fusion | flops 286187392 | bytes 2937376 | tf_op jit(solution)/shard_map/dot_general | solution.py:186
  165.9 0.1 fusion.67
  166.1 0.1 broadcast_in_dim.49
  166.2 1.4 collective-permute-start.13
  167.6 2.9 %collective-permute-start.14 = (bf16[136,1152]{1,0:T(8,128)(2,1)S(1)}, bf16[136,1152]{1,0:T(8,128)(2,1)S(1)}, u32[]{:S(2)}, u32[]{:S(2)}) collective-permute-start(bf16[136,1152]{1,0:T(8,128)(2,1)S(1)} %pad_maximum_fusion.6), channel_id=1, source_target_pairs={{0,2},{1,3},{2,0},{3,1},{4,6},{5,7},{6,4},{7,5},{8,10},{9,11},{10,... | collective-permute-start | bytes 940040 | tf_op jit(solution)/shard_map/ppermute | solution.py:113
  170.5 3.5 %collective-permute-done.13 = bf16[136,1152]{1,0:T(8,128)(2,1)S(1)} collective-permute-done((bf16[136,1152]{1,0:T(8,128)(2,1)S(1)}, bf16[136,1152]{1,0:T(8,128)(2,1)S(1)}, u32[]{:S(2)}, u32[]{:S(2)}) %collective-permute-start.13) | collective-permute-done | bytes 313376 | tf_op jit(solution)/shard_map/ppermute | solution.py:113
  174.0 10.3 %collective-permute-done.14 = bf16[136,1152]{1,0:T(8,128)(2,1)S(1)} collective-permute-done((bf16[136,1152]{1,0:T(8,128)(2,1)S(1)}, bf16[136,1152]{1,0:T(8,128)(2,1)S(1)}, u32[]{:S(2)}, u32[]{:S(2)}) %collective-permute-start.14) | collective-permute-done | bytes 313376 | tf_op jit(solution)/shard_map/ppermute | solution.py:113
  184.2 0.6 collective-permute-done.15
  184.8 0.3 fusion.72
  185.1 3.5 %fusion.59 = f32[544,16]{0,1:T(8,128)S(1)} fusion(bf16[2,1024,1024]{2,1,0:T(8,128)(2,1)} %param.17, f32[1024]{0:T(1024)S(1)} %bitcast.63, bf16[2,1024,16]{1,2,0:T(8,128)(2,1)S(1)} %copy-done.12, pred[544]{0:T(1024)(128)(4,1)S(1)} %get-tuple-element.85, bf16[136,1152]{1,0:T(8,128)(2,1)S(1)} %collective-permute-done.15, ...), kind=kOutput, calls=%fused_computation.59 | convolution fusion | flops 1169826304 | bytes 3423232 | tf_op jit(solution)/shard_map/dot_general | solution.py:200
  188.6 3.5 %fusion.62 = f32[544,16]{0,1:T(8,128)S(1)} fusion(f32[544,16]{0,1:T(8,128)S(1)} %fusion.59, bf16[2,1024,1024]{2,1,0:T(8,128)(2,1)} %param.17, f32[1024]{0:T(1024)S(1)} %bitcast.62, bf16[2,1024,16]{1,2,0:T(8,128)(2,1)S(1)} %copy-done.12, pred[544]{0:T(1024)(128)(4,1)S(1)} %get-tuple-element.84, bf16[136,1152]{1,0:T(8,128)(2,1)S(1)} %collective-permute-done.15, ...), kind=kOutput, calls=%fused_computation.60 | convolution fusion | flops 1169826304 | bytes 3464192 | tf_op jit(solution)/shard_map/dot_general | solution.py:200
  192.2 0.1 fusion.105
  192.3 0.2 collective-permute-start.17
  192.5 0.7 collective-permute-start.18
  193.2 0.3 collective-permute-done.16
  193.5 3.0 %collective-permute-done.17 = f32[136,16]{0,1:T(8,128)S(1)} collective-permute-done((f32[136,16]{0,1:T(8,128)S(1)}, f32[136,16]{0,1:T(8,128)S(1)}, u32[]{:S(2)}, u32[]{:S(2)}) %collective-permute-start.17) | collective-permute-done | bytes 8736 | tf_op jit(solution)/shard_map/ppermute | solution.py:113
  196.5 1.2 collective-permute-done.18
  197.6 0.6 fusion.79
  (53 shorter events, 0.7 us)
Async XLA Ops:
  7.2 156.5 %all-gather.2.cloned.1.call-start = ((), (), s32[]{:S(2)}) async-start(), calls=%async_computation.1 | async-start | bytes 2621440 | tf_op jit(solution)/shard_map/all_gather | solution.py:174
  10.2 10.3 %collective-permute-start = (bf16[136,1024]{1,0:T(8,128)(2,1)S(1)}, bf16[136,1024]{1,0:T(8,128)(2,1)S(1)}, u32[]{:S(2)}, u32[]{:S(2)}) collective-permute-start(bf16[136,1024]{1,0:T(8,128)(2,1)S(1)} %fusion.71), channel_id=1, source_target_pairs={{0,1},{1,2},{2,3},{3,0},{4,5},{5,6},{6,7},{7,4},{8,9},{9,10},{10,1... | collective-permute-start | bytes 835592 | tf_op jit(solution)/shard_map/ppermute | solution.py:113
  14.6 12.2 %collective-permute-start.1 = (bf16[136,1024]{1,0:T(8,128)(2,1)S(1)}, bf16[136,1024]{1,0:T(8,128)(2,1)S(1)}, u32[]{:S(2)}, u32[]{:S(2)}) collective-permute-start(bf16[136,1024]{1,0:T(8,128)(2,1)S(1)} %fusion.71), channel_id=1, source_target_pairs={{0,2},{1,3},{2,0},{3,1},{4,6},{5,7},{6,4},{7,5},{8,10},{9,11},{10,... | collective-permute-start | bytes 835592 | tf_op jit(solution)/shard_map/ppermute | solution.py:113
  14.6 12.8 %collective-permute-start.2 = (bf16[136,1024]{1,0:T(8,128)(2,1)S(1)}, bf16[136,1024]{1,0:T(8,128)(2,1)S(1)}, u32[]{:S(2)}, u32[]{:S(2)}) collective-permute-start(bf16[136,1024]{1,0:T(8,128)(2,1)S(1)} %fusion.71), channel_id=1, source_target_pairs={{0,3},{1,0},{2,1},{3,2},{4,7},{5,4},{6,5},{7,6},{8,11},{9,8},{10,9... | collective-permute-start | bytes 835592 | tf_op jit(solution)/shard_map/ppermute | solution.py:113
  30.5 9.6 %collective-permute-start.3 = (bf16[544,256]{1,0:T(8,128)(2,1)S(1)}, bf16[544,256]{1,0:T(8,128)(2,1)S(1)}, u32[]{:S(2)}, u32[]{:S(2)}) collective-permute-start(bf16[544,256]{1,0:T(8,128)(2,1)S(1)} %get-tuple-element.94), channel_id=1, source_target_pairs={{0,8},{8,16},{16,24},{24,0},{1,9},{9,17},{17,25},{25,1},{2,10},{10... | collective-permute-start | bytes 835592 | tf_op jit(solution)/shard_map/ppermute | solution.py:113
  31.8 15.4 %collective-permute-start.4 = (bf16[544,256]{1,0:T(8,128)(2,1)S(1)}, bf16[544,256]{1,0:T(8,128)(2,1)S(1)}, u32[]{:S(2)}, u32[]{:S(2)}) collective-permute-start(bf16[544,256]{1,0:T(8,128)(2,1)S(1)} %get-tuple-element.93), channel_id=1, source_target_pairs={{0,16},{8,24},{16,0},{24,8},{1,17},{9,25},{17,1},{25,9},{2,18},{10... | collective-permute-start | bytes 835592 | tf_op jit(solution)/shard_map/ppermute | solution.py:113
  34.3 12.9 %collective-permute-start.5 = (bf16[544,256]{1,0:T(8,128)(2,1)S(1)}, bf16[544,256]{1,0:T(8,128)(2,1)S(1)}, u32[]{:S(2)}, u32[]{:S(2)}) collective-permute-start(bf16[544,256]{1,0:T(8,128)(2,1)S(1)} %get-tuple-element.92), channel_id=1, source_target_pairs={{0,24},{8,0},{16,8},{24,16},{1,25},{9,1},{17,9},{25,17},{2,26},{10... | collective-permute-start | bytes 835592 | tf_op jit(solution)/shard_map/ppermute | solution.py:113
  48.2 4.5 %copy-start.2 = (bf16[2176,128]{1,0:T(8,128)(2,1)}, bf16[2176,128]{1,0:T(8,128)(2,1)S(1)}, u32[]{:S(2)}) copy-start(bf16[2176,128]{1,0:T(8,128)(2,1)S(1)} %get-tuple-element.89.refs_1_) | copy-start | bytes 1671172
  48.2 16.1 %collective-permute-start.6 = (bf16[2176,128]{1,0:T(8,128)(2,1)S(1)}, bf16[2176,128]{1,0:T(8,128)(2,1)S(1)}, u32[]{:S(2)}, u32[]{:S(2)}) collective-permute-start(bf16[2176,128]{1,0:T(8,128)(2,1)S(1)} %get-tuple-element.89.refs_1_), channel_id=1, source_target_pairs={{0,32},{32,64},{64,96},{96,0},{1,33},{33,65},{65,97},{97,1},{2,34}... | collective-permute-start | bytes 1671176 | tf_op jit(solution)/shard_map/ppermute | solution.py:153
  49.9 14.5 %collective-permute-start.7 = (bf16[2176,128]{1,0:T(8,128)(2,1)S(1)}, bf16[2176,128]{1,0:T(8,128)(2,1)S(1)}, u32[]{:S(2)}, u32[]{:S(2)}) collective-permute-start(bf16[2176,128]{1,0:T(8,128)(2,1)S(1)} %get-tuple-element.89.refs_1_), channel_id=1, source_target_pairs={{0,96},{32,0},{64,32},{96,64},{1,97},{33,1},{65,33},{97,65},{2,98}... | collective-permute-start | bytes 1671176 | tf_op jit(solution)/shard_map/ppermute | solution.py:154
  52.0 13.2 %collective-permute-start.8 = (bf16[2176,128]{1,0:T(8,128)(2,1)S(1)}, bf16[2176,128]{1,0:T(8,128)(2,1)S(1)}, u32[]{:S(2)}, u32[]{:S(2)}) collective-permute-start(bf16[2176,128]{1,0:T(8,128)(2,1)S(1)} %get-tuple-element.89.refs_1_), channel_id=1, source_target_pairs={{0,4},{4,0},{1,5},{5,1},{2,6},{6,2},{3,7},{7,3},{8,12},{12,8},{9,1... | collective-permute-start | bytes 1671176 | tf_op jit(solution)/shard_map/ppermute | solution.py:155
  64.3 3.7 %copy-start.6 = (bf16[2176,128]{1,0:T(8,128)(2,1)}, bf16[2176,128]{1,0:T(8,128)(2,1)S(1)}, u32[]{:S(2)}) copy-start(bf16[2176,128]{1,0:T(8,128)(2,1)S(1)} %collective-permute-done.6.refs_1_) | copy-start | bytes 1671172
  64.3 14.0 %copy-start.10 = (bf16[2176,128]{1,0:T(8,128)(2,1)}, bf16[2176,128]{1,0:T(8,128)(2,1)S(1)}, u32[]{:S(2)}) copy-start(bf16[2176,128]{1,0:T(8,128)(2,1)S(1)} %collective-permute-done.7.refs_1_) | copy-start | bytes 1671172
  65.2 13.2 %copy-start.8 = (bf16[2176,128]{1,0:T(8,128)(2,1)}, bf16[2176,128]{1,0:T(8,128)(2,1)S(1)}, u32[]{:S(2)}) copy-start(bf16[2176,128]{1,0:T(8,128)(2,1)S(1)} %collective-permute-done.8.refs_1_) | copy-start | bytes 1671172
  65.3 33.7 %collective-permute-start.10 = (bf16[2176,128]{1,0:T(8,128)(2,1)S(1)}, bf16[2176,128]{1,0:T(8,128)(2,1)S(1)}, u32[]{:S(2)}, u32[]{:S(2)}) collective-permute-start(bf16[2176,128]{1,0:T(8,128)(2,1)S(1)} %collective-permute-done.8.refs_1_), channel_id=1, source_target_pairs={{0,32},{32,64},{64,96},{96,0},{1,33},{33,65},{65,97},{97,1},{2,34}... | collective-permute-start | bytes 1671176 | tf_op jit(solution)/shard_map/ppermute | solution.py:160
  65.3 33.7 %collective-permute-start.11 = (bf16[2176,128]{1,0:T(8,128)(2,1)S(1)}, bf16[2176,128]{1,0:T(8,128)(2,1)S(1)}, u32[]{:S(2)}, u32[]{:S(2)}) collective-permute-start(bf16[2176,128]{1,0:T(8,128)(2,1)S(1)} %collective-permute-done.8.refs_1_), channel_id=1, source_target_pairs={{0,96},{32,0},{64,32},{96,64},{1,97},{33,1},{65,33},{97,65},{2,98}... | collective-permute-start | bytes 1671176 | tf_op jit(solution)/shard_map/ppermute | solution.py:161
  68.0 31.0 %collective-permute-start.9 = (bf16[2176,128]{1,0:T(8,128)(2,1)S(1)}, bf16[2176,128]{1,0:T(8,128)(2,1)}, u32[]{:S(2)}, u32[]{:S(2)}) collective-permute-start(bf16[2176,128]{1,0:T(8,128)(2,1)S(1)} %collective-permute-done.6.refs_1_), channel_id=1, source_target_pairs={{0,32},{32,64},{64,96},{96,0},{1,33},{33,65},{65,97},{97,1},{2,34}... | collective-permute-start | bytes 1671176 | tf_op jit(solution)/shard_map/ppermute | solution.py:159
  99.0 10.7 %copy-start.7 = (bf16[2176,128]{1,0:T(8,128)(2,1)}, bf16[2176,128]{1,0:T(8,128)(2,1)S(1)}, u32[]{:S(2)}) copy-start(bf16[2176,128]{1,0:T(8,128)(2,1)S(1)} %collective-permute-done.10.refs_1_) | copy-start | bytes 1671172
  99.0 10.7 %copy-start.9 = (bf16[2176,128]{1,0:T(8,128)(2,1)}, bf16[2176,128]{1,0:T(8,128)(2,1)S(1)}, u32[]{:S(2)}) copy-start(bf16[2176,128]{1,0:T(8,128)(2,1)S(1)} %collective-permute-done.11.refs_1_) | copy-start | bytes 1671172
  99.0 31.3 %collective-permute-start.12 = (bf16[2176,128]{1,0:T(8,128)(2,1)S(1)}, bf16[2176,128]{1,0:T(8,128)(2,1)S(1)}, u32[]{:S(2)}, u32[]{:S(2)}) collective-permute-start(bf16[2176,128]{1,0:T(8,128)(2,1)S(1)} %collective-permute-done.10.refs_1_), channel_id=1, source_target_pairs={{0,32},{32,64},{64,96},{96,0},{1,33},{33,65},{65,97},{97,1},{2,34}... | collective-permute-start | bytes 1671176 | tf_op jit(solution)/shard_map/ppermute | solution.py:164
  130.3 0.8 copy-start.11
  142.2 9.3 %copy-start.13 = (s32[136,1]{0,1:T(1,128)S(1)}, s32[136,1]{0,1:T(1,128)}, u32[]{:S(2)}) copy-start(s32[136,1]{0,1:T(1,128)} %param.16) | copy-start | bytes 1636
  143.2 20.5 %copy-start = (bf16[136,1024]{1,0:T(8,128)(2,1)S(1)}, bf16[136,1024]{1,0:T(8,128)(2,1)}, u32[]{:S(2)}) copy-start(bf16[136,1024]{1,0:T(8,128)(2,1)} %param.10) | copy-start | bytes 835588
  143.2 20.5 %copy-start.4 = (f32[1024]{0:T(1024)S(1)}, f32[1024]{0:T(1024)}, u32[]{:S(2)}) copy-start(f32[1024]{0:T(1024)} %param.12) | copy-start | bytes 12292
  144.1 18.5 %all-to-all-start = ((bf16[16,136,64]{1,2,0:T(8,128)(2,1)}), bf16[16,136,64]{1,2,0:T(8,128)(2,1)S(1)}, u32[]{:S(2)}, u32[]{:S(2)}) async-start(bf16[16,136,64]{1,2,0:T(8,128)(2,1)} %broadcast_select_fusion), calls=%async_computation | async-start | bytes 1048576 | tf_op jit(solution)/shard_map/all_to_all | solution.py:183
  163.3 2.7 %copy-start.5 = (f32[1024]{0:T(1024)S(1)}, f32[1024]{0:T(1024)}, u32[]{:S(2)}) copy-start(f32[1024]{0:T(1024)} %param.13) | copy-start | bytes 12292
  163.6 6.8 %copy-start.3 = (bf16[2,1024]{1,0:T(2,128)(2,1)S(1)}, bf16[2,1024]{1,0:T(2,128)(2,1)}, u32[]{:S(2)}) copy-start(bf16[2,1024]{1,0:T(2,128)(2,1)} %param.18) | copy-start | bytes 12292
  163.6 21.5 %copy-start.12 = (bf16[2,1024,16]{1,2,0:T(8,128)(2,1)S(1)}, bf16[2,1024,16]{1,2,0:T(8,128)(2,1)}, u32[]{:S(2)}) copy-start(bf16[2,1024,16]{1,2,0:T(8,128)(2,1)} %param.19) | copy-start | bytes 196612
  165.9 22.7 %copy-start.1 = (bf16[136,1024]{1,0:T(8,128)(2,1)}, bf16[136,1024]{1,0:T(8,128)(2,1)S(1)}, u32[]{:S(2)}) copy-start(bf16[136,1024]{1,0:T(8,128)(2,1)S(1)} %get-tuple-element.103) | copy-start | bytes 835588
  166.2 7.7 %collective-permute-start.13 = (bf16[136,1152]{1,0:T(8,128)(2,1)S(1)}, bf16[136,1152]{1,0:T(8,128)(2,1)S(1)}, u32[]{:S(2)}, u32[]{:S(2)}) collective-permute-start(bf16[136,1152]{1,0:T(8,128)(2,1)S(1)} %pad_maximum_fusion.6), channel_id=1, source_target_pairs={{0,1},{1,2},{2,3},{3,0},{4,5},{5,6},{6,7},{7,4},{8,9},{9,10},{10,1... | collective-permute-start | bytes 940040 | tf_op jit(solution)/shard_map/ppermute | solution.py:113
  167.6 16.6 %collective-permute-start.14 = (bf16[136,1152]{1,0:T(8,128)(2,1)S(1)}, bf16[136,1152]{1,0:T(8,128)(2,1)S(1)}, u32[]{:S(2)}, u32[]{:S(2)}) collective-permute-start(bf16[136,1152]{1,0:T(8,128)(2,1)S(1)} %pad_maximum_fusion.6), channel_id=1, source_target_pairs={{0,2},{1,3},{2,0},{3,1},{4,6},{5,7},{6,4},{7,5},{8,10},{9,11},{10,... | collective-permute-start | bytes 940040 | tf_op jit(solution)/shard_map/ppermute | solution.py:113
  170.5 14.4 %collective-permute-start.15 = (bf16[136,1152]{1,0:T(8,128)(2,1)S(1)}, bf16[136,1152]{1,0:T(8,128)(2,1)S(1)}, u32[]{:S(2)}, u32[]{:S(2)}) collective-permute-start(bf16[136,1152]{1,0:T(8,128)(2,1)S(1)} %pad_maximum_fusion.6), channel_id=1, source_target_pairs={{0,3},{1,0},{2,1},{3,2},{4,7},{5,4},{6,5},{7,6},{8,11},{9,8},{10,9... | collective-permute-start | bytes 940040 | tf_op jit(solution)/shard_map/ppermute | solution.py:113
  192.3 1.2 collective-permute-start.16
  192.3 4.2 %collective-permute-start.17 = (f32[136,16]{0,1:T(8,128)S(1)}, f32[136,16]{0,1:T(8,128)S(1)}, u32[]{:S(2)}, u32[]{:S(2)}) collective-permute-start(f32[136,16]{0,1:T(8,128)S(1)} %get-tuple-element.97), channel_id=1, source_target_pairs={{0,2},{1,3},{2,0},{3,1},{4,6},{5,7},{6,4},{7,5},{8,10},{9,11},{10,... | collective-permute-start | bytes 26120 | tf_op jit(solution)/shard_map/ppermute | solution.py:113
  192.5 5.2 %collective-permute-start.18 = (f32[136,16]{0,1:T(8,128)S(1)}, f32[136,16]{0,1:T(8,128)S(1)}, u32[]{:S(2)}, u32[]{:S(2)}) collective-permute-start(f32[136,16]{0,1:T(8,128)S(1)} %get-tuple-element.96), channel_id=1, source_target_pairs={{0,3},{1,0},{2,1},{3,2},{4,7},{5,4},{6,5},{7,6},{8,11},{9,8},{10,9... | collective-permute-start | bytes 26120 | tf_op jit(solution)/shard_map/ppermute | solution.py:113
Sparse Core Ops, SparseCore 0:
  65.3 26.3 all-gather.1

commit v8 on v7

--- a/solution.py
+++ b/solution.py
@@ -28,14 +28,19 @@
         rest = refs[5:]
     m_s, l_s, acc_s = rest[-3:]
     outs = rest[:-3]
-    if first:
-        m_s[...] = jnp.full(m_s.shape, -jnp.inf, jnp.float32)
-        l_s[...] = jnp.zeros(l_s.shape, jnp.float32)
-        acc_s[...] = jnp.zeros(acc_s.shape, jnp.float32)
-    else:
-        m_s[...] = m_in[...]
-        l_s[...] = l_in[...]
-        acc_s[...] = acc_in[...]
+    chunk = pl.program_id(1)
+
+    @pl.when(chunk == 0)
+    def _():
+        if first:
+            m_s[...] = jnp.full(m_s.shape, -jnp.inf, jnp.float32)
+            l_s[...] = jnp.zeros(l_s.shape, jnp.float32)
+            acc_s[...] = jnp.zeros(acc_s.shape, jnp.float32)
+        else:
+            m_s[...] = m_in[...]
+            l_s[...] = l_in[...]
+            acc_s[...] = acc_in[...]
+
     kv = kv_ref[...]
     rows = q_ref.shape[0] // ROW_SPLIT
     scores = []
@@ -59,21 +64,24 @@
             weights.astype(jnp.bfloat16), kv, preferred_element_type=jnp.float32
         )
         m_s[part, :] = m_new
-    if last:
-        outs[0][...] = (acc_s[...] / l_s[...]).astype(outs[0].dtype)
-    else:
-        outs[0][...] = m_s[...]
-        outs[1][...] = l_s[...]
-        outs[2][...] = acc_s[...]
+
+    @pl.when(chunk == pl.num_programs(1) - 1)
+    def _():
+        if last:
+            outs[0][...] = (acc_s[...] / l_s[...]).astype(outs[0].dtype)
+        else:
+            outs[0][...] = m_s[...]
+            outs[1][...] = l_s[...]
+            outs[2][...] = acc_s[...]
 
 
 def flash_step(q_pad, kv, state, first, last):
     rows, width = q_pad.shape
-    chunk = kv.shape[0]
+    chunks, chunk = kv.shape[:2]
     block = QUERY_BLOCK
-    row_block = pl.BlockSpec((block, width), lambda i: (i, 0))
-    stat_block = pl.BlockSpec((block, 1), lambda i: (i, 0))
-    in_specs = [row_block, pl.BlockSpec((chunk, width), lambda i: (0, 0))]
+    row_block = pl.BlockSpec((block, width), lambda i, c: (i, 0))
+    stat_block = pl.BlockSpec((block, 1), lambda i, c: (i, 0))
+    in_specs = [row_block, pl.BlockSpec((None, chunk, width), lambda i, c: (c, 0, 0))]
     operands = [q_pad, kv]
     if not first:
         in_specs += [stat_block, stat_block, row_block]
@@ -90,7 +98,7 @@
         ]
     return pl.pallas_call(
         functools.partial(step_kernel, first, last),
-        grid=(rows // block,),
+        grid=(rows // block, chunks),
         in_specs=in_specs,
         out_specs=out_specs,
         out_shape=out_shape,
@@ -99,11 +107,11 @@
             pltpu.VMEM((block, 1), jnp.float32),
             pltpu.VMEM((block, width), jnp.float32),
         ],
-        compiler_params=pltpu.CompilerParams(dimension_semantics=("arbitrary",)),
+        compiler_params=pltpu.CompilerParams(dimension_semantics=("arbitrary", "arbitrary")),
         cost_estimate=pl.CostEstimate(
-            flops=4 * rows * chunk * width,
-            transcendentals=rows * chunk,
-            bytes_accessed=rows * width * 14 + chunk * width * 2,
+            flops=4 * rows * chunks * chunk * width,
+            transcendentals=rows * chunks * chunk,
+            bytes_accessed=rows * width * 14 + (rows // block) * chunks * chunk * width * 2,
         ),
     )(*operands)
 
@@ -144,8 +152,6 @@
     yy = [(0, 1), (1, 0)]
     held = [chunk]
     state = None
-    done = 0
-    total = 2 * z_n
     w_out_all = None
     for stage in range(4):
         if stage == 0:
@@ -164,9 +170,7 @@
             following = [lax.ppermute(held[1], "z", zr)]
         else:
             following = []
-        for piece in held:
-            state = flash_step(q_pad, piece, state, done == 0, done == total - 1)
-            done += 1
+        state = flash_step(q_pad, jnp.stack(held), state, stage == 0, stage == 3)
         if following:
             held, state = lax.optimization_barrier((following, state))
         if stage == 0:

time: 206 us -> 199 us (0.966)
  Pallas kernels: 81.8 us -> 72.2 us
  other arithmetic: 5.41 us -> 8.13 us
    pallas_call x8 -> x4, Pallas kernels: 81.8 us -> 72.2 us  [flash_step(): pl.pallas_call(functools.partial(step_kernel, first, last), grid=(rows //...]
    another operation x0 -> x2, other arithmetic: none -> 2.73 us  [body(): state = flash_step(q_pad, jnp.stack(held), state, stage == 0, stage == 3)]
  transfers between devices with their start and end apart: 21 -> 21, of which waited for: 14 -> 14; matrix products, arithmetic and copies ran while one was open for 5% -> 6% of each run, Pallas kernels for 40% -> 36%
where the time goes in v8:
time: 199 us; the launch traced here: 198 us
  Pallas kernels  72.2 us (36%)
  waiting for transfers between devices  51.3 us (26%)
  starting transfers between devices  29.7 us (15%)
  between operations  14.4 us (7%)
  matrix products  12.2 us (6%)
  local copies, waits for them, and re-layouts  10.4 us (5%)
  other arithmetic  8.13 us (4%)
    pallas_call x4, Pallas kernels, flash_step(): pl.pallas_call(functools.partial(step_kernel, first, last), grid=(rows //...  72.2 us
    ppermute x12, waiting for transfers between devices, shifted(): return lax.ppermute(value, axis, [(i, (i + k) % n) for i in range(n)])  37.7 us
    ppermute x12, starting transfers between devices, shifted(): return lax.ppermute(value, axis, [(i, (i + k) % n) for i in range(n)])  14.9 us
    all_to_all x1, waiting for transfers between devices, body(): back = lax.all_to_all(attended, ('x', 'type'), 0, 0, tiled=True)  11.1 us
    all_to_all x1, starting transfers between devices, body(): back = lax.all_to_all(attended, ('x', 'type'), 0, 0, tiled=True)  7.46 us
    dot_general x2, matrix products, body(): answer = jnp.dot(hidden, head_w2[which], preferred_element_type=jnp.float32)  7.06 us
  transfers between devices with their start and end apart: 21, of which 14 were waited for; matrix products, arithmetic and copies ran while one was open for 6% of the time, Pallas kernels for 36%

profile of v8, /device:TPU:1, one launch (start us, length us, event | category | flops | bytes accessed | tf_op | source)
XLA Modules:
  0.0 198.4 jit_solution(13943954271651873872)
XLA Ops:
  7.2 0.8 slice_add_fusion.1
  8.0 1.1 fusion.68
  9.1 1.1 fusion.71
  10.2 4.4 %collective-permute-start = (bf16[136,1024]{1,0:T(8,128)(2,1)S(1)}, bf16[136,1024]{1,0:T(8,128)(2,1)S(1)}, u32[]{:S(2)}, u32[]{:S(2)}) collective-permute-start(bf16[136,1024]{1,0:T(8,128)(2,1)S(1)} %fusion.71), channel_id=1, source_target_pairs={{0,1},{1,2},{2,3},{3,0},{4,5},{5,6},{6,7},{7,4},{8,9},{9,10},{10,1... | collective-permute-start | bytes 835592 | tf_op jit(solution)/shard_map/ppermute | solution.py:121
  14.6 0.5 collective-permute-start.2
  15.1 1.5 fusion.103
  16.5 0.2 copy.36
  16.8 0.2 copy.37
  17.0 0.2 copy.38
  17.3 0.1 pad.20.clone
  17.3 0.2 pad_maximum_fusion
  17.6 0.2 copy.31
  17.8 2.6 %copy.32 = bf16[1024,4,256]{2,0,1:T(8,128)(2,1)} copy(bf16[1024,4,256]{0,2,1:T(8,128)(2,1)S(1)} %bitcast.63) | data formatting | bytes 4194304 | tf_op jit(solution)/shard_map/reshape | solution.py:139
  20.4 0.1 collective-permute-done
  20.5 6.4 %collective-permute-done.1 = bf16[136,1024]{1,0:T(8,128)(2,1)S(1)} collective-permute-done((bf16[136,1024]{1,0:T(8,128)(2,1)S(1)}, bf16[136,1024]{1,0:T(8,128)(2,1)S(1)}, u32[]{:S(2)}, u32[]{:S(2)}) %collective-permute-start.1) | collective-permute-done | bytes 278560 | tf_op jit(solution)/shard_map/ppermute | solution.py:121
  26.8 0.6 collective-permute-done.2
  27.4 3.0 %fusion.28 = bf16[4,544,256]{2,1,0:T(8,128)(2,1)S(1)} fusion(s32[]{:T(128)S(6)} %select_n.108, bf16[1024,4,256]{2,0,1:T(8,128)(2,1)} %copy.32, bf16[136,1024]{1,0:T(8,128)(2,1)S(1)} %collective-permute-done.2, bf16[136,1024]{1,0:T(8,128)(2,1)S(1)} %collective-permute-done.1, bf16[136,1024]{1,0:T(8,128)(2,1)S(1)} %collective-permute-done, ...), kind=kOutput, calls=%fused_computation.33 | convolution fusion | flops 1150058496 | bytes 4325380 | tf_op jit(solution)/shard_map/rd,dje->jre/dot_general | solution.py:141
  30.5 1.3 collective-permute-start.3
  31.8 2.5 %collective-permute-start.4 = (bf16[544,256]{1,0:T(8,128)(2,1)S(1)}, bf16[544,256]{1,0:T(8,128)(2,1)S(1)}, u32[]{:S(2)}, u32[]{:S(2)}) collective-permute-start(bf16[544,256]{1,0:T(8,128)(2,1)S(1)} %get-tuple-element.70), channel_id=1, source_target_pairs={{0,16},{8,24},{16,0},{24,8},{1,17},{9,25},{17,1},{25,9},{2,18},{10... | collective-permute-start | bytes 835592 | tf_op jit(solution)/shard_map/ppermute | solution.py:121
  34.3 1.1 collective-permute-start.5
  35.4 4.7 %collective-permute-done.3 = bf16[544,256]{1,0:T(8,128)(2,1)S(1)} collective-permute-done((bf16[544,256]{1,0:T(8,128)(2,1)S(1)}, bf16[544,256]{1,0:T(8,128)(2,1)S(1)}, u32[]{:S(2)}, u32[]{:S(2)}) %collective-permute-start.3) | collective-permute-done | bytes 278560 | tf_op jit(solution)/shard_map/ppermute | solution.py:121
  40.1 7.1 %collective-permute-done.4 = bf16[544,256]{1,0:T(8,128)(2,1)S(1)} collective-permute-done((bf16[544,256]{1,0:T(8,128)(2,1)S(1)}, bf16[544,256]{1,0:T(8,128)(2,1)S(1)}, u32[]{:S(2)}, u32[]{:S(2)}) %collective-permute-start.4) | collective-permute-done | bytes 278560 | tf_op jit(solution)/shard_map/ppermute | solution.py:121
  47.3 1.3 slice_bitcast_fusion.4
  48.6 1.7 collective-permute-start.6
  50.2 2.1 %collective-permute-start.7 = (bf16[2176,128]{1,0:T(8,128)(2,1)S(1)}, bf16[2176,128]{1,0:T(8,128)(2,1)S(1)}, u32[]{:S(2)}, u32[]{:S(2)}) collective-permute-start(bf16[2176,128]{1,0:T(8,128)(2,1)S(1)} %get-tuple-element.66), channel_id=1, source_target_pairs={{0,96},{32,0},{64,32},{96,64},{1,97},{33,1},{65,33},{97,65},{2,98}... | collective-permute-start | bytes 1671176 | tf_op jit(solution)/shard_map/ppermute | solution.py:160
  52.3 0.7 collective-permute-start.8
  53.0 10.0 %shard_map.113 = (f32[2176,1]{1,0:T(8,128)}, f32[2176,1]{1,0:T(8,128)}, f32[2176,128]{1,0:T(8,128)}) custom-call(bf16[2176,128]{1,0:T(8,128)(2,1)} %get-tuple-element.67.refs_0_, bf16[1,2176,128]{2,1,0:T(8,128)(2,1)} %get-tuple-element.65.refs_1_), custom_call_target="tpu_custom_call" | custom-call | flops 2424307712 | bytes 6127616 | tf_op jit(solution)/shard_map/pallas_call | solution.py:99
  63.1 1.6 collective-permute-done.6
  64.7 0.8 collective-permute-done.8
  65.6 0.1 collective-permute-start.10
  65.7 2.7 %collective-permute-start.11 = (bf16[2176,128]{1,0:T(8,128)(2,1)S(1)}, bf16[2176,128]{1,0:T(8,128)(2,1)S(1)}, u32[]{:S(2)}, u32[]{:S(2)}) collective-permute-start(bf16[2176,128]{1,0:T(8,128)(2,1)S(1)} %collective-permute-done.8), channel_id=1, source_target_pairs={{0,96},{32,0},{64,32},{96,64},{1,97},{33,1},{65,33},{97,65},{2,98}... | collective-permute-start | bytes 1671176 | tf_op jit(solution)/shard_map/ppermute | solution.py:167
  68.4 1.4 pad_maximum_fusion.1.refs_1_
  69.7 26.2 %shard_map.114 = (f32[2176,1]{1,0:T(8,128)}, f32[2176,1]{1,0:T(8,128)}, f32[2176,128]{1,0:T(8,128)}) custom-call(bf16[2176,128]{1,0:T(8,128)(2,1)} %get-tuple-element.67.refs_0_, bf16[3,2176,128]{2,1,0:T(8,128)(2,1)} %pad_maximum_fusion.1.refs_1_, f32[2176,1]{1,0:T(8,128)} %get-tuple-element.40.refs_2_, f32[2176,1]{1,0:T(8,128)} %get-tuple-element.41.refs_3_, ...), custom_call_target="tpu_custom_call" | custom-call | flops 7272923136 | bytes 10584064 | tf_op jit(solution)/shard_map/pallas_call | solution.py:99
  95.9 0.1 collective-permute-start.12
  96.0 1.4 pad_maximum_fusion.2.refs_1_
  97.3 26.2 %shard_map.115 = (f32[2176,1]{1,0:T(8,128)}, f32[2176,1]{1,0:T(8,128)}, f32[2176,128]{1,0:T(8,128)}) custom-call(bf16[2176,128]{1,0:T(8,128)(2,1)} %get-tuple-element.67.refs_0_, bf16[3,2176,128]{2,1,0:T(8,128)(2,1)} %pad_maximum_fusion.2.refs_1_, f32[2176,1]{1,0:T(8,128)} %get-tuple-element.49.refs_2_, f32[2176,1]{1,0:T(8,128)} %get-tuple-element.50.refs_3_, ...), custom_call_target="tpu_custom_call" | custom-call | flops 7272923136 | bytes 10584064 | tf_op jit(solution)/shard_map/pallas_call | solution.py:99
  123.5 0.8 copy-done.5
  124.4 9.8 %shard_map.116 = bf16[2176,128]{1,0:T(8,128)(2,1)} custom-call(bf16[2176,128]{1,0:T(8,128)(2,1)} %get-tuple-element.67.refs_0_, bf16[1,2176,128]{2,1,0:T(8,128)(2,1)} %bitcast.79, f32[2176,1]{1,0:T(8,128)} %get-tuple-element.56.refs_2_, f32[2176,1]{1,0:T(8,128)} %get-tuple-element.57.refs_3_, f32[2176,128]{1,0:T(8,128)} %get-tuple-element.58.refs_4_), custom_call_target="tpu_custom_call" | custom-call | flops 2424307712 | bytes 6127616 | tf_op jit(solution)/shard_map/pallas_call | solution.py:99
  134.2 1.3 slice.111
  135.5 0.3 copy.34
  135.8 0.6 gather_fusion
  136.4 0.9 broadcast_select_fusion
  137.3 7.5 %all-to-all-start = ((bf16[16,136,64]{1,2,0:T(8,128)(2,1)}), bf16[16,136,64]{1,2,0:T(8,128)(2,1)S(1)}, u32[]{:S(2)}, u32[]{:S(2)}) async-start(bf16[16,136,64]{1,2,0:T(8,128)(2,1)} %broadcast_select_fusion), calls=%async_computation | async-start | bytes 1048576 | tf_op jit(solution)/shard_map/all_to_all | solution.py:187
  144.8 11.1 %all-to-all-done = bf16[16,136,64]{1,2,0:T(8,128)(2,1)S(1)} async-done(((bf16[16,136,64]{1,2,0:T(8,128)(2,1)}), bf16[16,136,64]{1,2,0:T(8,128)(2,1)S(1)}, u32[]{:S(2)}, u32[]{:S(2)}) %all-to-all-start) | async-done | bytes 278560 | tf_op jit(solution)/shard_map/all_to_all | solution.py:187
  155.9 0.6 copy.35
  156.5 0.4 reshape.206
  157.0 2.2 %fusion.65 = (f32[136]{0:T(256)S(1)}, bf16[136,1024]{1,0:T(8,128)(2,1)S(1)}) fusion(bf16[136,1024]{1,0:T(8,128)(2,1)S(1)} %reshape.206, bf16[1024,1024]{1,0:T(8,128)(2,1)} %all-gather.2.cloned.1.call-done, f32[1024]{0:T(1024)S(1)} %copy-done.3, bf16[136,1024]{1,0:T(8,128)(2,1)S(1)} %copy-done), kind=kOutput, calls=%fused_computation.67 | convolution fusion | flops 286187392 | bytes 2937376 | tf_op jit(solution)/shard_map/dot_general | solution.py:190
  159.2 0.1 fusion.67
  159.3 0.1 broadcast_in_dim.49
  159.5 1.4 collective-permute-start.13
  160.8 2.9 %collective-permute-start.14 = (bf16[136,1152]{1,0:T(8,128)(2,1)S(1)}, bf16[136,1152]{1,0:T(8,128)(2,1)S(1)}, u32[]{:S(2)}, u32[]{:S(2)}) collective-permute-start(bf16[136,1152]{1,0:T(8,128)(2,1)S(1)} %pad_maximum_fusion.8), channel_id=1, source_target_pairs={{0,2},{1,3},{2,0},{3,1},{4,6},{5,7},{6,4},{7,5},{8,10},{9,11},{10,... | collective-permute-start | bytes 940040 | tf_op jit(solution)/shard_map/ppermute | solution.py:121
  163.7 3.5 %collective-permute-done.13 = bf16[136,1152]{1,0:T(8,128)(2,1)S(1)} collective-permute-done((bf16[136,1152]{1,0:T(8,128)(2,1)S(1)}, bf16[136,1152]{1,0:T(8,128)(2,1)S(1)}, u32[]{:S(2)}, u32[]{:S(2)}) %collective-permute-start.13) | collective-permute-done | bytes 313376 | tf_op jit(solution)/shard_map/ppermute | solution.py:121
  167.2 10.3 %collective-permute-done.14 = bf16[136,1152]{1,0:T(8,128)(2,1)S(1)} collective-permute-done((bf16[136,1152]{1,0:T(8,128)(2,1)S(1)}, bf16[136,1152]{1,0:T(8,128)(2,1)S(1)}, u32[]{:S(2)}, u32[]{:S(2)}) %collective-permute-start.14) | collective-permute-done | bytes 313376 | tf_op jit(solution)/shard_map/ppermute | solution.py:121
  177.5 0.6 collective-permute-done.15
  178.1 0.3 fusion.72
  178.4 3.5 %fusion.59 = f32[544,16]{0,1:T(8,128)S(1)} fusion(bf16[2,1024,1024]{2,1,0:T(8,128)(2,1)} %param.17, f32[1024]{0:T(1024)S(1)} %bitcast.78, bf16[2,1024,16]{1,2,0:T(8,128)(2,1)S(1)} %copy-done.6, pred[544]{0:T(1024)(128)(4,1)S(1)} %get-tuple-element.61, bf16[136,1152]{1,0:T(8,128)(2,1)S(1)} %collective-permute-done.15, ...), kind=kOutput, calls=%fused_computation.61 | convolution fusion | flops 1169826304 | bytes 3423232 | tf_op jit(solution)/shard_map/dot_general | solution.py:204
  181.9 3.5 %fusion.62 = f32[544,16]{0,1:T(8,128)S(1)} fusion(f32[544,16]{0,1:T(8,128)S(1)} %fusion.59, bf16[2,1024,1024]{2,1,0:T(8,128)(2,1)} %param.17, f32[1024]{0:T(1024)S(1)} %bitcast.77, bf16[2,1024,16]{1,2,0:T(8,128)(2,1)S(1)} %copy-done.6, pred[544]{0:T(1024)(128)(4,1)S(1)} %get-tuple-element.60, bf16[136,1152]{1,0:T(8,128)(2,1)S(1)} %collective-permute-done.15, ...), kind=kOutput, calls=%fused_computation.62 | convolution fusion | flops 1169826304 | bytes 3464192 | tf_op jit(solution)/shard_map/dot_general | solution.py:204
  185.4 0.1 fusion.104
  185.6 0.2 collective-permute-start.17
  185.7 0.7 collective-permute-start.18
  186.4 0.3 collective-permute-done.16
  186.7 3.0 %collective-permute-done.17 = f32[136,16]{0,1:T(8,128)S(1)} collective-permute-done((f32[136,16]{0,1:T(8,128)S(1)}, f32[136,16]{0,1:T(8,128)S(1)}, u32[]{:S(2)}, u32[]{:S(2)}) %collective-permute-start.17) | collective-permute-done | bytes 8736 | tf_op jit(solution)/shard_map/ppermute | solution.py:121
  189.7 1.2 collective-permute-done.18
  190.9 0.6 fusion.79
  (39 shorter events, 0.5 us)
Async XLA Ops:
  7.2 149.8 %all-gather.2.cloned.1.call-start = ((), (), s32[]{:S(2)}) async-start(), calls=%async_computation.1 | async-start | bytes 2621440 | tf_op jit(solution)/shard_map/all_gather | solution.py:178
  10.2 10.3 %collective-permute-start = (bf16[136,1024]{1,0:T(8,128)(2,1)S(1)}, bf16[136,1024]{1,0:T(8,128)(2,1)S(1)}, u32[]{:S(2)}, u32[]{:S(2)}) collective-permute-start(bf16[136,1024]{1,0:T(8,128)(2,1)S(1)} %fusion.71), channel_id=1, source_target_pairs={{0,1},{1,2},{2,3},{3,0},{4,5},{5,6},{6,7},{7,4},{8,9},{9,10},{10,1... | collective-permute-start | bytes 835592 | tf_op jit(solution)/shard_map/ppermute | solution.py:121
  14.6 12.2 %collective-permute-start.1 = (bf16[136,1024]{1,0:T(8,128)(2,1)S(1)}, bf16[136,1024]{1,0:T(8,128)(2,1)S(1)}, u32[]{:S(2)}, u32[]{:S(2)}) collective-permute-start(bf16[136,1024]{1,0:T(8,128)(2,1)S(1)} %fusion.71), channel_id=1, source_target_pairs={{0,2},{1,3},{2,0},{3,1},{4,6},{5,7},{6,4},{7,5},{8,10},{9,11},{10,... | collective-permute-start | bytes 835592 | tf_op jit(solution)/shard_map/ppermute | solution.py:121
  14.6 12.8 %collective-permute-start.2 = (bf16[136,1024]{1,0:T(8,128)(2,1)S(1)}, bf16[136,1024]{1,0:T(8,128)(2,1)S(1)}, u32[]{:S(2)}, u32[]{:S(2)}) collective-permute-start(bf16[136,1024]{1,0:T(8,128)(2,1)S(1)} %fusion.71), channel_id=1, source_target_pairs={{0,3},{1,0},{2,1},{3,2},{4,7},{5,4},{6,5},{7,6},{8,11},{9,8},{10,9... | collective-permute-start | bytes 835592 | tf_op jit(solution)/shard_map/ppermute | solution.py:121
  30.5 9.6 %collective-permute-start.3 = (bf16[544,256]{1,0:T(8,128)(2,1)S(1)}, bf16[544,256]{1,0:T(8,128)(2,1)S(1)}, u32[]{:S(2)}, u32[]{:S(2)}) collective-permute-start(bf16[544,256]{1,0:T(8,128)(2,1)S(1)} %get-tuple-element.71), channel_id=1, source_target_pairs={{0,8},{8,16},{16,24},{24,0},{1,9},{9,17},{17,25},{25,1},{2,10},{10... | collective-permute-start | bytes 835592 | tf_op jit(solution)/shard_map/ppermute | solution.py:121
  31.8 15.4 %collective-permute-start.4 = (bf16[544,256]{1,0:T(8,128)(2,1)S(1)}, bf16[544,256]{1,0:T(8,128)(2,1)S(1)}, u32[]{:S(2)}, u32[]{:S(2)}) collective-permute-start(bf16[544,256]{1,0:T(8,128)(2,1)S(1)} %get-tuple-element.70), channel_id=1, source_target_pairs={{0,16},{8,24},{16,0},{24,8},{1,17},{9,25},{17,1},{25,9},{2,18},{10... | collective-permute-start | bytes 835592 | tf_op jit(solution)/shard_map/ppermute | solution.py:121
  34.3 12.9 %collective-permute-start.5 = (bf16[544,256]{1,0:T(8,128)(2,1)S(1)}, bf16[544,256]{1,0:T(8,128)(2,1)S(1)}, u32[]{:S(2)}, u32[]{:S(2)}) collective-permute-start(bf16[544,256]{1,0:T(8,128)(2,1)S(1)} %get-tuple-element.69), channel_id=1, source_target_pairs={{0,24},{8,0},{16,8},{24,16},{1,25},{9,1},{17,9},{25,17},{2,26},{10... | collective-permute-start | bytes 835592 | tf_op jit(solution)/shard_map/ppermute | solution.py:121
  48.6 16.1 %collective-permute-start.6 = (bf16[2176,128]{1,0:T(8,128)(2,1)S(1)}, bf16[2176,128]{1,0:T(8,128)(2,1)S(1)}, u32[]{:S(2)}, u32[]{:S(2)}) collective-permute-start(bf16[2176,128]{1,0:T(8,128)(2,1)S(1)} %get-tuple-element.66), channel_id=1, source_target_pairs={{0,32},{32,64},{64,96},{96,0},{1,33},{33,65},{65,97},{97,1},{2,34}... | collective-permute-start | bytes 1671176 | tf_op jit(solution)/shard_map/ppermute | solution.py:159
  50.2 14.5 %collective-permute-start.7 = (bf16[2176,128]{1,0:T(8,128)(2,1)S(1)}, bf16[2176,128]{1,0:T(8,128)(2,1)S(1)}, u32[]{:S(2)}, u32[]{:S(2)}) collective-permute-start(bf16[2176,128]{1,0:T(8,128)(2,1)S(1)} %get-tuple-element.66), channel_id=1, source_target_pairs={{0,96},{32,0},{64,32},{96,64},{1,97},{33,1},{65,33},{97,65},{2,98}... | collective-permute-start | bytes 1671176 | tf_op jit(solution)/shard_map/ppermute | solution.py:160
  52.3 13.2 %collective-permute-start.8 = (bf16[2176,128]{1,0:T(8,128)(2,1)S(1)}, bf16[2176,128]{1,0:T(8,128)(2,1)S(1)}, u32[]{:S(2)}, u32[]{:S(2)}) collective-permute-start(bf16[2176,128]{1,0:T(8,128)(2,1)S(1)} %get-tuple-element.66), channel_id=1, source_target_pairs={{0,4},{4,0},{1,5},{5,1},{2,6},{6,2},{3,7},{7,3},{8,12},{12,8},{9,1... | collective-permute-start | bytes 1671176 | tf_op jit(solution)/shard_map/ppermute | solution.py:161
  65.6 30.3 %collective-permute-start.10 = (bf16[2176,128]{1,0:T(8,128)(2,1)S(1)}, bf16[2176,128]{1,0:T(8,128)(2,1)S(1)}, u32[]{:S(2)}, u32[]{:S(2)}) collective-permute-start(bf16[2176,128]{1,0:T(8,128)(2,1)S(1)} %collective-permute-done.8), channel_id=1, source_target_pairs={{0,32},{32,64},{64,96},{96,0},{1,33},{33,65},{65,97},{97,1},{2,34}... | collective-permute-start | bytes 1671176 | tf_op jit(solution)/shard_map/ppermute | solution.py:166
  65.7 30.2 %collective-permute-start.11 = (bf16[2176,128]{1,0:T(8,128)(2,1)S(1)}, bf16[2176,128]{1,0:T(8,128)(2,1)S(1)}, u32[]{:S(2)}, u32[]{:S(2)}) collective-permute-start(bf16[2176,128]{1,0:T(8,128)(2,1)S(1)} %collective-permute-done.8), channel_id=1, source_target_pairs={{0,96},{32,0},{64,32},{96,64},{1,97},{33,1},{65,33},{97,65},{2,98}... | collective-permute-start | bytes 1671176 | tf_op jit(solution)/shard_map/ppermute | solution.py:167
  68.3 27.5 %collective-permute-start.9 = (bf16[2176,128]{1,0:T(8,128)(2,1)S(1)}, bf16[2176,128]{1,0:T(8,128)(2,1)S(1)}, u32[]{:S(2)}, u32[]{:S(2)}) collective-permute-start(bf16[2176,128]{1,0:T(8,128)(2,1)S(1)} %collective-permute-done.6), channel_id=1, source_target_pairs={{0,32},{32,64},{64,96},{96,0},{1,33},{33,65},{65,97},{97,1},{2,34}... | collective-permute-start | bytes 1671176 | tf_op jit(solution)/shard_map/ppermute | solution.py:165
  95.9 27.6 %collective-permute-start.12 = (bf16[2176,128]{1,0:T(8,128)(2,1)S(1)}, bf16[2176,128]{1,0:T(8,128)(2,1)S(1)}, u32[]{:S(2)}, u32[]{:S(2)}) collective-permute-start(bf16[2176,128]{1,0:T(8,128)(2,1)S(1)} %collective-permute-done.10), channel_id=1, source_target_pairs={{0,32},{32,64},{64,96},{96,0},{1,33},{33,65},{65,97},{97,1},{2,34}... | collective-permute-start | bytes 1671176 | tf_op jit(solution)/shard_map/ppermute | solution.py:170
  123.5 0.8 copy-start.5
  135.4 9.4 %copy-start.7 = (s32[136,1]{0,1:T(1,128)S(1)}, s32[136,1]{0,1:T(1,128)}, u32[]{:S(2)}) copy-start(s32[136,1]{0,1:T(1,128)} %param.16) | copy-start | bytes 1636
  136.4 20.5 %copy-start = (bf16[136,1024]{1,0:T(8,128)(2,1)S(1)}, bf16[136,1024]{1,0:T(8,128)(2,1)}, u32[]{:S(2)}) copy-start(bf16[136,1024]{1,0:T(8,128)(2,1)} %param.10) | copy-start | bytes 835588
  136.4 20.5 %copy-start.3 = (f32[1024]{0:T(1024)S(1)}, f32[1024]{0:T(1024)}, u32[]{:S(2)}) copy-start(f32[1024]{0:T(1024)} %param.12) | copy-start | bytes 12292
  137.3 18.6 %all-to-all-start = ((bf16[16,136,64]{1,2,0:T(8,128)(2,1)}), bf16[16,136,64]{1,2,0:T(8,128)(2,1)S(1)}, u32[]{:S(2)}, u32[]{:S(2)}) async-start(bf16[16,136,64]{1,2,0:T(8,128)(2,1)} %broadcast_select_fusion), calls=%async_computation | async-start | bytes 1048576 | tf_op jit(solution)/shard_map/all_to_all | solution.py:187
  156.5 2.7 %copy-start.4 = (f32[1024]{0:T(1024)S(1)}, f32[1024]{0:T(1024)}, u32[]{:S(2)}) copy-start(f32[1024]{0:T(1024)} %param.13) | copy-start | bytes 12292
  156.9 6.8 %copy-start.2 = (bf16[2,1024]{1,0:T(2,128)(2,1)S(1)}, bf16[2,1024]{1,0:T(2,128)(2,1)}, u32[]{:S(2)}) copy-start(bf16[2,1024]{1,0:T(2,128)(2,1)} %param.18) | copy-start | bytes 12292
  156.9 21.5 %copy-start.6 = (bf16[2,1024,16]{1,2,0:T(8,128)(2,1)S(1)}, bf16[2,1024,16]{1,2,0:T(8,128)(2,1)}, u32[]{:S(2)}) copy-start(bf16[2,1024,16]{1,2,0:T(8,128)(2,1)} %param.19) | copy-start | bytes 196612
  159.2 22.7 %copy-start.1 = (bf16[136,1024]{1,0:T(8,128)(2,1)}, bf16[136,1024]{1,0:T(8,128)(2,1)S(1)}, u32[]{:S(2)}) copy-start(bf16[136,1024]{1,0:T(8,128)(2,1)S(1)} %get-tuple-element.80) | copy-start | bytes 835588
  159.5 7.7 %collective-permute-start.13 = (bf16[136,1152]{1,0:T(8,128)(2,1)S(1)}, bf16[136,1152]{1,0:T(8,128)(2,1)S(1)}, u32[]{:S(2)}, u32[]{:S(2)}) collective-permute-start(bf16[136,1152]{1,0:T(8,128)(2,1)S(1)} %pad_maximum_fusion.8), channel_id=1, source_target_pairs={{0,1},{1,2},{2,3},{3,0},{4,5},{5,6},{6,7},{7,4},{8,9},{9,10},{10,1... | collective-permute-start | bytes 940040 | tf_op jit(solution)/shard_map/ppermute | solution.py:121
  160.8 16.6 %collective-permute-start.14 = (bf16[136,1152]{1,0:T(8,128)(2,1)S(1)}, bf16[136,1152]{1,0:T(8,128)(2,1)S(1)}, u32[]{:S(2)}, u32[]{:S(2)}) collective-permute-start(bf16[136,1152]{1,0:T(8,128)(2,1)S(1)} %pad_maximum_fusion.8), channel_id=1, source_target_pairs={{0,2},{1,3},{2,0},{3,1},{4,6},{5,7},{6,4},{7,5},{8,10},{9,11},{10,... | collective-permute-start | bytes 940040 | tf_op jit(solution)/shard_map/ppermute | solution.py:121
  163.7 14.4 %collective-permute-start.15 = (bf16[136,1152]{1,0:T(8,128)(2,1)S(1)}, bf16[136,1152]{1,0:T(8,128)(2,1)S(1)}, u32[]{:S(2)}, u32[]{:S(2)}) collective-permute-start(bf16[136,1152]{1,0:T(8,128)(2,1)S(1)} %pad_maximum_fusion.8), channel_id=1, source_target_pairs={{0,3},{1,0},{2,1},{3,2},{4,7},{5,4},{6,5},{7,6},{8,11},{9,8},{10,9... | collective-permute-start | bytes 940040 | tf_op jit(solution)/shard_map/ppermute | solution.py:121
  185.5 1.2 collective-permute-start.16
  185.6 4.2 %collective-permute-start.17 = (f32[136,16]{0,1:T(8,128)S(1)}, f32[136,16]{0,1:T(8,128)S(1)}, u32[]{:S(2)}, u32[]{:S(2)}) collective-permute-start(f32[136,16]{0,1:T(8,128)S(1)} %get-tuple-element.74), channel_id=1, source_target_pairs={{0,2},{1,3},{2,0},{3,1},{4,6},{5,7},{6,4},{7,5},{8,10},{9,11},{10,... | collective-permute-start | bytes 26120 | tf_op jit(solution)/shard_map/ppermute | solution.py:121
  185.7 5.2 %collective-permute-start.18 = (f32[136,16]{0,1:T(8,128)S(1)}, f32[136,16]{0,1:T(8,128)S(1)}, u32[]{:S(2)}, u32[]{:S(2)}) collective-permute-start(f32[136,16]{0,1:T(8,128)S(1)} %get-tuple-element.73), channel_id=1, source_target_pairs={{0,3},{1,0},{2,1},{3,2},{4,7},{5,4},{6,5},{7,6},{8,11},{9,8},{10,9... | collective-permute-start | bytes 26120 | tf_op jit(solution)/shard_map/ppermute | solution.py:121
Sparse Core Ops, SparseCore 0:
  65.7 26.3 all-gather.1

commit v9 on v8

--- a/solution.py
+++ b/solution.py
@@ -42,6 +42,8 @@
             acc_s[...] = acc_in[...]
 
     kv = kv_ref[...]
+    lane = lax.broadcasted_iota(jnp.int32, kv.shape, 1)
+    kv_sums = jnp.where(lane < HD, jnp.ones_like(kv), kv)
     rows = q_ref.shape[0] // ROW_SPLIT
     scores = []
     for g in range(ROW_SPLIT):
@@ -58,17 +60,16 @@
         m_old = m_s[part, :]
         m_new = jnp.maximum(m_old, jnp.max(scores[g], axis=1, keepdims=True))
         decay = jnp.exp(m_old - m_new)
-        weights = jnp.exp(scores[g] - m_new)
-        l_s[part, :] = decay * l_s[part, :] + jnp.sum(weights, axis=1, keepdims=True)
+        weights = jnp.exp(scores[g] - m_new).astype(jnp.bfloat16)
         acc_s[part, :] = decay * acc_s[part, :] + jnp.dot(
-            weights.astype(jnp.bfloat16), kv, preferred_element_type=jnp.float32
+            weights, kv_sums, preferred_element_type=jnp.float32
         )
         m_s[part, :] = m_new
 
     @pl.when(chunk == pl.num_programs(1) - 1)
     def _():
         if last:
-            outs[0][...] = (acc_s[...] / l_s[...]).astype(outs[0].dtype)
+            outs[0][...] = (acc_s[...] / acc_s[:, 0:1]).astype(outs[0].dtype)
         else:
             outs[0][...] = m_s[...]
             outs[1][...] = l_s[...]

time: 199 us -> 193 us (0.970)
  Pallas kernels: 72.2 us -> 65.5 us
    pallas_call x4, Pallas kernels: 72.2 us -> 65.5 us  [flash_step(): pl.pallas_call(functools.partial(step_kernel, first, last), grid=(rows //...]
  transfers between devices with their start and end apart: 21 -> 21, of which waited for: 14 -> 14; matrix products, arithmetic and copies ran while one was open for 6% -> 6% of each run, Pallas kernels for 36% -> 34%
where the time goes in v9:
time: 193 us
  Pallas kernels  65.5 us (34%)
  waiting for transfers between devices  52.3 us (27%)
  starting transfers between devices  29.7 us (15%)
  between operations  14.4 us (7%)
  matrix products  12.2 us (6%)
  local copies, waits for them, and re-layouts  10.4 us (5%)
  other arithmetic  8.13 us (4%)
    pallas_call x4, Pallas kernels, flash_step(): pl.pallas_call(functools.partial(step_kernel, first, last), grid=(rows //...  65.5 us
    ppermute x12, waiting for transfers between devices, shifted(): return lax.ppermute(value, axis, [(i, (i + k) % n) for i in range(n)])  37.7 us
    ppermute x12, starting transfers between devices, shifted(): return lax.ppermute(value, axis, [(i, (i + k) % n) for i in range(n)])  14.9 us
    all_to_all x1, waiting for transfers between devices, body(): back = lax.all_to_all(attended, ('x', 'type'), 0, 0, tiled=True)  11.1 us
    all_to_all x1, starting transfers between devices, body(): back = lax.all_to_all(attended, ('x', 'type'), 0, 0, tiled=True)  7.45 us
    dot_general x2, matrix products, body(): answer = jnp.dot(hidden, head_w2[which], preferred_element_type=jnp.float32)  7.05 us
  transfers between devices with their start and end apart: 21, of which 14 were waited for; matrix products, arithmetic and copies ran while one was open for 6% of the time, Pallas kernels for 34%

profile of v9, /device:TPU:1, one launch (start us, length us, event | category | flops | bytes accessed | tf_op | source)
XLA Modules:
  0.0 192.7 jit_solution(6114566953899283756)
XLA Ops:
  7.2 0.8 slice_add_fusion.1
  8.0 1.1 fusion.68
  9.1 1.1 fusion.71
  10.2 4.4 %collective-permute-start = (bf16[136,1024]{1,0:T(8,128)(2,1)S(1)}, bf16[136,1024]{1,0:T(8,128)(2,1)S(1)}, u32[]{:S(2)}, u32[]{:S(2)}) collective-permute-start(bf16[136,1024]{1,0:T(8,128)(2,1)S(1)} %fusion.71), channel_id=1, source_target_pairs={{0,1},{1,2},{2,3},{3,0},{4,5},{5,6},{6,7},{7,4},{8,9},{9,10},{10,1... | collective-permute-start | bytes 835592 | tf_op jit(solution)/shard_map/ppermute | solution.py:122
  14.6 0.5 collective-permute-start.2
  15.1 1.5 fusion.103
  16.5 0.2 copy.36
  16.8 0.2 copy.37
  17.0 0.2 copy.38
  17.3 0.1 pad.20.clone
  17.3 0.2 pad_maximum_fusion
  17.6 0.2 copy.31
  17.8 2.6 %copy.32 = bf16[1024,4,256]{2,0,1:T(8,128)(2,1)} copy(bf16[1024,4,256]{0,2,1:T(8,128)(2,1)S(1)} %bitcast.63) | data formatting | bytes 4194304 | tf_op jit(solution)/shard_map/reshape | solution.py:140
  20.4 0.1 collective-permute-done
  20.5 6.4 %collective-permute-done.1 = bf16[136,1024]{1,0:T(8,128)(2,1)S(1)} collective-permute-done((bf16[136,1024]{1,0:T(8,128)(2,1)S(1)}, bf16[136,1024]{1,0:T(8,128)(2,1)S(1)}, u32[]{:S(2)}, u32[]{:S(2)}) %collective-permute-start.1) | collective-permute-done | bytes 278560 | tf_op jit(solution)/shard_map/ppermute | solution.py:122
  26.8 0.6 collective-permute-done.2
  27.4 3.0 %fusion.28 = bf16[4,544,256]{2,1,0:T(8,128)(2,1)S(1)} fusion(s32[]{:T(128)S(6)} %select_n.108, bf16[1024,4,256]{2,0,1:T(8,128)(2,1)} %copy.32, bf16[136,1024]{1,0:T(8,128)(2,1)S(1)} %collective-permute-done.2, bf16[136,1024]{1,0:T(8,128)(2,1)S(1)} %collective-permute-done.1, bf16[136,1024]{1,0:T(8,128)(2,1)S(1)} %collective-permute-done, ...), kind=kOutput, calls=%fused_computation.33 | convolution fusion | flops 1150058496 | bytes 4325380 | tf_op jit(solution)/shard_map/rd,dje->jre/dot_general | solution.py:142
  30.5 1.3 collective-permute-start.3
  31.8 2.5 %collective-permute-start.4 = (bf16[544,256]{1,0:T(8,128)(2,1)S(1)}, bf16[544,256]{1,0:T(8,128)(2,1)S(1)}, u32[]{:S(2)}, u32[]{:S(2)}) collective-permute-start(bf16[544,256]{1,0:T(8,128)(2,1)S(1)} %get-tuple-element.70), channel_id=1, source_target_pairs={{0,16},{8,24},{16,0},{24,8},{1,17},{9,25},{17,1},{25,9},{2,18},{10... | collective-permute-start | bytes 835592 | tf_op jit(solution)/shard_map/ppermute | solution.py:122
  34.3 1.1 collective-permute-start.5
  35.4 4.7 %collective-permute-done.3 = bf16[544,256]{1,0:T(8,128)(2,1)S(1)} collective-permute-done((bf16[544,256]{1,0:T(8,128)(2,1)S(1)}, bf16[544,256]{1,0:T(8,128)(2,1)S(1)}, u32[]{:S(2)}, u32[]{:S(2)}) %collective-permute-start.3) | collective-permute-done | bytes 278560 | tf_op jit(solution)/shard_map/ppermute | solution.py:122
  40.1 7.1 %collective-permute-done.4 = bf16[544,256]{1,0:T(8,128)(2,1)S(1)} collective-permute-done((bf16[544,256]{1,0:T(8,128)(2,1)S(1)}, bf16[544,256]{1,0:T(8,128)(2,1)S(1)}, u32[]{:S(2)}, u32[]{:S(2)}) %collective-permute-start.4) | collective-permute-done | bytes 278560 | tf_op jit(solution)/shard_map/ppermute | solution.py:122
  47.3 1.3 slice_bitcast_fusion.4
  48.6 1.7 collective-permute-start.6
  50.2 2.1 %collective-permute-start.7 = (bf16[2176,128]{1,0:T(8,128)(2,1)S(1)}, bf16[2176,128]{1,0:T(8,128)(2,1)S(1)}, u32[]{:S(2)}, u32[]{:S(2)}) collective-permute-start(bf16[2176,128]{1,0:T(8,128)(2,1)S(1)} %get-tuple-element.66), channel_id=1, source_target_pairs={{0,96},{32,0},{64,32},{96,64},{1,97},{33,1},{65,33},{97,65},{2,98}... | collective-permute-start | bytes 1671176 | tf_op jit(solution)/shard_map/ppermute | solution.py:161
  52.3 0.7 collective-permute-start.8
  53.0 9.0 %shard_map.113 = (f32[2176,1]{1,0:T(8,128)}, f32[2176,1]{1,0:T(8,128)}, f32[2176,128]{1,0:T(8,128)}) custom-call(bf16[2176,128]{1,0:T(8,128)(2,1)} %get-tuple-element.67.refs_0_, bf16[1,2176,128]{2,1,0:T(8,128)(2,1)} %get-tuple-element.65.refs_1_), custom_call_target="tpu_custom_call" | custom-call | flops 2424307712 | bytes 6127616 | tf_op jit(solution)/shard_map/pallas_call | solution.py:100
  62.1 2.6 %collective-permute-done.6 = bf16[2176,128]{1,0:T(8,128)(2,1)S(1)} collective-permute-done((bf16[2176,128]{1,0:T(8,128)(2,1)S(1)}, bf16[2176,128]{1,0:T(8,128)(2,1)S(1)}, u32[]{:S(2)}, u32[]{:S(2)}) %collective-permute-start.6) | collective-permute-done | bytes 557088 | tf_op jit(solution)/shard_map/ppermute | solution.py:160
  64.7 0.8 collective-permute-done.8
  65.6 0.1 collective-permute-start.10
  65.7 2.7 %collective-permute-start.11 = (bf16[2176,128]{1,0:T(8,128)(2,1)S(1)}, bf16[2176,128]{1,0:T(8,128)(2,1)S(1)}, u32[]{:S(2)}, u32[]{:S(2)}) collective-permute-start(bf16[2176,128]{1,0:T(8,128)(2,1)S(1)} %collective-permute-done.8), channel_id=1, source_target_pairs={{0,96},{32,0},{64,32},{96,64},{1,97},{33,1},{65,33},{97,65},{2,98}... | collective-permute-start | bytes 1671176 | tf_op jit(solution)/shard_map/ppermute | solution.py:168
  68.4 1.4 pad_maximum_fusion.1.refs_1_
  69.7 23.6 %shard_map.114 = (f32[2176,1]{1,0:T(8,128)}, f32[2176,1]{1,0:T(8,128)}, f32[2176,128]{1,0:T(8,128)}) custom-call(bf16[2176,128]{1,0:T(8,128)(2,1)} %get-tuple-element.67.refs_0_, bf16[3,2176,128]{2,1,0:T(8,128)(2,1)} %pad_maximum_fusion.1.refs_1_, f32[2176,1]{1,0:T(8,128)} %get-tuple-element.40.refs_2_, f32[2176,1]{1,0:T(8,128)} %get-tuple-element.41.refs_3_, ...), custom_call_target="tpu_custom_call" | custom-call | flops 7272923136 | bytes 10584064 | tf_op jit(solution)/shard_map/pallas_call | solution.py:100
  93.3 0.1 collective-permute-start.12
  93.4 1.4 pad_maximum_fusion.2.refs_1_
  94.8 23.6 %shard_map.115 = (f32[2176,1]{1,0:T(8,128)}, f32[2176,1]{1,0:T(8,128)}, f32[2176,128]{1,0:T(8,128)}) custom-call(bf16[2176,128]{1,0:T(8,128)(2,1)} %get-tuple-element.67.refs_0_, bf16[3,2176,128]{2,1,0:T(8,128)(2,1)} %pad_maximum_fusion.2.refs_1_, f32[2176,1]{1,0:T(8,128)} %get-tuple-element.49.refs_2_, f32[2176,1]{1,0:T(8,128)} %get-tuple-element.50.refs_3_, ...), custom_call_target="tpu_custom_call" | custom-call | flops 7272923136 | bytes 10584064 | tf_op jit(solution)/shard_map/pallas_call | solution.py:100
  118.4 0.8 copy-done.5
  119.2 9.3 %shard_map.116 = bf16[2176,128]{1,0:T(8,128)(2,1)} custom-call(bf16[2176,128]{1,0:T(8,128)(2,1)} %get-tuple-element.67.refs_0_, bf16[1,2176,128]{2,1,0:T(8,128)(2,1)} %bitcast.79, f32[2176,1]{1,0:T(8,128)} %get-tuple-element.56.refs_2_, f32[2176,1]{1,0:T(8,128)} %get-tuple-element.57.refs_3_, f32[2176,128]{1,0:T(8,128)} %get-tuple-element.58.refs_4_), custom_call_target="tpu_custom_call" | custom-call | flops 2424307712 | bytes 6127616 | tf_op jit(solution)/shard_map/pallas_call | solution.py:100
  128.5 1.3 slice.111
  129.8 0.3 copy.34
  130.1 0.6 gather_fusion
  130.7 0.9 broadcast_select_fusion
  131.7 7.4 %all-to-all-start = ((bf16[16,136,64]{1,2,0:T(8,128)(2,1)}), bf16[16,136,64]{1,2,0:T(8,128)(2,1)S(1)}, u32[]{:S(2)}, u32[]{:S(2)}) async-start(bf16[16,136,64]{1,2,0:T(8,128)(2,1)} %broadcast_select_fusion), calls=%async_computation | async-start | bytes 1048576 | tf_op jit(solution)/shard_map/all_to_all | solution.py:188
  139.1 11.1 %all-to-all-done = bf16[16,136,64]{1,2,0:T(8,128)(2,1)S(1)} async-done(((bf16[16,136,64]{1,2,0:T(8,128)(2,1)}), bf16[16,136,64]{1,2,0:T(8,128)(2,1)S(1)}, u32[]{:S(2)}, u32[]{:S(2)}) %all-to-all-start) | async-done | bytes 278560 | tf_op jit(solution)/shard_map/all_to_all | solution.py:188
  150.2 0.6 copy.35
  150.8 0.4 reshape.206
  151.3 2.2 %fusion.65 = (f32[136]{0:T(256)S(1)}, bf16[136,1024]{1,0:T(8,128)(2,1)S(1)}) fusion(bf16[136,1024]{1,0:T(8,128)(2,1)S(1)} %reshape.206, bf16[1024,1024]{1,0:T(8,128)(2,1)} %all-gather.2.cloned.1.call-done, f32[1024]{0:T(1024)S(1)} %copy-done.3, bf16[136,1024]{1,0:T(8,128)(2,1)S(1)} %copy-done), kind=kOutput, calls=%fused_computation.67 | convolution fusion | flops 286187392 | bytes 2937376 | tf_op jit(solution)/shard_map/dot_general | solution.py:191
  153.5 0.1 fusion.67
  153.6 0.1 broadcast_in_dim.49
  153.8 1.4 collective-permute-start.13
  155.1 2.9 %collective-permute-start.14 = (bf16[136,1152]{1,0:T(8,128)(2,1)S(1)}, bf16[136,1152]{1,0:T(8,128)(2,1)S(1)}, u32[]{:S(2)}, u32[]{:S(2)}) collective-permute-start(bf16[136,1152]{1,0:T(8,128)(2,1)S(1)} %pad_maximum_fusion.8), channel_id=1, source_target_pairs={{0,2},{1,3},{2,0},{3,1},{4,6},{5,7},{6,4},{7,5},{8,10},{9,11},{10,... | collective-permute-start | bytes 940040 | tf_op jit(solution)/shard_map/ppermute | solution.py:122
  158.0 3.5 %collective-permute-done.13 = bf16[136,1152]{1,0:T(8,128)(2,1)S(1)} collective-permute-done((bf16[136,1152]{1,0:T(8,128)(2,1)S(1)}, bf16[136,1152]{1,0:T(8,128)(2,1)S(1)}, u32[]{:S(2)}, u32[]{:S(2)}) %collective-permute-start.13) | collective-permute-done | bytes 313376 | tf_op jit(solution)/shard_map/ppermute | solution.py:122
  161.5 10.3 %collective-permute-done.14 = bf16[136,1152]{1,0:T(8,128)(2,1)S(1)} collective-permute-done((bf16[136,1152]{1,0:T(8,128)(2,1)S(1)}, bf16[136,1152]{1,0:T(8,128)(2,1)S(1)}, u32[]{:S(2)}, u32[]{:S(2)}) %collective-permute-start.14) | collective-permute-done | bytes 313376 | tf_op jit(solution)/shard_map/ppermute | solution.py:122
  171.8 0.6 collective-permute-done.15
  172.4 0.3 fusion.72
  172.7 3.5 %fusion.59 = f32[544,16]{0,1:T(8,128)S(1)} fusion(bf16[2,1024,1024]{2,1,0:T(8,128)(2,1)} %param.17, f32[1024]{0:T(1024)S(1)} %bitcast.78, bf16[2,1024,16]{1,2,0:T(8,128)(2,1)S(1)} %copy-done.6, pred[544]{0:T(1024)(128)(4,1)S(1)} %get-tuple-element.61, bf16[136,1152]{1,0:T(8,128)(2,1)S(1)} %collective-permute-done.15, ...), kind=kOutput, calls=%fused_computation.61 | convolution fusion | flops 1169826304 | bytes 3423232 | tf_op jit(solution)/shard_map/dot_general | solution.py:205
  176.2 3.5 %fusion.62 = f32[544,16]{0,1:T(8,128)S(1)} fusion(f32[544,16]{0,1:T(8,128)S(1)} %fusion.59, bf16[2,1024,1024]{2,1,0:T(8,128)(2,1)} %param.17, f32[1024]{0:T(1024)S(1)} %bitcast.77, bf16[2,1024,16]{1,2,0:T(8,128)(2,1)S(1)} %copy-done.6, pred[544]{0:T(1024)(128)(4,1)S(1)} %get-tuple-element.60, bf16[136,1152]{1,0:T(8,128)(2,1)S(1)} %collective-permute-done.15, ...), kind=kOutput, calls=%fused_computation.62 | convolution fusion | flops 1169826304 | bytes 3464192 | tf_op jit(solution)/shard_map/dot_general | solution.py:205
  179.7 0.1 fusion.104
  179.9 0.2 collective-permute-start.17
  180.0 0.7 collective-permute-start.18
  180.7 0.3 collective-permute-done.16
  181.0 3.0 %collective-permute-done.17 = f32[136,16]{0,1:T(8,128)S(1)} collective-permute-done((f32[136,16]{0,1:T(8,128)S(1)}, f32[136,16]{0,1:T(8,128)S(1)}, u32[]{:S(2)}, u32[]{:S(2)}) %collective-permute-start.17) | collective-permute-done | bytes 8736 | tf_op jit(solution)/shard_map/ppermute | solution.py:122
  184.0 1.2 collective-permute-done.18
  185.2 0.6 fusion.79
  (39 shorter events, 0.5 us)
Async XLA Ops:
  7.2 144.1 %all-gather.2.cloned.1.call-start = ((), (), s32[]{:S(2)}) async-start(), calls=%async_computation.1 | async-start | bytes 2621440 | tf_op jit(solution)/shard_map/all_gather | solution.py:179
  10.2 10.3 %collective-permute-start = (bf16[136,1024]{1,0:T(8,128)(2,1)S(1)}, bf16[136,1024]{1,0:T(8,128)(2,1)S(1)}, u32[]{:S(2)}, u32[]{:S(2)}) collective-permute-start(bf16[136,1024]{1,0:T(8,128)(2,1)S(1)} %fusion.71), channel_id=1, source_target_pairs={{0,1},{1,2},{2,3},{3,0},{4,5},{5,6},{6,7},{7,4},{8,9},{9,10},{10,1... | collective-permute-start | bytes 835592 | tf_op jit(solution)/shard_map/ppermute | solution.py:122
  14.6 12.2 %collective-permute-start.1 = (bf16[136,1024]{1,0:T(8,128)(2,1)S(1)}, bf16[136,1024]{1,0:T(8,128)(2,1)S(1)}, u32[]{:S(2)}, u32[]{:S(2)}) collective-permute-start(bf16[136,1024]{1,0:T(8,128)(2,1)S(1)} %fusion.71), channel_id=1, source_target_pairs={{0,2},{1,3},{2,0},{3,1},{4,6},{5,7},{6,4},{7,5},{8,10},{9,11},{10,... | collective-permute-start | bytes 835592 | tf_op jit(solution)/shard_map/ppermute | solution.py:122
  14.6 12.8 %collective-permute-start.2 = (bf16[136,1024]{1,0:T(8,128)(2,1)S(1)}, bf16[136,1024]{1,0:T(8,128)(2,1)S(1)}, u32[]{:S(2)}, u32[]{:S(2)}) collective-permute-start(bf16[136,1024]{1,0:T(8,128)(2,1)S(1)} %fusion.71), channel_id=1, source_target_pairs={{0,3},{1,0},{2,1},{3,2},{4,7},{5,4},{6,5},{7,6},{8,11},{9,8},{10,9... | collective-permute-start | bytes 835592 | tf_op jit(solution)/shard_map/ppermute | solution.py:122
  30.5 9.6 %collective-permute-start.3 = (bf16[544,256]{1,0:T(8,128)(2,1)S(1)}, bf16[544,256]{1,0:T(8,128)(2,1)S(1)}, u32[]{:S(2)}, u32[]{:S(2)}) collective-permute-start(bf16[544,256]{1,0:T(8,128)(2,1)S(1)} %get-tuple-element.71), channel_id=1, source_target_pairs={{0,8},{8,16},{16,24},{24,0},{1,9},{9,17},{17,25},{25,1},{2,10},{10... | collective-permute-start | bytes 835592 | tf_op jit(solution)/shard_map/ppermute | solution.py:122
  31.8 15.4 %collective-permute-start.4 = (bf16[544,256]{1,0:T(8,128)(2,1)S(1)}, bf16[544,256]{1,0:T(8,128)(2,1)S(1)}, u32[]{:S(2)}, u32[]{:S(2)}) collective-permute-start(bf16[544,256]{1,0:T(8,128)(2,1)S(1)} %get-tuple-element.70), channel_id=1, source_target_pairs={{0,16},{8,24},{16,0},{24,8},{1,17},{9,25},{17,1},{25,9},{2,18},{10... | collective-permute-start | bytes 835592 | tf_op jit(solution)/shard_map/ppermute | solution.py:122
  34.3 12.9 %collective-permute-start.5 = (bf16[544,256]{1,0:T(8,128)(2,1)S(1)}, bf16[544,256]{1,0:T(8,128)(2,1)S(1)}, u32[]{:S(2)}, u32[]{:S(2)}) collective-permute-start(bf16[544,256]{1,0:T(8,128)(2,1)S(1)} %get-tuple-element.69), channel_id=1, source_target_pairs={{0,24},{8,0},{16,8},{24,16},{1,25},{9,1},{17,9},{25,17},{2,26},{10... | collective-permute-start | bytes 835592 | tf_op jit(solution)/shard_map/ppermute | solution.py:122
  48.6 16.1 %collective-permute-start.6 = (bf16[2176,128]{1,0:T(8,128)(2,1)S(1)}, bf16[2176,128]{1,0:T(8,128)(2,1)S(1)}, u32[]{:S(2)}, u32[]{:S(2)}) collective-permute-start(bf16[2176,128]{1,0:T(8,128)(2,1)S(1)} %get-tuple-element.66), channel_id=1, source_target_pairs={{0,32},{32,64},{64,96},{96,0},{1,33},{33,65},{65,97},{97,1},{2,34}... | collective-permute-start | bytes 1671176 | tf_op jit(solution)/shard_map/ppermute | solution.py:160
  50.2 14.5 %collective-permute-start.7 = (bf16[2176,128]{1,0:T(8,128)(2,1)S(1)}, bf16[2176,128]{1,0:T(8,128)(2,1)S(1)}, u32[]{:S(2)}, u32[]{:S(2)}) collective-permute-start(bf16[2176,128]{1,0:T(8,128)(2,1)S(1)} %get-tuple-element.66), channel_id=1, source_target_pairs={{0,96},{32,0},{64,32},{96,64},{1,97},{33,1},{65,33},{97,65},{2,98}... | collective-permute-start | bytes 1671176 | tf_op jit(solution)/shard_map/ppermute | solution.py:161
  52.3 13.2 %collective-permute-start.8 = (bf16[2176,128]{1,0:T(8,128)(2,1)S(1)}, bf16[2176,128]{1,0:T(8,128)(2,1)S(1)}, u32[]{:S(2)}, u32[]{:S(2)}) collective-permute-start(bf16[2176,128]{1,0:T(8,128)(2,1)S(1)} %get-tuple-element.66), channel_id=1, source_target_pairs={{0,4},{4,0},{1,5},{5,1},{2,6},{6,2},{3,7},{7,3},{8,12},{12,8},{9,1... | collective-permute-start | bytes 1671176 | tf_op jit(solution)/shard_map/ppermute | solution.py:162
  65.6 27.7 %collective-permute-start.10 = (bf16[2176,128]{1,0:T(8,128)(2,1)S(1)}, bf16[2176,128]{1,0:T(8,128)(2,1)S(1)}, u32[]{:S(2)}, u32[]{:S(2)}) collective-permute-start(bf16[2176,128]{1,0:T(8,128)(2,1)S(1)} %collective-permute-done.8), channel_id=1, source_target_pairs={{0,32},{32,64},{64,96},{96,0},{1,33},{33,65},{65,97},{97,1},{2,34}... | collective-permute-start | bytes 1671176 | tf_op jit(solution)/shard_map/ppermute | solution.py:167
  65.7 27.6 %collective-permute-start.11 = (bf16[2176,128]{1,0:T(8,128)(2,1)S(1)}, bf16[2176,128]{1,0:T(8,128)(2,1)S(1)}, u32[]{:S(2)}, u32[]{:S(2)}) collective-permute-start(bf16[2176,128]{1,0:T(8,128)(2,1)S(1)} %collective-permute-done.8), channel_id=1, source_target_pairs={{0,96},{32,0},{64,32},{96,64},{1,97},{33,1},{65,33},{97,65},{2,98}... | collective-permute-start | bytes 1671176 | tf_op jit(solution)/shard_map/ppermute | solution.py:168
  68.3 25.0 %collective-permute-start.9 = (bf16[2176,128]{1,0:T(8,128)(2,1)S(1)}, bf16[2176,128]{1,0:T(8,128)(2,1)S(1)}, u32[]{:S(2)}, u32[]{:S(2)}) collective-permute-start(bf16[2176,128]{1,0:T(8,128)(2,1)S(1)} %collective-permute-done.6), channel_id=1, source_target_pairs={{0,32},{32,64},{64,96},{96,0},{1,33},{33,65},{65,97},{97,1},{2,34}... | collective-permute-start | bytes 1671176 | tf_op jit(solution)/shard_map/ppermute | solution.py:166
  93.3 25.1 %collective-permute-start.12 = (bf16[2176,128]{1,0:T(8,128)(2,1)S(1)}, bf16[2176,128]{1,0:T(8,128)(2,1)S(1)}, u32[]{:S(2)}, u32[]{:S(2)}) collective-permute-start(bf16[2176,128]{1,0:T(8,128)(2,1)S(1)} %collective-permute-done.10), channel_id=1, source_target_pairs={{0,32},{32,64},{64,96},{96,0},{1,33},{33,65},{65,97},{97,1},{2,34}... | collective-permute-start | bytes 1671176 | tf_op jit(solution)/shard_map/ppermute | solution.py:171
  118.4 0.8 copy-start.5
  129.8 9.3 %copy-start.7 = (s32[136,1]{0,1:T(1,128)S(1)}, s32[136,1]{0,1:T(1,128)}, u32[]{:S(2)}) copy-start(s32[136,1]{0,1:T(1,128)} %param.16) | copy-start | bytes 1636
  130.7 20.5 %copy-start = (bf16[136,1024]{1,0:T(8,128)(2,1)S(1)}, bf16[136,1024]{1,0:T(8,128)(2,1)}, u32[]{:S(2)}) copy-start(bf16[136,1024]{1,0:T(8,128)(2,1)} %param.10) | copy-start | bytes 835588
  130.7 20.5 %copy-start.3 = (f32[1024]{0:T(1024)S(1)}, f32[1024]{0:T(1024)}, u32[]{:S(2)}) copy-start(f32[1024]{0:T(1024)} %param.12) | copy-start | bytes 12292
  131.7 18.6 %all-to-all-start = ((bf16[16,136,64]{1,2,0:T(8,128)(2,1)}), bf16[16,136,64]{1,2,0:T(8,128)(2,1)S(1)}, u32[]{:S(2)}, u32[]{:S(2)}) async-start(bf16[16,136,64]{1,2,0:T(8,128)(2,1)} %broadcast_select_fusion), calls=%async_computation | async-start | bytes 1048576 | tf_op jit(solution)/shard_map/all_to_all | solution.py:188
  150.8 2.7 %copy-start.4 = (f32[1024]{0:T(1024)S(1)}, f32[1024]{0:T(1024)}, u32[]{:S(2)}) copy-start(f32[1024]{0:T(1024)} %param.13) | copy-start | bytes 12292
  151.2 6.8 %copy-start.2 = (bf16[2,1024]{1,0:T(2,128)(2,1)S(1)}, bf16[2,1024]{1,0:T(2,128)(2,1)}, u32[]{:S(2)}) copy-start(bf16[2,1024]{1,0:T(2,128)(2,1)} %param.18) | copy-start | bytes 12292
  151.2 21.5 %copy-start.6 = (bf16[2,1024,16]{1,2,0:T(8,128)(2,1)S(1)}, bf16[2,1024,16]{1,2,0:T(8,128)(2,1)}, u32[]{:S(2)}) copy-start(bf16[2,1024,16]{1,2,0:T(8,128)(2,1)} %param.19) | copy-start | bytes 196612
  153.5 22.7 %copy-start.1 = (bf16[136,1024]{1,0:T(8,128)(2,1)}, bf16[136,1024]{1,0:T(8,128)(2,1)S(1)}, u32[]{:S(2)}) copy-start(bf16[136,1024]{1,0:T(8,128)(2,1)S(1)} %get-tuple-element.80) | copy-start | bytes 835588
  153.8 7.7 %collective-permute-start.13 = (bf16[136,1152]{1,0:T(8,128)(2,1)S(1)}, bf16[136,1152]{1,0:T(8,128)(2,1)S(1)}, u32[]{:S(2)}, u32[]{:S(2)}) collective-permute-start(bf16[136,1152]{1,0:T(8,128)(2,1)S(1)} %pad_maximum_fusion.8), channel_id=1, source_target_pairs={{0,1},{1,2},{2,3},{3,0},{4,5},{5,6},{6,7},{7,4},{8,9},{9,10},{10,1... | collective-permute-start | bytes 940040 | tf_op jit(solution)/shard_map/ppermute | solution.py:122
  155.1 16.6 %collective-permute-start.14 = (bf16[136,1152]{1,0:T(8,128)(2,1)S(1)}, bf16[136,1152]{1,0:T(8,128)(2,1)S(1)}, u32[]{:S(2)}, u32[]{:S(2)}) collective-permute-start(bf16[136,1152]{1,0:T(8,128)(2,1)S(1)} %pad_maximum_fusion.8), channel_id=1, source_target_pairs={{0,2},{1,3},{2,0},{3,1},{4,6},{5,7},{6,4},{7,5},{8,10},{9,11},{10,... | collective-permute-start | bytes 940040 | tf_op jit(solution)/shard_map/ppermute | solution.py:122
  158.0 14.4 %collective-permute-start.15 = (bf16[136,1152]{1,0:T(8,128)(2,1)S(1)}, bf16[136,1152]{1,0:T(8,128)(2,1)S(1)}, u32[]{:S(2)}, u32[]{:S(2)}) collective-permute-start(bf16[136,1152]{1,0:T(8,128)(2,1)S(1)} %pad_maximum_fusion.8), channel_id=1, source_target_pairs={{0,3},{1,0},{2,1},{3,2},{4,7},{5,4},{6,5},{7,6},{8,11},{9,8},{10,9... | collective-permute-start | bytes 940040 | tf_op jit(solution)/shard_map/ppermute | solution.py:122
  179.8 1.2 collective-permute-start.16
  179.9 4.2 %collective-permute-start.17 = (f32[136,16]{0,1:T(8,128)S(1)}, f32[136,16]{0,1:T(8,128)S(1)}, u32[]{:S(2)}, u32[]{:S(2)}) collective-permute-start(f32[136,16]{0,1:T(8,128)S(1)} %get-tuple-element.74), channel_id=1, source_target_pairs={{0,2},{1,3},{2,0},{3,1},{4,6},{5,7},{6,4},{7,5},{8,10},{9,11},{10,... | collective-permute-start | bytes 26120 | tf_op jit(solution)/shard_map/ppermute | solution.py:122
  180.0 5.2 %collective-permute-start.18 = (f32[136,16]{0,1:T(8,128)S(1)}, f32[136,16]{0,1:T(8,128)S(1)}, u32[]{:S(2)}, u32[]{:S(2)}) collective-permute-start(f32[136,16]{0,1:T(8,128)S(1)} %get-tuple-element.73), channel_id=1, source_target_pairs={{0,3},{1,0},{2,1},{3,2},{4,7},{5,4},{6,5},{7,6},{8,11},{9,8},{10,9... | collective-permute-start | bytes 26120 | tf_op jit(solution)/shard_map/ppermute | solution.py:122
Sparse Core Ops, SparseCore 0:
  65.7 26.3 all-gather.1

commit v10 on v9

--- a/solution.py
+++ b/solution.py
@@ -21,24 +21,17 @@
 
 def step_kernel(first, last, *refs):
     if first:
-        q_ref, kv_ref = refs[:2]
-        rest = refs[2:]
+        q_ref, kv_ref, out_ref, acc_s = refs
     else:
-        q_ref, kv_ref, m_in, l_in, acc_in = refs[:5]
-        rest = refs[5:]
-    m_s, l_s, acc_s = rest[-3:]
-    outs = rest[:-3]
+        q_ref, kv_ref, acc_in, out_ref, acc_s = refs
     chunk = pl.program_id(1)
 
     @pl.when(chunk == 0)
     def _():
         if first:
-            m_s[...] = jnp.full(m_s.shape, -jnp.inf, jnp.float32)
-            l_s[...] = jnp.zeros(l_s.shape, jnp.float32)
-            acc_s[...] = jnp.zeros(acc_s.shape, jnp.float32)
+            lane = lax.broadcasted_iota(jnp.int32, acc_s.shape, 1)
+            acc_s[...] = jnp.where(lane == 1, -jnp.inf, 0.0).astype(jnp.float32)
         else:
-            m_s[...] = m_in[...]
-            l_s[...] = l_in[...]
             acc_s[...] = acc_in[...]
 
     kv = kv_ref[...]
@@ -57,23 +50,21 @@
         )
     for g in range(ROW_SPLIT):
         part = slice(g * rows, (g + 1) * rows)
-        m_old = m_s[part, :]
+        held = acc_s[part, :]
+        m_old = held[:, 1:2]
         m_new = jnp.maximum(m_old, jnp.max(scores[g], axis=1, keepdims=True))
         decay = jnp.exp(m_old - m_new)
         weights = jnp.exp(scores[g] - m_new).astype(jnp.bfloat16)
-        acc_s[part, :] = decay * acc_s[part, :] + jnp.dot(
-            weights, kv_sums, preferred_element_type=jnp.float32
-        )
-        m_s[part, :] = m_new
+        fresh = decay * held + jnp.dot(weights, kv_sums, preferred_element_type=jnp.float32)
+        lane_row = lax.broadcasted_iota(jnp.int32, fresh.shape, 1)
+        acc_s[part, :] = jnp.where(lane_row == 1, m_new, fresh)
 
     @pl.when(chunk == pl.num_programs(1) - 1)
     def _():
         if last:
-            outs[0][...] = (acc_s[...] / acc_s[:, 0:1]).astype(outs[0].dtype)
+            out_ref[...] = (acc_s[...] / acc_s[:, 0:1]).astype(out_ref.dtype)
         else:
-            outs[0][...] = m_s[...]
-            outs[1][...] = l_s[...]
-            outs[2][...] = acc_s[...]
+            out_ref[...] = acc_s[...]
 
 
 def flash_step(q_pad, kv, state, first, last):
@@ -81,38 +72,24 @@
     chunks, chunk = kv.shape[:2]
     block = QUERY_BLOCK
     row_block = pl.BlockSpec((block, width), lambda i, c: (i, 0))
-    stat_block = pl.BlockSpec((block, 1), lambda i, c: (i, 0))
     in_specs = [row_block, pl.BlockSpec((None, chunk, width), lambda i, c: (c, 0, 0))]
     operands = [q_pad, kv]
     if not first:
-        in_specs += [stat_block, stat_block, row_block]
-        operands += list(state)
-    if last:
-        out_specs = row_block
-        out_shape = jax.ShapeDtypeStruct((rows, width), jnp.bfloat16)
-    else:
-        out_specs = [stat_block, stat_block, row_block]
-        out_shape = [
-            jax.ShapeDtypeStruct((rows, 1), jnp.float32),
-            jax.ShapeDtypeStruct((rows, 1), jnp.float32),
-            jax.ShapeDtypeStruct((rows, width), jnp.float32),
-        ]
+        in_specs.append(row_block)
+        operands.append(state)
+    out_type = jnp.bfloat16 if last else jnp.float32
     return pl.pallas_call(
         functools.partial(step_kernel, first, last),
         grid=(rows // block, chunks),
         in_specs=in_specs,
-        out_specs=out_specs,
-        out_shape=out_shape,
-        scratch_shapes=[
-            pltpu.VMEM((block, 1), jnp.float32),
-            pltpu.VMEM((block, 1), jnp.float32),
-            pltpu.VMEM((block, width), jnp.float32),
-        ],
+        out_specs=row_block,
+        out_shape=jax.ShapeDtypeStruct((rows, width), out_type),
+        scratch_shapes=[pltpu.VMEM((block, width), jnp.float32)],
         compiler_params=pltpu.CompilerParams(dimension_semantics=("arbitrary", "arbitrary")),
         cost_estimate=pl.CostEstimate(
             flops=4 * rows * chunks * chunk * width,
             transcendentals=rows * chunks * chunk,
-            bytes_accessed=rows * width * 14 + (rows // block) * chunks * chunk * width * 2,
+            bytes_accessed=rows * width * 10 + (rows // block) * chunks * chunk * width * 2,
         ),
     )(*operands)
 

time: 193 us -> 191 us (0.990)
  Pallas kernels: 65.5 us -> 63 us
    pallas_call x4, Pallas kernels: 65.5 us -> 63 us  [flash_step(): pl.pallas_call(functools.partial(step_kernel, first, last), grid=(rows //...]
  transfers between devices with their start and end apart: 21 -> 21, of which waited for: 14 -> 14; matrix products, arithmetic and copies ran while one was open for 6% -> 6% of each run, Pallas kernels for 34% -> 33%
where the time goes in v10:
time: 191 us
  Pallas kernels  63 us (33%)
  waiting for transfers between devices  52.8 us (28%)
  starting transfers between devices  29.9 us (16%)
  between operations  14.4 us (8%)
  matrix products  12.2 us (6%)
  local copies, waits for them, and re-layouts  10.4 us (5%)
  other arithmetic  8.09 us (4%)
    pallas_call x4, Pallas kernels, flash_step(): pl.pallas_call(functools.partial(step_kernel, first, last), grid=(rows //...  63 us
    ppermute x12, waiting for transfers between devices, shifted(): return lax.ppermute(value, axis, [(i, (i + k) % n) for i in range(n)])  37.8 us
    ppermute x12, starting transfers between devices, shifted(): return lax.ppermute(value, axis, [(i, (i + k) % n) for i in range(n)])  14.9 us
    all_to_all x1, waiting for transfers between devices, body(): back = lax.all_to_all(attended, ('x', 'type'), 0, 0, tiled=True)  11.1 us
    all_to_all x1, starting transfers between devices, body(): back = lax.all_to_all(attended, ('x', 'type'), 0, 0, tiled=True)  7.45 us
    dot_general x2, matrix products, body(): answer = jnp.dot(hidden, head_w2[which], preferred_element_type=jnp.float32)  7.05 us
  transfers between devices with their start and end apart: 21, of which 14 were waited for; matrix products, arithmetic and copies ran while one was open for 6% of the time, Pallas kernels for 33%

profile of v10, /device:TPU:1, one launch (start us, length us, event | category | flops | bytes accessed | tf_op | source)
XLA Modules:
  0.0 190.7 jit_solution(12472447693639465381)
XLA Ops:
  7.2 0.8 slice_add_fusion.1
  8.0 1.1 fusion.68
  9.1 1.1 fusion.71
  10.2 4.4 %collective-permute-start = (bf16[136,1024]{1,0:T(8,128)(2,1)S(1)}, bf16[136,1024]{1,0:T(8,128)(2,1)S(1)}, u32[]{:S(2)}, u32[]{:S(2)}) collective-permute-start(bf16[136,1024]{1,0:T(8,128)(2,1)S(1)} %fusion.71), channel_id=1, source_target_pairs={{0,1},{1,2},{2,3},{3,0},{4,5},{5,6},{6,7},{7,4},{8,9},{9,10},{10,1... | collective-permute-start | bytes 835592 | tf_op jit(solution)/shard_map/ppermute | solution.py:99
  14.6 0.5 collective-permute-start.2
  15.1 1.5 fusion.103
  16.5 0.2 copy.36
  16.8 0.2 copy.37
  17.0 0.2 copy.38
  17.3 0.1 pad.20.clone
  17.3 0.2 pad_maximum_fusion
  17.6 0.2 copy.31
  17.8 2.6 %copy.32 = bf16[1024,4,256]{2,0,1:T(8,128)(2,1)} copy(bf16[1024,4,256]{0,2,1:T(8,128)(2,1)S(1)} %bitcast.63) | data formatting | bytes 4194304 | tf_op jit(solution)/shard_map/reshape | solution.py:117
  20.3 0.2 collective-permute-done
  20.5 6.4 %collective-permute-done.1 = bf16[136,1024]{1,0:T(8,128)(2,1)S(1)} collective-permute-done((bf16[136,1024]{1,0:T(8,128)(2,1)S(1)}, bf16[136,1024]{1,0:T(8,128)(2,1)S(1)}, u32[]{:S(2)}, u32[]{:S(2)}) %collective-permute-start.1) | collective-permute-done | bytes 278560 | tf_op jit(solution)/shard_map/ppermute | solution.py:99
  26.8 0.6 collective-permute-done.2
  27.4 3.0 %fusion.28 = bf16[4,544,256]{2,1,0:T(8,128)(2,1)S(1)} fusion(s32[]{:T(128)S(6)} %select_n.108, bf16[1024,4,256]{2,0,1:T(8,128)(2,1)} %copy.32, bf16[136,1024]{1,0:T(8,128)(2,1)S(1)} %collective-permute-done.2, bf16[136,1024]{1,0:T(8,128)(2,1)S(1)} %collective-permute-done.1, bf16[136,1024]{1,0:T(8,128)(2,1)S(1)} %collective-permute-done, ...), kind=kOutput, calls=%fused_computation.33 | convolution fusion | flops 1150058496 | bytes 4325380 | tf_op jit(solution)/shard_map/rd,dje->jre/dot_general | solution.py:119
  30.5 1.3 collective-permute-start.3
  31.8 2.5 %collective-permute-start.4 = (bf16[544,256]{1,0:T(8,128)(2,1)S(1)}, bf16[544,256]{1,0:T(8,128)(2,1)S(1)}, u32[]{:S(2)}, u32[]{:S(2)}) collective-permute-start(bf16[544,256]{1,0:T(8,128)(2,1)S(1)} %get-tuple-element.40), channel_id=1, source_target_pairs={{0,16},{8,24},{16,0},{24,8},{1,17},{9,25},{17,1},{25,9},{2,18},{10... | collective-permute-start | bytes 835592 | tf_op jit(solution)/shard_map/ppermute | solution.py:99
  34.3 1.1 collective-permute-start.5
  35.4 4.7 %collective-permute-done.3 = bf16[544,256]{1,0:T(8,128)(2,1)S(1)} collective-permute-done((bf16[544,256]{1,0:T(8,128)(2,1)S(1)}, bf16[544,256]{1,0:T(8,128)(2,1)S(1)}, u32[]{:S(2)}, u32[]{:S(2)}) %collective-permute-start.3) | collective-permute-done | bytes 278560 | tf_op jit(solution)/shard_map/ppermute | solution.py:99
  40.1 7.1 %collective-permute-done.4 = bf16[544,256]{1,0:T(8,128)(2,1)S(1)} collective-permute-done((bf16[544,256]{1,0:T(8,128)(2,1)S(1)}, bf16[544,256]{1,0:T(8,128)(2,1)S(1)}, u32[]{:S(2)}, u32[]{:S(2)}) %collective-permute-start.4) | collective-permute-done | bytes 278560 | tf_op jit(solution)/shard_map/ppermute | solution.py:99
  47.3 1.3 slice_bitcast_fusion.4
  48.6 1.7 collective-permute-start.6
  50.2 2.1 %collective-permute-start.7 = (bf16[2176,128]{1,0:T(8,128)(2,1)S(1)}, bf16[2176,128]{1,0:T(8,128)(2,1)S(1)}, u32[]{:S(2)}, u32[]{:S(2)}) collective-permute-start(bf16[2176,128]{1,0:T(8,128)(2,1)S(1)} %get-tuple-element.36), channel_id=1, source_target_pairs={{0,96},{32,0},{64,32},{96,64},{1,97},{33,1},{65,33},{97,65},{2,98}... | collective-permute-start | bytes 1671176 | tf_op jit(solution)/shard_map/ppermute | solution.py:138
  52.3 0.7 collective-permute-start.8
  53.1 8.6 %shard_map.113.refs_2_ = f32[2176,128]{1,0:T(8,128)} custom-call(bf16[2176,128]{1,0:T(8,128)(2,1)} %get-tuple-element.37.refs_0_, bf16[1,2176,128]{2,1,0:T(8,128)(2,1)} %get-tuple-element.35.refs_1_), custom_call_target="tpu_custom_call" | custom-call | flops 2424307712 | bytes 5013504 | tf_op jit(solution)/shard_map/pallas_call | solution.py:81
  61.7 3.0 %collective-permute-done.6 = bf16[2176,128]{1,0:T(8,128)(2,1)S(1)} collective-permute-done((bf16[2176,128]{1,0:T(8,128)(2,1)S(1)}, bf16[2176,128]{1,0:T(8,128)(2,1)S(1)}, u32[]{:S(2)}, u32[]{:S(2)}) %collective-permute-start.6) | collective-permute-done | bytes 557088 | tf_op jit(solution)/shard_map/ppermute | solution.py:137
  64.7 0.8 collective-permute-done.8
  65.6 0.1 collective-permute-start.10
  65.7 2.7 %collective-permute-start.11 = (bf16[2176,128]{1,0:T(8,128)(2,1)S(1)}, bf16[2176,128]{1,0:T(8,128)(2,1)S(1)}, u32[]{:S(2)}, u32[]{:S(2)}) collective-permute-start(bf16[2176,128]{1,0:T(8,128)(2,1)S(1)} %collective-permute-done.8), channel_id=1, source_target_pairs={{0,96},{32,0},{64,32},{96,64},{1,97},{33,1},{65,33},{97,65},{2,98}... | collective-permute-start | bytes 1671176 | tf_op jit(solution)/shard_map/ppermute | solution.py:145
  68.4 1.3 pad_maximum_fusion.1.refs_1_
  69.7 22.7 %shard_map.114.refs_2_ = f32[2176,128]{1,0:T(8,128)} custom-call(bf16[2176,128]{1,0:T(8,128)(2,1)} %get-tuple-element.37.refs_0_, bf16[3,2176,128]{2,1,0:T(8,128)(2,1)} %pad_maximum_fusion.1.refs_1_, f32[2176,128]{1,0:T(8,128)} %shard_map.113.refs_2_), custom_call_target="tpu_custom_call" | custom-call | flops 7272923136 | bytes 9469952 | tf_op jit(solution)/shard_map/pallas_call | solution.py:81
  92.4 0.3 collective-permute-start.12
  92.7 1.4 pad_maximum_fusion.2.refs_1_
  94.0 22.7 %shard_map.115.refs_2_ = f32[2176,128]{1,0:T(8,128)} custom-call(bf16[2176,128]{1,0:T(8,128)(2,1)} %get-tuple-element.37.refs_0_, bf16[3,2176,128]{2,1,0:T(8,128)(2,1)} %pad_maximum_fusion.2.refs_1_, f32[2176,128]{1,0:T(8,128)} %shard_map.114.refs_2_), custom_call_target="tpu_custom_call" | custom-call | flops 7272923136 | bytes 9469952 | tf_op jit(solution)/shard_map/pallas_call | solution.py:81
  116.8 0.8 copy-done.5
  117.6 9.0 %shard_map.116 = bf16[2176,128]{1,0:T(8,128)(2,1)} custom-call(bf16[2176,128]{1,0:T(8,128)(2,1)} %get-tuple-element.37.refs_0_, bf16[1,2176,128]{2,1,0:T(8,128)(2,1)} %bitcast.79, f32[2176,128]{1,0:T(8,128)} %shard_map.115.refs_2_), custom_call_target="tpu_custom_call" | custom-call | flops 2424307712 | bytes 5013504 | tf_op jit(solution)/shard_map/pallas_call | solution.py:81
  126.6 1.3 slice.111
  127.8 0.3 copy.34
  128.2 0.6 gather_fusion
  128.8 0.9 broadcast_select_fusion
  129.7 7.4 %all-to-all-start = ((bf16[16,136,64]{1,2,0:T(8,128)(2,1)}), bf16[16,136,64]{1,2,0:T(8,128)(2,1)S(1)}, u32[]{:S(2)}, u32[]{:S(2)}) async-start(bf16[16,136,64]{1,2,0:T(8,128)(2,1)} %broadcast_select_fusion), calls=%async_computation | async-start | bytes 1048576 | tf_op jit(solution)/shard_map/all_to_all | solution.py:165
  137.2 11.1 %all-to-all-done = bf16[16,136,64]{1,2,0:T(8,128)(2,1)S(1)} async-done(((bf16[16,136,64]{1,2,0:T(8,128)(2,1)}), bf16[16,136,64]{1,2,0:T(8,128)(2,1)S(1)}, u32[]{:S(2)}, u32[]{:S(2)}) %all-to-all-start) | async-done | bytes 278560 | tf_op jit(solution)/shard_map/all_to_all | solution.py:165
  148.3 0.6 copy.35
  148.9 0.4 reshape.206
  149.3 2.2 %fusion.65 = (f32[136]{0:T(256)S(1)}, bf16[136,1024]{1,0:T(8,128)(2,1)S(1)}) fusion(bf16[136,1024]{1,0:T(8,128)(2,1)S(1)} %reshape.206, bf16[1024,1024]{1,0:T(8,128)(2,1)} %all-gather.2.cloned.1.call-done, f32[1024]{0:T(1024)S(1)} %copy-done.3, bf16[136,1024]{1,0:T(8,128)(2,1)S(1)} %copy-done), kind=kOutput, calls=%fused_computation.67 | convolution fusion | flops 286187392 | bytes 2937376 | tf_op jit(solution)/shard_map/dot_general | solution.py:168
  151.5 0.1 fusion.67
  151.7 0.1 broadcast_in_dim.49
  151.8 1.4 collective-permute-start.13
  153.2 2.9 %collective-permute-start.14 = (bf16[136,1152]{1,0:T(8,128)(2,1)S(1)}, bf16[136,1152]{1,0:T(8,128)(2,1)S(1)}, u32[]{:S(2)}, u32[]{:S(2)}) collective-permute-start(bf16[136,1152]{1,0:T(8,128)(2,1)S(1)} %pad_maximum_fusion.8), channel_id=1, source_target_pairs={{0,2},{1,3},{2,0},{3,1},{4,6},{5,7},{6,4},{7,5},{8,10},{9,11},{10,... | collective-permute-start | bytes 940040 | tf_op jit(solution)/shard_map/ppermute | solution.py:99
  156.1 3.5 %collective-permute-done.13 = bf16[136,1152]{1,0:T(8,128)(2,1)S(1)} collective-permute-done((bf16[136,1152]{1,0:T(8,128)(2,1)S(1)}, bf16[136,1152]{1,0:T(8,128)(2,1)S(1)}, u32[]{:S(2)}, u32[]{:S(2)}) %collective-permute-start.13) | collective-permute-done | bytes 313376 | tf_op jit(solution)/shard_map/ppermute | solution.py:99
  159.5 10.3 %collective-permute-done.14 = bf16[136,1152]{1,0:T(8,128)(2,1)S(1)} collective-permute-done((bf16[136,1152]{1,0:T(8,128)(2,1)S(1)}, bf16[136,1152]{1,0:T(8,128)(2,1)S(1)}, u32[]{:S(2)}, u32[]{:S(2)}) %collective-permute-start.14) | collective-permute-done | bytes 313376 | tf_op jit(solution)/shard_map/ppermute | solution.py:99
  169.8 0.6 collective-permute-done.15
  170.4 0.3 fusion.72
  170.7 3.5 %fusion.59 = f32[544,16]{0,1:T(8,128)S(1)} fusion(bf16[2,1024,1024]{2,1,0:T(8,128)(2,1)} %param.17, f32[1024]{0:T(1024)S(1)} %bitcast.78, bf16[2,1024,16]{1,2,0:T(8,128)(2,1)S(1)} %copy-done.6, pred[544]{0:T(1024)(128)(4,1)S(1)} %get-tuple-element.31, bf16[136,1152]{1,0:T(8,128)(2,1)S(1)} %collective-permute-done.15, ...), kind=kOutput, calls=%fused_computation.61 | convolution fusion | flops 1169826304 | bytes 3423232 | tf_op jit(solution)/shard_map/dot_general | solution.py:182
  174.2 3.5 %fusion.62 = f32[544,16]{0,1:T(8,128)S(1)} fusion(f32[544,16]{0,1:T(8,128)S(1)} %fusion.59, bf16[2,1024,1024]{2,1,0:T(8,128)(2,1)} %param.17, f32[1024]{0:T(1024)S(1)} %bitcast.77, bf16[2,1024,16]{1,2,0:T(8,128)(2,1)S(1)} %copy-done.6, pred[544]{0:T(1024)(128)(4,1)S(1)} %get-tuple-element.30, bf16[136,1152]{1,0:T(8,128)(2,1)S(1)} %collective-permute-done.15, ...), kind=kOutput, calls=%fused_computation.62 | convolution fusion | flops 1169826304 | bytes 3464192 | tf_op jit(solution)/shard_map/dot_general | solution.py:182
  177.8 0.1 fusion.104
  177.9 0.2 collective-permute-start.17
  178.1 0.7 collective-permute-start.18
  178.8 0.3 collective-permute-done.16
  179.1 3.0 %collective-permute-done.17 = f32[136,16]{0,1:T(8,128)S(1)} collective-permute-done((f32[136,16]{0,1:T(8,128)S(1)}, f32[136,16]{0,1:T(8,128)S(1)}, u32[]{:S(2)}, u32[]{:S(2)}) %collective-permute-start.17) | collective-permute-done | bytes 8736 | tf_op jit(solution)/shard_map/ppermute | solution.py:99
  182.1 1.2 collective-permute-done.18
  183.2 0.6 fusion.79
  (39 shorter events, 0.5 us)
Async XLA Ops:
  7.2 142.1 %all-gather.2.cloned.1.call-start = ((), (), s32[]{:S(2)}) async-start(), calls=%async_computation.1 | async-start | bytes 2621440 | tf_op jit(solution)/shard_map/all_gather | solution.py:156
  10.2 10.3 %collective-permute-start = (bf16[136,1024]{1,0:T(8,128)(2,1)S(1)}, bf16[136,1024]{1,0:T(8,128)(2,1)S(1)}, u32[]{:S(2)}, u32[]{:S(2)}) collective-permute-start(bf16[136,1024]{1,0:T(8,128)(2,1)S(1)} %fusion.71), channel_id=1, source_target_pairs={{0,1},{1,2},{2,3},{3,0},{4,5},{5,6},{6,7},{7,4},{8,9},{9,10},{10,1... | collective-permute-start | bytes 835592 | tf_op jit(solution)/shard_map/ppermute | solution.py:99
  14.6 12.2 %collective-permute-start.1 = (bf16[136,1024]{1,0:T(8,128)(2,1)S(1)}, bf16[136,1024]{1,0:T(8,128)(2,1)S(1)}, u32[]{:S(2)}, u32[]{:S(2)}) collective-permute-start(bf16[136,1024]{1,0:T(8,128)(2,1)S(1)} %fusion.71), channel_id=1, source_target_pairs={{0,2},{1,3},{2,0},{3,1},{4,6},{5,7},{6,4},{7,5},{8,10},{9,11},{10,... | collective-permute-start | bytes 835592 | tf_op jit(solution)/shard_map/ppermute | solution.py:99
  14.6 12.8 %collective-permute-start.2 = (bf16[136,1024]{1,0:T(8,128)(2,1)S(1)}, bf16[136,1024]{1,0:T(8,128)(2,1)S(1)}, u32[]{:S(2)}, u32[]{:S(2)}) collective-permute-start(bf16[136,1024]{1,0:T(8,128)(2,1)S(1)} %fusion.71), channel_id=1, source_target_pairs={{0,3},{1,0},{2,1},{3,2},{4,7},{5,4},{6,5},{7,6},{8,11},{9,8},{10,9... | collective-permute-start | bytes 835592 | tf_op jit(solution)/shard_map/ppermute | solution.py:99
  30.5 9.6 %collective-permute-start.3 = (bf16[544,256]{1,0:T(8,128)(2,1)S(1)}, bf16[544,256]{1,0:T(8,128)(2,1)S(1)}, u32[]{:S(2)}, u32[]{:S(2)}) collective-permute-start(bf16[544,256]{1,0:T(8,128)(2,1)S(1)} %get-tuple-element.41), channel_id=1, source_target_pairs={{0,8},{8,16},{16,24},{24,0},{1,9},{9,17},{17,25},{25,1},{2,10},{10... | collective-permute-start | bytes 835592 | tf_op jit(solution)/shard_map/ppermute | solution.py:99
  31.8 15.4 %collective-permute-start.4 = (bf16[544,256]{1,0:T(8,128)(2,1)S(1)}, bf16[544,256]{1,0:T(8,128)(2,1)S(1)}, u32[]{:S(2)}, u32[]{:S(2)}) collective-permute-start(bf16[544,256]{1,0:T(8,128)(2,1)S(1)} %get-tuple-element.40), channel_id=1, source_target_pairs={{0,16},{8,24},{16,0},{24,8},{1,17},{9,25},{17,1},{25,9},{2,18},{10... | collective-permute-start | bytes 835592 | tf_op jit(solution)/shard_map/ppermute | solution.py:99
  34.3 12.9 %collective-permute-start.5 = (bf16[544,256]{1,0:T(8,128)(2,1)S(1)}, bf16[544,256]{1,0:T(8,128)(2,1)S(1)}, u32[]{:S(2)}, u32[]{:S(2)}) collective-permute-start(bf16[544,256]{1,0:T(8,128)(2,1)S(1)} %get-tuple-element.39), channel_id=1, source_target_pairs={{0,24},{8,0},{16,8},{24,16},{1,25},{9,1},{17,9},{25,17},{2,26},{10... | collective-permute-start | bytes 835592 | tf_op jit(solution)/shard_map/ppermute | solution.py:99
  48.6 16.1 %collective-permute-start.6 = (bf16[2176,128]{1,0:T(8,128)(2,1)S(1)}, bf16[2176,128]{1,0:T(8,128)(2,1)S(1)}, u32[]{:S(2)}, u32[]{:S(2)}) collective-permute-start(bf16[2176,128]{1,0:T(8,128)(2,1)S(1)} %get-tuple-element.36), channel_id=1, source_target_pairs={{0,32},{32,64},{64,96},{96,0},{1,33},{33,65},{65,97},{97,1},{2,34}... | collective-permute-start | bytes 1671176 | tf_op jit(solution)/shard_map/ppermute | solution.py:137
  50.2 14.5 %collective-permute-start.7 = (bf16[2176,128]{1,0:T(8,128)(2,1)S(1)}, bf16[2176,128]{1,0:T(8,128)(2,1)S(1)}, u32[]{:S(2)}, u32[]{:S(2)}) collective-permute-start(bf16[2176,128]{1,0:T(8,128)(2,1)S(1)} %get-tuple-element.36), channel_id=1, source_target_pairs={{0,96},{32,0},{64,32},{96,64},{1,97},{33,1},{65,33},{97,65},{2,98}... | collective-permute-start | bytes 1671176 | tf_op jit(solution)/shard_map/ppermute | solution.py:138
  52.3 13.2 %collective-permute-start.8 = (bf16[2176,128]{1,0:T(8,128)(2,1)S(1)}, bf16[2176,128]{1,0:T(8,128)(2,1)S(1)}, u32[]{:S(2)}, u32[]{:S(2)}) collective-permute-start(bf16[2176,128]{1,0:T(8,128)(2,1)S(1)} %get-tuple-element.36), channel_id=1, source_target_pairs={{0,4},{4,0},{1,5},{5,1},{2,6},{6,2},{3,7},{7,3},{8,12},{12,8},{9,1... | collective-permute-start | bytes 1671176 | tf_op jit(solution)/shard_map/ppermute | solution.py:139
  65.6 26.8 %collective-permute-start.10 = (bf16[2176,128]{1,0:T(8,128)(2,1)S(1)}, bf16[2176,128]{1,0:T(8,128)(2,1)S(1)}, u32[]{:S(2)}, u32[]{:S(2)}) collective-permute-start(bf16[2176,128]{1,0:T(8,128)(2,1)S(1)} %collective-permute-done.8), channel_id=1, source_target_pairs={{0,32},{32,64},{64,96},{96,0},{1,33},{33,65},{65,97},{97,1},{2,34}... | collective-permute-start | bytes 1671176 | tf_op jit(solution)/shard_map/ppermute | solution.py:144
  65.7 26.7 %collective-permute-start.11 = (bf16[2176,128]{1,0:T(8,128)(2,1)S(1)}, bf16[2176,128]{1,0:T(8,128)(2,1)S(1)}, u32[]{:S(2)}, u32[]{:S(2)}) collective-permute-start(bf16[2176,128]{1,0:T(8,128)(2,1)S(1)} %collective-permute-done.8), channel_id=1, source_target_pairs={{0,96},{32,0},{64,32},{96,64},{1,97},{33,1},{65,33},{97,65},{2,98}... | collective-permute-start | bytes 1671176 | tf_op jit(solution)/shard_map/ppermute | solution.py:145
  68.4 24.0 %collective-permute-start.9 = (bf16[2176,128]{1,0:T(8,128)(2,1)S(1)}, bf16[2176,128]{1,0:T(8,128)(2,1)S(1)}, u32[]{:S(2)}, u32[]{:S(2)}) collective-permute-start(bf16[2176,128]{1,0:T(8,128)(2,1)S(1)} %collective-permute-done.6), channel_id=1, source_target_pairs={{0,32},{32,64},{64,96},{96,0},{1,33},{33,65},{65,97},{97,1},{2,34}... | collective-permute-start | bytes 1671176 | tf_op jit(solution)/shard_map/ppermute | solution.py:143
  92.4 24.3 %collective-permute-start.12 = (bf16[2176,128]{1,0:T(8,128)(2,1)S(1)}, bf16[2176,128]{1,0:T(8,128)(2,1)S(1)}, u32[]{:S(2)}, u32[]{:S(2)}) collective-permute-start(bf16[2176,128]{1,0:T(8,128)(2,1)S(1)} %collective-permute-done.10), channel_id=1, source_target_pairs={{0,32},{32,64},{64,96},{96,0},{1,33},{33,65},{65,97},{97,1},{2,34}... | collective-permute-start | bytes 1671176 | tf_op jit(solution)/shard_map/ppermute | solution.py:148
  116.8 0.8 copy-start.5
  127.8 9.3 %copy-start.7 = (s32[136,1]{0,1:T(1,128)S(1)}, s32[136,1]{0,1:T(1,128)}, u32[]{:S(2)}) copy-start(s32[136,1]{0,1:T(1,128)} %param.16) | copy-start | bytes 1636
  128.8 20.5 %copy-start = (bf16[136,1024]{1,0:T(8,128)(2,1)S(1)}, bf16[136,1024]{1,0:T(8,128)(2,1)}, u32[]{:S(2)}) copy-start(bf16[136,1024]{1,0:T(8,128)(2,1)} %param.10) | copy-start | bytes 835588
  128.8 20.5 %copy-start.3 = (f32[1024]{0:T(1024)S(1)}, f32[1024]{0:T(1024)}, u32[]{:S(2)}) copy-start(f32[1024]{0:T(1024)} %param.12) | copy-start | bytes 12292
  129.7 18.6 %all-to-all-start = ((bf16[16,136,64]{1,2,0:T(8,128)(2,1)}), bf16[16,136,64]{1,2,0:T(8,128)(2,1)S(1)}, u32[]{:S(2)}, u32[]{:S(2)}) async-start(bf16[16,136,64]{1,2,0:T(8,128)(2,1)} %broadcast_select_fusion), calls=%async_computation | async-start | bytes 1048576 | tf_op jit(solution)/shard_map/all_to_all | solution.py:165
  148.3 3.2 %copy-start.4 = (f32[1024]{0:T(1024)S(1)}, f32[1024]{0:T(1024)}, u32[]{:S(2)}) copy-start(f32[1024]{0:T(1024)} %param.13) | copy-start | bytes 12292
  149.2 6.8 %copy-start.2 = (bf16[2,1024]{1,0:T(2,128)(2,1)S(1)}, bf16[2,1024]{1,0:T(2,128)(2,1)}, u32[]{:S(2)}) copy-start(bf16[2,1024]{1,0:T(2,128)(2,1)} %param.18) | copy-start | bytes 12292
  149.2 21.5 %copy-start.6 = (bf16[2,1024,16]{1,2,0:T(8,128)(2,1)S(1)}, bf16[2,1024,16]{1,2,0:T(8,128)(2,1)}, u32[]{:S(2)}) copy-start(bf16[2,1024,16]{1,2,0:T(8,128)(2,1)} %param.19) | copy-start | bytes 196612
  151.5 22.7 %copy-start.1 = (bf16[136,1024]{1,0:T(8,128)(2,1)}, bf16[136,1024]{1,0:T(8,128)(2,1)S(1)}, u32[]{:S(2)}) copy-start(bf16[136,1024]{1,0:T(8,128)(2,1)S(1)} %get-tuple-element.50) | copy-start | bytes 835588
  151.8 7.7 %collective-permute-start.13 = (bf16[136,1152]{1,0:T(8,128)(2,1)S(1)}, bf16[136,1152]{1,0:T(8,128)(2,1)S(1)}, u32[]{:S(2)}, u32[]{:S(2)}) collective-permute-start(bf16[136,1152]{1,0:T(8,128)(2,1)S(1)} %pad_maximum_fusion.8), channel_id=1, source_target_pairs={{0,1},{1,2},{2,3},{3,0},{4,5},{5,6},{6,7},{7,4},{8,9},{9,10},{10,1... | collective-permute-start | bytes 940040 | tf_op jit(solution)/shard_map/ppermute | solution.py:99
  153.2 16.6 %collective-permute-start.14 = (bf16[136,1152]{1,0:T(8,128)(2,1)S(1)}, bf16[136,1152]{1,0:T(8,128)(2,1)S(1)}, u32[]{:S(2)}, u32[]{:S(2)}) collective-permute-start(bf16[136,1152]{1,0:T(8,128)(2,1)S(1)} %pad_maximum_fusion.8), channel_id=1, source_target_pairs={{0,2},{1,3},{2,0},{3,1},{4,6},{5,7},{6,4},{7,5},{8,10},{9,11},{10,... | collective-permute-start | bytes 940040 | tf_op jit(solution)/shard_map/ppermute | solution.py:99
  156.1 14.4 %collective-permute-start.15 = (bf16[136,1152]{1,0:T(8,128)(2,1)S(1)}, bf16[136,1152]{1,0:T(8,128)(2,1)S(1)}, u32[]{:S(2)}, u32[]{:S(2)}) collective-permute-start(bf16[136,1152]{1,0:T(8,128)(2,1)S(1)} %pad_maximum_fusion.8), channel_id=1, source_target_pairs={{0,3},{1,0},{2,1},{3,2},{4,7},{5,4},{6,5},{7,6},{8,11},{9,8},{10,9... | collective-permute-start | bytes 940040 | tf_op jit(solution)/shard_map/ppermute | solution.py:99
  177.9 1.2 collective-permute-start.16
  177.9 4.2 %collective-permute-start.17 = (f32[136,16]{0,1:T(8,128)S(1)}, f32[136,16]{0,1:T(8,128)S(1)}, u32[]{:S(2)}, u32[]{:S(2)}) collective-permute-start(f32[136,16]{0,1:T(8,128)S(1)} %get-tuple-element.44), channel_id=1, source_target_pairs={{0,2},{1,3},{2,0},{3,1},{4,6},{5,7},{6,4},{7,5},{8,10},{9,11},{10,... | collective-permute-start | bytes 26120 | tf_op jit(solution)/shard_map/ppermute | solution.py:99
  178.1 5.2 %collective-permute-start.18 = (f32[136,16]{0,1:T(8,128)S(1)}, f32[136,16]{0,1:T(8,128)S(1)}, u32[]{:S(2)}, u32[]{:S(2)}) collective-permute-start(f32[136,16]{0,1:T(8,128)S(1)} %get-tuple-element.43), channel_id=1, source_target_pairs={{0,3},{1,0},{2,1},{3,2},{4,7},{5,4},{6,5},{7,6},{8,11},{9,8},{10,9... | collective-permute-start | bytes 26120 | tf_op jit(solution)/shard_map/ppermute | solution.py:99
Sparse Core Ops, SparseCore 0:
  65.7 26.3 all-gather.1

commit v11 on v10

--- a/solution.py
+++ b/solution.py
@@ -170,21 +170,24 @@
     final = (rms_normalize(updated.astype(jnp.float32)) * final_gain).astype(jnp.bfloat16)
     ids = jnp.broadcast_to(type_ids.astype(jnp.bfloat16), (rows, 128))
     ext = jnp.concatenate([final, ids], axis=1)
-    joined = jnp.concatenate([ext] + [shifted(ext, "type", k) for k in range(1, kinds)], axis=0)
-    final_all = joined[:, : final.shape[1]]
-    kinds_all = joined[:, final.shape[1]].astype(jnp.int32)
     owned = head_w1.shape[0]
     first_kind = lax.axis_index("type") * owned
-    result = jnp.zeros((final_all.shape[0], head_w2.shape[2]), jnp.float32)
-    for which in range(owned):
-        hidden = jnp.dot(final_all, head_w1[which], preferred_element_type=jnp.float32)
-        hidden = jax.nn.gelu(hidden + head_b1[which].astype(jnp.float32)).astype(jnp.bfloat16)
-        answer = jnp.dot(hidden, head_w2[which], preferred_element_type=jnp.float32)
-        result = jnp.where((kinds_all == first_kind + which)[:, None], answer, result)
-    result = result.reshape(kinds, rows, -1)
-    head_out = result[0]
+
+    def heads_of(block):
+        features = block[:, : final.shape[1]]
+        block_kinds = block[:, final.shape[1]].astype(jnp.int32)
+        result = jnp.zeros((rows, head_w2.shape[2]), jnp.float32)
+        for which in range(owned):
+            hidden = jnp.dot(features, head_w1[which], preferred_element_type=jnp.float32)
+            hidden = jax.nn.gelu(hidden + head_b1[which].astype(jnp.float32)).astype(jnp.bfloat16)
+            answer = jnp.dot(hidden, head_w2[which], preferred_element_type=jnp.float32)
+            result = jnp.where((block_kinds == first_kind + which)[:, None], answer, result)
+        return result
+
+    arriving = [shifted(ext, "type", k) for k in range(1, kinds)]
+    head_out = heads_of(ext)
     for k in range(1, kinds):
-        head_out = head_out + shifted(result[(-k) % kinds], "type", k)
+        head_out = head_out + shifted(heads_of(arriving[k - 1]), "type", -k)
     return (updated, head_out)
 
 

time: 191 us -> 194 us (1.016)
  waiting for transfers between devices: 52.8 us -> 38 us
  matrix products: 12.2 us -> 23.8 us
  starting transfers between devices: 29.9 us -> 35.3 us
    ppermute x12, waiting for transfers between devices: 37.8 us -> 23.2 us  [shifted(): return lax.ppermute(value, axis, [(i, (i + k) % n) for i in range(n)])]
    dot_general x2 -> x8, matrix products: 7.05 us -> 18.6 us  [heads_of(): answer = jnp.dot(hidden, head_w2[which], preferred_element_type=jnp.float32)]
    ppermute x12, starting transfers between devices: 14.9 us -> 20.3 us  [shifted(): return lax.ppermute(value, axis, [(i, (i + k) % n) for i in range(n)])]
  transfers between devices with their start and end apart: 21 -> 21, of which waited for: 14 -> 10; matrix products, arithmetic and copies ran while one was open for 6% -> 15% of each run, Pallas kernels for 33% -> 33%
where the time goes in v11:
time: 194 us; the launch traced here: 193 us
  Pallas kernels  63 us (32%)
  waiting for transfers between devices  38 us (20%)
  starting transfers between devices  35.3 us (18%)
  matrix products  23.8 us (12%)
  between operations  14.4 us (7%)
  local copies, waits for them, and re-layouts  10.3 us (5%)
  other arithmetic  8.09 us (4%)
    pallas_call x4, Pallas kernels, flash_step(): pl.pallas_call(functools.partial(step_kernel, first, last), grid=(rows //...  63 us
    ppermute x12, waiting for transfers between devices, shifted(): return lax.ppermute(value, axis, [(i, (i + k) % n) for i in range(n)])  23.2 us
    ppermute x12, starting transfers between devices, shifted(): return lax.ppermute(value, axis, [(i, (i + k) % n) for i in range(n)])  20.3 us
    dot_general x8, matrix products, heads_of(): answer = jnp.dot(hidden, head_w2[which], preferred_element_type=jnp.float32)  18.6 us
    all_to_all x1, waiting for transfers between devices, body(): back = lax.all_to_all(attended, ('x', 'type'), 0, 0, tiled=True)  10.9 us
    all_to_all x1, starting transfers between devices, body(): back = lax.all_to_all(attended, ('x', 'type'), 0, 0, tiled=True)  7.45 us
  transfers between devices with their start and end apart: 21, of which 10 were waited for; matrix products, arithmetic and copies ran while one was open for 15% of the time, Pallas kernels for 33%

profile of v11, /device:TPU:1, one launch (start us, length us, event | category | flops | bytes accessed | tf_op | source)
XLA Modules:
  0.0 192.9 jit_solution(1701880533004590927)
XLA Ops:
  7.2 0.8 slice_add_fusion
  8.0 1.1 fusion.72
  9.1 1.1 fusion.75
  10.2 4.4 %collective-permute-start = (bf16[136,1024]{1,0:T(8,128)(2,1)S(1)}, bf16[136,1024]{1,0:T(8,128)(2,1)S(1)}, u32[]{:S(2)}, u32[]{:S(2)}) collective-permute-start(bf16[136,1024]{1,0:T(8,128)(2,1)S(1)} %fusion.75), channel_id=1, source_target_pairs={{0,1},{1,2},{2,3},{3,0},{4,5},{5,6},{6,7},{7,4},{8,9},{9,10},{10,1... | collective-permute-start | bytes 835592 | tf_op jit(solution)/shard_map/ppermute | solution.py:99
  14.6 0.5 collective-permute-start.2
  15.1 1.5 fusion.336
  16.5 0.2 copy.40
  16.8 0.2 copy.41
  17.0 0.2 copy.42
  17.3 0.2 pad_maximum_fusion
  17.6 0.2 copy.34
  17.8 2.6 %copy.35 = bf16[1024,4,256]{2,0,1:T(8,128)(2,1)} copy(bf16[1024,4,256]{0,2,1:T(8,128)(2,1)S(1)} %bitcast.153) | data formatting | bytes 4194304 | tf_op jit(solution)/shard_map/reshape | solution.py:117
  20.3 0.1 collective-permute-done
  20.5 6.4 %collective-permute-done.1 = bf16[136,1024]{1,0:T(8,128)(2,1)S(1)} collective-permute-done((bf16[136,1024]{1,0:T(8,128)(2,1)S(1)}, bf16[136,1024]{1,0:T(8,128)(2,1)S(1)}, u32[]{:S(2)}, u32[]{:S(2)}) %collective-permute-start.1) | collective-permute-done | bytes 278560 | tf_op jit(solution)/shard_map/ppermute | solution.py:99
  26.8 0.6 collective-permute-done.2
  27.4 3.0 %fusion.22 = bf16[4,544,256]{2,1,0:T(8,128)(2,1)S(1)} fusion(s32[]{:T(128)S(6)} %select_n.126, bf16[1024,4,256]{2,0,1:T(8,128)(2,1)} %copy.35, bf16[136,1024]{1,0:T(8,128)(2,1)S(1)} %collective-permute-done.2, bf16[136,1024]{1,0:T(8,128)(2,1)S(1)} %collective-permute-done.1, bf16[136,1024]{1,0:T(8,128)(2,1)S(1)} %collective-permute-done, ...), kind=kOutput, calls=%fused_computation.25 | convolution fusion | flops 1150058496 | bytes 4325380 | tf_op jit(solution)/shard_map/rd,dje->jre/dot_general | solution.py:119
  30.5 1.3 collective-permute-start.3
  31.8 2.5 %collective-permute-start.4 = (bf16[544,256]{1,0:T(8,128)(2,1)S(1)}, bf16[544,256]{1,0:T(8,128)(2,1)S(1)}, u32[]{:S(2)}, u32[]{:S(2)}) collective-permute-start(bf16[544,256]{1,0:T(8,128)(2,1)S(1)} %get-tuple-element.46), channel_id=1, source_target_pairs={{0,16},{8,24},{16,0},{24,8},{1,17},{9,25},{17,1},{25,9},{2,18},{10... | collective-permute-start | bytes 835592 | tf_op jit(solution)/shard_map/ppermute | solution.py:99
  34.3 1.1 collective-permute-start.5
  35.4 4.7 %collective-permute-done.3 = bf16[544,256]{1,0:T(8,128)(2,1)S(1)} collective-permute-done((bf16[544,256]{1,0:T(8,128)(2,1)S(1)}, bf16[544,256]{1,0:T(8,128)(2,1)S(1)}, u32[]{:S(2)}, u32[]{:S(2)}) %collective-permute-start.3) | collective-permute-done | bytes 278560 | tf_op jit(solution)/shard_map/ppermute | solution.py:99
  40.1 7.1 %collective-permute-done.4 = bf16[544,256]{1,0:T(8,128)(2,1)S(1)} collective-permute-done((bf16[544,256]{1,0:T(8,128)(2,1)S(1)}, bf16[544,256]{1,0:T(8,128)(2,1)S(1)}, u32[]{:S(2)}, u32[]{:S(2)}) %collective-permute-start.4) | collective-permute-done | bytes 278560 | tf_op jit(solution)/shard_map/ppermute | solution.py:99
  47.3 1.2 slice_bitcast_fusion.4
  48.5 1.7 collective-permute-start.6
  50.2 2.1 %collective-permute-start.7 = (bf16[2176,128]{1,0:T(8,128)(2,1)S(1)}, bf16[2176,128]{1,0:T(8,128)(2,1)S(1)}, u32[]{:S(2)}, u32[]{:S(2)}) collective-permute-start(bf16[2176,128]{1,0:T(8,128)(2,1)S(1)} %get-tuple-element.42), channel_id=1, source_target_pairs={{0,96},{32,0},{64,32},{96,64},{1,97},{33,1},{65,33},{97,65},{2,98}... | collective-permute-start | bytes 1671176 | tf_op jit(solution)/shard_map/ppermute | solution.py:138
  52.3 0.7 collective-permute-start.8
  53.0 8.6 %shard_map.113.refs_2_ = f32[2176,128]{1,0:T(8,128)} custom-call(bf16[2176,128]{1,0:T(8,128)(2,1)} %get-tuple-element.43.refs_0_, bf16[1,2176,128]{2,1,0:T(8,128)(2,1)} %get-tuple-element.41.refs_1_), custom_call_target="tpu_custom_call" | custom-call | flops 2424307712 | bytes 5013504 | tf_op jit(solution)/shard_map/pallas_call | solution.py:81
  61.6 3.0 %collective-permute-done.6 = bf16[2176,128]{1,0:T(8,128)(2,1)S(1)} collective-permute-done((bf16[2176,128]{1,0:T(8,128)(2,1)S(1)}, bf16[2176,128]{1,0:T(8,128)(2,1)S(1)}, u32[]{:S(2)}, u32[]{:S(2)}) %collective-permute-start.6) | collective-permute-done | bytes 557088 | tf_op jit(solution)/shard_map/ppermute | solution.py:137
  64.7 0.8 collective-permute-done.8
  65.7 2.7 %collective-permute-start.11 = (bf16[2176,128]{1,0:T(8,128)(2,1)S(1)}, bf16[2176,128]{1,0:T(8,128)(2,1)S(1)}, u32[]{:S(2)}, u32[]{:S(2)}) collective-permute-start(bf16[2176,128]{1,0:T(8,128)(2,1)S(1)} %collective-permute-done.8), channel_id=1, source_target_pairs={{0,96},{32,0},{64,32},{96,64},{1,97},{33,1},{65,33},{97,65},{2,98}... | collective-permute-start | bytes 1671176 | tf_op jit(solution)/shard_map/ppermute | solution.py:145
  68.3 1.4 pad_maximum_fusion.1.refs_1_
  69.7 22.7 %shard_map.114.refs_2_ = f32[2176,128]{1,0:T(8,128)} custom-call(bf16[2176,128]{1,0:T(8,128)(2,1)} %get-tuple-element.43.refs_0_, bf16[3,2176,128]{2,1,0:T(8,128)(2,1)} %pad_maximum_fusion.1.refs_1_, f32[2176,128]{1,0:T(8,128)} %shard_map.113.refs_2_), custom_call_target="tpu_custom_call" | custom-call | flops 7272923136 | bytes 9469952 | tf_op jit(solution)/shard_map/pallas_call | solution.py:81
  92.4 0.3 collective-permute-start.12
  92.7 1.4 pad_maximum_fusion.2.refs_1_
  94.1 22.7 %shard_map.115.refs_2_ = f32[2176,128]{1,0:T(8,128)} custom-call(bf16[2176,128]{1,0:T(8,128)(2,1)} %get-tuple-element.43.refs_0_, bf16[3,2176,128]{2,1,0:T(8,128)(2,1)} %pad_maximum_fusion.2.refs_1_, f32[2176,128]{1,0:T(8,128)} %shard_map.114.refs_2_), custom_call_target="tpu_custom_call" | custom-call | flops 7272923136 | bytes 9469952 | tf_op jit(solution)/shard_map/pallas_call | solution.py:81
  116.8 0.8 copy-done.6
  117.6 9.0 %shard_map.116 = bf16[2176,128]{1,0:T(8,128)(2,1)} custom-call(bf16[2176,128]{1,0:T(8,128)(2,1)} %get-tuple-element.43.refs_0_, bf16[1,2176,128]{2,1,0:T(8,128)(2,1)} %bitcast.175, f32[2176,128]{1,0:T(8,128)} %shard_map.115.refs_2_), custom_call_target="tpu_custom_call" | custom-call | flops 2424307712 | bytes 5013504 | tf_op jit(solution)/shard_map/pallas_call | solution.py:81
  126.6 1.3 slice.126
  127.9 0.3 copy.37
  128.2 0.6 gather_fusion
  128.8 0.9 broadcast_select_fusion
  129.7 7.4 %all-to-all-start = ((bf16[16,136,64]{1,2,0:T(8,128)(2,1)}), bf16[16,136,64]{1,2,0:T(8,128)(2,1)S(1)}, u32[]{:S(2)}, u32[]{:S(2)}) async-start(bf16[16,136,64]{1,2,0:T(8,128)(2,1)} %broadcast_select_fusion), calls=%async_computation | async-start | bytes 1048576 | tf_op jit(solution)/shard_map/all_to_all | solution.py:165
  137.4 10.9 %all-to-all-done = bf16[16,136,64]{1,2,0:T(8,128)(2,1)S(1)} async-done(((bf16[16,136,64]{1,2,0:T(8,128)(2,1)}), bf16[16,136,64]{1,2,0:T(8,128)(2,1)S(1)}, u32[]{:S(2)}, u32[]{:S(2)}) %all-to-all-start) | async-done | bytes 278560 | tf_op jit(solution)/shard_map/all_to_all | solution.py:165
  148.3 0.6 copy.38
  148.9 0.4 reshape.201
  149.3 2.2 %fusion.69 = (f32[136]{0:T(256)S(1)}, bf16[136,1024]{1,0:T(8,128)(2,1)S(1)}) fusion(bf16[136,1024]{1,0:T(8,128)(2,1)S(1)} %reshape.201, bf16[1024,1024]{1,0:T(8,128)(2,1)} %all-gather.2.cloned.1.call-done, f32[1024]{0:T(1024)S(1)} %copy-done.3, bf16[136,1024]{1,0:T(8,128)(2,1)S(1)} %copy-done), kind=kOutput, calls=%fused_computation.70 | convolution fusion | flops 286187392 | bytes 2937376 | tf_op jit(solution)/shard_map/dot_general | solution.py:168
  151.6 0.1 fusion.71
  151.9 1.4 collective-permute-start.13
  153.2 0.2 fusion.247
  153.4 3.0 %collective-permute-start.15 = (bf16[136,1152]{1,0:T(8,128)(2,1)S(1)}, bf16[136,1152]{1,0:T(8,128)(2,1)S(1)}, u32[]{:S(2)}, u32[]{:S(2)}) collective-permute-start(bf16[136,1152]{1,0:T(8,128)(2,1)S(1)} %pad_maximum_fusion.4), channel_id=1, source_target_pairs={{0,2},{1,3},{2,0},{3,1},{4,6},{5,7},{6,4},{7,5},{8,10},{9,11},{10,... | collective-permute-start | bytes 940040 | tf_op jit(solution)/shard_map/ppermute | solution.py:99
  156.4 2.9 %collective-permute-done.13 = bf16[136,1152]{1,0:T(8,128)(2,1)S(1)} collective-permute-done((bf16[136,1152]{1,0:T(8,128)(2,1)S(1)}, bf16[136,1152]{1,0:T(8,128)(2,1)S(1)}, u32[]{:S(2)}, u32[]{:S(2)}) %collective-permute-start.13) | collective-permute-done | bytes 313376 | tf_op jit(solution)/shard_map/ppermute | solution.py:99
  159.3 2.2 %fusion.133 = f32[136,16]{0,1:T(8,128)S(1)} fusion(bf16[2,1024,1024]{2,1,0:T(8,128)(2,1)} %param.17, f32[1024]{0:T(1024)S(1)} %bitcast.167, bf16[136,1152]{1,0:T(8,128)(2,1)S(1)} %collective-permute-done.13, bf16[2,1024,16]{1,2,0:T(8,128)(2,1)S(1)} %copy-done.7), kind=kOutput, calls=%fused_computation.111 | convolution fusion | flops 291061760 | bytes 2421248 | tf_op jit(solution)/shard_map/dot_general | solution.py:183
  161.5 0.2 fusion.249
  161.7 2.2 %select_select_fusion.2 = f32[136,16]{0,1:T(8,128)S(1)} fusion(f32[136,16]{0,1:T(8,128)S(1)} %fusion.133, pred[136]{0:T(512)(128)(4,1)S(1)} %get-tuple-element.31, pred[136]{0:T(512)(128)(4,1)S(1)} %get-tuple-element.30, bf16[2,1024,16]{1,2,0:T(8,128)(2,1)S(1)} %copy-done.7, bf16[2,1024,1024]{2,1,0:T(8,128)(2,1)} %param.17, f32[1024]{0:T(1024)S(1)} %bitcast.171, ...), kind=kOutput, calls=%fused_computation.235 | convolution fusion | flops 291066112 | bytes 2438656 | tf_op jit(solution)/shard_map/dot_general | solution.py:183
  164.0 4.4 %collective-permute-start.14 = (f32[136,16]{0,1:T(8,128)S(1)}, f32[136,16]{0,1:T(8,128)S(1)}, u32[]{:S(2)}, u32[]{:S(2)}) collective-permute-start(f32[136,16]{0,1:T(8,128)S(1)} %select_select_fusion.2), channel_id=1, source_target_pairs={{0,3},{1,0},{2,1},{3,2},{4,7},{5,4},{6,5},{7,6},{8,11},{9,8},{10,9... | collective-permute-start | bytes 26120 | tf_op jit(solution)/shard_map/ppermute | solution.py:99
  168.3 1.3 collective-permute-done.15
  169.7 2.2 %fusion.163 = f32[136,16]{0,1:T(8,128)S(1)} fusion(bf16[2,1024,1024]{2,1,0:T(8,128)(2,1)} %param.17, f32[1024]{0:T(1024)S(1)} %bitcast.168, bf16[136,1152]{1,0:T(8,128)(2,1)S(1)} %collective-permute-done.15, bf16[2,1024,16]{1,2,0:T(8,128)(2,1)S(1)} %copy-done.7), kind=kOutput, calls=%fused_computation.129 | convolution fusion | flops 291061760 | bytes 2421248 | tf_op jit(solution)/shard_map/dot_general | solution.py:183
  171.9 0.2 fusion.251
  172.1 2.2 %select_select_fusion.1 = f32[136,16]{0,1:T(8,128)S(1)} fusion(f32[136,16]{0,1:T(8,128)S(1)} %fusion.163, pred[136]{0:T(512)(128)(4,1)S(1)} %get-tuple-element.33, pred[136]{0:T(512)(128)(4,1)S(1)} %get-tuple-element.32, bf16[2,1024,16]{1,2,0:T(8,128)(2,1)S(1)} %copy-done.7, bf16[2,1024,1024]{2,1,0:T(8,128)(2,1)} %param.17, f32[1024]{0:T(1024)S(1)} %bitcast.172, ...), kind=kOutput, calls=%fused_computation.234 | convolution fusion | flops 291066112 | bytes 2438656 | tf_op jit(solution)/shard_map/dot_general | solution.py:183
  174.4 2.2 %fusion.193 = f32[136,16]{0,1:T(8,128)S(1)} fusion(bf16[2,1024,1024]{2,1,0:T(8,128)(2,1)} %param.17, f32[1024]{0:T(1024)S(1)} %bitcast.169, bf16[136,1152]{1,0:T(8,128)(2,1)S(1)} %collective-permute-done.17, bf16[2,1024,16]{1,2,0:T(8,128)(2,1)S(1)} %copy-done.7), kind=kOutput, calls=%fused_computation.147 | convolution fusion | flops 291061760 | bytes 2421248 | tf_op jit(solution)/shard_map/dot_general | solution.py:183
  176.6 0.2 fusion.253
  176.8 2.2 %select_select_fusion = f32[136,16]{0,1:T(8,128)S(1)} fusion(f32[136,16]{0,1:T(8,128)S(1)} %fusion.193, pred[136]{0:T(512)(128)(4,1)S(1)} %get-tuple-element.35, pred[136]{0:T(512)(128)(4,1)S(1)} %get-tuple-element.34, bf16[2,1024,16]{1,2,0:T(8,128)(2,1)S(1)} %copy-done.7, bf16[2,1024,1024]{2,1,0:T(8,128)(2,1)} %param.17, f32[1024]{0:T(1024)S(1)} %bitcast.173, ...), kind=kOutput, calls=%fused_computation.233 | convolution fusion | flops 291066112 | bytes 2438656 | tf_op jit(solution)/shard_map/dot_general | solution.py:183
  179.0 1.8 collective-permute-start.18
  180.9 2.2 %fusion.89 = f32[136,16]{0,1:T(8,128)S(1)} fusion(bf16[136,1024]{1,0:T(8,128)(2,1)S(1)} %fusion.71, bf16[2,1024,1024]{2,1,0:T(8,128)(2,1)} %param.17, f32[1024]{0:T(1024)S(1)} %bitcast.174, bf16[2,1024,16]{1,2,0:T(8,128)(2,1)S(1)} %copy-done.7), kind=kOutput, calls=%fused_computation.85 | convolution fusion | flops 291061760 | bytes 2421248 | tf_op jit(solution)/shard_map/dot_general | solution.py:183
  183.2 2.9 %fusion.68 = f32[136,16]{0,1:T(8,128)} fusion(f32[136,16]{0,1:T(8,128)S(1)} %collective-permute-done.18, f32[136,16]{0,1:T(8,128)S(1)} %collective-permute-done.16, f32[136,16]{0,1:T(8,128)S(1)} %collective-permute-done.14, f32[136,16]{0,1:T(8,128)S(1)} %fusion.89, bf16[136,1024]{1,0:T(8,128)(2,1)S(1)} %fusion.71, bf16[2,1024,1024]{2,1,0:T(8,128)(2,1)} %param.17, ...), kind=kOutput, calls=%fused_computation.57 | convolution fusion | flops 291072640 | bytes 2487808 | tf_op jit(solution)/shard_map/dot_general | solution.py:183
  (47 shorter events, 0.9 us)
Async XLA Ops:
  7.2 142.1 %all-gather.2.cloned.1.call-start = ((), (), s32[]{:S(2)}) async-start(), calls=%async_computation.1 | async-start | bytes 2621440 | tf_op jit(solution)/shard_map/all_gather | solution.py:156
  10.2 10.3 %collective-permute-start = (bf16[136,1024]{1,0:T(8,128)(2,1)S(1)}, bf16[136,1024]{1,0:T(8,128)(2,1)S(1)}, u32[]{:S(2)}, u32[]{:S(2)}) collective-permute-start(bf16[136,1024]{1,0:T(8,128)(2,1)S(1)} %fusion.75), channel_id=1, source_target_pairs={{0,1},{1,2},{2,3},{3,0},{4,5},{5,6},{6,7},{7,4},{8,9},{9,10},{10,1... | collective-permute-start | bytes 835592 | tf_op jit(solution)/shard_map/ppermute | solution.py:99
  14.6 12.2 %collective-permute-start.1 = (bf16[136,1024]{1,0:T(8,128)(2,1)S(1)}, bf16[136,1024]{1,0:T(8,128)(2,1)S(1)}, u32[]{:S(2)}, u32[]{:S(2)}) collective-permute-start(bf16[136,1024]{1,0:T(8,128)(2,1)S(1)} %fusion.75), channel_id=1, source_target_pairs={{0,2},{1,3},{2,0},{3,1},{4,6},{5,7},{6,4},{7,5},{8,10},{9,11},{10,... | collective-permute-start | bytes 835592 | tf_op jit(solution)/shard_map/ppermute | solution.py:99
  14.6 12.8 %collective-permute-start.2 = (bf16[136,1024]{1,0:T(8,128)(2,1)S(1)}, bf16[136,1024]{1,0:T(8,128)(2,1)S(1)}, u32[]{:S(2)}, u32[]{:S(2)}) collective-permute-start(bf16[136,1024]{1,0:T(8,128)(2,1)S(1)} %fusion.75), channel_id=1, source_target_pairs={{0,3},{1,0},{2,1},{3,2},{4,7},{5,4},{6,5},{7,6},{8,11},{9,8},{10,9... | collective-permute-start | bytes 835592 | tf_op jit(solution)/shard_map/ppermute | solution.py:99
  30.5 9.6 %collective-permute-start.3 = (bf16[544,256]{1,0:T(8,128)(2,1)S(1)}, bf16[544,256]{1,0:T(8,128)(2,1)S(1)}, u32[]{:S(2)}, u32[]{:S(2)}) collective-permute-start(bf16[544,256]{1,0:T(8,128)(2,1)S(1)} %get-tuple-element.47), channel_id=1, source_target_pairs={{0,8},{8,16},{16,24},{24,0},{1,9},{9,17},{17,25},{25,1},{2,10},{10... | collective-permute-start | bytes 835592 | tf_op jit(solution)/shard_map/ppermute | solution.py:99
  31.8 15.4 %collective-permute-start.4 = (bf16[544,256]{1,0:T(8,128)(2,1)S(1)}, bf16[544,256]{1,0:T(8,128)(2,1)S(1)}, u32[]{:S(2)}, u32[]{:S(2)}) collective-permute-start(bf16[544,256]{1,0:T(8,128)(2,1)S(1)} %get-tuple-element.46), channel_id=1, source_target_pairs={{0,16},{8,24},{16,0},{24,8},{1,17},{9,25},{17,1},{25,9},{2,18},{10... | collective-permute-start | bytes 835592 | tf_op jit(solution)/shard_map/ppermute | solution.py:99
  34.3 12.9 %collective-permute-start.5 = (bf16[544,256]{1,0:T(8,128)(2,1)S(1)}, bf16[544,256]{1,0:T(8,128)(2,1)S(1)}, u32[]{:S(2)}, u32[]{:S(2)}) collective-permute-start(bf16[544,256]{1,0:T(8,128)(2,1)S(1)} %get-tuple-element.45), channel_id=1, source_target_pairs={{0,24},{8,0},{16,8},{24,16},{1,25},{9,1},{17,9},{25,17},{2,26},{10... | collective-permute-start | bytes 835592 | tf_op jit(solution)/shard_map/ppermute | solution.py:99
  48.5 16.1 %collective-permute-start.6 = (bf16[2176,128]{1,0:T(8,128)(2,1)S(1)}, bf16[2176,128]{1,0:T(8,128)(2,1)S(1)}, u32[]{:S(2)}, u32[]{:S(2)}) collective-permute-start(bf16[2176,128]{1,0:T(8,128)(2,1)S(1)} %get-tuple-element.42), channel_id=1, source_target_pairs={{0,32},{32,64},{64,96},{96,0},{1,33},{33,65},{65,97},{97,1},{2,34}... | collective-permute-start | bytes 1671176 | tf_op jit(solution)/shard_map/ppermute | solution.py:137
  50.2 14.5 %collective-permute-start.7 = (bf16[2176,128]{1,0:T(8,128)(2,1)S(1)}, bf16[2176,128]{1,0:T(8,128)(2,1)S(1)}, u32[]{:S(2)}, u32[]{:S(2)}) collective-permute-start(bf16[2176,128]{1,0:T(8,128)(2,1)S(1)} %get-tuple-element.42), channel_id=1, source_target_pairs={{0,96},{32,0},{64,32},{96,64},{1,97},{33,1},{65,33},{97,65},{2,98}... | collective-permute-start | bytes 1671176 | tf_op jit(solution)/shard_map/ppermute | solution.py:138
  52.3 13.2 %collective-permute-start.8 = (bf16[2176,128]{1,0:T(8,128)(2,1)S(1)}, bf16[2176,128]{1,0:T(8,128)(2,1)S(1)}, u32[]{:S(2)}, u32[]{:S(2)}) collective-permute-start(bf16[2176,128]{1,0:T(8,128)(2,1)S(1)} %get-tuple-element.42), channel_id=1, source_target_pairs={{0,4},{4,0},{1,5},{5,1},{2,6},{6,2},{3,7},{7,3},{8,12},{12,8},{9,1... | collective-permute-start | bytes 1671176 | tf_op jit(solution)/shard_map/ppermute | solution.py:139
  65.6 26.8 %collective-permute-start.10 = (bf16[2176,128]{1,0:T(8,128)(2,1)S(1)}, bf16[2176,128]{1,0:T(8,128)(2,1)S(1)}, u32[]{:S(2)}, u32[]{:S(2)}) collective-permute-start(bf16[2176,128]{1,0:T(8,128)(2,1)S(1)} %collective-permute-done.8), channel_id=1, source_target_pairs={{0,32},{32,64},{64,96},{96,0},{1,33},{33,65},{65,97},{97,1},{2,34}... | collective-permute-start | bytes 1671176 | tf_op jit(solution)/shard_map/ppermute | solution.py:144
  65.7 26.7 %collective-permute-start.11 = (bf16[2176,128]{1,0:T(8,128)(2,1)S(1)}, bf16[2176,128]{1,0:T(8,128)(2,1)S(1)}, u32[]{:S(2)}, u32[]{:S(2)}) collective-permute-start(bf16[2176,128]{1,0:T(8,128)(2,1)S(1)} %collective-permute-done.8), channel_id=1, source_target_pairs={{0,96},{32,0},{64,32},{96,64},{1,97},{33,1},{65,33},{97,65},{2,98}... | collective-permute-start | bytes 1671176 | tf_op jit(solution)/shard_map/ppermute | solution.py:145
  68.3 24.1 %collective-permute-start.9 = (bf16[2176,128]{1,0:T(8,128)(2,1)S(1)}, bf16[2176,128]{1,0:T(8,128)(2,1)S(1)}, u32[]{:S(2)}, u32[]{:S(2)}) collective-permute-start(bf16[2176,128]{1,0:T(8,128)(2,1)S(1)} %collective-permute-done.6), channel_id=1, source_target_pairs={{0,32},{32,64},{64,96},{96,0},{1,33},{33,65},{65,97},{97,1},{2,34}... | collective-permute-start | bytes 1671176 | tf_op jit(solution)/shard_map/ppermute | solution.py:143
  92.4 24.3 %collective-permute-start.12 = (bf16[2176,128]{1,0:T(8,128)(2,1)S(1)}, bf16[2176,128]{1,0:T(8,128)(2,1)S(1)}, u32[]{:S(2)}, u32[]{:S(2)}) collective-permute-start(bf16[2176,128]{1,0:T(8,128)(2,1)S(1)} %collective-permute-done.10), channel_id=1, source_target_pairs={{0,32},{32,64},{64,96},{96,0},{1,33},{33,65},{65,97},{97,1},{2,34}... | collective-permute-start | bytes 1671176 | tf_op jit(solution)/shard_map/ppermute | solution.py:148
  116.8 0.8 copy-start.6
  127.8 9.3 %copy-start.5 = (s32[136,1]{0,1:T(1,128)S(1)}, s32[136,1]{0,1:T(1,128)}, u32[]{:S(2)}) copy-start(s32[136,1]{0,1:T(1,128)} %param.16) | copy-start | bytes 1636
  128.8 20.5 %copy-start = (bf16[136,1024]{1,0:T(8,128)(2,1)S(1)}, bf16[136,1024]{1,0:T(8,128)(2,1)}, u32[]{:S(2)}) copy-start(bf16[136,1024]{1,0:T(8,128)(2,1)} %param.10) | copy-start | bytes 835588
  128.8 20.5 %copy-start.3 = (f32[1024]{0:T(1024)S(1)}, f32[1024]{0:T(1024)}, u32[]{:S(2)}) copy-start(f32[1024]{0:T(1024)} %param.12) | copy-start | bytes 12292
  129.7 18.6 %all-to-all-start = ((bf16[16,136,64]{1,2,0:T(8,128)(2,1)}), bf16[16,136,64]{1,2,0:T(8,128)(2,1)S(1)}, u32[]{:S(2)}, u32[]{:S(2)}) async-start(bf16[16,136,64]{1,2,0:T(8,128)(2,1)} %broadcast_select_fusion), calls=%async_computation | async-start | bytes 1048576 | tf_op jit(solution)/shard_map/all_to_all | solution.py:165
  148.9 2.7 %copy-start.4 = (f32[1024]{0:T(1024)S(1)}, f32[1024]{0:T(1024)}, u32[]{:S(2)}) copy-start(f32[1024]{0:T(1024)} %param.13) | copy-start | bytes 12292
  149.3 4.1 %copy-start.2 = (bf16[2,1024]{1,0:T(2,128)(2,1)S(1)}, bf16[2,1024]{1,0:T(2,128)(2,1)}, u32[]{:S(2)}) copy-start(bf16[2,1024]{1,0:T(2,128)(2,1)} %param.18) | copy-start | bytes 12292
  149.3 10.0 %copy-start.7 = (bf16[2,1024,16]{1,2,0:T(8,128)(2,1)S(1)}, bf16[2,1024,16]{1,2,0:T(8,128)(2,1)}, u32[]{:S(2)}) copy-start(bf16[2,1024,16]{1,2,0:T(8,128)(2,1)} %param.19) | copy-start | bytes 196612
  151.6 10.0 %copy-start.1 = (bf16[136,1024]{1,0:T(8,128)(2,1)}, bf16[136,1024]{1,0:T(8,128)(2,1)S(1)}, u32[]{:S(2)}) copy-start(bf16[136,1024]{1,0:T(8,128)(2,1)S(1)} %get-tuple-element.53) | copy-start | bytes 835588
  151.9 7.5 %collective-permute-start.13 = (bf16[136,1152]{1,0:T(8,128)(2,1)S(1)}, bf16[136,1152]{1,0:T(8,128)(2,1)S(1)}, u32[]{:S(2)}, u32[]{:S(2)}) collective-permute-start(bf16[136,1152]{1,0:T(8,128)(2,1)S(1)} %pad_maximum_fusion.4), channel_id=1, source_target_pairs={{0,1},{1,2},{2,3},{3,0},{4,5},{5,6},{6,7},{7,4},{8,9},{9,10},{10,1... | collective-permute-start | bytes 940040 | tf_op jit(solution)/shard_map/ppermute | solution.py:99
  153.4 16.2 %collective-permute-start.15 = (bf16[136,1152]{1,0:T(8,128)(2,1)S(1)}, bf16[136,1152]{1,0:T(8,128)(2,1)S(1)}, u32[]{:S(2)}, u32[]{:S(2)}) collective-permute-start(bf16[136,1152]{1,0:T(8,128)(2,1)S(1)} %pad_maximum_fusion.4), channel_id=1, source_target_pairs={{0,2},{1,3},{2,0},{3,1},{4,6},{5,7},{6,4},{7,5},{8,10},{9,11},{10,... | collective-permute-start | bytes 940040 | tf_op jit(solution)/shard_map/ppermute | solution.py:99
  156.4 18.0 %collective-permute-start.17 = (bf16[136,1152]{1,0:T(8,128)(2,1)S(1)}, bf16[136,1152]{1,0:T(8,128)(2,1)S(1)}, u32[]{:S(2)}, u32[]{:S(2)}) collective-permute-start(bf16[136,1152]{1,0:T(8,128)(2,1)S(1)} %pad_maximum_fusion.4), channel_id=1, source_target_pairs={{0,3},{1,0},{2,1},{3,2},{4,7},{5,4},{6,5},{7,6},{8,11},{9,8},{10,9... | collective-permute-start | bytes 940040 | tf_op jit(solution)/shard_map/ppermute | solution.py:99
  164.0 19.2 %collective-permute-start.14 = (f32[136,16]{0,1:T(8,128)S(1)}, f32[136,16]{0,1:T(8,128)S(1)}, u32[]{:S(2)}, u32[]{:S(2)}) collective-permute-start(f32[136,16]{0,1:T(8,128)S(1)} %select_select_fusion.2), channel_id=1, source_target_pairs={{0,3},{1,0},{2,1},{3,2},{4,7},{5,4},{6,5},{7,6},{8,11},{9,8},{10,9... | collective-permute-start | bytes 26120 | tf_op jit(solution)/shard_map/ppermute | solution.py:99
  174.3 8.8 %collective-permute-start.16 = (f32[136,16]{0,1:T(8,128)S(1)}, f32[136,16]{0,1:T(8,128)S(1)}, u32[]{:S(2)}, u32[]{:S(2)}) collective-permute-start(f32[136,16]{0,1:T(8,128)S(1)} %select_select_fusion.1), channel_id=1, source_target_pairs={{0,2},{1,3},{2,0},{3,1},{4,6},{5,7},{6,4},{7,5},{8,10},{9,11},{10,... | collective-permute-start | bytes 26120 | tf_op jit(solution)/shard_map/ppermute | solution.py:99
  179.0 4.1 %collective-permute-start.18 = (f32[136,16]{0,1:T(8,128)S(1)}, f32[136,16]{0,1:T(8,128)S(1)}, u32[]{:S(2)}, u32[]{:S(2)}) collective-permute-start(f32[136,16]{0,1:T(8,128)S(1)} %select_select_fusion), channel_id=1, source_target_pairs={{0,1},{1,2},{2,3},{3,0},{4,5},{5,6},{6,7},{7,4},{8,9},{9,10},{10,1... | collective-permute-start | bytes 26120 | tf_op jit(solution)/shard_map/ppermute | solution.py:99
Sparse Core Ops, SparseCore 0:
  65.7 26.3 all-gather.1

commit v12 on v10

--- a/solution.py
+++ b/solution.py
@@ -10,7 +10,7 @@
 
 HD = 64
 SCALE = HD ** (-0.5)
-QUERY_BLOCK = 544
+QUERY_BLOCK = 1088
 ROW_SPLIT = 2
 
 

time: 191 us -> 189 us (0.990)
  Pallas kernels: 63 us -> 58.7 us
    pallas_call x4, Pallas kernels: 63 us -> 58.7 us  [flash_step(): pl.pallas_call(functools.partial(step_kernel, first, last), grid=(rows //...]
  transfers between devices with their start and end apart: 21 -> 21, of which waited for: 14 -> 15; matrix products, arithmetic and copies ran while one was open for 6% -> 6% of each run, Pallas kernels for 33% -> 31%
where the time goes in v12:
time: 189 us; the launch traced here: 188 us
  Pallas kernels  58.7 us (31%)
  waiting for transfers between devices  53.5 us (28%)
  starting transfers between devices  30.8 us (16%)
  between operations  14.3 us (8%)
  matrix products  12.2 us (6%)
  local copies, waits for them, and re-layouts  10.4 us (6%)
  other arithmetic  8.09 us (4%)
    pallas_call x4, Pallas kernels, flash_step(): pl.pallas_call(functools.partial(step_kernel, first, last), grid=(rows //...  58.7 us
    ppermute x12, waiting for transfers between devices, shifted(): return lax.ppermute(value, axis, [(i, (i + k) % n) for i in range(n)])  37.8 us
    ppermute x12, starting transfers between devices, shifted(): return lax.ppermute(value, axis, [(i, (i + k) % n) for i in range(n)])  14.9 us
    all_to_all x1, waiting for transfers between devices, body(): back = lax.all_to_all(attended, ('x', 'type'), 0, 0, tiled=True)  11.1 us
    all_to_all x1, starting transfers between devices, body(): back = lax.all_to_all(attended, ('x', 'type'), 0, 0, tiled=True)  8.62 us
    dot_general x2, matrix products, body(): answer = jnp.dot(hidden, head_w2[which], preferred_element_type=jnp.float32)  7.06 us
  transfers between devices with their start and end apart: 21, of which 15 were waited for; matrix products, arithmetic and copies ran while one was open for 6% of the time, Pallas kernels for 31%

profile of v12, /device:TPU:1, one launch (start us, length us, event | category | flops | bytes accessed | tf_op | source)
XLA Modules:
  0.0 188.1 jit_solution(13097137149592021918)
XLA Ops:
  7.2 0.8 slice_add_fusion.1
  8.0 1.1 fusion.68
  9.1 1.1 fusion.71
  10.2 4.4 %collective-permute-start = (bf16[136,1024]{1,0:T(8,128)(2,1)S(1)}, bf16[136,1024]{1,0:T(8,128)(2,1)S(1)}, u32[]{:S(2)}, u32[]{:S(2)}) collective-permute-start(bf16[136,1024]{1,0:T(8,128)(2,1)S(1)} %fusion.71), channel_id=1, source_target_pairs={{0,1},{1,2},{2,3},{3,0},{4,5},{5,6},{6,7},{7,4},{8,9},{9,10},{10,1... | collective-permute-start | bytes 835592 | tf_op jit(solution)/shard_map/ppermute | solution.py:99
  14.6 0.5 collective-permute-start.2
  15.1 1.5 fusion.103
  16.5 0.2 copy.36
  16.8 0.2 copy.37
  17.0 0.2 copy.38
  17.3 0.1 pad.20.clone
  17.3 0.2 pad_maximum_fusion
  17.6 0.2 copy.31
  17.8 2.6 %copy.32 = bf16[1024,4,256]{2,0,1:T(8,128)(2,1)} copy(bf16[1024,4,256]{0,2,1:T(8,128)(2,1)S(1)} %bitcast.63) | data formatting | bytes 4194304 | tf_op jit(solution)/shard_map/reshape | solution.py:117
  20.3 0.2 collective-permute-done
  20.5 6.4 %collective-permute-done.1 = bf16[136,1024]{1,0:T(8,128)(2,1)S(1)} collective-permute-done((bf16[136,1024]{1,0:T(8,128)(2,1)S(1)}, bf16[136,1024]{1,0:T(8,128)(2,1)S(1)}, u32[]{:S(2)}, u32[]{:S(2)}) %collective-permute-start.1) | collective-permute-done | bytes 278560 | tf_op jit(solution)/shard_map/ppermute | solution.py:99
  26.8 0.6 collective-permute-done.2
  27.4 3.0 %fusion.28 = bf16[4,544,256]{2,1,0:T(8,128)(2,1)S(1)} fusion(s32[]{:T(128)S(6)} %select_n.108, bf16[1024,4,256]{2,0,1:T(8,128)(2,1)} %copy.32, bf16[136,1024]{1,0:T(8,128)(2,1)S(1)} %collective-permute-done.2, bf16[136,1024]{1,0:T(8,128)(2,1)S(1)} %collective-permute-done.1, bf16[136,1024]{1,0:T(8,128)(2,1)S(1)} %collective-permute-done, ...), kind=kOutput, calls=%fused_computation.33 | convolution fusion | flops 1150058496 | bytes 4325380 | tf_op jit(solution)/shard_map/rd,dje->jre/dot_general | solution.py:119
  30.5 1.3 collective-permute-start.3
  31.8 2.5 %collective-permute-start.4 = (bf16[544,256]{1,0:T(8,128)(2,1)S(1)}, bf16[544,256]{1,0:T(8,128)(2,1)S(1)}, u32[]{:S(2)}, u32[]{:S(2)}) collective-permute-start(bf16[544,256]{1,0:T(8,128)(2,1)S(1)} %get-tuple-element.40), channel_id=1, source_target_pairs={{0,16},{8,24},{16,0},{24,8},{1,17},{9,25},{17,1},{25,9},{2,18},{10... | collective-permute-start | bytes 835592 | tf_op jit(solution)/shard_map/ppermute | solution.py:99
  34.3 1.1 collective-permute-start.5
  35.4 4.7 %collective-permute-done.3 = bf16[544,256]{1,0:T(8,128)(2,1)S(1)} collective-permute-done((bf16[544,256]{1,0:T(8,128)(2,1)S(1)}, bf16[544,256]{1,0:T(8,128)(2,1)S(1)}, u32[]{:S(2)}, u32[]{:S(2)}) %collective-permute-start.3) | collective-permute-done | bytes 278560 | tf_op jit(solution)/shard_map/ppermute | solution.py:99
  40.1 7.1 %collective-permute-done.4 = bf16[544,256]{1,0:T(8,128)(2,1)S(1)} collective-permute-done((bf16[544,256]{1,0:T(8,128)(2,1)S(1)}, bf16[544,256]{1,0:T(8,128)(2,1)S(1)}, u32[]{:S(2)}, u32[]{:S(2)}) %collective-permute-start.4) | collective-permute-done | bytes 278560 | tf_op jit(solution)/shard_map/ppermute | solution.py:99
  47.3 1.3 slice_bitcast_fusion.4
  48.6 1.7 collective-permute-start.6
  50.2 2.1 %collective-permute-start.7 = (bf16[2176,128]{1,0:T(8,128)(2,1)S(1)}, bf16[2176,128]{1,0:T(8,128)(2,1)S(1)}, u32[]{:S(2)}, u32[]{:S(2)}) collective-permute-start(bf16[2176,128]{1,0:T(8,128)(2,1)S(1)} %get-tuple-element.36), channel_id=1, source_target_pairs={{0,96},{32,0},{64,32},{96,64},{1,97},{33,1},{65,33},{97,65},{2,98}... | collective-permute-start | bytes 1671176 | tf_op jit(solution)/shard_map/ppermute | solution.py:138
  52.3 0.7 collective-permute-start.8
  53.1 8.2 %shard_map.113.refs_2_ = f32[2176,128]{1,0:T(8,128)} custom-call(bf16[2176,128]{1,0:T(8,128)(2,1)} %get-tuple-element.37.refs_0_, bf16[1,2176,128]{2,1,0:T(8,128)(2,1)} %get-tuple-element.35.refs_1_), custom_call_target="tpu_custom_call" | custom-call | flops 2424307712 | bytes 3899392 | tf_op jit(solution)/shard_map/pallas_call | solution.py:81
  61.3 3.5 %collective-permute-done.6 = bf16[2176,128]{1,0:T(8,128)(2,1)S(1)} collective-permute-done((bf16[2176,128]{1,0:T(8,128)(2,1)S(1)}, bf16[2176,128]{1,0:T(8,128)(2,1)S(1)}, u32[]{:S(2)}, u32[]{:S(2)}) %collective-permute-start.6) | collective-permute-done | bytes 557088 | tf_op jit(solution)/shard_map/ppermute | solution.py:137
  64.7 0.8 collective-permute-done.8
  65.6 0.1 collective-permute-start.10
  65.7 2.7 %collective-permute-start.11 = (bf16[2176,128]{1,0:T(8,128)(2,1)S(1)}, bf16[2176,128]{1,0:T(8,128)(2,1)S(1)}, u32[]{:S(2)}, u32[]{:S(2)}) collective-permute-start(bf16[2176,128]{1,0:T(8,128)(2,1)S(1)} %collective-permute-done.8), channel_id=1, source_target_pairs={{0,96},{32,0},{64,32},{96,64},{1,97},{33,1},{65,33},{97,65},{2,98}... | collective-permute-start | bytes 1671176 | tf_op jit(solution)/shard_map/ppermute | solution.py:145
  68.4 1.3 pad_maximum_fusion.1.refs_1_
  69.7 21.1 %shard_map.114.refs_2_ = f32[2176,128]{1,0:T(8,128)} custom-call(bf16[2176,128]{1,0:T(8,128)(2,1)} %get-tuple-element.37.refs_0_, bf16[3,2176,128]{2,1,0:T(8,128)(2,1)} %pad_maximum_fusion.1.refs_1_, f32[2176,128]{1,0:T(8,128)} %shard_map.113.refs_2_), custom_call_target="tpu_custom_call" | custom-call | flops 7272923136 | bytes 6127616 | tf_op jit(solution)/shard_map/pallas_call | solution.py:81
  90.8 0.3 collective-permute-done.9
  91.1 1.3 pad_maximum_fusion.2.refs_1_
  92.5 21.1 %shard_map.115.refs_2_ = f32[2176,128]{1,0:T(8,128)} custom-call(bf16[2176,128]{1,0:T(8,128)(2,1)} %get-tuple-element.37.refs_0_, bf16[3,2176,128]{2,1,0:T(8,128)(2,1)} %pad_maximum_fusion.2.refs_1_, f32[2176,128]{1,0:T(8,128)} %shard_map.114.refs_2_), custom_call_target="tpu_custom_call" | custom-call | flops 7272923136 | bytes 6127616 | tf_op jit(solution)/shard_map/pallas_call | solution.py:81
  113.6 0.8 copy-done.5
  114.4 8.4 %shard_map.116 = bf16[2176,128]{1,0:T(8,128)(2,1)} custom-call(bf16[2176,128]{1,0:T(8,128)(2,1)} %get-tuple-element.37.refs_0_, bf16[1,2176,128]{2,1,0:T(8,128)(2,1)} %bitcast.79, f32[2176,128]{1,0:T(8,128)} %shard_map.115.refs_2_), custom_call_target="tpu_custom_call" | custom-call | flops 2424307712 | bytes 3899392 | tf_op jit(solution)/shard_map/pallas_call | solution.py:81
  122.8 1.3 slice.111
  124.1 0.3 copy.34
  124.4 0.6 gather_fusion
  125.0 0.9 broadcast_select_fusion
  125.9 8.6 %all-to-all-start = ((bf16[16,136,64]{1,2,0:T(8,128)(2,1)}), bf16[16,136,64]{1,2,0:T(8,128)(2,1)S(1)}, u32[]{:S(2)}, u32[]{:S(2)}) async-start(bf16[16,136,64]{1,2,0:T(8,128)(2,1)} %broadcast_select_fusion), calls=%async_computation | async-start | bytes 1048576 | tf_op jit(solution)/shard_map/all_to_all | solution.py:165
  134.6 11.1 %all-to-all-done = bf16[16,136,64]{1,2,0:T(8,128)(2,1)S(1)} async-done(((bf16[16,136,64]{1,2,0:T(8,128)(2,1)}), bf16[16,136,64]{1,2,0:T(8,128)(2,1)S(1)}, u32[]{:S(2)}, u32[]{:S(2)}) %all-to-all-start) | async-done | bytes 278560 | tf_op jit(solution)/shard_map/all_to_all | solution.py:165
  145.7 0.6 copy.35
  146.2 0.4 reshape.206
  146.7 2.2 %fusion.65 = (f32[136]{0:T(256)S(1)}, bf16[136,1024]{1,0:T(8,128)(2,1)S(1)}) fusion(bf16[136,1024]{1,0:T(8,128)(2,1)S(1)} %reshape.206, bf16[1024,1024]{1,0:T(8,128)(2,1)} %all-gather.2.cloned.1.call-done, f32[1024]{0:T(1024)S(1)} %copy-done.3, bf16[136,1024]{1,0:T(8,128)(2,1)S(1)} %copy-done), kind=kOutput, calls=%fused_computation.67 | convolution fusion | flops 286187392 | bytes 2937376 | tf_op jit(solution)/shard_map/dot_general | solution.py:168
  148.9 0.1 fusion.67
  149.1 0.1 broadcast_in_dim.49
  149.2 1.4 collective-permute-start.13
  150.6 2.9 %collective-permute-start.14 = (bf16[136,1152]{1,0:T(8,128)(2,1)S(1)}, bf16[136,1152]{1,0:T(8,128)(2,1)S(1)}, u32[]{:S(2)}, u32[]{:S(2)}) collective-permute-start(bf16[136,1152]{1,0:T(8,128)(2,1)S(1)} %pad_maximum_fusion.8), channel_id=1, source_target_pairs={{0,2},{1,3},{2,0},{3,1},{4,6},{5,7},{6,4},{7,5},{8,10},{9,11},{10,... | collective-permute-start | bytes 940040 | tf_op jit(solution)/shard_map/ppermute | solution.py:99
  153.5 3.5 %collective-permute-done.13 = bf16[136,1152]{1,0:T(8,128)(2,1)S(1)} collective-permute-done((bf16[136,1152]{1,0:T(8,128)(2,1)S(1)}, bf16[136,1152]{1,0:T(8,128)(2,1)S(1)}, u32[]{:S(2)}, u32[]{:S(2)}) %collective-permute-start.13) | collective-permute-done | bytes 313376 | tf_op jit(solution)/shard_map/ppermute | solution.py:99
  156.9 10.3 %collective-permute-done.14 = bf16[136,1152]{1,0:T(8,128)(2,1)S(1)} collective-permute-done((bf16[136,1152]{1,0:T(8,128)(2,1)S(1)}, bf16[136,1152]{1,0:T(8,128)(2,1)S(1)}, u32[]{:S(2)}, u32[]{:S(2)}) %collective-permute-start.14) | collective-permute-done | bytes 313376 | tf_op jit(solution)/shard_map/ppermute | solution.py:99
  167.2 0.6 collective-permute-done.15
  167.8 0.3 fusion.72
  168.1 3.5 %fusion.59 = f32[544,16]{0,1:T(8,128)S(1)} fusion(bf16[2,1024,1024]{2,1,0:T(8,128)(2,1)} %param.17, f32[1024]{0:T(1024)S(1)} %bitcast.78, bf16[2,1024,16]{1,2,0:T(8,128)(2,1)S(1)} %copy-done.6, pred[544]{0:T(1024)(128)(4,1)S(1)} %get-tuple-element.31, bf16[136,1152]{1,0:T(8,128)(2,1)S(1)} %collective-permute-done.15, ...), kind=kOutput, calls=%fused_computation.61 | convolution fusion | flops 1169826304 | bytes 3423232 | tf_op jit(solution)/shard_map/dot_general | solution.py:182
  171.6 3.5 %fusion.62 = f32[544,16]{0,1:T(8,128)S(1)} fusion(f32[544,16]{0,1:T(8,128)S(1)} %fusion.59, bf16[2,1024,1024]{2,1,0:T(8,128)(2,1)} %param.17, f32[1024]{0:T(1024)S(1)} %bitcast.77, bf16[2,1024,16]{1,2,0:T(8,128)(2,1)S(1)} %copy-done.6, pred[544]{0:T(1024)(128)(4,1)S(1)} %get-tuple-element.30, bf16[136,1152]{1,0:T(8,128)(2,1)S(1)} %collective-permute-done.15, ...), kind=kOutput, calls=%fused_computation.62 | convolution fusion | flops 1169826304 | bytes 3464192 | tf_op jit(solution)/shard_map/dot_general | solution.py:182
  175.2 0.1 fusion.104
  175.3 0.2 collective-permute-start.17
  175.5 0.7 collective-permute-start.18
  176.1 0.3 collective-permute-done.16
  176.4 3.0 %collective-permute-done.17 = f32[136,16]{0,1:T(8,128)S(1)} collective-permute-done((f32[136,16]{0,1:T(8,128)S(1)}, f32[136,16]{0,1:T(8,128)S(1)}, u32[]{:S(2)}, u32[]{:S(2)}) %collective-permute-start.17) | collective-permute-done | bytes 8736 | tf_op jit(solution)/shard_map/ppermute | solution.py:99
  179.5 1.2 collective-permute-done.18
  180.6 0.6 fusion.79
  (39 shorter events, 0.5 us)
Async XLA Ops:
  7.2 139.5 %all-gather.2.cloned.1.call-start = ((), (), s32[]{:S(2)}) async-start(), calls=%async_computation.1 | async-start | bytes 2621440 | tf_op jit(solution)/shard_map/all_gather | solution.py:156
  10.2 10.3 %collective-permute-start = (bf16[136,1024]{1,0:T(8,128)(2,1)S(1)}, bf16[136,1024]{1,0:T(8,128)(2,1)S(1)}, u32[]{:S(2)}, u32[]{:S(2)}) collective-permute-start(bf16[136,1024]{1,0:T(8,128)(2,1)S(1)} %fusion.71), channel_id=1, source_target_pairs={{0,1},{1,2},{2,3},{3,0},{4,5},{5,6},{6,7},{7,4},{8,9},{9,10},{10,1... | collective-permute-start | bytes 835592 | tf_op jit(solution)/shard_map/ppermute | solution.py:99
  14.6 12.2 %collective-permute-start.1 = (bf16[136,1024]{1,0:T(8,128)(2,1)S(1)}, bf16[136,1024]{1,0:T(8,128)(2,1)S(1)}, u32[]{:S(2)}, u32[]{:S(2)}) collective-permute-start(bf16[136,1024]{1,0:T(8,128)(2,1)S(1)} %fusion.71), channel_id=1, source_target_pairs={{0,2},{1,3},{2,0},{3,1},{4,6},{5,7},{6,4},{7,5},{8,10},{9,11},{10,... | collective-permute-start | bytes 835592 | tf_op jit(solution)/shard_map/ppermute | solution.py:99
  14.6 12.8 %collective-permute-start.2 = (bf16[136,1024]{1,0:T(8,128)(2,1)S(1)}, bf16[136,1024]{1,0:T(8,128)(2,1)S(1)}, u32[]{:S(2)}, u32[]{:S(2)}) collective-permute-start(bf16[136,1024]{1,0:T(8,128)(2,1)S(1)} %fusion.71), channel_id=1, source_target_pairs={{0,3},{1,0},{2,1},{3,2},{4,7},{5,4},{6,5},{7,6},{8,11},{9,8},{10,9... | collective-permute-start | bytes 835592 | tf_op jit(solution)/shard_map/ppermute | solution.py:99
  30.5 9.6 %collective-permute-start.3 = (bf16[544,256]{1,0:T(8,128)(2,1)S(1)}, bf16[544,256]{1,0:T(8,128)(2,1)S(1)}, u32[]{:S(2)}, u32[]{:S(2)}) collective-permute-start(bf16[544,256]{1,0:T(8,128)(2,1)S(1)} %get-tuple-element.41), channel_id=1, source_target_pairs={{0,8},{8,16},{16,24},{24,0},{1,9},{9,17},{17,25},{25,1},{2,10},{10... | collective-permute-start | bytes 835592 | tf_op jit(solution)/shard_map/ppermute | solution.py:99
  31.8 15.4 %collective-permute-start.4 = (bf16[544,256]{1,0:T(8,128)(2,1)S(1)}, bf16[544,256]{1,0:T(8,128)(2,1)S(1)}, u32[]{:S(2)}, u32[]{:S(2)}) collective-permute-start(bf16[544,256]{1,0:T(8,128)(2,1)S(1)} %get-tuple-element.40), channel_id=1, source_target_pairs={{0,16},{8,24},{16,0},{24,8},{1,17},{9,25},{17,1},{25,9},{2,18},{10... | collective-permute-start | bytes 835592 | tf_op jit(solution)/shard_map/ppermute | solution.py:99
  34.3 12.9 %collective-permute-start.5 = (bf16[544,256]{1,0:T(8,128)(2,1)S(1)}, bf16[544,256]{1,0:T(8,128)(2,1)S(1)}, u32[]{:S(2)}, u32[]{:S(2)}) collective-permute-start(bf16[544,256]{1,0:T(8,128)(2,1)S(1)} %get-tuple-element.39), channel_id=1, source_target_pairs={{0,24},{8,0},{16,8},{24,16},{1,25},{9,1},{17,9},{25,17},{2,26},{10... | collective-permute-start | bytes 835592 | tf_op jit(solution)/shard_map/ppermute | solution.py:99
  48.6 16.1 %collective-permute-start.6 = (bf16[2176,128]{1,0:T(8,128)(2,1)S(1)}, bf16[2176,128]{1,0:T(8,128)(2,1)S(1)}, u32[]{:S(2)}, u32[]{:S(2)}) collective-permute-start(bf16[2176,128]{1,0:T(8,128)(2,1)S(1)} %get-tuple-element.36), channel_id=1, source_target_pairs={{0,32},{32,64},{64,96},{96,0},{1,33},{33,65},{65,97},{97,1},{2,34}... | collective-permute-start | bytes 1671176 | tf_op jit(solution)/shard_map/ppermute | solution.py:137
  50.2 14.5 %collective-permute-start.7 = (bf16[2176,128]{1,0:T(8,128)(2,1)S(1)}, bf16[2176,128]{1,0:T(8,128)(2,1)S(1)}, u32[]{:S(2)}, u32[]{:S(2)}) collective-permute-start(bf16[2176,128]{1,0:T(8,128)(2,1)S(1)} %get-tuple-element.36), channel_id=1, source_target_pairs={{0,96},{32,0},{64,32},{96,64},{1,97},{33,1},{65,33},{97,65},{2,98}... | collective-permute-start | bytes 1671176 | tf_op jit(solution)/shard_map/ppermute | solution.py:138
  52.3 13.2 %collective-permute-start.8 = (bf16[2176,128]{1,0:T(8,128)(2,1)S(1)}, bf16[2176,128]{1,0:T(8,128)(2,1)S(1)}, u32[]{:S(2)}, u32[]{:S(2)}) collective-permute-start(bf16[2176,128]{1,0:T(8,128)(2,1)S(1)} %get-tuple-element.36), channel_id=1, source_target_pairs={{0,4},{4,0},{1,5},{5,1},{2,6},{6,2},{3,7},{7,3},{8,12},{12,8},{9,1... | collective-permute-start | bytes 1671176 | tf_op jit(solution)/shard_map/ppermute | solution.py:139
  65.6 25.2 %collective-permute-start.10 = (bf16[2176,128]{1,0:T(8,128)(2,1)S(1)}, bf16[2176,128]{1,0:T(8,128)(2,1)S(1)}, u32[]{:S(2)}, u32[]{:S(2)}) collective-permute-start(bf16[2176,128]{1,0:T(8,128)(2,1)S(1)} %collective-permute-done.8), channel_id=1, source_target_pairs={{0,32},{32,64},{64,96},{96,0},{1,33},{33,65},{65,97},{97,1},{2,34}... | collective-permute-start | bytes 1671176 | tf_op jit(solution)/shard_map/ppermute | solution.py:144
  65.7 25.1 %collective-permute-start.11 = (bf16[2176,128]{1,0:T(8,128)(2,1)S(1)}, bf16[2176,128]{1,0:T(8,128)(2,1)S(1)}, u32[]{:S(2)}, u32[]{:S(2)}) collective-permute-start(bf16[2176,128]{1,0:T(8,128)(2,1)S(1)} %collective-permute-done.8), channel_id=1, source_target_pairs={{0,96},{32,0},{64,32},{96,64},{1,97},{33,1},{65,33},{97,65},{2,98}... | collective-permute-start | bytes 1671176 | tf_op jit(solution)/shard_map/ppermute | solution.py:145
  68.4 22.7 %collective-permute-start.9 = (bf16[2176,128]{1,0:T(8,128)(2,1)S(1)}, bf16[2176,128]{1,0:T(8,128)(2,1)S(1)}, u32[]{:S(2)}, u32[]{:S(2)}) collective-permute-start(bf16[2176,128]{1,0:T(8,128)(2,1)S(1)} %collective-permute-done.6), channel_id=1, source_target_pairs={{0,32},{32,64},{64,96},{96,0},{1,33},{33,65},{65,97},{97,1},{2,34}... | collective-permute-start | bytes 1671176 | tf_op jit(solution)/shard_map/ppermute | solution.py:143
  91.1 22.4 %collective-permute-start.12 = (bf16[2176,128]{1,0:T(8,128)(2,1)S(1)}, bf16[2176,128]{1,0:T(8,128)(2,1)S(1)}, u32[]{:S(2)}, u32[]{:S(2)}) collective-permute-start(bf16[2176,128]{1,0:T(8,128)(2,1)S(1)} %collective-permute-done.10), channel_id=1, source_target_pairs={{0,32},{32,64},{64,96},{96,0},{1,33},{33,65},{65,97},{97,1},{2,34}... | collective-permute-start | bytes 1671176 | tf_op jit(solution)/shard_map/ppermute | solution.py:148
  113.6 0.8 copy-start.5
  124.0 10.5 %copy-start.7 = (s32[136,1]{0,1:T(1,128)S(1)}, s32[136,1]{0,1:T(1,128)}, u32[]{:S(2)}) copy-start(s32[136,1]{0,1:T(1,128)} %param.16) | copy-start | bytes 1636
  125.0 21.7 %copy-start = (bf16[136,1024]{1,0:T(8,128)(2,1)S(1)}, bf16[136,1024]{1,0:T(8,128)(2,1)}, u32[]{:S(2)}) copy-start(bf16[136,1024]{1,0:T(8,128)(2,1)} %param.10) | copy-start | bytes 835588
  125.0 21.7 %copy-start.3 = (f32[1024]{0:T(1024)S(1)}, f32[1024]{0:T(1024)}, u32[]{:S(2)}) copy-start(f32[1024]{0:T(1024)} %param.12) | copy-start | bytes 12292
  125.9 19.8 %all-to-all-start = ((bf16[16,136,64]{1,2,0:T(8,128)(2,1)}), bf16[16,136,64]{1,2,0:T(8,128)(2,1)S(1)}, u32[]{:S(2)}, u32[]{:S(2)}) async-start(bf16[16,136,64]{1,2,0:T(8,128)(2,1)} %broadcast_select_fusion), calls=%async_computation | async-start | bytes 1048576 | tf_op jit(solution)/shard_map/all_to_all | solution.py:165
  145.7 3.2 %copy-start.4 = (f32[1024]{0:T(1024)S(1)}, f32[1024]{0:T(1024)}, u32[]{:S(2)}) copy-start(f32[1024]{0:T(1024)} %param.13) | copy-start | bytes 12292
  146.6 6.8 %copy-start.2 = (bf16[2,1024]{1,0:T(2,128)(2,1)S(1)}, bf16[2,1024]{1,0:T(2,128)(2,1)}, u32[]{:S(2)}) copy-start(bf16[2,1024]{1,0:T(2,128)(2,1)} %param.18) | copy-start | bytes 12292
  146.6 21.5 %copy-start.6 = (bf16[2,1024,16]{1,2,0:T(8,128)(2,1)S(1)}, bf16[2,1024,16]{1,2,0:T(8,128)(2,1)}, u32[]{:S(2)}) copy-start(bf16[2,1024,16]{1,2,0:T(8,128)(2,1)} %param.19) | copy-start | bytes 196612
  148.9 22.7 %copy-start.1 = (bf16[136,1024]{1,0:T(8,128)(2,1)}, bf16[136,1024]{1,0:T(8,128)(2,1)S(1)}, u32[]{:S(2)}) copy-start(bf16[136,1024]{1,0:T(8,128)(2,1)S(1)} %get-tuple-element.50) | copy-start | bytes 835588
  149.2 7.7 %collective-permute-start.13 = (bf16[136,1152]{1,0:T(8,128)(2,1)S(1)}, bf16[136,1152]{1,0:T(8,128)(2,1)S(1)}, u32[]{:S(2)}, u32[]{:S(2)}) collective-permute-start(bf16[136,1152]{1,0:T(8,128)(2,1)S(1)} %pad_maximum_fusion.8), channel_id=1, source_target_pairs={{0,1},{1,2},{2,3},{3,0},{4,5},{5,6},{6,7},{7,4},{8,9},{9,10},{10,1... | collective-permute-start | bytes 940040 | tf_op jit(solution)/shard_map/ppermute | solution.py:99
  150.6 16.6 %collective-permute-start.14 = (bf16[136,1152]{1,0:T(8,128)(2,1)S(1)}, bf16[136,1152]{1,0:T(8,128)(2,1)S(1)}, u32[]{:S(2)}, u32[]{:S(2)}) collective-permute-start(bf16[136,1152]{1,0:T(8,128)(2,1)S(1)} %pad_maximum_fusion.8), channel_id=1, source_target_pairs={{0,2},{1,3},{2,0},{3,1},{4,6},{5,7},{6,4},{7,5},{8,10},{9,11},{10,... | collective-permute-start | bytes 940040 | tf_op jit(solution)/shard_map/ppermute | solution.py:99
  153.4 14.4 %collective-permute-start.15 = (bf16[136,1152]{1,0:T(8,128)(2,1)S(1)}, bf16[136,1152]{1,0:T(8,128)(2,1)S(1)}, u32[]{:S(2)}, u32[]{:S(2)}) collective-permute-start(bf16[136,1152]{1,0:T(8,128)(2,1)S(1)} %pad_maximum_fusion.8), channel_id=1, source_target_pairs={{0,3},{1,0},{2,1},{3,2},{4,7},{5,4},{6,5},{7,6},{8,11},{9,8},{10,9... | collective-permute-start | bytes 940040 | tf_op jit(solution)/shard_map/ppermute | solution.py:99
  175.2 1.2 collective-permute-start.16
  175.3 4.2 %collective-permute-start.17 = (f32[136,16]{0,1:T(8,128)S(1)}, f32[136,16]{0,1:T(8,128)S(1)}, u32[]{:S(2)}, u32[]{:S(2)}) collective-permute-start(f32[136,16]{0,1:T(8,128)S(1)} %get-tuple-element.44), channel_id=1, source_target_pairs={{0,2},{1,3},{2,0},{3,1},{4,6},{5,7},{6,4},{7,5},{8,10},{9,11},{10,... | collective-permute-start | bytes 26120 | tf_op jit(solution)/shard_map/ppermute | solution.py:99
  175.5 5.2 %collective-permute-start.18 = (f32[136,16]{0,1:T(8,128)S(1)}, f32[136,16]{0,1:T(8,128)S(1)}, u32[]{:S(2)}, u32[]{:S(2)}) collective-permute-start(f32[136,16]{0,1:T(8,128)S(1)} %get-tuple-element.43), channel_id=1, source_target_pairs={{0,3},{1,0},{2,1},{3,2},{4,7},{5,4},{6,5},{7,6},{8,11},{9,8},{10,9... | collective-permute-start | bytes 26120 | tf_op jit(solution)/shard_map/ppermute | solution.py:99
Sparse Core Ops, SparseCore 0:
  65.7 26.3 all-gather.1

commit v13 on v11

--- a/solution.py
+++ b/solution.py
@@ -10,7 +10,7 @@
 
 HD = 64
 SCALE = HD ** (-0.5)
-QUERY_BLOCK = 544
+QUERY_BLOCK = 1088
 ROW_SPLIT = 2
 
 
@@ -176,7 +176,7 @@
     def heads_of(block):
         features = block[:, : final.shape[1]]
         block_kinds = block[:, final.shape[1]].astype(jnp.int32)
-        result = jnp.zeros((rows, head_w2.shape[2]), jnp.float32)
+        result = jnp.zeros((block.shape[0], head_w2.shape[2]), jnp.float32)
         for which in range(owned):
             hidden = jnp.dot(features, head_w1[which], preferred_element_type=jnp.float32)
             hidden = jax.nn.gelu(hidden + head_b1[which].astype(jnp.float32)).astype(jnp.bfloat16)
@@ -184,10 +184,11 @@
             result = jnp.where((block_kinds == first_kind + which)[:, None], answer, result)
         return result
 
-    arriving = [shifted(ext, "type", k) for k in range(1, kinds)]
+    arriving = jnp.concatenate([shifted(ext, "type", k) for k in range(1, kinds)], axis=0)
     head_out = heads_of(ext)
+    others = heads_of(arriving).reshape(kinds - 1, rows, -1)
     for k in range(1, kinds):
-        head_out = head_out + shifted(heads_of(arriving[k - 1]), "type", -k)
+        head_out = head_out + shifted(others[k - 1], "type", -k)
     return (updated, head_out)
 
 

time: 194 us -> 190 us (0.979)
  waiting for transfers between devices: 38 us -> 46.5 us
  matrix products: 23.8 us -> 16 us
  Pallas kernels: 63 us -> 58.8 us
    dot_general x8 -> x4, matrix products: 18.6 us -> 10.9 us  [heads_of(): answer = jnp.dot(hidden, head_w2[which], preferred_element_type=jnp.float32)]
    ppermute x12, waiting for transfers between devices: 23.2 us -> 30.9 us  [shifted(): return lax.ppermute(value, axis, [(i, (i + k) % n) for i in range(n)])]
    pallas_call x4, Pallas kernels: 63 us -> 58.8 us  [flash_step(): pl.pallas_call(functools.partial(step_kernel, first, last), grid=(rows //...]
    ppermute x12, starting transfers between devices: 20.3 us -> 17.7 us  [shifted(): return lax.ppermute(value, axis, [(i, (i + k) % n) for i in range(n)])]
  transfers between devices with their start and end apart: 21 -> 21, of which waited for: 10 -> 12; matrix products, arithmetic and copies ran while one was open for 15% -> 9% of each run, Pallas kernels for 33% -> 31%
where the time goes in v13:
time: 190 us; the launch traced here: 188 us
  Pallas kernels  58.8 us (31%)
  waiting for transfers between devices  46.5 us (24%)
  starting transfers between devices  33.8 us (18%)
  matrix products  16 us (8%)
  between operations  14.4 us (8%)
  local copies, waits for them, and re-layouts  10.5 us (6%)
  other arithmetic  8.08 us (4%)
    pallas_call x4, Pallas kernels, flash_step(): pl.pallas_call(functools.partial(step_kernel, first, last), grid=(rows //...  58.8 us
    ppermute x12, waiting for transfers between devices, shifted(): return lax.ppermute(value, axis, [(i, (i + k) % n) for i in range(n)])  30.9 us
    ppermute x12, starting transfers between devices, shifted(): return lax.ppermute(value, axis, [(i, (i + k) % n) for i in range(n)])  17.7 us
    all_to_all x1, waiting for transfers between devices, body(): back = lax.all_to_all(attended, ('x', 'type'), 0, 0, tiled=True)  11.1 us
    dot_general x4, matrix products, heads_of(): answer = jnp.dot(hidden, head_w2[which], preferred_element_type=jnp.float32)  10.9 us
    all_to_all x1, starting transfers between devices, body(): back = lax.all_to_all(attended, ('x', 'type'), 0, 0, tiled=True)  8.75 us
  transfers between devices with their start and end apart: 21, of which 12 were waited for; matrix products, arithmetic and copies ran while one was open for 9% of the time, Pallas kernels for 31%

profile of v13, /device:TPU:1, one launch (start us, length us, event | category | flops | bytes accessed | tf_op | source)
XLA Modules:
  0.0 188.1 jit_solution(12784371109991495722)
XLA Ops:
  7.2 0.8 slice_add_fusion
  8.0 1.1 fusion.85
  9.1 1.1 fusion.88
  10.2 4.4 %collective-permute-start = (bf16[136,1024]{1,0:T(8,128)(2,1)S(1)}, bf16[136,1024]{1,0:T(8,128)(2,1)S(1)}, u32[]{:S(2)}, u32[]{:S(2)}) collective-permute-start(bf16[136,1024]{1,0:T(8,128)(2,1)S(1)} %fusion.88), channel_id=1, source_target_pairs={{0,1},{1,2},{2,3},{3,0},{4,5},{5,6},{6,7},{7,4},{8,9},{9,10},{10,1... | collective-permute-start | bytes 835592 | tf_op jit(solution)/shard_map/ppermute | solution.py:99
  14.6 0.5 collective-permute-start.2
  15.1 1.5 fusion.169
  16.5 0.2 copy.36
  16.8 0.2 copy.37
  17.0 0.2 copy.38
  17.3 0.1 pad.15.clone
  17.3 0.2 pad_maximum_fusion
  17.6 0.2 copy.31
  17.8 2.6 %copy.32 = bf16[1024,4,256]{2,0,1:T(8,128)(2,1)} copy(bf16[1024,4,256]{0,2,1:T(8,128)(2,1)S(1)} %bitcast.89) | data formatting | bytes 4194304 | tf_op jit(solution)/shard_map/reshape | solution.py:117
  20.4 0.1 collective-permute-done
  20.5 6.4 %collective-permute-done.1 = bf16[136,1024]{1,0:T(8,128)(2,1)S(1)} collective-permute-done((bf16[136,1024]{1,0:T(8,128)(2,1)S(1)}, bf16[136,1024]{1,0:T(8,128)(2,1)S(1)}, u32[]{:S(2)}, u32[]{:S(2)}) %collective-permute-start.1) | collective-permute-done | bytes 278560 | tf_op jit(solution)/shard_map/ppermute | solution.py:99
  26.8 0.6 collective-permute-done.2
  27.4 3.0 %fusion.38 = bf16[4,544,256]{2,1,0:T(8,128)(2,1)S(1)} fusion(s32[]{:T(128)S(6)} %select_n.115, bf16[1024,4,256]{2,0,1:T(8,128)(2,1)} %copy.32, bf16[136,1024]{1,0:T(8,128)(2,1)S(1)} %collective-permute-done.2, bf16[136,1024]{1,0:T(8,128)(2,1)S(1)} %collective-permute-done.1, bf16[136,1024]{1,0:T(8,128)(2,1)S(1)} %collective-permute-done, ...), kind=kOutput, calls=%fused_computation.39 | convolution fusion | flops 1150058496 | bytes 4325380 | tf_op jit(solution)/shard_map/rd,dje->jre/dot_general | solution.py:119
  30.4 0.1 slice_bitcast_fusion.3
  30.5 1.3 collective-permute-start.3
  31.8 2.5 %collective-permute-start.4 = (bf16[544,256]{1,0:T(8,128)(2,1)S(1)}, bf16[544,256]{1,0:T(8,128)(2,1)S(1)}, u32[]{:S(2)}, u32[]{:S(2)}) collective-permute-start(bf16[544,256]{1,0:T(8,128)(2,1)S(1)} %get-tuple-element.42), channel_id=1, source_target_pairs={{0,16},{8,24},{16,0},{24,8},{1,17},{9,25},{17,1},{25,9},{2,18},{10... | collective-permute-start | bytes 835592 | tf_op jit(solution)/shard_map/ppermute | solution.py:99
  34.3 1.1 collective-permute-start.5
  35.4 4.7 %collective-permute-done.3 = bf16[544,256]{1,0:T(8,128)(2,1)S(1)} collective-permute-done((bf16[544,256]{1,0:T(8,128)(2,1)S(1)}, bf16[544,256]{1,0:T(8,128)(2,1)S(1)}, u32[]{:S(2)}, u32[]{:S(2)}) %collective-permute-start.3) | collective-permute-done | bytes 278560 | tf_op jit(solution)/shard_map/ppermute | solution.py:99
  40.1 7.1 %collective-permute-done.4 = bf16[544,256]{1,0:T(8,128)(2,1)S(1)} collective-permute-done((bf16[544,256]{1,0:T(8,128)(2,1)S(1)}, bf16[544,256]{1,0:T(8,128)(2,1)S(1)}, u32[]{:S(2)}, u32[]{:S(2)}) %collective-permute-start.4) | collective-permute-done | bytes 278560 | tf_op jit(solution)/shard_map/ppermute | solution.py:99
  47.3 1.3 slice_bitcast_fusion.4
  48.6 1.7 collective-permute-start.6
  50.3 2.1 %collective-permute-start.7 = (bf16[2176,128]{1,0:T(8,128)(2,1)S(1)}, bf16[2176,128]{1,0:T(8,128)(2,1)S(1)}, u32[]{:S(2)}, u32[]{:S(2)}) collective-permute-start(bf16[2176,128]{1,0:T(8,128)(2,1)S(1)} %get-tuple-element.38), channel_id=1, source_target_pairs={{0,96},{32,0},{64,32},{96,64},{1,97},{33,1},{65,33},{97,65},{2,98}... | collective-permute-start | bytes 1671176 | tf_op jit(solution)/shard_map/ppermute | solution.py:138
  52.4 0.7 collective-permute-start.8
  53.1 8.2 %shard_map.113.refs_2_ = f32[2176,128]{1,0:T(8,128)} custom-call(bf16[2176,128]{1,0:T(8,128)(2,1)} %get-tuple-element.39.refs_0_, bf16[1,2176,128]{2,1,0:T(8,128)(2,1)} %get-tuple-element.37.refs_1_), custom_call_target="tpu_custom_call" | custom-call | flops 2424307712 | bytes 3899392 | tf_op jit(solution)/shard_map/pallas_call | solution.py:81
  61.3 3.4 %collective-permute-done.6 = bf16[2176,128]{1,0:T(8,128)(2,1)S(1)} collective-permute-done((bf16[2176,128]{1,0:T(8,128)(2,1)S(1)}, bf16[2176,128]{1,0:T(8,128)(2,1)S(1)}, u32[]{:S(2)}, u32[]{:S(2)}) %collective-permute-start.6) | collective-permute-done | bytes 557088 | tf_op jit(solution)/shard_map/ppermute | solution.py:137
  64.7 0.8 collective-permute-done.8
  65.6 0.1 collective-permute-start.10
  65.7 2.7 %collective-permute-start.11 = (bf16[2176,128]{1,0:T(8,128)(2,1)S(1)}, bf16[2176,128]{1,0:T(8,128)(2,1)S(1)}, u32[]{:S(2)}, u32[]{:S(2)}) collective-permute-start(bf16[2176,128]{1,0:T(8,128)(2,1)S(1)} %collective-permute-done.8), channel_id=1, source_target_pairs={{0,96},{32,0},{64,32},{96,64},{1,97},{33,1},{65,33},{97,65},{2,98}... | collective-permute-start | bytes 1671176 | tf_op jit(solution)/shard_map/ppermute | solution.py:145
  68.4 1.3 pad_maximum_fusion.1.refs_1_
  69.7 21.1 %shard_map.114.refs_2_ = f32[2176,128]{1,0:T(8,128)} custom-call(bf16[2176,128]{1,0:T(8,128)(2,1)} %get-tuple-element.39.refs_0_, bf16[3,2176,128]{2,1,0:T(8,128)(2,1)} %pad_maximum_fusion.1.refs_1_, f32[2176,128]{1,0:T(8,128)} %shard_map.113.refs_2_), custom_call_target="tpu_custom_call" | custom-call | flops 7272923136 | bytes 6127616 | tf_op jit(solution)/shard_map/pallas_call | solution.py:81
  90.8 0.3 collective-permute-done.9
  91.1 1.3 pad_maximum_fusion.2.refs_1_
  92.5 21.1 %shard_map.115.refs_2_ = f32[2176,128]{1,0:T(8,128)} custom-call(bf16[2176,128]{1,0:T(8,128)(2,1)} %get-tuple-element.39.refs_0_, bf16[3,2176,128]{2,1,0:T(8,128)(2,1)} %pad_maximum_fusion.2.refs_1_, f32[2176,128]{1,0:T(8,128)} %shard_map.114.refs_2_), custom_call_target="tpu_custom_call" | custom-call | flops 7272923136 | bytes 6127616 | tf_op jit(solution)/shard_map/pallas_call | solution.py:81
  113.6 0.8 copy-done.6
  114.4 8.4 %shard_map.116 = bf16[2176,128]{1,0:T(8,128)(2,1)} custom-call(bf16[2176,128]{1,0:T(8,128)(2,1)} %get-tuple-element.39.refs_0_, bf16[1,2176,128]{2,1,0:T(8,128)(2,1)} %bitcast.107, f32[2176,128]{1,0:T(8,128)} %shard_map.115.refs_2_), custom_call_target="tpu_custom_call" | custom-call | flops 2424307712 | bytes 3899392 | tf_op jit(solution)/shard_map/pallas_call | solution.py:81
  122.8 1.3 slice.113
  124.1 0.3 copy.34
  124.4 0.6 gather_fusion
  125.0 0.9 broadcast_select_fusion
  125.9 8.7 %all-to-all-start = ((bf16[16,136,64]{1,2,0:T(8,128)(2,1)}), bf16[16,136,64]{1,2,0:T(8,128)(2,1)S(1)}, u32[]{:S(2)}, u32[]{:S(2)}) async-start(bf16[16,136,64]{1,2,0:T(8,128)(2,1)} %broadcast_select_fusion), calls=%async_computation | async-start | bytes 1048576 | tf_op jit(solution)/shard_map/all_to_all | solution.py:165
  134.7 11.1 %all-to-all-done = bf16[16,136,64]{1,2,0:T(8,128)(2,1)S(1)} async-done(((bf16[16,136,64]{1,2,0:T(8,128)(2,1)}), bf16[16,136,64]{1,2,0:T(8,128)(2,1)S(1)}, u32[]{:S(2)}, u32[]{:S(2)}) %all-to-all-start) | async-done | bytes 278560 | tf_op jit(solution)/shard_map/all_to_all | solution.py:165
  145.8 0.6 copy.35
  146.4 0.4 reshape.208
  146.8 2.2 %fusion.82 = (f32[136]{0:T(256)S(1)}, bf16[136,1024]{1,0:T(8,128)(2,1)S(1)}) fusion(bf16[136,1024]{1,0:T(8,128)(2,1)S(1)} %reshape.208, bf16[1024,1024]{1,0:T(8,128)(2,1)} %all-gather.2.cloned.1.call-done, f32[1024]{0:T(1024)S(1)} %copy-done.3, bf16[136,1024]{1,0:T(8,128)(2,1)S(1)} %copy-done), kind=kOutput, calls=%fused_computation.77 | convolution fusion | flops 286187392 | bytes 2937376 | tf_op jit(solution)/shard_map/dot_general | solution.py:168
  149.1 0.1 fusion.84
  149.2 0.1 broadcast_in_dim.78
  149.3 1.4 collective-permute-start.13
  150.7 3.0 %collective-permute-start.14 = (bf16[136,1152]{1,0:T(8,128)(2,1)S(1)}, bf16[136,1152]{1,0:T(8,128)(2,1)S(1)}, u32[]{:S(2)}, u32[]{:S(2)}) collective-permute-start(bf16[136,1152]{1,0:T(8,128)(2,1)S(1)} %pad_maximum_fusion.4), channel_id=1, source_target_pairs={{0,2},{1,3},{2,0},{3,1},{4,6},{5,7},{6,4},{7,5},{8,10},{9,11},{10,... | collective-permute-start | bytes 940040 | tf_op jit(solution)/shard_map/ppermute | solution.py:99
  153.7 2.2 %fusion.102 = f32[136,16]{0,1:T(8,128)S(1)} fusion(bf16[136,1024]{1,0:T(8,128)(2,1)S(1)} %fusion.84, bf16[2,1024,1024]{2,1,0:T(8,128)(2,1)} %param.17, f32[1024]{0:T(1024)S(1)} %bitcast.105, bf16[2,1024,16]{1,2,0:T(8,128)(2,1)S(1)} %copy-done.7), kind=kOutput, calls=%fused_computation.92 | convolution fusion | flops 291061760 | bytes 2421248 | tf_op jit(solution)/shard_map/dot_general | solution.py:183
  155.9 1.0 collective-permute-done.13
  157.0 10.3 %collective-permute-done.14 = bf16[136,1152]{1,0:T(8,128)(2,1)S(1)} collective-permute-done((bf16[136,1152]{1,0:T(8,128)(2,1)S(1)}, bf16[136,1152]{1,0:T(8,128)(2,1)S(1)}, u32[]{:S(2)}, u32[]{:S(2)}) %collective-permute-start.14) | collective-permute-done | bytes 313376 | tf_op jit(solution)/shard_map/ppermute | solution.py:99
  167.3 0.6 collective-permute-done.15
  168.0 0.2 fusion.128
  168.2 3.2 %fusion.64 = f32[408,16]{0,1:T(8,128)S(1)} fusion(bf16[2,1024,1024]{2,1,0:T(8,128)(2,1)} %param.17, f32[1024]{0:T(1024)S(1)} %bitcast.103, bf16[408,1152]{1,0:T(8,128)(2,1)S(1)} %constant_dynamic-update-slice_fusion, bf16[2,1024,16]{1,2,0:T(8,128)(2,1)S(1)} %copy-done.7, pred[408]{0:T(512)(128)(4,1)S(1)} %get-tuple-element.31), kind=kOutput, calls=%fused_computation.56 | convolution fusion | flops 873191808 | bytes 2996224 | tf_op jit(solution)/shard_map/dot_general | solution.py:183
  171.4 3.2 %fusion.61 = f32[408,16]{0,1:T(8,128)S(1)} fusion(f32[408,16]{0,1:T(8,128)S(1)} %fusion.64, bf16[2,1024,1024]{2,1,0:T(8,128)(2,1)} %param.17, f32[1024]{0:T(1024)S(1)} %bitcast.106, bf16[408,1152]{1,0:T(8,128)(2,1)S(1)} %constant_dynamic-update-slice_fusion, bf16[2,1024,16]{1,2,0:T(8,128)(2,1)S(1)} %copy-done.7, pred[408]{0:T(512)(128)(4,1)S(1)} %get-tuple-element.30), kind=kOutput, calls=%fused_computation.55 | convolution fusion | flops 873191808 | bytes 3028992 | tf_op jit(solution)/shard_map/dot_general | solution.py:183
  174.6 0.1 fusion.170
  174.7 0.2 collective-permute-start.17
  174.9 3.4 %collective-permute-start.18 = (f32[136,16]{0,1:T(8,128)S(1)}, f32[136,16]{0,1:T(8,128)S(1)}, u32[]{:S(2)}, u32[]{:S(2)}) collective-permute-start(f32[136,16]{0,1:T(8,128)S(1)} %get-tuple-element.45), channel_id=1, source_target_pairs={{0,1},{1,2},{2,3},{3,0},{4,5},{5,6},{6,7},{7,4},{8,9},{9,10},{10,1... | collective-permute-start | bytes 26120 | tf_op jit(solution)/shard_map/ppermute | solution.py:99
  178.3 2.2 %fusion.67 = f32[136,16]{0,1:T(8,128)S(1)} fusion(f32[136,16]{0,1:T(8,128)S(1)} %fusion.102, bf16[136,1024]{1,0:T(8,128)(2,1)S(1)} %fusion.84, bf16[2,1024,1024]{2,1,0:T(8,128)(2,1)} %param.17, f32[1024]{0:T(1024)S(1)} %bitcast.104, bf16[2,1024,16]{1,2,0:T(8,128)(2,1)S(1)} %copy-done.7, pred[136]{0:T(512)(128)(4,1)S(1)} %get-tuple-element.33, ...), kind=kOutput, calls=%fused_computation.58 | convolution fusion | flops 291066112 | bytes 2438656 | tf_op jit(solution)/shard_map/dot_general | solution.py:183
  180.6 0.6 add_add_fusion
  (45 shorter events, 0.5 us)
Async XLA Ops:
  7.2 139.6 %all-gather.2.cloned.1.call-start = ((), (), s32[]{:S(2)}) async-start(), calls=%async_computation.1 | async-start | bytes 2621440 | tf_op jit(solution)/shard_map/all_gather | solution.py:156
  10.2 10.3 %collective-permute-start = (bf16[136,1024]{1,0:T(8,128)(2,1)S(1)}, bf16[136,1024]{1,0:T(8,128)(2,1)S(1)}, u32[]{:S(2)}, u32[]{:S(2)}) collective-permute-start(bf16[136,1024]{1,0:T(8,128)(2,1)S(1)} %fusion.88), channel_id=1, source_target_pairs={{0,1},{1,2},{2,3},{3,0},{4,5},{5,6},{6,7},{7,4},{8,9},{9,10},{10,1... | collective-permute-start | bytes 835592 | tf_op jit(solution)/shard_map/ppermute | solution.py:99
  14.6 12.2 %collective-permute-start.1 = (bf16[136,1024]{1,0:T(8,128)(2,1)S(1)}, bf16[136,1024]{1,0:T(8,128)(2,1)S(1)}, u32[]{:S(2)}, u32[]{:S(2)}) collective-permute-start(bf16[136,1024]{1,0:T(8,128)(2,1)S(1)} %fusion.88), channel_id=1, source_target_pairs={{0,2},{1,3},{2,0},{3,1},{4,6},{5,7},{6,4},{7,5},{8,10},{9,11},{10,... | collective-permute-start | bytes 835592 | tf_op jit(solution)/shard_map/ppermute | solution.py:99
  14.6 12.8 %collective-permute-start.2 = (bf16[136,1024]{1,0:T(8,128)(2,1)S(1)}, bf16[136,1024]{1,0:T(8,128)(2,1)S(1)}, u32[]{:S(2)}, u32[]{:S(2)}) collective-permute-start(bf16[136,1024]{1,0:T(8,128)(2,1)S(1)} %fusion.88), channel_id=1, source_target_pairs={{0,3},{1,0},{2,1},{3,2},{4,7},{5,4},{6,5},{7,6},{8,11},{9,8},{10,9... | collective-permute-start | bytes 835592 | tf_op jit(solution)/shard_map/ppermute | solution.py:99
  30.5 9.6 %collective-permute-start.3 = (bf16[544,256]{1,0:T(8,128)(2,1)S(1)}, bf16[544,256]{1,0:T(8,128)(2,1)S(1)}, u32[]{:S(2)}, u32[]{:S(2)}) collective-permute-start(bf16[544,256]{1,0:T(8,128)(2,1)S(1)} %get-tuple-element.43), channel_id=1, source_target_pairs={{0,8},{8,16},{16,24},{24,0},{1,9},{9,17},{17,25},{25,1},{2,10},{10... | collective-permute-start | bytes 835592 | tf_op jit(solution)/shard_map/ppermute | solution.py:99
  31.8 15.4 %collective-permute-start.4 = (bf16[544,256]{1,0:T(8,128)(2,1)S(1)}, bf16[544,256]{1,0:T(8,128)(2,1)S(1)}, u32[]{:S(2)}, u32[]{:S(2)}) collective-permute-start(bf16[544,256]{1,0:T(8,128)(2,1)S(1)} %get-tuple-element.42), channel_id=1, source_target_pairs={{0,16},{8,24},{16,0},{24,8},{1,17},{9,25},{17,1},{25,9},{2,18},{10... | collective-permute-start | bytes 835592 | tf_op jit(solution)/shard_map/ppermute | solution.py:99
  34.3 12.9 %collective-permute-start.5 = (bf16[544,256]{1,0:T(8,128)(2,1)S(1)}, bf16[544,256]{1,0:T(8,128)(2,1)S(1)}, u32[]{:S(2)}, u32[]{:S(2)}) collective-permute-start(bf16[544,256]{1,0:T(8,128)(2,1)S(1)} %get-tuple-element.41), channel_id=1, source_target_pairs={{0,24},{8,0},{16,8},{24,16},{1,25},{9,1},{17,9},{25,17},{2,26},{10... | collective-permute-start | bytes 835592 | tf_op jit(solution)/shard_map/ppermute | solution.py:99
  48.6 16.1 %collective-permute-start.6 = (bf16[2176,128]{1,0:T(8,128)(2,1)S(1)}, bf16[2176,128]{1,0:T(8,128)(2,1)S(1)}, u32[]{:S(2)}, u32[]{:S(2)}) collective-permute-start(bf16[2176,128]{1,0:T(8,128)(2,1)S(1)} %get-tuple-element.38), channel_id=1, source_target_pairs={{0,32},{32,64},{64,96},{96,0},{1,33},{33,65},{65,97},{97,1},{2,34}... | collective-permute-start | bytes 1671176 | tf_op jit(solution)/shard_map/ppermute | solution.py:137
  50.3 14.5 %collective-permute-start.7 = (bf16[2176,128]{1,0:T(8,128)(2,1)S(1)}, bf16[2176,128]{1,0:T(8,128)(2,1)S(1)}, u32[]{:S(2)}, u32[]{:S(2)}) collective-permute-start(bf16[2176,128]{1,0:T(8,128)(2,1)S(1)} %get-tuple-element.38), channel_id=1, source_target_pairs={{0,96},{32,0},{64,32},{96,64},{1,97},{33,1},{65,33},{97,65},{2,98}... | collective-permute-start | bytes 1671176 | tf_op jit(solution)/shard_map/ppermute | solution.py:138
  52.4 13.2 %collective-permute-start.8 = (bf16[2176,128]{1,0:T(8,128)(2,1)S(1)}, bf16[2176,128]{1,0:T(8,128)(2,1)S(1)}, u32[]{:S(2)}, u32[]{:S(2)}) collective-permute-start(bf16[2176,128]{1,0:T(8,128)(2,1)S(1)} %get-tuple-element.38), channel_id=1, source_target_pairs={{0,4},{4,0},{1,5},{5,1},{2,6},{6,2},{3,7},{7,3},{8,12},{12,8},{9,1... | collective-permute-start | bytes 1671176 | tf_op jit(solution)/shard_map/ppermute | solution.py:139
  65.6 25.2 %collective-permute-start.10 = (bf16[2176,128]{1,0:T(8,128)(2,1)S(1)}, bf16[2176,128]{1,0:T(8,128)(2,1)S(1)}, u32[]{:S(2)}, u32[]{:S(2)}) collective-permute-start(bf16[2176,128]{1,0:T(8,128)(2,1)S(1)} %collective-permute-done.8), channel_id=1, source_target_pairs={{0,32},{32,64},{64,96},{96,0},{1,33},{33,65},{65,97},{97,1},{2,34}... | collective-permute-start | bytes 1671176 | tf_op jit(solution)/shard_map/ppermute | solution.py:144
  65.7 25.1 %collective-permute-start.11 = (bf16[2176,128]{1,0:T(8,128)(2,1)S(1)}, bf16[2176,128]{1,0:T(8,128)(2,1)S(1)}, u32[]{:S(2)}, u32[]{:S(2)}) collective-permute-start(bf16[2176,128]{1,0:T(8,128)(2,1)S(1)} %collective-permute-done.8), channel_id=1, source_target_pairs={{0,96},{32,0},{64,32},{96,64},{1,97},{33,1},{65,33},{97,65},{2,98}... | collective-permute-start | bytes 1671176 | tf_op jit(solution)/shard_map/ppermute | solution.py:145
  68.4 22.7 %collective-permute-start.9 = (bf16[2176,128]{1,0:T(8,128)(2,1)S(1)}, bf16[2176,128]{1,0:T(8,128)(2,1)S(1)}, u32[]{:S(2)}, u32[]{:S(2)}) collective-permute-start(bf16[2176,128]{1,0:T(8,128)(2,1)S(1)} %collective-permute-done.6), channel_id=1, source_target_pairs={{0,32},{32,64},{64,96},{96,0},{1,33},{33,65},{65,97},{97,1},{2,34}... | collective-permute-start | bytes 1671176 | tf_op jit(solution)/shard_map/ppermute | solution.py:143
  91.1 22.4 %collective-permute-start.12 = (bf16[2176,128]{1,0:T(8,128)(2,1)S(1)}, bf16[2176,128]{1,0:T(8,128)(2,1)S(1)}, u32[]{:S(2)}, u32[]{:S(2)}) collective-permute-start(bf16[2176,128]{1,0:T(8,128)(2,1)S(1)} %collective-permute-done.10), channel_id=1, source_target_pairs={{0,32},{32,64},{64,96},{96,0},{1,33},{33,65},{65,97},{97,1},{2,34}... | collective-permute-start | bytes 1671176 | tf_op jit(solution)/shard_map/ppermute | solution.py:148
  113.5 0.8 copy-start.6
  124.4 10.3 %copy-start.5 = (s32[136,1]{0,1:T(1,128)S(1)}, s32[136,1]{0,1:T(1,128)}, u32[]{:S(2)}) copy-start(s32[136,1]{0,1:T(1,128)} %param.16) | copy-start | bytes 1636
  124.4 10.3 %copy-start.2 = (bf16[2,1024]{1,0:T(2,128)(2,1)S(1)}, bf16[2,1024]{1,0:T(2,128)(2,1)}, u32[]{:S(2)}) copy-start(bf16[2,1024]{1,0:T(2,128)(2,1)} %param.18) | copy-start | bytes 12292
  125.9 20.9 %copy-start = (bf16[136,1024]{1,0:T(8,128)(2,1)S(1)}, bf16[136,1024]{1,0:T(8,128)(2,1)}, u32[]{:S(2)}) copy-start(bf16[136,1024]{1,0:T(8,128)(2,1)} %param.10) | copy-start | bytes 835588
  125.9 20.9 %copy-start.3 = (f32[1024]{0:T(1024)S(1)}, f32[1024]{0:T(1024)}, u32[]{:S(2)}) copy-start(f32[1024]{0:T(1024)} %param.12) | copy-start | bytes 12292
  125.9 19.9 %all-to-all-start = ((bf16[16,136,64]{1,2,0:T(8,128)(2,1)}), bf16[16,136,64]{1,2,0:T(8,128)(2,1)S(1)}, u32[]{:S(2)}, u32[]{:S(2)}) async-start(bf16[16,136,64]{1,2,0:T(8,128)(2,1)} %broadcast_select_fusion), calls=%async_computation | async-start | bytes 1048576 | tf_op jit(solution)/shard_map/all_to_all | solution.py:165
  146.8 2.3 %copy-start.4 = (f32[1024]{0:T(1024)S(1)}, f32[1024]{0:T(1024)}, u32[]{:S(2)}) copy-start(f32[1024]{0:T(1024)} %param.13) | copy-start | bytes 12292
  146.8 6.9 %copy-start.7 = (bf16[2,1024,16]{1,2,0:T(8,128)(2,1)S(1)}, bf16[2,1024,16]{1,2,0:T(8,128)(2,1)}, u32[]{:S(2)}) copy-start(bf16[2,1024,16]{1,2,0:T(8,128)(2,1)} %param.19) | copy-start | bytes 196612
  149.0 6.9 %copy-start.1 = (bf16[136,1024]{1,0:T(8,128)(2,1)}, bf16[136,1024]{1,0:T(8,128)(2,1)S(1)}, u32[]{:S(2)}) copy-start(bf16[136,1024]{1,0:T(8,128)(2,1)S(1)} %get-tuple-element.52) | copy-start | bytes 835588
  149.3 7.6 %collective-permute-start.13 = (bf16[136,1152]{1,0:T(8,128)(2,1)S(1)}, bf16[136,1152]{1,0:T(8,128)(2,1)S(1)}, u32[]{:S(2)}, u32[]{:S(2)}) collective-permute-start(bf16[136,1152]{1,0:T(8,128)(2,1)S(1)} %pad_maximum_fusion.4), channel_id=1, source_target_pairs={{0,1},{1,2},{2,3},{3,0},{4,5},{5,6},{6,7},{7,4},{8,9},{9,10},{10,1... | collective-permute-start | bytes 940040 | tf_op jit(solution)/shard_map/ppermute | solution.py:99
  150.7 16.6 %collective-permute-start.14 = (bf16[136,1152]{1,0:T(8,128)(2,1)S(1)}, bf16[136,1152]{1,0:T(8,128)(2,1)S(1)}, u32[]{:S(2)}, u32[]{:S(2)}) collective-permute-start(bf16[136,1152]{1,0:T(8,128)(2,1)S(1)} %pad_maximum_fusion.4), channel_id=1, source_target_pairs={{0,2},{1,3},{2,0},{3,1},{4,6},{5,7},{6,4},{7,5},{8,10},{9,11},{10,... | collective-permute-start | bytes 940040 | tf_op jit(solution)/shard_map/ppermute | solution.py:99
  153.7 14.3 %collective-permute-start.15 = (bf16[136,1152]{1,0:T(8,128)(2,1)S(1)}, bf16[136,1152]{1,0:T(8,128)(2,1)S(1)}, u32[]{:S(2)}, u32[]{:S(2)}) collective-permute-start(bf16[136,1152]{1,0:T(8,128)(2,1)S(1)} %pad_maximum_fusion.4), channel_id=1, source_target_pairs={{0,3},{1,0},{2,1},{3,2},{4,7},{5,4},{6,5},{7,6},{8,11},{9,8},{10,9... | collective-permute-start | bytes 940040 | tf_op jit(solution)/shard_map/ppermute | solution.py:99
  174.7 5.9 %collective-permute-start.16 = (f32[136,16]{0,1:T(8,128)S(1)}, f32[136,16]{0,1:T(8,128)S(1)}, u32[]{:S(2)}, u32[]{:S(2)}) collective-permute-start(f32[136,16]{0,1:T(8,128)S(1)} %get-tuple-element.44), channel_id=1, source_target_pairs={{0,3},{1,0},{2,1},{3,2},{4,7},{5,4},{6,5},{7,6},{8,11},{9,8},{10,9... | collective-permute-start | bytes 26120 | tf_op jit(solution)/shard_map/ppermute | solution.py:99
  174.7 5.9 %collective-permute-start.17 = (f32[136,16]{0,1:T(8,128)S(1)}, f32[136,16]{0,1:T(8,128)S(1)}, u32[]{:S(2)}, u32[]{:S(2)}) collective-permute-start(f32[136,16]{0,1:T(8,128)S(1)} %get-tuple-element.46), channel_id=1, source_target_pairs={{0,2},{1,3},{2,0},{3,1},{4,6},{5,7},{6,4},{7,5},{8,10},{9,11},{10,... | collective-permute-start | bytes 26120 | tf_op jit(solution)/shard_map/ppermute | solution.py:99
  174.9 5.7 %collective-permute-start.18 = (f32[136,16]{0,1:T(8,128)S(1)}, f32[136,16]{0,1:T(8,128)S(1)}, u32[]{:S(2)}, u32[]{:S(2)}) collective-permute-start(f32[136,16]{0,1:T(8,128)S(1)} %get-tuple-element.45), channel_id=1, source_target_pairs={{0,1},{1,2},{2,3},{3,0},{4,5},{5,6},{6,7},{7,4},{8,9},{9,10},{10,1... | collective-permute-start | bytes 26120 | tf_op jit(solution)/shard_map/ppermute | solution.py:99
Sparse Core Ops, SparseCore 0:
  65.7 26.3 all-gather.1

commit v14 on v12

--- a/solution.py
+++ b/solution.py
@@ -62,7 +62,7 @@
     @pl.when(chunk == pl.num_programs(1) - 1)
     def _():
         if last:
-            out_ref[...] = (acc_s[...] / acc_s[:, 0:1]).astype(out_ref.dtype)
+            out_ref[...] = (acc_s[:, HD:] / acc_s[:, 0:1]).astype(out_ref.dtype)
         else:
             out_ref[...] = acc_s[...]
 
@@ -77,13 +77,18 @@
     if not first:
         in_specs.append(row_block)
         operands.append(state)
-    out_type = jnp.bfloat16 if last else jnp.float32
+    if last:
+        out_specs = pl.BlockSpec((block, HD), lambda i, c: (i, 0))
+        out_shape = jax.ShapeDtypeStruct((rows, HD), jnp.bfloat16)
+    else:
+        out_specs = row_block
+        out_shape = jax.ShapeDtypeStruct((rows, width), jnp.float32)
     return pl.pallas_call(
         functools.partial(step_kernel, first, last),
         grid=(rows // block, chunks),
         in_specs=in_specs,
-        out_specs=row_block,
-        out_shape=jax.ShapeDtypeStruct((rows, width), out_type),
+        out_specs=out_specs,
+        out_shape=out_shape,
         scratch_shapes=[pltpu.VMEM((block, width), jnp.float32)],
         compiler_params=pltpu.CompilerParams(dimension_semantics=("arbitrary", "arbitrary")),
         cost_estimate=pl.CostEstimate(
@@ -154,7 +159,7 @@
         if stage == 0:
             w_out_dep, held = lax.optimization_barrier((w_out, held))
             w_out_all = lax.all_gather(w_out_dep, "type", axis=0, tiled=True)
-    attended = state[:, HD:]
+    attended = state
     rows = tokens.shape[0]
     attended = attended.reshape(-1, rows, HD)
     owner = jnp.arange(local_heads * kinds)

time: 189 us -> 189 us (level)
  no operation moved by 1% of the time
where the time goes in v14:
time: 189 us; the launch traced here: 188 us
  Pallas kernels  58.9 us (31%)
  waiting for transfers between devices  53.5 us (28%)
  starting transfers between devices  30.8 us (16%)
  between operations  14.3 us (8%)
  matrix products  12.2 us (6%)
  local copies, waits for them, and re-layouts  10.1 us (5%)
  other arithmetic  8.09 us (4%)
    pallas_call x4, Pallas kernels, flash_step(): pl.pallas_call(functools.partial(step_kernel, first, last), grid=(rows //...  58.9 us
    ppermute x12, waiting for transfers between devices, shifted(): return lax.ppermute(value, axis, [(i, (i + k) % n) for i in range(n)])  37.7 us
    ppermute x12, starting transfers between devices, shifted(): return lax.ppermute(value, axis, [(i, (i + k) % n) for i in range(n)])  14.9 us
    all_to_all x1, waiting for transfers between devices, body(): back = lax.all_to_all(attended, ('x', 'type'), 0, 0, tiled=True)  11.1 us
    all_to_all x1, starting transfers between devices, body(): back = lax.all_to_all(attended, ('x', 'type'), 0, 0, tiled=True)  8.62 us
    dot_general x2, matrix products, body(): answer = jnp.dot(hidden, head_w2[which], preferred_element_type=jnp.float32)  7.04 us
  transfers between devices with their start and end apart: 21, of which 15 were waited for; matrix products, arithmetic and copies ran while one was open for 6% of the time, Pallas kernels for 31%

profile of v14, /device:TPU:1, one launch (start us, length us, event | category | flops | bytes accessed | tf_op | source)
XLA Modules:
  0.0 188.0 jit_solution(9276298327436381086)
XLA Ops:
  7.2 0.8 slice_add_fusion.1
  8.0 1.1 fusion.68
  9.1 1.1 fusion.71
  10.2 4.4 %collective-permute-start = (bf16[136,1024]{1,0:T(8,128)(2,1)S(1)}, bf16[136,1024]{1,0:T(8,128)(2,1)S(1)}, u32[]{:S(2)}, u32[]{:S(2)}) collective-permute-start(bf16[136,1024]{1,0:T(8,128)(2,1)S(1)} %fusion.71), channel_id=1, source_target_pairs={{0,1},{1,2},{2,3},{3,0},{4,5},{5,6},{6,7},{7,4},{8,9},{9,10},{10,1... | collective-permute-start | bytes 835592 | tf_op jit(solution)/shard_map/ppermute | solution.py:104
  14.6 0.5 collective-permute-start.2
  15.1 1.5 fusion.103
  16.5 0.2 copy.36
  16.8 0.2 copy.37
  17.0 0.2 copy.38
  17.3 0.1 pad.20.clone
  17.3 0.2 pad_maximum_fusion
  17.6 0.2 copy.31
  17.8 2.6 %copy.32 = bf16[1024,4,256]{2,0,1:T(8,128)(2,1)} copy(bf16[1024,4,256]{0,2,1:T(8,128)(2,1)S(1)} %bitcast.63) | data formatting | bytes 4194304 | tf_op jit(solution)/shard_map/reshape | solution.py:122
  20.3 0.2 collective-permute-done
  20.5 6.4 %collective-permute-done.1 = bf16[136,1024]{1,0:T(8,128)(2,1)S(1)} collective-permute-done((bf16[136,1024]{1,0:T(8,128)(2,1)S(1)}, bf16[136,1024]{1,0:T(8,128)(2,1)S(1)}, u32[]{:S(2)}, u32[]{:S(2)}) %collective-permute-start.1) | collective-permute-done | bytes 278560 | tf_op jit(solution)/shard_map/ppermute | solution.py:104
  26.8 0.6 collective-permute-done.2
  27.4 3.0 %fusion.28 = bf16[4,544,256]{2,1,0:T(8,128)(2,1)S(1)} fusion(s32[]{:T(128)S(6)} %select_n.108, bf16[1024,4,256]{2,0,1:T(8,128)(2,1)} %copy.32, bf16[136,1024]{1,0:T(8,128)(2,1)S(1)} %collective-permute-done.2, bf16[136,1024]{1,0:T(8,128)(2,1)S(1)} %collective-permute-done.1, bf16[136,1024]{1,0:T(8,128)(2,1)S(1)} %collective-permute-done, ...), kind=kOutput, calls=%fused_computation.33 | convolution fusion | flops 1150058496 | bytes 4325380 | tf_op jit(solution)/shard_map/rd,dje->jre/dot_general | solution.py:124
  30.4 0.1 slice_bitcast_fusion.3
  30.5 1.3 collective-permute-start.3
  31.8 2.5 %collective-permute-start.4 = (bf16[544,256]{1,0:T(8,128)(2,1)S(1)}, bf16[544,256]{1,0:T(8,128)(2,1)S(1)}, u32[]{:S(2)}, u32[]{:S(2)}) collective-permute-start(bf16[544,256]{1,0:T(8,128)(2,1)S(1)} %get-tuple-element.40), channel_id=1, source_target_pairs={{0,16},{8,24},{16,0},{24,8},{1,17},{9,25},{17,1},{25,9},{2,18},{10... | collective-permute-start | bytes 835592 | tf_op jit(solution)/shard_map/ppermute | solution.py:104
  34.3 1.1 collective-permute-start.5
  35.4 4.7 %collective-permute-done.3 = bf16[544,256]{1,0:T(8,128)(2,1)S(1)} collective-permute-done((bf16[544,256]{1,0:T(8,128)(2,1)S(1)}, bf16[544,256]{1,0:T(8,128)(2,1)S(1)}, u32[]{:S(2)}, u32[]{:S(2)}) %collective-permute-start.3) | collective-permute-done | bytes 278560 | tf_op jit(solution)/shard_map/ppermute | solution.py:104
  40.1 7.1 %collective-permute-done.4 = bf16[544,256]{1,0:T(8,128)(2,1)S(1)} collective-permute-done((bf16[544,256]{1,0:T(8,128)(2,1)S(1)}, bf16[544,256]{1,0:T(8,128)(2,1)S(1)}, u32[]{:S(2)}, u32[]{:S(2)}) %collective-permute-start.4) | collective-permute-done | bytes 278560 | tf_op jit(solution)/shard_map/ppermute | solution.py:104
  47.3 1.3 slice_bitcast_fusion.4
  48.6 1.7 collective-permute-start.6
  50.2 2.1 %collective-permute-start.7 = (bf16[2176,128]{1,0:T(8,128)(2,1)S(1)}, bf16[2176,128]{1,0:T(8,128)(2,1)S(1)}, u32[]{:S(2)}, u32[]{:S(2)}) collective-permute-start(bf16[2176,128]{1,0:T(8,128)(2,1)S(1)} %get-tuple-element.36), channel_id=1, source_target_pairs={{0,96},{32,0},{64,32},{96,64},{1,97},{33,1},{65,33},{97,65},{2,98}... | collective-permute-start | bytes 1671176 | tf_op jit(solution)/shard_map/ppermute | solution.py:143
  52.3 0.7 collective-permute-start.8
  53.1 8.2 %shard_map.113.refs_2_ = f32[2176,128]{1,0:T(8,128)} custom-call(bf16[2176,128]{1,0:T(8,128)(2,1)} %get-tuple-element.37.refs_0_, bf16[1,2176,128]{2,1,0:T(8,128)(2,1)} %get-tuple-element.35.refs_1_), custom_call_target="tpu_custom_call" | custom-call | flops 2424307712 | bytes 3899392 | tf_op jit(solution)/shard_map/pallas_call | solution.py:86
  61.3 3.5 %collective-permute-done.6 = bf16[2176,128]{1,0:T(8,128)(2,1)S(1)} collective-permute-done((bf16[2176,128]{1,0:T(8,128)(2,1)S(1)}, bf16[2176,128]{1,0:T(8,128)(2,1)S(1)}, u32[]{:S(2)}, u32[]{:S(2)}) %collective-permute-start.6) | collective-permute-done | bytes 557088 | tf_op jit(solution)/shard_map/ppermute | solution.py:142
  64.7 0.8 collective-permute-done.8
  65.6 0.1 collective-permute-start.10
  65.7 2.7 %collective-permute-start.11 = (bf16[2176,128]{1,0:T(8,128)(2,1)S(1)}, bf16[2176,128]{1,0:T(8,128)(2,1)S(1)}, u32[]{:S(2)}, u32[]{:S(2)}) collective-permute-start(bf16[2176,128]{1,0:T(8,128)(2,1)S(1)} %collective-permute-done.8), channel_id=1, source_target_pairs={{0,96},{32,0},{64,32},{96,64},{1,97},{33,1},{65,33},{97,65},{2,98}... | collective-permute-start | bytes 1671176 | tf_op jit(solution)/shard_map/ppermute | solution.py:150
  68.4 1.3 pad_maximum_fusion.1.refs_1_
  69.7 21.1 %shard_map.114.refs_2_ = f32[2176,128]{1,0:T(8,128)} custom-call(bf16[2176,128]{1,0:T(8,128)(2,1)} %get-tuple-element.37.refs_0_, bf16[3,2176,128]{2,1,0:T(8,128)(2,1)} %pad_maximum_fusion.1.refs_1_, f32[2176,128]{1,0:T(8,128)} %shard_map.113.refs_2_), custom_call_target="tpu_custom_call" | custom-call | flops 7272923136 | bytes 6127616 | tf_op jit(solution)/shard_map/pallas_call | solution.py:86
  90.8 0.3 collective-permute-done.9
  91.1 1.3 pad_maximum_fusion.2.refs_1_
  92.5 21.1 %shard_map.115.refs_2_ = f32[2176,128]{1,0:T(8,128)} custom-call(bf16[2176,128]{1,0:T(8,128)(2,1)} %get-tuple-element.37.refs_0_, bf16[3,2176,128]{2,1,0:T(8,128)(2,1)} %pad_maximum_fusion.2.refs_1_, f32[2176,128]{1,0:T(8,128)} %shard_map.114.refs_2_), custom_call_target="tpu_custom_call" | custom-call | flops 7272923136 | bytes 6127616 | tf_op jit(solution)/shard_map/pallas_call | solution.py:86
  113.6 0.8 copy-done.5
  114.4 8.5 %shard_map.116 = bf16[2176,64]{1,0:T(8,128)(2,1)} custom-call(bf16[2176,128]{1,0:T(8,128)(2,1)} %get-tuple-element.37.refs_0_, bf16[1,2176,128]{2,1,0:T(8,128)(2,1)} %bitcast.79, f32[2176,128]{1,0:T(8,128)} %shard_map.115.refs_2_), custom_call_target="tpu_custom_call" | custom-call | flops 2424307712 | bytes 3899392 | tf_op jit(solution)/shard_map/pallas_call | solution.py:86
  122.9 1.4 copy.34
  124.3 0.6 gather_fusion
  124.9 0.9 broadcast_select_fusion
  125.8 8.6 %all-to-all-start = ((bf16[16,136,64]{1,2,0:T(8,128)(2,1)}), bf16[16,136,64]{1,2,0:T(8,128)(2,1)S(1)}, u32[]{:S(2)}, u32[]{:S(2)}) async-start(bf16[16,136,64]{1,2,0:T(8,128)(2,1)} %broadcast_select_fusion), calls=%async_computation | async-start | bytes 1048576 | tf_op jit(solution)/shard_map/all_to_all | solution.py:170
  134.5 11.1 %all-to-all-done = bf16[16,136,64]{1,2,0:T(8,128)(2,1)S(1)} async-done(((bf16[16,136,64]{1,2,0:T(8,128)(2,1)}), bf16[16,136,64]{1,2,0:T(8,128)(2,1)S(1)}, u32[]{:S(2)}, u32[]{:S(2)}) %all-to-all-start) | async-done | bytes 278560 | tf_op jit(solution)/shard_map/all_to_all | solution.py:170
  145.6 0.6 copy.35
  146.2 0.4 reshape.206
  146.6 2.2 %fusion.65 = (f32[136]{0:T(256)S(1)}, bf16[136,1024]{1,0:T(8,128)(2,1)S(1)}) fusion(bf16[136,1024]{1,0:T(8,128)(2,1)S(1)} %reshape.206, bf16[1024,1024]{1,0:T(8,128)(2,1)} %all-gather.2.cloned.1.call-done, f32[1024]{0:T(1024)S(1)} %copy-done.3, bf16[136,1024]{1,0:T(8,128)(2,1)S(1)} %copy-done), kind=kOutput, calls=%fused_computation.67 | convolution fusion | flops 286187392 | bytes 2937376 | tf_op jit(solution)/shard_map/dot_general | solution.py:173
  148.9 0.1 fusion.67
  149.0 0.1 broadcast_in_dim.49
  149.1 1.4 collective-permute-start.13
  150.5 2.9 %collective-permute-start.14 = (bf16[136,1152]{1,0:T(8,128)(2,1)S(1)}, bf16[136,1152]{1,0:T(8,128)(2,1)S(1)}, u32[]{:S(2)}, u32[]{:S(2)}) collective-permute-start(bf16[136,1152]{1,0:T(8,128)(2,1)S(1)} %pad_maximum_fusion.8), channel_id=1, source_target_pairs={{0,2},{1,3},{2,0},{3,1},{4,6},{5,7},{6,4},{7,5},{8,10},{9,11},{10,... | collective-permute-start | bytes 940040 | tf_op jit(solution)/shard_map/ppermute | solution.py:104
  153.4 3.5 %collective-permute-done.13 = bf16[136,1152]{1,0:T(8,128)(2,1)S(1)} collective-permute-done((bf16[136,1152]{1,0:T(8,128)(2,1)S(1)}, bf16[136,1152]{1,0:T(8,128)(2,1)S(1)}, u32[]{:S(2)}, u32[]{:S(2)}) %collective-permute-start.13) | collective-permute-done | bytes 313376 | tf_op jit(solution)/shard_map/ppermute | solution.py:104
  156.9 10.3 %collective-permute-done.14 = bf16[136,1152]{1,0:T(8,128)(2,1)S(1)} collective-permute-done((bf16[136,1152]{1,0:T(8,128)(2,1)S(1)}, bf16[136,1152]{1,0:T(8,128)(2,1)S(1)}, u32[]{:S(2)}, u32[]{:S(2)}) %collective-permute-start.14) | collective-permute-done | bytes 313376 | tf_op jit(solution)/shard_map/ppermute | solution.py:104
  167.1 0.6 collective-permute-done.15
  167.7 0.3 fusion.72
  168.0 3.5 %fusion.59 = f32[544,16]{0,1:T(8,128)S(1)} fusion(bf16[2,1024,1024]{2,1,0:T(8,128)(2,1)} %param.17, f32[1024]{0:T(1024)S(1)} %bitcast.78, bf16[2,1024,16]{1,2,0:T(8,128)(2,1)S(1)} %copy-done.6, pred[544]{0:T(1024)(128)(4,1)S(1)} %get-tuple-element.31, bf16[136,1152]{1,0:T(8,128)(2,1)S(1)} %collective-permute-done.15, ...), kind=kOutput, calls=%fused_computation.61 | convolution fusion | flops 1169826304 | bytes 3423232 | tf_op jit(solution)/shard_map/dot_general | solution.py:187
  171.5 3.5 %fusion.62 = f32[544,16]{0,1:T(8,128)S(1)} fusion(f32[544,16]{0,1:T(8,128)S(1)} %fusion.59, bf16[2,1024,1024]{2,1,0:T(8,128)(2,1)} %param.17, f32[1024]{0:T(1024)S(1)} %bitcast.77, bf16[2,1024,16]{1,2,0:T(8,128)(2,1)S(1)} %copy-done.6, pred[544]{0:T(1024)(128)(4,1)S(1)} %get-tuple-element.30, bf16[136,1152]{1,0:T(8,128)(2,1)S(1)} %collective-permute-done.15, ...), kind=kOutput, calls=%fused_computation.62 | convolution fusion | flops 1169826304 | bytes 3464192 | tf_op jit(solution)/shard_map/dot_general | solution.py:187
  175.1 0.1 fusion.104
  175.2 0.2 collective-permute-start.17
  175.4 0.7 collective-permute-start.18
  176.1 0.3 collective-permute-done.16
  176.4 3.0 %collective-permute-done.17 = f32[136,16]{0,1:T(8,128)S(1)} collective-permute-done((f32[136,16]{0,1:T(8,128)S(1)}, f32[136,16]{0,1:T(8,128)S(1)}, u32[]{:S(2)}, u32[]{:S(2)}) %collective-permute-start.17) | collective-permute-done | bytes 8736 | tf_op jit(solution)/shard_map/ppermute | solution.py:104
  179.4 1.2 collective-permute-done.18
  180.5 0.6 fusion.79
  (38 shorter events, 0.4 us)
Async XLA Ops:
  7.2 139.4 %all-gather.2.cloned.1.call-start = ((), (), s32[]{:S(2)}) async-start(), calls=%async_computation.1 | async-start | bytes 2621440 | tf_op jit(solution)/shard_map/all_gather | solution.py:161
  10.2 10.3 %collective-permute-start = (bf16[136,1024]{1,0:T(8,128)(2,1)S(1)}, bf16[136,1024]{1,0:T(8,128)(2,1)S(1)}, u32[]{:S(2)}, u32[]{:S(2)}) collective-permute-start(bf16[136,1024]{1,0:T(8,128)(2,1)S(1)} %fusion.71), channel_id=1, source_target_pairs={{0,1},{1,2},{2,3},{3,0},{4,5},{5,6},{6,7},{7,4},{8,9},{9,10},{10,1... | collective-permute-start | bytes 835592 | tf_op jit(solution)/shard_map/ppermute | solution.py:104
  14.6 12.2 %collective-permute-start.1 = (bf16[136,1024]{1,0:T(8,128)(2,1)S(1)}, bf16[136,1024]{1,0:T(8,128)(2,1)S(1)}, u32[]{:S(2)}, u32[]{:S(2)}) collective-permute-start(bf16[136,1024]{1,0:T(8,128)(2,1)S(1)} %fusion.71), channel_id=1, source_target_pairs={{0,2},{1,3},{2,0},{3,1},{4,6},{5,7},{6,4},{7,5},{8,10},{9,11},{10,... | collective-permute-start | bytes 835592 | tf_op jit(solution)/shard_map/ppermute | solution.py:104
  14.6 12.8 %collective-permute-start.2 = (bf16[136,1024]{1,0:T(8,128)(2,1)S(1)}, bf16[136,1024]{1,0:T(8,128)(2,1)S(1)}, u32[]{:S(2)}, u32[]{:S(2)}) collective-permute-start(bf16[136,1024]{1,0:T(8,128)(2,1)S(1)} %fusion.71), channel_id=1, source_target_pairs={{0,3},{1,0},{2,1},{3,2},{4,7},{5,4},{6,5},{7,6},{8,11},{9,8},{10,9... | collective-permute-start | bytes 835592 | tf_op jit(solution)/shard_map/ppermute | solution.py:104
  30.5 9.6 %collective-permute-start.3 = (bf16[544,256]{1,0:T(8,128)(2,1)S(1)}, bf16[544,256]{1,0:T(8,128)(2,1)S(1)}, u32[]{:S(2)}, u32[]{:S(2)}) collective-permute-start(bf16[544,256]{1,0:T(8,128)(2,1)S(1)} %get-tuple-element.41), channel_id=1, source_target_pairs={{0,8},{8,16},{16,24},{24,0},{1,9},{9,17},{17,25},{25,1},{2,10},{10... | collective-permute-start | bytes 835592 | tf_op jit(solution)/shard_map/ppermute | solution.py:104
  31.8 15.4 %collective-permute-start.4 = (bf16[544,256]{1,0:T(8,128)(2,1)S(1)}, bf16[544,256]{1,0:T(8,128)(2,1)S(1)}, u32[]{:S(2)}, u32[]{:S(2)}) collective-permute-start(bf16[544,256]{1,0:T(8,128)(2,1)S(1)} %get-tuple-element.40), channel_id=1, source_target_pairs={{0,16},{8,24},{16,0},{24,8},{1,17},{9,25},{17,1},{25,9},{2,18},{10... | collective-permute-start | bytes 835592 | tf_op jit(solution)/shard_map/ppermute | solution.py:104
  34.3 12.9 %collective-permute-start.5 = (bf16[544,256]{1,0:T(8,128)(2,1)S(1)}, bf16[544,256]{1,0:T(8,128)(2,1)S(1)}, u32[]{:S(2)}, u32[]{:S(2)}) collective-permute-start(bf16[544,256]{1,0:T(8,128)(2,1)S(1)} %get-tuple-element.39), channel_id=1, source_target_pairs={{0,24},{8,0},{16,8},{24,16},{1,25},{9,1},{17,9},{25,17},{2,26},{10... | collective-permute-start | bytes 835592 | tf_op jit(solution)/shard_map/ppermute | solution.py:104
  48.6 16.1 %collective-permute-start.6 = (bf16[2176,128]{1,0:T(8,128)(2,1)S(1)}, bf16[2176,128]{1,0:T(8,128)(2,1)S(1)}, u32[]{:S(2)}, u32[]{:S(2)}) collective-permute-start(bf16[2176,128]{1,0:T(8,128)(2,1)S(1)} %get-tuple-element.36), channel_id=1, source_target_pairs={{0,32},{32,64},{64,96},{96,0},{1,33},{33,65},{65,97},{97,1},{2,34}... | collective-permute-start | bytes 1671176 | tf_op jit(solution)/shard_map/ppermute | solution.py:142
  50.2 14.5 %collective-permute-start.7 = (bf16[2176,128]{1,0:T(8,128)(2,1)S(1)}, bf16[2176,128]{1,0:T(8,128)(2,1)S(1)}, u32[]{:S(2)}, u32[]{:S(2)}) collective-permute-start(bf16[2176,128]{1,0:T(8,128)(2,1)S(1)} %get-tuple-element.36), channel_id=1, source_target_pairs={{0,96},{32,0},{64,32},{96,64},{1,97},{33,1},{65,33},{97,65},{2,98}... | collective-permute-start | bytes 1671176 | tf_op jit(solution)/shard_map/ppermute | solution.py:143
  52.3 13.2 %collective-permute-start.8 = (bf16[2176,128]{1,0:T(8,128)(2,1)S(1)}, bf16[2176,128]{1,0:T(8,128)(2,1)S(1)}, u32[]{:S(2)}, u32[]{:S(2)}) collective-permute-start(bf16[2176,128]{1,0:T(8,128)(2,1)S(1)} %get-tuple-element.36), channel_id=1, source_target_pairs={{0,4},{4,0},{1,5},{5,1},{2,6},{6,2},{3,7},{7,3},{8,12},{12,8},{9,1... | collective-permute-start | bytes 1671176 | tf_op jit(solution)/shard_map/ppermute | solution.py:144
  65.6 25.2 %collective-permute-start.10 = (bf16[2176,128]{1,0:T(8,128)(2,1)S(1)}, bf16[2176,128]{1,0:T(8,128)(2,1)S(1)}, u32[]{:S(2)}, u32[]{:S(2)}) collective-permute-start(bf16[2176,128]{1,0:T(8,128)(2,1)S(1)} %collective-permute-done.8), channel_id=1, source_target_pairs={{0,32},{32,64},{64,96},{96,0},{1,33},{33,65},{65,97},{97,1},{2,34}... | collective-permute-start | bytes 1671176 | tf_op jit(solution)/shard_map/ppermute | solution.py:149
  65.7 25.1 %collective-permute-start.11 = (bf16[2176,128]{1,0:T(8,128)(2,1)S(1)}, bf16[2176,128]{1,0:T(8,128)(2,1)S(1)}, u32[]{:S(2)}, u32[]{:S(2)}) collective-permute-start(bf16[2176,128]{1,0:T(8,128)(2,1)S(1)} %collective-permute-done.8), channel_id=1, source_target_pairs={{0,96},{32,0},{64,32},{96,64},{1,97},{33,1},{65,33},{97,65},{2,98}... | collective-permute-start | bytes 1671176 | tf_op jit(solution)/shard_map/ppermute | solution.py:150
  68.4 22.7 %collective-permute-start.9 = (bf16[2176,128]{1,0:T(8,128)(2,1)S(1)}, bf16[2176,128]{1,0:T(8,128)(2,1)S(1)}, u32[]{:S(2)}, u32[]{:S(2)}) collective-permute-start(bf16[2176,128]{1,0:T(8,128)(2,1)S(1)} %collective-permute-done.6), channel_id=1, source_target_pairs={{0,32},{32,64},{64,96},{96,0},{1,33},{33,65},{65,97},{97,1},{2,34}... | collective-permute-start | bytes 1671176 | tf_op jit(solution)/shard_map/ppermute | solution.py:148
  91.1 22.4 %collective-permute-start.12 = (bf16[2176,128]{1,0:T(8,128)(2,1)S(1)}, bf16[2176,128]{1,0:T(8,128)(2,1)S(1)}, u32[]{:S(2)}, u32[]{:S(2)}) collective-permute-start(bf16[2176,128]{1,0:T(8,128)(2,1)S(1)} %collective-permute-done.10), channel_id=1, source_target_pairs={{0,32},{32,64},{64,96},{96,0},{1,33},{33,65},{65,97},{97,1},{2,34}... | collective-permute-start | bytes 1671176 | tf_op jit(solution)/shard_map/ppermute | solution.py:153
  113.6 0.8 copy-start.5
  122.9 11.5 %copy-start.7 = (s32[136,1]{0,1:T(1,128)S(1)}, s32[136,1]{0,1:T(1,128)}, u32[]{:S(2)}) copy-start(s32[136,1]{0,1:T(1,128)} %param.16) | copy-start | bytes 1636
  124.9 21.7 %copy-start = (bf16[136,1024]{1,0:T(8,128)(2,1)S(1)}, bf16[136,1024]{1,0:T(8,128)(2,1)}, u32[]{:S(2)}) copy-start(bf16[136,1024]{1,0:T(8,128)(2,1)} %param.10) | copy-start | bytes 835588
  124.9 21.7 %copy-start.3 = (f32[1024]{0:T(1024)S(1)}, f32[1024]{0:T(1024)}, u32[]{:S(2)}) copy-start(f32[1024]{0:T(1024)} %param.12) | copy-start | bytes 12292
  125.8 19.8 %all-to-all-start = ((bf16[16,136,64]{1,2,0:T(8,128)(2,1)}), bf16[16,136,64]{1,2,0:T(8,128)(2,1)S(1)}, u32[]{:S(2)}, u32[]{:S(2)}) async-start(bf16[16,136,64]{1,2,0:T(8,128)(2,1)} %broadcast_select_fusion), calls=%async_computation | async-start | bytes 1048576 | tf_op jit(solution)/shard_map/all_to_all | solution.py:170
  145.6 3.3 %copy-start.4 = (f32[1024]{0:T(1024)S(1)}, f32[1024]{0:T(1024)}, u32[]{:S(2)}) copy-start(f32[1024]{0:T(1024)} %param.13) | copy-start | bytes 12292
  146.5 6.8 %copy-start.2 = (bf16[2,1024]{1,0:T(2,128)(2,1)S(1)}, bf16[2,1024]{1,0:T(2,128)(2,1)}, u32[]{:S(2)}) copy-start(bf16[2,1024]{1,0:T(2,128)(2,1)} %param.18) | copy-start | bytes 12292
  146.5 21.5 %copy-start.6 = (bf16[2,1024,16]{1,2,0:T(8,128)(2,1)S(1)}, bf16[2,1024,16]{1,2,0:T(8,128)(2,1)}, u32[]{:S(2)}) copy-start(bf16[2,1024,16]{1,2,0:T(8,128)(2,1)} %param.19) | copy-start | bytes 196612
  148.8 22.7 %copy-start.1 = (bf16[136,1024]{1,0:T(8,128)(2,1)}, bf16[136,1024]{1,0:T(8,128)(2,1)S(1)}, u32[]{:S(2)}) copy-start(bf16[136,1024]{1,0:T(8,128)(2,1)S(1)} %get-tuple-element.50) | copy-start | bytes 835588
  149.1 7.7 %collective-permute-start.13 = (bf16[136,1152]{1,0:T(8,128)(2,1)S(1)}, bf16[136,1152]{1,0:T(8,128)(2,1)S(1)}, u32[]{:S(2)}, u32[]{:S(2)}) collective-permute-start(bf16[136,1152]{1,0:T(8,128)(2,1)S(1)} %pad_maximum_fusion.8), channel_id=1, source_target_pairs={{0,1},{1,2},{2,3},{3,0},{4,5},{5,6},{6,7},{7,4},{8,9},{9,10},{10,1... | collective-permute-start | bytes 940040 | tf_op jit(solution)/shard_map/ppermute | solution.py:104
  150.5 16.6 %collective-permute-start.14 = (bf16[136,1152]{1,0:T(8,128)(2,1)S(1)}, bf16[136,1152]{1,0:T(8,128)(2,1)S(1)}, u32[]{:S(2)}, u32[]{:S(2)}) collective-permute-start(bf16[136,1152]{1,0:T(8,128)(2,1)S(1)} %pad_maximum_fusion.8), channel_id=1, source_target_pairs={{0,2},{1,3},{2,0},{3,1},{4,6},{5,7},{6,4},{7,5},{8,10},{9,11},{10,... | collective-permute-start | bytes 940040 | tf_op jit(solution)/shard_map/ppermute | solution.py:104
  153.4 14.4 %collective-permute-start.15 = (bf16[136,1152]{1,0:T(8,128)(2,1)S(1)}, bf16[136,1152]{1,0:T(8,128)(2,1)S(1)}, u32[]{:S(2)}, u32[]{:S(2)}) collective-permute-start(bf16[136,1152]{1,0:T(8,128)(2,1)S(1)} %pad_maximum_fusion.8), channel_id=1, source_target_pairs={{0,3},{1,0},{2,1},{3,2},{4,7},{5,4},{6,5},{7,6},{8,11},{9,8},{10,9... | collective-permute-start | bytes 940040 | tf_op jit(solution)/shard_map/ppermute | solution.py:104
  175.2 1.2 collective-permute-start.16
  175.2 4.2 %collective-permute-start.17 = (f32[136,16]{0,1:T(8,128)S(1)}, f32[136,16]{0,1:T(8,128)S(1)}, u32[]{:S(2)}, u32[]{:S(2)}) collective-permute-start(f32[136,16]{0,1:T(8,128)S(1)} %get-tuple-element.44), channel_id=1, source_target_pairs={{0,2},{1,3},{2,0},{3,1},{4,6},{5,7},{6,4},{7,5},{8,10},{9,11},{10,... | collective-permute-start | bytes 26120 | tf_op jit(solution)/shard_map/ppermute | solution.py:104
  175.4 5.2 %collective-permute-start.18 = (f32[136,16]{0,1:T(8,128)S(1)}, f32[136,16]{0,1:T(8,128)S(1)}, u32[]{:S(2)}, u32[]{:S(2)}) collective-permute-start(f32[136,16]{0,1:T(8,128)S(1)} %get-tuple-element.43), channel_id=1, source_target_pairs={{0,3},{1,0},{2,1},{3,2},{4,7},{5,4},{6,5},{7,6},{8,11},{9,8},{10,9... | collective-permute-start | bytes 26120 | tf_op jit(solution)/shard_map/ppermute | solution.py:104
Sparse Core Ops, SparseCore 0:
  65.7 26.3 all-gather.1

commit v15 on v12

--- a/solution.py
+++ b/solution.py
@@ -139,11 +139,8 @@
                 lax.ppermute(chunk, "y", yy),
             ]
         elif stage == 1:
-            following = [
-                lax.ppermute(held[0], "z", zr),
-                lax.ppermute(held[2], "z", zr),
-                lax.ppermute(held[2], "z", zl),
-            ]
+            pair = lax.ppermute(jnp.stack([held[0], held[2]]), "z", zr)
+            following = [pair[0], pair[1], lax.ppermute(held[2], "z", zl)]
         elif stage == 2:
             following = [lax.ppermute(held[1], "z", zr)]
         else:

time: 189 us -> 190 us (level)
  other arithmetic: 8.09 us -> 10.3 us
    another operation x2, other arithmetic: 2.7 us -> 4.82 us  [body(): state = flash_step(q_pad, jnp.stack(held), state, stage == 0, stage == 3)]
  transfers between devices with their start and end apart: 21 -> 20, of which waited for: 15 -> 14; matrix products, arithmetic and copies ran while one was open for 6% -> 7% of each run, Pallas kernels for 31% -> 31%
where the time goes in v15:
time: 190 us; the launch traced here: 189 us
  Pallas kernels  58.7 us (31%)
  waiting for transfers between devices  53.1 us (28%)
  starting transfers between devices  30.1 us (16%)
  between operations  14.3 us (8%)
  matrix products  12.2 us (6%)
  local copies, waits for them, and re-layouts  10.4 us (5%)
  other arithmetic  10.3 us (5%)
    pallas_call x4, Pallas kernels, flash_step(): pl.pallas_call(functools.partial(step_kernel, first, last), grid=(rows //...  58.7 us
    ppermute x12, waiting for transfers between devices, shifted(): return lax.ppermute(value, axis, [(i, (i + k) % n) for i in range(n)])  37.7 us
    ppermute x12, starting transfers between devices, shifted(): return lax.ppermute(value, axis, [(i, (i + k) % n) for i in range(n)])  14.9 us
    all_to_all x1, waiting for transfers between devices, body(): back = lax.all_to_all(attended, ('x', 'type'), 0, 0, tiled=True)  11.1 us
    all_to_all x1, starting transfers between devices, body(): back = lax.all_to_all(attended, ('x', 'type'), 0, 0, tiled=True)  7.6 us
    dot_general x2, matrix products, body(): answer = jnp.dot(hidden, head_w2[which], preferred_element_type=jnp.float32)  7.05 us
    another operation x2, other arithmetic, body(): state = flash_step(q_pad, jnp.stack(held), state, stage == 0, stage == 3)  4.82 us
  transfers between devices with their start and end apart: 20, of which 14 were waited for; matrix products, arithmetic and copies ran while one was open for 7% of the time, Pallas kernels for 31%

profile of v15, /device:TPU:1, one launch (start us, length us, event | category | flops | bytes accessed | tf_op | source)
XLA Modules:
  0.0 189.3 jit_solution(3935979942726533737)
XLA Ops:
  7.2 0.8 slice_add_fusion.1
  8.0 1.1 fusion.68
  9.1 1.1 fusion.71
  10.2 4.4 %collective-permute-start = (bf16[136,1024]{1,0:T(8,128)(2,1)S(1)}, bf16[136,1024]{1,0:T(8,128)(2,1)S(1)}, u32[]{:S(2)}, u32[]{:S(2)}) collective-permute-start(bf16[136,1024]{1,0:T(8,128)(2,1)S(1)} %fusion.71), channel_id=1, source_target_pairs={{0,1},{1,2},{2,3},{3,0},{4,5},{5,6},{6,7},{7,4},{8,9},{9,10},{10,1... | collective-permute-start | bytes 835592 | tf_op jit(solution)/shard_map/ppermute | solution.py:99
  14.6 0.5 collective-permute-start.2
  15.1 1.5 fusion.103
  16.5 0.2 copy.36
  16.8 0.2 copy.37
  17.0 0.2 copy.38
  17.3 0.1 pad.22.clone
  17.3 0.2 pad_maximum_fusion
  17.6 0.2 copy.31
  17.8 2.6 %copy.32 = bf16[1024,4,256]{2,0,1:T(8,128)(2,1)} copy(bf16[1024,4,256]{0,2,1:T(8,128)(2,1)S(1)} %bitcast.67) | data formatting | bytes 4194304 | tf_op jit(solution)/shard_map/reshape | solution.py:117
  20.3 0.1 collective-permute-done
  20.5 6.4 %collective-permute-done.1 = bf16[136,1024]{1,0:T(8,128)(2,1)S(1)} collective-permute-done((bf16[136,1024]{1,0:T(8,128)(2,1)S(1)}, bf16[136,1024]{1,0:T(8,128)(2,1)S(1)}, u32[]{:S(2)}, u32[]{:S(2)}) %collective-permute-start.1) | collective-permute-done | bytes 278560 | tf_op jit(solution)/shard_map/ppermute | solution.py:99
  26.8 0.6 collective-permute-done.2
  27.4 3.0 %fusion.28 = bf16[4,544,256]{2,1,0:T(8,128)(2,1)S(1)} fusion(s32[]{:T(128)S(6)} %select_n.108, bf16[1024,4,256]{2,0,1:T(8,128)(2,1)} %copy.32, bf16[136,1024]{1,0:T(8,128)(2,1)S(1)} %collective-permute-done.2, bf16[136,1024]{1,0:T(8,128)(2,1)S(1)} %collective-permute-done.1, bf16[136,1024]{1,0:T(8,128)(2,1)S(1)} %collective-permute-done, ...), kind=kOutput, calls=%fused_computation.33 | convolution fusion | flops 1150058496 | bytes 4325380 | tf_op jit(solution)/shard_map/rd,dje->jre/dot_general | solution.py:119
  30.5 1.3 collective-permute-start.3
  31.8 2.5 %collective-permute-start.4 = (bf16[544,256]{1,0:T(8,128)(2,1)S(1)}, bf16[544,256]{1,0:T(8,128)(2,1)S(1)}, u32[]{:S(2)}, u32[]{:S(2)}) collective-permute-start(bf16[544,256]{1,0:T(8,128)(2,1)S(1)} %get-tuple-element.42), channel_id=1, source_target_pairs={{0,16},{8,24},{16,0},{24,8},{1,17},{9,25},{17,1},{25,9},{2,18},{10... | collective-permute-start | bytes 835592 | tf_op jit(solution)/shard_map/ppermute | solution.py:99
  34.3 1.1 collective-permute-start.5
  35.4 4.7 %collective-permute-done.3 = bf16[544,256]{1,0:T(8,128)(2,1)S(1)} collective-permute-done((bf16[544,256]{1,0:T(8,128)(2,1)S(1)}, bf16[544,256]{1,0:T(8,128)(2,1)S(1)}, u32[]{:S(2)}, u32[]{:S(2)}) %collective-permute-start.3) | collective-permute-done | bytes 278560 | tf_op jit(solution)/shard_map/ppermute | solution.py:99
  40.1 7.1 %collective-permute-done.4 = bf16[544,256]{1,0:T(8,128)(2,1)S(1)} collective-permute-done((bf16[544,256]{1,0:T(8,128)(2,1)S(1)}, bf16[544,256]{1,0:T(8,128)(2,1)S(1)}, u32[]{:S(2)}, u32[]{:S(2)}) %collective-permute-start.4) | collective-permute-done | bytes 278560 | tf_op jit(solution)/shard_map/ppermute | solution.py:99
  47.3 1.3 slice_bitcast_fusion.6
  48.6 1.7 collective-permute-start.6
  50.2 2.1 %collective-permute-start.7 = (bf16[2176,128]{1,0:T(8,128)(2,1)S(1)}, bf16[2176,128]{1,0:T(8,128)(2,1)S(1)}, u32[]{:S(2)}, u32[]{:S(2)}) collective-permute-start(bf16[2176,128]{1,0:T(8,128)(2,1)S(1)} %get-tuple-element.38), channel_id=1, source_target_pairs={{0,96},{32,0},{64,32},{96,64},{1,97},{33,1},{65,33},{97,65},{2,98}... | collective-permute-start | bytes 1671176 | tf_op jit(solution)/shard_map/ppermute | solution.py:138
  52.3 0.7 collective-permute-start.8
  53.1 8.2 %shard_map.113.refs_2_ = f32[2176,128]{1,0:T(8,128)} custom-call(bf16[2176,128]{1,0:T(8,128)(2,1)} %get-tuple-element.39.refs_0_, bf16[1,2176,128]{2,1,0:T(8,128)(2,1)} %get-tuple-element.37.refs_1_), custom_call_target="tpu_custom_call" | custom-call | flops 2424307712 | bytes 3899392 | tf_op jit(solution)/shard_map/pallas_call | solution.py:81
  61.3 3.4 %collective-permute-done.6 = bf16[2176,128]{1,0:T(8,128)(2,1)S(1)} collective-permute-done((bf16[2176,128]{1,0:T(8,128)(2,1)S(1)}, bf16[2176,128]{1,0:T(8,128)(2,1)S(1)}, u32[]{:S(2)}, u32[]{:S(2)}) %collective-permute-start.6) | collective-permute-done | bytes 557088 | tf_op jit(solution)/shard_map/ppermute | solution.py:137
  64.7 0.8 collective-permute-done.8
  65.5 0.1 pad_maximum_fusion.8
  65.6 0.4 collective-permute-start.9
  66.0 2.6 %collective-permute-start.10 = (bf16[2176,128]{1,0:T(8,128)(2,1)S(1)}, bf16[2176,128]{1,0:T(8,128)(2,1)}, u32[]{:S(2)}, u32[]{:S(2)}) collective-permute-start(bf16[2176,128]{1,0:T(8,128)(2,1)S(1)} %collective-permute-done.8), channel_id=1, source_target_pairs={{0,96},{32,0},{64,32},{96,64},{1,97},{33,1},{65,33},{97,65},{2,98}... | collective-permute-start | bytes 1671176 | tf_op jit(solution)/shard_map/ppermute | solution.py:143
  68.7 2.4 %pad_maximum_fusion.1.refs_1_ = bf16[3,2176,128]{2,1,0:T(8,128)(2,1)} fusion(bf16[1,2176,128]{2,1,0:T(8,128)(2,1)S(1)} %bitcast.69, bf16[1,2176,128]{2,1,0:T(8,128)(2,1)} %bitcast.79, bf16[1,2176,128]{2,1,0:T(8,128)(2,1)S(1)} %bitcast.71), kind=kLoop, calls=%fused_computation.30 | loop fusion | flops 1671168 | bytes 3342336 | tf_op jit(solution)/shard_map/stack | solution.py:148
  71.1 21.1 %shard_map.114.refs_2_ = f32[2176,128]{1,0:T(8,128)} custom-call(bf16[2176,128]{1,0:T(8,128)(2,1)} %get-tuple-element.39.refs_0_, bf16[3,2176,128]{2,1,0:T(8,128)(2,1)} %pad_maximum_fusion.1.refs_1_, f32[2176,128]{1,0:T(8,128)} %shard_map.113.refs_2_), custom_call_target="tpu_custom_call" | custom-call | flops 7272923136 | bytes 6127616 | tf_op jit(solution)/shard_map/pallas_call | solution.py:81
  92.3 2.4 %pad_maximum_fusion.2.refs_1_ = bf16[3,2176,128]{2,1,0:T(8,128)(2,1)} fusion(bf16[1,2176,128]{2,1,0:T(8,128)(2,1)} %bitcast.20, bf16[1,2176,128]{2,1,0:T(8,128)(2,1)S(1)} %bitcast.72, bf16[1,2176,128]{2,1,0:T(8,128)(2,1)S(1)} %bitcast.73), kind=kLoop, calls=%fused_computation.31 | loop fusion | flops 1671168 | bytes 3342336 | tf_op jit(solution)/shard_map/stack | solution.py:148
  94.7 21.1 %shard_map.115.refs_2_ = f32[2176,128]{1,0:T(8,128)} custom-call(bf16[2176,128]{1,0:T(8,128)(2,1)} %get-tuple-element.39.refs_0_, bf16[3,2176,128]{2,1,0:T(8,128)(2,1)} %pad_maximum_fusion.2.refs_1_, f32[2176,128]{1,0:T(8,128)} %shard_map.114.refs_2_), custom_call_target="tpu_custom_call" | custom-call | flops 7272923136 | bytes 6127616 | tf_op jit(solution)/shard_map/pallas_call | solution.py:81
  115.8 0.8 copy-done.6
  116.6 8.4 %shard_map.116 = bf16[2176,128]{1,0:T(8,128)(2,1)} custom-call(bf16[2176,128]{1,0:T(8,128)(2,1)} %get-tuple-element.39.refs_0_, bf16[1,2176,128]{2,1,0:T(8,128)(2,1)} %bitcast.84, f32[2176,128]{1,0:T(8,128)} %shard_map.115.refs_2_), custom_call_target="tpu_custom_call" | custom-call | flops 2424307712 | bytes 3899392 | tf_op jit(solution)/shard_map/pallas_call | solution.py:81
  125.0 1.3 slice.121
  126.3 0.3 copy.34
  126.7 0.6 gather_fusion
  127.3 0.9 broadcast_select_fusion
  128.2 7.6 %all-to-all-start = ((bf16[16,136,64]{1,2,0:T(8,128)(2,1)}), bf16[16,136,64]{1,2,0:T(8,128)(2,1)S(1)}, u32[]{:S(2)}, u32[]{:S(2)}) async-start(bf16[16,136,64]{1,2,0:T(8,128)(2,1)} %broadcast_select_fusion), calls=%async_computation | async-start | bytes 1048576 | tf_op jit(solution)/shard_map/all_to_all | solution.py:162
  135.8 11.1 %all-to-all-done = bf16[16,136,64]{1,2,0:T(8,128)(2,1)S(1)} async-done(((bf16[16,136,64]{1,2,0:T(8,128)(2,1)}), bf16[16,136,64]{1,2,0:T(8,128)(2,1)S(1)}, u32[]{:S(2)}, u32[]{:S(2)}) %all-to-all-start) | async-done | bytes 278560 | tf_op jit(solution)/shard_map/all_to_all | solution.py:162
  146.9 0.6 copy.35
  147.5 0.4 reshape.206
  147.9 2.2 %fusion.65 = (f32[136]{0:T(256)S(1)}, bf16[136,1024]{1,0:T(8,128)(2,1)S(1)}) fusion(bf16[136,1024]{1,0:T(8,128)(2,1)S(1)} %reshape.206, bf16[1024,1024]{1,0:T(8,128)(2,1)} %all-gather.2.cloned.1.call-done, f32[1024]{0:T(1024)S(1)} %copy-done.4, bf16[136,1024]{1,0:T(8,128)(2,1)S(1)} %copy-done), kind=kOutput, calls=%fused_computation.68 | convolution fusion | flops 286187392 | bytes 2937376 | tf_op jit(solution)/shard_map/dot_general | solution.py:165
  150.2 0.1 fusion.67
  150.3 0.1 broadcast_in_dim.49
  150.5 1.4 collective-permute-start.12
  151.8 2.9 %collective-permute-start.13 = (bf16[136,1152]{1,0:T(8,128)(2,1)S(1)}, bf16[136,1152]{1,0:T(8,128)(2,1)S(1)}, u32[]{:S(2)}, u32[]{:S(2)}) collective-permute-start(bf16[136,1152]{1,0:T(8,128)(2,1)S(1)} %pad_maximum_fusion.9), channel_id=1, source_target_pairs={{0,2},{1,3},{2,0},{3,1},{4,6},{5,7},{6,4},{7,5},{8,10},{9,11},{10,... | collective-permute-start | bytes 940040 | tf_op jit(solution)/shard_map/ppermute | solution.py:99
  154.7 3.5 %collective-permute-done.12 = bf16[136,1152]{1,0:T(8,128)(2,1)S(1)} collective-permute-done((bf16[136,1152]{1,0:T(8,128)(2,1)S(1)}, bf16[136,1152]{1,0:T(8,128)(2,1)S(1)}, u32[]{:S(2)}, u32[]{:S(2)}) %collective-permute-start.12) | collective-permute-done | bytes 313376 | tf_op jit(solution)/shard_map/ppermute | solution.py:99
  158.2 10.3 %collective-permute-done.13 = bf16[136,1152]{1,0:T(8,128)(2,1)S(1)} collective-permute-done((bf16[136,1152]{1,0:T(8,128)(2,1)S(1)}, bf16[136,1152]{1,0:T(8,128)(2,1)S(1)}, u32[]{:S(2)}, u32[]{:S(2)}) %collective-permute-start.13) | collective-permute-done | bytes 313376 | tf_op jit(solution)/shard_map/ppermute | solution.py:99
  168.5 0.6 collective-permute-done.14
  169.1 0.3 fusion.72
  169.3 3.5 %fusion.59 = f32[544,16]{0,1:T(8,128)S(1)} fusion(bf16[2,1024,1024]{2,1,0:T(8,128)(2,1)} %param.17, f32[1024]{0:T(1024)S(1)} %bitcast.83, bf16[2,1024,16]{1,2,0:T(8,128)(2,1)S(1)} %copy-done.7, pred[544]{0:T(1024)(128)(4,1)S(1)} %get-tuple-element.31, bf16[136,1152]{1,0:T(8,128)(2,1)S(1)} %collective-permute-done.14, ...), kind=kOutput, calls=%fused_computation.62 | convolution fusion | flops 1169826304 | bytes 3423232 | tf_op jit(solution)/shard_map/dot_general | solution.py:179
  172.9 3.5 %fusion.62 = f32[544,16]{0,1:T(8,128)S(1)} fusion(f32[544,16]{0,1:T(8,128)S(1)} %fusion.59, bf16[2,1024,1024]{2,1,0:T(8,128)(2,1)} %param.17, f32[1024]{0:T(1024)S(1)} %bitcast.82, bf16[2,1024,16]{1,2,0:T(8,128)(2,1)S(1)} %copy-done.7, pred[544]{0:T(1024)(128)(4,1)S(1)} %get-tuple-element.30, bf16[136,1152]{1,0:T(8,128)(2,1)S(1)} %collective-permute-done.14, ...), kind=kOutput, calls=%fused_computation.63 | convolution fusion | flops 1169826304 | bytes 3464192 | tf_op jit(solution)/shard_map/dot_general | solution.py:179
  176.4 0.1 fusion.104
  176.5 0.2 collective-permute-start.16
  176.7 0.7 collective-permute-start.17
  177.4 0.3 collective-permute-done.15
  177.7 3.0 %collective-permute-done.16 = f32[136,16]{0,1:T(8,128)S(1)} collective-permute-done((f32[136,16]{0,1:T(8,128)S(1)}, f32[136,16]{0,1:T(8,128)S(1)}, u32[]{:S(2)}, u32[]{:S(2)}) %collective-permute-start.16) | collective-permute-done | bytes 8736 | tf_op jit(solution)/shard_map/ppermute | solution.py:99
  180.7 1.2 collective-permute-done.17
  181.9 0.6 fusion.79
  (41 shorter events, 0.6 us)
Async XLA Ops:
  7.2 140.8 %all-gather.2.cloned.1.call-start = ((), (), s32[]{:S(2)}) async-start(), calls=%async_computation.1 | async-start | bytes 2621440 | tf_op jit(solution)/shard_map/all_gather | solution.py:153
  10.2 10.3 %collective-permute-start = (bf16[136,1024]{1,0:T(8,128)(2,1)S(1)}, bf16[136,1024]{1,0:T(8,128)(2,1)S(1)}, u32[]{:S(2)}, u32[]{:S(2)}) collective-permute-start(bf16[136,1024]{1,0:T(8,128)(2,1)S(1)} %fusion.71), channel_id=1, source_target_pairs={{0,1},{1,2},{2,3},{3,0},{4,5},{5,6},{6,7},{7,4},{8,9},{9,10},{10,1... | collective-permute-start | bytes 835592 | tf_op jit(solution)/shard_map/ppermute | solution.py:99
  14.6 12.2 %collective-permute-start.1 = (bf16[136,1024]{1,0:T(8,128)(2,1)S(1)}, bf16[136,1024]{1,0:T(8,128)(2,1)S(1)}, u32[]{:S(2)}, u32[]{:S(2)}) collective-permute-start(bf16[136,1024]{1,0:T(8,128)(2,1)S(1)} %fusion.71), channel_id=1, source_target_pairs={{0,2},{1,3},{2,0},{3,1},{4,6},{5,7},{6,4},{7,5},{8,10},{9,11},{10,... | collective-permute-start | bytes 835592 | tf_op jit(solution)/shard_map/ppermute | solution.py:99
  14.6 12.8 %collective-permute-start.2 = (bf16[136,1024]{1,0:T(8,128)(2,1)S(1)}, bf16[136,1024]{1,0:T(8,128)(2,1)S(1)}, u32[]{:S(2)}, u32[]{:S(2)}) collective-permute-start(bf16[136,1024]{1,0:T(8,128)(2,1)S(1)} %fusion.71), channel_id=1, source_target_pairs={{0,3},{1,0},{2,1},{3,2},{4,7},{5,4},{6,5},{7,6},{8,11},{9,8},{10,9... | collective-permute-start | bytes 835592 | tf_op jit(solution)/shard_map/ppermute | solution.py:99
  30.5 9.6 %collective-permute-start.3 = (bf16[544,256]{1,0:T(8,128)(2,1)S(1)}, bf16[544,256]{1,0:T(8,128)(2,1)S(1)}, u32[]{:S(2)}, u32[]{:S(2)}) collective-permute-start(bf16[544,256]{1,0:T(8,128)(2,1)S(1)} %get-tuple-element.43), channel_id=1, source_target_pairs={{0,8},{8,16},{16,24},{24,0},{1,9},{9,17},{17,25},{25,1},{2,10},{10... | collective-permute-start | bytes 835592 | tf_op jit(solution)/shard_map/ppermute | solution.py:99
  31.8 15.4 %collective-permute-start.4 = (bf16[544,256]{1,0:T(8,128)(2,1)S(1)}, bf16[544,256]{1,0:T(8,128)(2,1)S(1)}, u32[]{:S(2)}, u32[]{:S(2)}) collective-permute-start(bf16[544,256]{1,0:T(8,128)(2,1)S(1)} %get-tuple-element.42), channel_id=1, source_target_pairs={{0,16},{8,24},{16,0},{24,8},{1,17},{9,25},{17,1},{25,9},{2,18},{10... | collective-permute-start | bytes 835592 | tf_op jit(solution)/shard_map/ppermute | solution.py:99
  34.3 12.9 %collective-permute-start.5 = (bf16[544,256]{1,0:T(8,128)(2,1)S(1)}, bf16[544,256]{1,0:T(8,128)(2,1)S(1)}, u32[]{:S(2)}, u32[]{:S(2)}) collective-permute-start(bf16[544,256]{1,0:T(8,128)(2,1)S(1)} %get-tuple-element.41), channel_id=1, source_target_pairs={{0,24},{8,0},{16,8},{24,16},{1,25},{9,1},{17,9},{25,17},{2,26},{10... | collective-permute-start | bytes 835592 | tf_op jit(solution)/shard_map/ppermute | solution.py:99
  48.6 16.1 %collective-permute-start.6 = (bf16[2176,128]{1,0:T(8,128)(2,1)S(1)}, bf16[2176,128]{1,0:T(8,128)(2,1)S(1)}, u32[]{:S(2)}, u32[]{:S(2)}) collective-permute-start(bf16[2176,128]{1,0:T(8,128)(2,1)S(1)} %get-tuple-element.38), channel_id=1, source_target_pairs={{0,32},{32,64},{64,96},{96,0},{1,33},{33,65},{65,97},{97,1},{2,34}... | collective-permute-start | bytes 1671176 | tf_op jit(solution)/shard_map/ppermute | solution.py:137
  50.2 14.5 %collective-permute-start.7 = (bf16[2176,128]{1,0:T(8,128)(2,1)S(1)}, bf16[2176,128]{1,0:T(8,128)(2,1)S(1)}, u32[]{:S(2)}, u32[]{:S(2)}) collective-permute-start(bf16[2176,128]{1,0:T(8,128)(2,1)S(1)} %get-tuple-element.38), channel_id=1, source_target_pairs={{0,96},{32,0},{64,32},{96,64},{1,97},{33,1},{65,33},{97,65},{2,98}... | collective-permute-start | bytes 1671176 | tf_op jit(solution)/shard_map/ppermute | solution.py:138
  52.3 13.2 %collective-permute-start.8 = (bf16[2176,128]{1,0:T(8,128)(2,1)S(1)}, bf16[2176,128]{1,0:T(8,128)(2,1)S(1)}, u32[]{:S(2)}, u32[]{:S(2)}) collective-permute-start(bf16[2176,128]{1,0:T(8,128)(2,1)S(1)} %get-tuple-element.38), channel_id=1, source_target_pairs={{0,4},{4,0},{1,5},{5,1},{2,6},{6,2},{3,7},{7,3},{8,12},{12,8},{9,1... | collective-permute-start | bytes 1671176 | tf_op jit(solution)/shard_map/ppermute | solution.py:139
  64.7 0.8 copy-start.2
  65.6 26.5 %collective-permute-start.9 = (bf16[2,2176,128]{2,1,0:T(8,128)(2,1)S(1)}, bf16[2,2176,128]{2,1,0:T(8,128)(2,1)S(1)}, u32[]{:S(2)}, u32[]{:S(2)}) collective-permute-start(bf16[2,2176,128]{2,1,0:T(8,128)(2,1)S(1)} %pad_maximum_fusion.8), channel_id=1, source_target_pairs={{0,32},{32,64},{64,96},{96,0},{1,33},{33,65},{65,97},{97,1},{2,34}... | collective-permute-start | bytes 3342344 | tf_op jit(solution)/shard_map/ppermute | solution.py:142
  66.0 26.2 %collective-permute-start.10 = (bf16[2176,128]{1,0:T(8,128)(2,1)S(1)}, bf16[2176,128]{1,0:T(8,128)(2,1)}, u32[]{:S(2)}, u32[]{:S(2)}) collective-permute-start(bf16[2176,128]{1,0:T(8,128)(2,1)S(1)} %collective-permute-done.8), channel_id=1, source_target_pairs={{0,96},{32,0},{64,32},{96,64},{1,97},{33,1},{65,33},{97,65},{2,98}... | collective-permute-start | bytes 1671176 | tf_op jit(solution)/shard_map/ppermute | solution.py:143
  92.2 23.6 %collective-permute-start.11 = (bf16[2176,128]{1,0:T(8,128)(2,1)S(1)}, bf16[2176,128]{1,0:T(8,128)(2,1)S(1)}, u32[]{:S(2)}, u32[]{:S(2)}) collective-permute-start(bf16[2176,128]{1,0:T(8,128)(2,1)S(1)} %get-tuple-element.23), channel_id=1, source_target_pairs={{0,32},{32,64},{64,96},{96,0},{1,33},{33,65},{65,97},{97,1},{2,34}... | collective-permute-start | bytes 1671176 | tf_op jit(solution)/shard_map/ppermute | solution.py:145
  115.8 0.8 copy-start.6
  126.3 9.5 %copy-start.8 = (s32[136,1]{0,1:T(1,128)S(1)}, s32[136,1]{0,1:T(1,128)}, u32[]{:S(2)}) copy-start(s32[136,1]{0,1:T(1,128)} %param.16) | copy-start | bytes 1636
  127.2 20.7 %copy-start = (bf16[136,1024]{1,0:T(8,128)(2,1)S(1)}, bf16[136,1024]{1,0:T(8,128)(2,1)}, u32[]{:S(2)}) copy-start(bf16[136,1024]{1,0:T(8,128)(2,1)} %param.10) | copy-start | bytes 835588
  127.3 20.7 %copy-start.4 = (f32[1024]{0:T(1024)S(1)}, f32[1024]{0:T(1024)}, u32[]{:S(2)}) copy-start(f32[1024]{0:T(1024)} %param.12) | copy-start | bytes 12292
  128.2 18.7 %all-to-all-start = ((bf16[16,136,64]{1,2,0:T(8,128)(2,1)}), bf16[16,136,64]{1,2,0:T(8,128)(2,1)S(1)}, u32[]{:S(2)}, u32[]{:S(2)}) async-start(bf16[16,136,64]{1,2,0:T(8,128)(2,1)} %broadcast_select_fusion), calls=%async_computation | async-start | bytes 1048576 | tf_op jit(solution)/shard_map/all_to_all | solution.py:162
  147.5 2.7 %copy-start.5 = (f32[1024]{0:T(1024)S(1)}, f32[1024]{0:T(1024)}, u32[]{:S(2)}) copy-start(f32[1024]{0:T(1024)} %param.13) | copy-start | bytes 12292
  147.9 6.8 %copy-start.3 = (bf16[2,1024]{1,0:T(2,128)(2,1)S(1)}, bf16[2,1024]{1,0:T(2,128)(2,1)}, u32[]{:S(2)}) copy-start(bf16[2,1024]{1,0:T(2,128)(2,1)} %param.18) | copy-start | bytes 12292
  147.9 21.5 %copy-start.7 = (bf16[2,1024,16]{1,2,0:T(8,128)(2,1)S(1)}, bf16[2,1024,16]{1,2,0:T(8,128)(2,1)}, u32[]{:S(2)}) copy-start(bf16[2,1024,16]{1,2,0:T(8,128)(2,1)} %param.19) | copy-start | bytes 196612
  150.2 22.7 %copy-start.1 = (bf16[136,1024]{1,0:T(8,128)(2,1)}, bf16[136,1024]{1,0:T(8,128)(2,1)S(1)}, u32[]{:S(2)}) copy-start(bf16[136,1024]{1,0:T(8,128)(2,1)S(1)} %get-tuple-element.52) | copy-start | bytes 835588
  150.5 7.7 %collective-permute-start.12 = (bf16[136,1152]{1,0:T(8,128)(2,1)S(1)}, bf16[136,1152]{1,0:T(8,128)(2,1)S(1)}, u32[]{:S(2)}, u32[]{:S(2)}) collective-permute-start(bf16[136,1152]{1,0:T(8,128)(2,1)S(1)} %pad_maximum_fusion.9), channel_id=1, source_target_pairs={{0,1},{1,2},{2,3},{3,0},{4,5},{5,6},{6,7},{7,4},{8,9},{9,10},{10,1... | collective-permute-start | bytes 940040 | tf_op jit(solution)/shard_map/ppermute | solution.py:99
  151.8 16.6 %collective-permute-start.13 = (bf16[136,1152]{1,0:T(8,128)(2,1)S(1)}, bf16[136,1152]{1,0:T(8,128)(2,1)S(1)}, u32[]{:S(2)}, u32[]{:S(2)}) collective-permute-start(bf16[136,1152]{1,0:T(8,128)(2,1)S(1)} %pad_maximum_fusion.9), channel_id=1, source_target_pairs={{0,2},{1,3},{2,0},{3,1},{4,6},{5,7},{6,4},{7,5},{8,10},{9,11},{10,... | collective-permute-start | bytes 940040 | tf_op jit(solution)/shard_map/ppermute | solution.py:99
  154.7 14.4 %collective-permute-start.14 = (bf16[136,1152]{1,0:T(8,128)(2,1)S(1)}, bf16[136,1152]{1,0:T(8,128)(2,1)S(1)}, u32[]{:S(2)}, u32[]{:S(2)}) collective-permute-start(bf16[136,1152]{1,0:T(8,128)(2,1)S(1)} %pad_maximum_fusion.9), channel_id=1, source_target_pairs={{0,3},{1,0},{2,1},{3,2},{4,7},{5,4},{6,5},{7,6},{8,11},{9,8},{10,9... | collective-permute-start | bytes 940040 | tf_op jit(solution)/shard_map/ppermute | solution.py:99
  176.5 1.2 collective-permute-start.15
  176.5 4.2 %collective-permute-start.16 = (f32[136,16]{0,1:T(8,128)S(1)}, f32[136,16]{0,1:T(8,128)S(1)}, u32[]{:S(2)}, u32[]{:S(2)}) collective-permute-start(f32[136,16]{0,1:T(8,128)S(1)} %get-tuple-element.46), channel_id=1, source_target_pairs={{0,2},{1,3},{2,0},{3,1},{4,6},{5,7},{6,4},{7,5},{8,10},{9,11},{10,... | collective-permute-start | bytes 26120 | tf_op jit(solution)/shard_map/ppermute | solution.py:99
  176.7 5.2 %collective-permute-start.17 = (f32[136,16]{0,1:T(8,128)S(1)}, f32[136,16]{0,1:T(8,128)S(1)}, u32[]{:S(2)}, u32[]{:S(2)}) collective-permute-start(f32[136,16]{0,1:T(8,128)S(1)} %get-tuple-element.45), channel_id=1, source_target_pairs={{0,3},{1,0},{2,1},{3,2},{4,7},{5,4},{6,5},{7,6},{8,11},{9,8},{10,9... | collective-permute-start | bytes 26120 | tf_op jit(solution)/shard_map/ppermute | solution.py:99
Sparse Core Ops, SparseCore 0:
  68.8 26.2 all-gather.1
